TPU v7x, 512 devices: a whole 4x8x8 slice. The times are simulated.
512 devices in a mesh: space: 64 (over x, y_hi, z), chan: 8 (over y_lo, core).
Axes of the slice: x: 4, y: 8 (y_hi: 2, y_lo: 4; y = y_hi * 4 + y_lo), z: 8, core: 2. Of those that a mesh axis runs over, the one named last changes fastest.
Arguments:
- activation: float32 [64, 2, 512, 256], P('space', None, 'chan'), may hold values from -6 to 6
- weight: bfloat16 [3, 3, 3, 512, 512], P(None, None, None, 'chan'), may hold values from -0.0546875 to 0.0546875
- conv_bias: float32 [512], P('chan'), may hold values from -3 to 3
Outputs:
- output: float32 [64, 2, 512, 256], P('space', None, 'chan')
All inputs are finite; a program needn't handle non-finite values.
Results may differ from a plain program's by a relative error of at most 0.0026.
Values may be sent and summed in bfloat16 or wider, within the bound.
No kernel may reach another device: no remote copies, remote signals or barrier semaphores. Data moves between devices by JAX's collectives and lax.ppermute only.
A program may use at most 64 MiB of HBM per device.

v0:
```python
import jax
import jax.numpy as jnp
from jax import lax
from jax.sharding import PartitionSpec as P

CY = 8


negative_slope = 0.3


def shifted(value, axis, steps):
    count = lax.axis_size(axis)
    pairs = [(source, (source + steps) % count) for source in range(count)]
    return lax.ppermute(value, axis, pairs)


def haloed(own_block):
    below = shifted(own_block[-1:], "space", 8)
    above = shifted(own_block[:1], "space", -8)
    widened = jnp.concatenate([below, own_block, above], axis=0)
    lower_from = shifted(widened[:, -1:], "space", 1)
    upper_from = shifted(widened[:, :1], "space", -1)
    place_y = (lax.axis_index("space") + 4) % 8
    lower_rim = jnp.where(place_y > 0, lower_from, jnp.zeros_like(lower_from))
    upper_rim = jnp.where(place_y < 7, upper_from, jnp.zeros_like(upper_from))
    return jnp.concatenate([lower_rim, widened, upper_rim], axis=1)


def pad_depth(field):
    return jnp.pad(field, ((0, 0), (0, 0), (1, 1), (0, 0)))


def tap_sum(padded, kernel):
    size_x = padded.shape[0] - 2
    size_y = padded.shape[1] - 2
    size_z = padded.shape[2] - 2
    width_in = padded.shape[3]
    total = None
    for tap_x in range(3):
        for tap_y in range(3):
            columns = jnp.concatenate(
                [
                    padded[
                        tap_x : tap_x + size_x, tap_y : tap_y + size_y, tap_z : tap_z + size_z, :
                    ]
                    for tap_z in range(3)
                ],
                axis=-1,
            )
            columns = columns.reshape(-1, 3 * width_in)
            product = jnp.dot(
                columns,
                kernel[tap_x, tap_y].reshape(3 * width_in, -1),
                preferred_element_type=jnp.float32,
            )
            total = product if total is None else total + product
    return total


def body(activation, weight, conv_bias):
    size_x = activation.shape[1]
    width_in = activation.shape[2]
    size_y = CY
    size_z = activation.shape[3] // size_y
    own_block = (
        activation[0]
        .astype(jnp.bfloat16)
        .reshape(size_x, width_in, size_y, size_z)
        .transpose(0, 2, 3, 1)
    )
    kernel_all = weight.transpose(0, 1, 2, 4, 3)
    width_out = kernel_all.shape[4]
    gathered = lax.all_gather(own_block, "chan", axis=3, tiled=True)
    total = tap_sum(pad_depth(haloed(gathered)), kernel_all)
    before = total + conv_bias[None, :]
    result = jnp.maximum(before, negative_slope * before)
    result = result.reshape(size_x, size_y, size_z, width_out).transpose(0, 3, 1, 2)
    return result.reshape(1, size_x, width_out, size_y * size_z)


def solution(mesh):
    placed = (P("space", None, "chan", None), P(None, None, None, "chan", None), P("chan"))
    return jax.shard_map(
        body, mesh=mesh, in_specs=placed, out_specs=P("space", None, "chan", None), check_vma=False
    )
```

profile of v0, /device:TPU:1, one launch (start us, length us, event | category | flops | bytes accessed | tf_op | source)
XLA Modules:
  0.0 94.0 jit_solution(14746755892564685399)
XLA Ops:
  0.0 1.0 %copy.17 = bf16[1,2,64,256]{2,3,1,0:T(8,128)(2,1)S(1)} copy(f32[1,2,64,256]{3,2,1,0:T(8,128)} %param.3) | data formatting | bytes 196608 | tf_op args[0]
  1.0 0.3 copy.18
  1.3 27.3 %all_gather.3 = bf16[2,8,32,512]{2,1,0,3:T(8,128)(2,1)S(1)} all-gather(bf16[2,8,32,64]{2,1,0,3:T(8,128)(2,1)S(1)} %copy.18), channel_id=1, replica_groups=mesh['space'=64,'chan'=8] {'chan'}, dimensions={3}, use_global_device_ids=true | all-gather | bytes 589824 | tf_op jit(solution)/shard_map/all_gather | solution.py:74
  28.6 1.6 %copy.19 = bf16[2,8,32,512]{3,2,1,0:T(8,128)(2,1)S(1)} copy(bf16[2,8,32,512]{2,1,0,3:T(8,128)(2,1)S(1)} %all_gather.3) | data formatting | bytes 1048576 | tf_op jit(solution)/shard_map/all_gather | solution.py:74
  30.3 0.0 copy-start
  30.3 3.9 %collective-permute-start = (bf16[1,8,32,512]{3,2,1,0:T(8,128)(2,1)S(1)}, bf16[1,8,32,512]{3,2,1,0:T(8,128)(2,1)S(1)}, u32[]{:S(2)}, u32[]{:S(2)}) collective-permute-start(bf16[1,8,32,512]{3,2,1,0:T(8,128)(2,1)S(1)} %get-tuple-element.45), channel_id=1, source_target_pairs={{0,64},{8,72},{16,80},{24,88},{32,96},{40,104},{48,112},{56,120},{... | collective-permute-start | bytes 786440 | tf_op jit(solution)/shard_map/ppermute | solution.py:15
  34.2 7.5 %collective-permute-start.1 = (bf16[1,8,32,512]{3,2,1,0:T(8,128)(2,1)S(1)}, bf16[1,8,32,512]{3,2,1,0:T(8,128)(2,1)S(1)}, u32[]{:S(2)}, u32[]{:S(2)}) collective-permute-start(bf16[1,8,32,512]{3,2,1,0:T(8,128)(2,1)S(1)} %get-tuple-element.46), channel_id=1, source_target_pairs={{0,448},{8,456},{16,464},{24,472},{32,480},{40,488},{48,496},{56,5... | collective-permute-start | bytes 786440 | tf_op jit(solution)/shard_map/ppermute | solution.py:15
  41.7 12.2 %collective-permute-done = bf16[1,8,32,512]{3,2,1,0:T(8,128)(2,1)S(1)} collective-permute-done((bf16[1,8,32,512]{3,2,1,0:T(8,128)(2,1)S(1)}, bf16[1,8,32,512]{3,2,1,0:T(8,128)(2,1)S(1)}, u32[]{:S(2)}, u32[]{:S(2)}) %collective-permute-start) | collective-permute-done | bytes 262176 | tf_op jit(solution)/shard_map/ppermute | solution.py:15
  54.0 5.5 %collective-permute-done.1 = bf16[1,8,32,512]{3,2,1,0:T(8,128)(2,1)S(1)} collective-permute-done((bf16[1,8,32,512]{3,2,1,0:T(8,128)(2,1)S(1)}, bf16[1,8,32,512]{3,2,1,0:T(8,128)(2,1)S(1)}, u32[]{:S(2)}, u32[]{:S(2)}) %collective-permute-start.1) | collective-permute-done | bytes 262176 | tf_op jit(solution)/shard_map/ppermute | solution.py:15
  59.5 4.0 %collective-permute-start.2 = (bf16[4,1,32,512]{3,2,1,0:T(8,128)(2,1)S(1)}, bf16[4,1,32,512]{3,2,1,0:T(8,128)(2,1)S(1)}, u32[]{:S(2)}, u32[]{:S(2)}) collective-permute-start(bf16[4,1,32,512]{3,2,1,0:T(8,128)(2,1)S(1)} %get-tuple-element.40), channel_id=1, source_target_pairs={{0,8},{8,16},{16,24},{24,32},{32,40},{40,48},{48,56},{56,64},{64,7... | collective-permute-start | bytes 393224 | tf_op jit(solution)/shard_map/ppermute | solution.py:15
  63.5 0.0 copy-done
  63.5 0.1 fusion.12
  63.7 0.2 copy.24
  63.9 0.2 copy.22
  64.1 0.2 copy.25
  64.4 0.2 copy.26
  64.6 0.2 copy.28
  64.8 0.2 copy.29
  65.1 0.2 copy.30
  65.3 0.2 copy.33
  65.5 0.2 copy.32
  65.8 13.8 %collective-permute-start.3 = (bf16[4,1,32,512]{3,2,1,0:T(8,128)(2,1)S(1)}, bf16[4,1,32,512]{3,2,1,0:T(8,128)(2,1)S(1)}, u32[]{:S(2)}, u32[]{:S(2)}) collective-permute-start(bf16[4,1,32,512]{3,2,1,0:T(8,128)(2,1)S(1)} %get-tuple-element.41), channel_id=1, source_target_pairs={{0,504},{8,0},{16,8},{24,16},{32,24},{40,32},{48,40},{56,48},{64,5... | collective-permute-start | bytes 393224 | tf_op jit(solution)/shard_map/ppermute | solution.py:15
  79.5 0.7 collective-permute-done.2
  80.2 1.2 %collective-permute-done.3 = bf16[4,1,32,512]{3,2,1,0:T(8,128)(2,1)S(1)} collective-permute-done((bf16[4,1,32,512]{3,2,1,0:T(8,128)(2,1)S(1)}, bf16[4,1,32,512]{3,2,1,0:T(8,128)(2,1)S(1)}, u32[]{:S(2)}, u32[]{:S(2)}) %collective-permute-start.3) | collective-permute-done | bytes 131104 | tf_op jit(solution)/shard_map/ppermute | solution.py:15
  81.5 0.2 maximum_maximum_fusion
  81.7 0.2 fusion.14
  81.9 0.2 fusion.15
  82.0 1.0 %select_maximum_fusion = bf16[4,10,34,512]{3,2,1,0:T(8,128)(2,1)S(1)} fusion(bf16[4,1,32,512]{3,2,1,0:T(8,128)(2,1)S(1)} %broadcast_select_fusion, bf16[4,1,32,512]{3,2,1,0:T(8,128)(2,1)S(1)} %broadcast_select_fusion.1, bf16[1,8,32,512]{3,2,1,0:T(8,128)(2,1)S(1)} %collective-permute-done.1, bf16[2,8,32,512]{3,2,1,0:T(8,128)(2,1)S(1)} %copy.19, ...), kind=kLoop, calls=%fused_computation.3 | loop fusion | flops 12533760 | bytes 2703360 | tf_op jit(solution)/shard_map/concatenate | solution.py:27
  83.0 3.2 %fusion.13 = (bf16[2,8,32,512]{3,2,1,0:T(8,128)(2,1)S(1)}, bf16[2,8,32,512]{3,2,1,0:T(8,128)(2,1)S(1)}, bf16[2,8,32,512]{3,2,1,0:T(8,128)(2,1)S(1)}, bf16[2,8,32...) fusion(bf16[4,10,34,512]{3,2,1,0:T(8,128)(2,1)S(1)} %select_max, ...), kind=kLoop, calls=%fused_computation.41 | loop fusion | bytes 18874368 | tf_op jit(solution)/shard_map/slice | solution.py:44
  86.2 0.5 fusion.7
  86.7 0.6 fusion.17
  87.3 0.3 pad_maximum_fusion.7
  87.6 0.6 fusion.18
  88.2 0.3 pad_maximum_fusion.2
  88.5 0.6 convolution_add_fusion.6
  89.1 0.6 convolution_add_fusion.5
  89.7 0.3 pad_maximum_fusion.4
  90.0 0.6 convolution_add_fusion.4
  90.6 0.6 convolution_add_fusion.3
  91.2 0.0 copy-start.1
  91.2 0.6 convolution_add_fusion.2
  91.8 0.6 convolution_add_fusion.1
  92.4 0.0 copy-done.1
  92.5 0.6 multiply_maximum_fusion
  93.1 0.1 copy.34
  93.2 0.8 copy.35
  (13 shorter events, 0.5 us)
Async XLA Ops:
  30.3 33.3 %copy-start = (bf16[3,3,3,64,512]{4,3,2,1,0:T(8,128)(2,1)S(1)}, bf16[3,3,3,64,512]{4,3,2,1,0:T(8,128)(2,1)}, u32[]{:S(2)}) copy-start(bf16[3,3,3,64,512]{4,3,2,1,0:T(8,128)(2,1)} %param.4) | copy-start | bytes 5308420
  30.3 23.7 %collective-permute-start = (bf16[1,8,32,512]{3,2,1,0:T(8,128)(2,1)S(1)}, bf16[1,8,32,512]{3,2,1,0:T(8,128)(2,1)S(1)}, u32[]{:S(2)}, u32[]{:S(2)}) collective-permute-start(bf16[1,8,32,512]{3,2,1,0:T(8,128)(2,1)S(1)} %get-tuple-element.45), channel_id=1, source_target_pairs={{0,64},{8,72},{16,80},{24,88},{32,96},{40,104},{48,112},{56,120},{... | collective-permute-start | bytes 786440 | tf_op jit(solution)/shard_map/ppermute | solution.py:15
  34.2 25.3 %collective-permute-start.1 = (bf16[1,8,32,512]{3,2,1,0:T(8,128)(2,1)S(1)}, bf16[1,8,32,512]{3,2,1,0:T(8,128)(2,1)S(1)}, u32[]{:S(2)}, u32[]{:S(2)}) collective-permute-start(bf16[1,8,32,512]{3,2,1,0:T(8,128)(2,1)S(1)} %get-tuple-element.46), channel_id=1, source_target_pairs={{0,448},{8,456},{16,464},{24,472},{32,480},{40,488},{48,496},{56,5... | collective-permute-start | bytes 786440 | tf_op jit(solution)/shard_map/ppermute | solution.py:15
  59.5 20.7 %collective-permute-start.2 = (bf16[4,1,32,512]{3,2,1,0:T(8,128)(2,1)S(1)}, bf16[4,1,32,512]{3,2,1,0:T(8,128)(2,1)S(1)}, u32[]{:S(2)}, u32[]{:S(2)}) collective-permute-start(bf16[4,1,32,512]{3,2,1,0:T(8,128)(2,1)S(1)} %get-tuple-element.40), channel_id=1, source_target_pairs={{0,8},{8,16},{16,24},{24,32},{32,40},{40,48},{48,56},{56,64},{64,7... | collective-permute-start | bytes 393224 | tf_op jit(solution)/shard_map/ppermute | solution.py:15
  65.8 15.7 %collective-permute-start.3 = (bf16[4,1,32,512]{3,2,1,0:T(8,128)(2,1)S(1)}, bf16[4,1,32,512]{3,2,1,0:T(8,128)(2,1)S(1)}, u32[]{:S(2)}, u32[]{:S(2)}) collective-permute-start(bf16[4,1,32,512]{3,2,1,0:T(8,128)(2,1)S(1)} %get-tuple-element.41), channel_id=1, source_target_pairs={{0,504},{8,0},{16,8},{24,16},{32,24},{40,32},{48,40},{56,48},{64,5... | collective-permute-start | bytes 393224 | tf_op jit(solution)/shard_map/ppermute | solution.py:15
  91.2 1.2 %copy-start.1 = (f32[64]{0:T(128)S(1)}, f32[64]{0:T(128)}, u32[]{:S(2)}) copy-start(f32[64]{0:T(128)} %param.5) | copy-start | bytes 772
where the time goes:
time: 94.7 us; the launch traced here: 94 us
  starting transfers between devices  29.2 us (31%)
  blocking collectives  27.3 us (29%)
  waiting for transfers between devices  19.6 us (21%)
  local copies, waits for them, and re-layouts  9.53 us (10%)
  matrix products  5.38 us (6%)
  other arithmetic  2.59 us (3%)
    ppermute x4, starting transfers between devices, shifted(): return lax.ppermute(value, axis, pairs)  29.2 us
    all_gather x1, blocking collectives, body(): gathered = lax.all_gather(own_block, 'chan', axis=3, tiled=True)  27.3 us
    ppermute x4, waiting for transfers between devices, shifted(): return lax.ppermute(value, axis, pairs)  19.6 us
    dot_general x9, matrix products, tap_sum(): jnp.dot(columns, kernel[tap_x, tap_y].reshape(3 * width_in, -1), preferre...  5.38 us
    slice x3, local copies, waits for them, and re-layouts, tap_sum(): padded[tap_x:tap_x + size_x, tap_y:tap_y + size_y, tap_z:tap_z + size_z, :]  3.58 us
  transfers between devices with their start and end apart: 4, of which 4 were waited for; matrix products, arithmetic and copies ran while one was open for 2% of the time, Pallas kernels for 0%

commit v1 on v0

--- a/solution.py
+++ b/solution.py
@@ -16,14 +16,21 @@
 
 
 def haloed(own_block):
-    below = shifted(own_block[-1:], "space", 8)
-    above = shifted(own_block[:1], "space", -8)
-    widened = jnp.concatenate([below, own_block, above], axis=0)
-    lower_from = shifted(widened[:, -1:], "space", 1)
-    upper_from = shifted(widened[:, :1], "space", -1)
+    stride_x = CY
+    x_lo = shifted(own_block[-1:], "space", stride_x)
+    x_hi = shifted(own_block[:1], "space", -stride_x)
+    y_lo = shifted(own_block[:, -1:], "space", 1)
+    y_hi = shifted(own_block[:, :1], "space", -1)
+    c_ll = shifted(own_block[-1:, -1:], "space", stride_x + 1)
+    c_lh = shifted(own_block[-1:, :1], "space", stride_x - 1)
+    c_hl = shifted(own_block[:1, -1:], "space", 1 - stride_x)
+    c_hh = shifted(own_block[:1, :1], "space", -stride_x - 1)
+    lower_rim = jnp.concatenate([c_ll, y_lo, c_hl], axis=0)
+    upper_rim = jnp.concatenate([c_lh, y_hi, c_hh], axis=0)
     place_y = (lax.axis_index("space") + 4) % 8
-    lower_rim = jnp.where(place_y > 0, lower_from, jnp.zeros_like(lower_from))
-    upper_rim = jnp.where(place_y < 7, upper_from, jnp.zeros_like(upper_from))
+    lower_rim = jnp.where(place_y > 0, lower_rim, jnp.zeros_like(lower_rim))
+    upper_rim = jnp.where(place_y < 7, upper_rim, jnp.zeros_like(upper_rim))
+    widened = jnp.concatenate([x_lo, own_block, x_hi], axis=0)
     return jnp.concatenate([lower_rim, widened, upper_rim], axis=1)
 
 

time: 94.7 us -> 98 us (1.035)
  starting transfers between devices: 29.2 us -> 45.7 us
  waiting for transfers between devices: 19.6 us -> 3.6 us
  local copies, waits for them, and re-layouts: 9.53 us -> 11.8 us
    ppermute x4 -> x8, starting transfers between devices: 29.2 us -> 45.7 us  [shifted(): return lax.ppermute(value, axis, pairs)]
    ppermute x4 -> x8, waiting for transfers between devices: 19.6 us -> 3.6 us  [shifted(): return lax.ppermute(value, axis, pairs)]
    slice x10, local copies, waits for them, and re-layouts: 1.66 us -> 3.21 us  [tap_sum(): kernel[tap_x, tap_y].reshape(3 * width_in, -1)]
  transfers between devices with their start and end apart: 4 -> 8, of which waited for: 4 -> 1; matrix products, arithmetic and copies ran while one was open for 2% -> 5% of each run, Pallas kernels for 0% -> 0%
where the time goes in v1:
time: 98 us; the launch traced here: 97.6 us
  starting transfers between devices  45.7 us (47%)
  blocking collectives  27.3 us (28%)
  local copies, waits for them, and re-layouts  11.8 us (12%)
  matrix products  5.39 us (6%)
  waiting for transfers between devices  3.6 us (4%)
  other arithmetic  3.35 us (3%)
    ppermute x8, starting transfers between devices, shifted(): return lax.ppermute(value, axis, pairs)  45.7 us
    all_gather x1, blocking collectives, body(): gathered = lax.all_gather(own_block, 'chan', axis=3, tiled=True)  27.3 us
    dot_general x9, matrix products, tap_sum(): jnp.dot(columns, kernel[tap_x, tap_y].reshape(3 * width_in, -1), preferre...  5.39 us
    ppermute x8, waiting for transfers between devices, shifted(): return lax.ppermute(value, axis, pairs)  3.6 us
    slice x3, local copies, waits for them, and re-layouts, tap_sum(): padded[tap_x:tap_x + size_x, tap_y:tap_y + size_y, tap_z:tap_z + size_z, :]  3.58 us
    slice x10, local copies, waits for them, and re-layouts, tap_sum(): kernel[tap_x, tap_y].reshape(3 * width_in, -1)  3.21 us
  transfers between devices with their start and end apart: 8, of which 1 were waited for; matrix products, arithmetic and copies ran while one was open for 5% of the time, Pallas kernels for 0%

profile of v1, /device:TPU:1, one launch (start us, length us, event | category | flops | bytes accessed | tf_op | source)
XLA Modules:
  0.0 97.6 jit_solution(18041078308598012967)
XLA Ops:
  0.0 1.0 %copy.17 = bf16[1,2,64,256]{2,3,1,0:T(8,128)(2,1)S(1)} copy(f32[1,2,64,256]{3,2,1,0:T(8,128)} %param.3) | data formatting | bytes 196608 | tf_op args[0]
  1.0 0.3 copy.18
  1.3 27.3 %all_gather.3 = bf16[2,8,32,512]{2,1,0,3:T(8,128)(2,1)S(1)} all-gather(bf16[2,8,32,64]{2,1,0,3:T(8,128)(2,1)S(1)} %copy.18), channel_id=1, replica_groups=mesh['space'=64,'chan'=8] {'chan'}, dimensions={3}, use_global_device_ids=true | all-gather | bytes 589824 | tf_op jit(solution)/shard_map/all_gather | solution.py:81
  28.6 1.6 %copy.19 = bf16[2,8,32,512]{3,2,1,0:T(8,128)(2,1)S(1)} copy(bf16[2,8,32,512]{2,1,0,3:T(8,128)(2,1)S(1)} %all_gather.3) | data formatting | bytes 1048576 | tf_op jit(solution)/shard_map/all_gather | solution.py:81
  30.3 0.7 fusion.17
  30.9 5.6 %collective-permute-start = (bf16[1,1,32,512]{3,2,1,0:T(8,128)(2,1)}, bf16[1,1,32,512]{3,2,1,0:T(8,128)(2,1)}, u32[]{:S(2)}, u32[]{:S(2)}) collective-permute-start(bf16[1,1,32,512]{3,2,1,0:T(8,128)(2,1)} %get-tuple-element.45), channel_id=1, source_target_pairs={{0,72},{8,80},{16,88},{24,96},{32,104},{40,112},{48,120},{56,128},... | collective-permute-start | bytes 98312 | tf_op jit(solution)/shard_map/ppermute | solution.py:15
  36.5 7.0 %collective-permute-start.2 = (bf16[1,1,32,512]{3,2,1,0:T(8,128)(2,1)}, bf16[1,1,32,512]{3,2,1,0:T(8,128)(2,1)}, u32[]{:S(2)}, u32[]{:S(2)}) collective-permute-start(bf16[1,1,32,512]{3,2,1,0:T(8,128)(2,1)} %get-tuple-element.48), channel_id=1, source_target_pairs={{0,456},{8,464},{16,472},{24,480},{32,488},{40,496},{48,504},{56,0... | collective-permute-start | bytes 98312 | tf_op jit(solution)/shard_map/ppermute | solution.py:15
  43.5 4.0 %collective-permute-start.1 = (bf16[2,1,32,512]{3,2,1,0:T(8,128)(2,1)S(1)}, bf16[2,1,32,512]{3,2,1,0:T(8,128)(2,1)S(1)}, u32[]{:S(2)}, u32[]{:S(2)}) collective-permute-start(bf16[2,1,32,512]{3,2,1,0:T(8,128)(2,1)S(1)} %get-tuple-element.49), channel_id=1, source_target_pairs={{0,8},{8,16},{16,24},{24,32},{32,40},{40,48},{48,56},{56,64},{64,7... | collective-permute-start | bytes 196616 | tf_op jit(solution)/shard_map/ppermute | solution.py:15
  47.6 4.0 %collective-permute-start.3 = (bf16[1,8,32,512]{3,2,1,0:T(8,128)(2,1)S(1)}, bf16[1,8,32,512]{3,2,1,0:T(8,128)(2,1)S(1)}, u32[]{:S(2)}, u32[]{:S(2)}) collective-permute-start(bf16[1,8,32,512]{3,2,1,0:T(8,128)(2,1)S(1)} %get-tuple-element.43), channel_id=1, source_target_pairs={{0,64},{8,72},{16,80},{24,88},{32,96},{40,104},{48,112},{56,120},{... | collective-permute-start | bytes 786440 | tf_op jit(solution)/shard_map/ppermute | solution.py:15
  51.6 7.3 %collective-permute-start.4 = (bf16[1,8,32,512]{3,2,1,0:T(8,128)(2,1)S(1)}, bf16[1,8,32,512]{3,2,1,0:T(8,128)(2,1)S(1)}, u32[]{:S(2)}, u32[]{:S(2)}) collective-permute-start(bf16[1,8,32,512]{3,2,1,0:T(8,128)(2,1)S(1)} %get-tuple-element.44), channel_id=1, source_target_pairs={{0,448},{8,456},{16,464},{24,472},{32,480},{40,488},{48,496},{56,5... | collective-permute-start | bytes 786440 | tf_op jit(solution)/shard_map/ppermute | solution.py:15
  58.9 1.7 %fusion.12 = (bf16[1,1,3,512,64]{3,4,2,1,0:T(8,128)(2,1)S(1)}, bf16[1,1,3,512,64]{3,4,2,1,0:T(8,128)(2,1)S(1)}, bf16[1,1,3,512,64]{3,4,2,1,0:T(8,128)(2,1)S(1)},...) fusion(bf16[3,3,3,512,64]{3,4,2,1,0:T(8,128)(2,1)} %bitcast.90), kind=kLoop, calls=%fused_computation.37 | loop fusion | bytes 3538944 | tf_op jit(solution)/shard_map/slice | solution.py:61
  60.6 0.2 copy.30
  60.8 0.2 copy.28
  61.1 0.2 copy.31
  61.3 0.2 copy.32
  61.5 0.2 copy.34
  61.8 0.2 copy.35
  61.9 0.0 copy-start.1
  62.0 0.0 copy-start
  62.0 0.2 copy.36
  62.3 0.2 copy.39
  62.5 0.2 copy.38
  62.7 0.0 collective-permute-done
  62.7 0.0 copy-done.1
  62.7 4.3 %collective-permute-start.5 = (bf16[1,1,32,512]{3,2,1,0:T(8,128)(2,1)S(1)}, bf16[1,1,32,512]{3,2,1,0:T(8,128)(2,1)S(1)}, u32[]{:S(2)}, u32[]{:S(2)}) collective-permute-start(bf16[1,1,32,512]{3,2,1,0:T(8,128)(2,1)S(1)} %copy-done.1), channel_id=1, source_target_pairs={{0,56},{8,64},{16,72},{24,80},{32,88},{40,96},{48,104},{56,112},{6... | collective-permute-start | bytes 98312 | tf_op jit(solution)/shard_map/ppermute | solution.py:15
  67.0 0.0 collective-permute-done.2
  67.0 0.0 copy-done
  67.0 2.9 %collective-permute-start.7 = (bf16[1,1,32,512]{3,2,1,0:T(8,128)(2,1)S(1)}, bf16[1,1,32,512]{3,2,1,0:T(8,128)(2,1)S(1)}, u32[]{:S(2)}, u32[]{:S(2)}) collective-permute-start(bf16[1,1,32,512]{3,2,1,0:T(8,128)(2,1)S(1)} %copy-done), channel_id=1, source_target_pairs={{0,440},{8,448},{16,456},{24,464},{32,472},{40,480},{48,488},{56,4... | collective-permute-start | bytes 98312 | tf_op jit(solution)/shard_map/ppermute | solution.py:15
  69.9 0.0 collective-permute-done.1
  69.9 10.7 %collective-permute-start.6 = (bf16[2,1,32,512]{3,2,1,0:T(8,128)(2,1)S(1)}, bf16[2,1,32,512]{3,2,1,0:T(8,128)(2,1)S(1)}, u32[]{:S(2)}, u32[]{:S(2)}) collective-permute-start(bf16[2,1,32,512]{3,2,1,0:T(8,128)(2,1)S(1)} %get-tuple-element.50), channel_id=1, source_target_pairs={{0,504},{8,0},{16,8},{24,16},{32,24},{40,32},{48,40},{56,48},{64,5... | collective-permute-start | bytes 196616 | tf_op jit(solution)/shard_map/ppermute | solution.py:15
  80.6 0.8 maximum_select_fusion
  81.4 3.6 %collective-permute-done.5 = bf16[1,1,32,512]{3,2,1,0:T(8,128)(2,1)S(1)} collective-permute-done((bf16[1,1,32,512]{3,2,1,0:T(8,128)(2,1)S(1)}, bf16[1,1,32,512]{3,2,1,0:T(8,128)(2,1)S(1)}, u32[]{:S(2)}, u32[]{:S(2)}) %collective-permute-start.5) | collective-permute-done | bytes 32800 | tf_op jit(solution)/shard_map/ppermute | solution.py:15
  85.0 0.0 collective-permute-done.7
  85.0 0.0 collective-permute-done.6
  85.0 0.0 collective-permute-done.3
  85.0 0.0 collective-permute-done.4
  85.0 0.2 maximum_maximum_fusion
  85.3 0.2 fusion.14
  85.4 0.2 fusion.15
  85.6 1.0 select_maximum_fusion
  86.6 3.2 %fusion.13 = (bf16[2,8,32,512]{3,2,1,0:T(8,128)(2,1)S(1)}, bf16[2,8,32,512]{3,2,1,0:T(8,128)(2,1)S(1)}, bf16[2,8,32,512]{3,2,1,0:T(8,128)(2,1)S(1)}, bf16[2,8,32...) fusion(bf16[4,10,34,512]{3,2,1,0:T(8,128)(2,1)S(1)} %select_max, ...), kind=kLoop, calls=%fused_computation.38 | loop fusion | bytes 18874368 | tf_op jit(solution)/shard_map/slice | solution.py:51
  89.8 0.5 fusion.7
  90.3 0.6 fusion.19
  90.9 0.3 pad_maximum_fusion.7
  91.2 0.6 fusion.20
  91.8 0.3 pad_maximum_fusion.2
  92.1 0.6 convolution_add_fusion.6
  92.7 0.6 convolution_add_fusion.5
  93.3 0.3 pad_maximum_fusion.4
  93.6 0.6 convolution_add_fusion.4
  94.2 0.6 convolution_add_fusion.3
  94.8 0.0 copy-start.2
  94.8 0.6 convolution_add_fusion.2
  95.4 0.6 convolution_add_fusion.1
  96.0 0.0 copy-done.2
  96.0 0.6 multiply_maximum_fusion
  96.7 0.1 copy.40
  96.8 0.8 copy.41
  (12 shorter events, 0.5 us)
Async XLA Ops:
  30.9 31.8 %collective-permute-start = (bf16[1,1,32,512]{3,2,1,0:T(8,128)(2,1)}, bf16[1,1,32,512]{3,2,1,0:T(8,128)(2,1)}, u32[]{:S(2)}, u32[]{:S(2)}) collective-permute-start(bf16[1,1,32,512]{3,2,1,0:T(8,128)(2,1)} %get-tuple-element.45), channel_id=1, source_target_pairs={{0,72},{8,80},{16,88},{24,96},{32,104},{40,112},{48,120},{56,128},... | collective-permute-start | bytes 98312 | tf_op jit(solution)/shard_map/ppermute | solution.py:15
  36.5 30.5 %collective-permute-start.2 = (bf16[1,1,32,512]{3,2,1,0:T(8,128)(2,1)}, bf16[1,1,32,512]{3,2,1,0:T(8,128)(2,1)}, u32[]{:S(2)}, u32[]{:S(2)}) collective-permute-start(bf16[1,1,32,512]{3,2,1,0:T(8,128)(2,1)} %get-tuple-element.48), channel_id=1, source_target_pairs={{0,456},{8,464},{16,472},{24,480},{32,488},{40,496},{48,504},{56,0... | collective-permute-start | bytes 98312 | tf_op jit(solution)/shard_map/ppermute | solution.py:15
  43.5 26.4 %collective-permute-start.1 = (bf16[2,1,32,512]{3,2,1,0:T(8,128)(2,1)S(1)}, bf16[2,1,32,512]{3,2,1,0:T(8,128)(2,1)S(1)}, u32[]{:S(2)}, u32[]{:S(2)}) collective-permute-start(bf16[2,1,32,512]{3,2,1,0:T(8,128)(2,1)S(1)} %get-tuple-element.49), channel_id=1, source_target_pairs={{0,8},{8,16},{16,24},{24,32},{32,40},{40,48},{48,56},{56,64},{64,7... | collective-permute-start | bytes 196616 | tf_op jit(solution)/shard_map/ppermute | solution.py:15
  47.6 37.4 %collective-permute-start.3 = (bf16[1,8,32,512]{3,2,1,0:T(8,128)(2,1)S(1)}, bf16[1,8,32,512]{3,2,1,0:T(8,128)(2,1)S(1)}, u32[]{:S(2)}, u32[]{:S(2)}) collective-permute-start(bf16[1,8,32,512]{3,2,1,0:T(8,128)(2,1)S(1)} %get-tuple-element.43), channel_id=1, source_target_pairs={{0,64},{8,72},{16,80},{24,88},{32,96},{40,104},{48,112},{56,120},{... | collective-permute-start | bytes 786440 | tf_op jit(solution)/shard_map/ppermute | solution.py:15
  51.6 33.5 %collective-permute-start.4 = (bf16[1,8,32,512]{3,2,1,0:T(8,128)(2,1)S(1)}, bf16[1,8,32,512]{3,2,1,0:T(8,128)(2,1)S(1)}, u32[]{:S(2)}, u32[]{:S(2)}) collective-permute-start(bf16[1,8,32,512]{3,2,1,0:T(8,128)(2,1)S(1)} %get-tuple-element.44), channel_id=1, source_target_pairs={{0,448},{8,456},{16,464},{24,472},{32,480},{40,488},{48,496},{56,5... | collective-permute-start | bytes 786440 | tf_op jit(solution)/shard_map/ppermute | solution.py:15
  61.9 0.8 copy-start.1
  62.0 5.1 %copy-start = (bf16[1,1,32,512]{3,2,1,0:T(8,128)(2,1)S(1)}, bf16[1,1,32,512]{3,2,1,0:T(8,128)(2,1)}, u32[]{:S(2)}) copy-start(bf16[1,1,32,512]{3,2,1,0:T(8,128)(2,1)} %get-tuple-element.46) | copy-start | bytes 98308
  62.7 22.3 %collective-permute-start.5 = (bf16[1,1,32,512]{3,2,1,0:T(8,128)(2,1)S(1)}, bf16[1,1,32,512]{3,2,1,0:T(8,128)(2,1)S(1)}, u32[]{:S(2)}, u32[]{:S(2)}) collective-permute-start(bf16[1,1,32,512]{3,2,1,0:T(8,128)(2,1)S(1)} %copy-done.1), channel_id=1, source_target_pairs={{0,56},{8,64},{16,72},{24,80},{32,88},{40,96},{48,104},{56,112},{6... | collective-permute-start | bytes 98312 | tf_op jit(solution)/shard_map/ppermute | solution.py:15
  67.0 18.0 %collective-permute-start.7 = (bf16[1,1,32,512]{3,2,1,0:T(8,128)(2,1)S(1)}, bf16[1,1,32,512]{3,2,1,0:T(8,128)(2,1)S(1)}, u32[]{:S(2)}, u32[]{:S(2)}) collective-permute-start(bf16[1,1,32,512]{3,2,1,0:T(8,128)(2,1)S(1)} %copy-done), channel_id=1, source_target_pairs={{0,440},{8,448},{16,456},{24,464},{32,472},{40,480},{48,488},{56,4... | collective-permute-start | bytes 98312 | tf_op jit(solution)/shard_map/ppermute | solution.py:15
  69.9 15.1 %collective-permute-start.6 = (bf16[2,1,32,512]{3,2,1,0:T(8,128)(2,1)S(1)}, bf16[2,1,32,512]{3,2,1,0:T(8,128)(2,1)S(1)}, u32[]{:S(2)}, u32[]{:S(2)}) collective-permute-start(bf16[2,1,32,512]{3,2,1,0:T(8,128)(2,1)S(1)} %get-tuple-element.50), channel_id=1, source_target_pairs={{0,504},{8,0},{16,8},{24,16},{32,24},{40,32},{48,40},{56,48},{64,5... | collective-permute-start | bytes 196616 | tf_op jit(solution)/shard_map/ppermute | solution.py:15
  94.8 1.2 %copy-start.2 = (f32[64]{0:T(128)S(1)}, f32[64]{0:T(128)}, u32[]{:S(2)}) copy-start(f32[64]{0:T(128)} %param.5) | copy-start | bytes 772

commit v2 on v0

--- a/solution.py
+++ b/solution.py
@@ -71,8 +71,8 @@
     )
     kernel_all = weight.transpose(0, 1, 2, 4, 3)
     width_out = kernel_all.shape[4]
-    gathered = lax.all_gather(own_block, "chan", axis=3, tiled=True)
-    total = tap_sum(pad_depth(haloed(gathered)), kernel_all)
+    gathered = lax.all_gather(haloed(own_block), "chan", axis=3, tiled=True)
+    total = tap_sum(pad_depth(gathered), kernel_all)
     before = total + conv_bias[None, :]
     result = jnp.maximum(before, negative_slope * before)
     result = result.reshape(size_x, size_y, size_z, width_out).transpose(0, 3, 1, 2)

time: 94.7 us -> 142 us (1.50)
  waiting for transfers between devices: 19.6 us -> 78 us
  blocking collectives: 27.3 us -> 0 us
  between operations: 0.34 us -> 13.7 us
  local copies, waits for them, and re-layouts: 9.53 us -> 17.9 us
  starting transfers between devices: 29.2 us -> 24.1 us
    all_gather x0 -> x1, waiting for transfers between devices: none -> 56.6 us  [body(): gathered = lax.all_gather(haloed(own_block), 'chan', axis=3, tiled=True)]
    all_gather x1 -> x0, blocking collectives: 27.3 us -> none  [body(): gathered = lax.all_gather(own_block, 'chan', axis=3, tiled=True)]
    ppermute x4, starting transfers between devices: 29.2 us -> 24.1 us  [shifted(): return lax.ppermute(value, axis, pairs)]
    all_gather x1, local copies, waits for them, and re-layouts: 1.63 us -> 6.18 us  [body(): gathered = lax.all_gather(haloed(own_block), 'chan', axis=3, tiled=True)]
    slice x3 -> x2, local copies, waits for them, and re-layouts: 3.58 us -> 5.91 us  [tap_sum(): padded[tap_x:tap_x + size_x, tap_y:tap_y + size_y, tap_z:tap_z + size_z, :]]
    ppermute x4, waiting for transfers between devices: 19.6 us -> 21.4 us  [shifted(): return lax.ppermute(value, axis, pairs)]
  transfers between devices with their start and end apart: 4 -> 5, of which waited for: 4 -> 3; matrix products, arithmetic and copies ran while one was open for 2% -> 2% of each run, Pallas kernels for 0% -> 0%
where the time goes in v2:
time: 142 us; the launch traced here: 141 us
  waiting for transfers between devices  78 us (55%)
  starting transfers between devices  24.1 us (17%)
  local copies, waits for them, and re-layouts  17.9 us (13%)
  between operations  13.7 us (10%)
  matrix products  5.35 us (4%)
  other arithmetic  1.61 us (1%)
    all_gather x1, waiting for transfers between devices, body(): gathered = lax.all_gather(haloed(own_block), 'chan', axis=3, tiled=True)  56.6 us
    ppermute x4, starting transfers between devices, shifted(): return lax.ppermute(value, axis, pairs)  24.1 us
    ppermute x4, waiting for transfers between devices, shifted(): return lax.ppermute(value, axis, pairs)  21.4 us
    all_gather x1, local copies, waits for them, and re-layouts, body(): gathered = lax.all_gather(haloed(own_block), 'chan', axis=3, tiled=True)  6.18 us
    slice x2, local copies, waits for them, and re-layouts, tap_sum(): padded[tap_x:tap_x + size_x, tap_y:tap_y + size_y, tap_z:tap_z + size_z, :]  5.91 us
    dot_general x9, matrix products, tap_sum(): jnp.dot(columns, kernel[tap_x, tap_y].reshape(3 * width_in, -1), preferre...  5.35 us
  transfers between devices with their start and end apart: 5, of which 3 were waited for; matrix products, arithmetic and copies ran while one was open for 2% of the time, Pallas kernels for 0%

profile of v2, /device:TPU:1, one launch (start us, length us, event | category | flops | bytes accessed | tf_op | source)
XLA Modules:
  0.0 140.6 jit_solution(16022617028331609732)
XLA Ops:
  6.5 0.0 all-gather.2.cloned.1.call-start
  6.5 1.0 copy.17
  7.6 0.0 copy-start
  7.6 10.6 %collective-permute-start.1 = (bf16[1,8,32,64]{3,2,1,0:T(8,128)(2,1)S(1)}, bf16[1,8,32,64]{3,2,1,0:T(8,128)(2,1)S(1)}, u32[]{:S(2)}, u32[]{:S(2)}) collective-permute-start(bf16[1,8,32,64]{3,2,1,0:T(8,128)(2,1)S(1)} %get-tuple-element.44), channel_id=1, source_target_pairs={{0,448},{8,456},{16,464},{24,472},{32,480},{40,488},{48,496},{56,5... | collective-permute-start | bytes 98312 | tf_op jit(solution)/shard_map/ppermute | solution.py:15
  18.2 1.9 %collective-permute-start = (bf16[1,8,32,64]{3,2,1,0:T(8,128)(2,1)S(1)}, bf16[1,8,32,64]{3,2,1,0:T(8,128)(2,1)S(1)}, u32[]{:S(2)}, u32[]{:S(2)}) collective-permute-start(bf16[1,8,32,64]{3,2,1,0:T(8,128)(2,1)S(1)} %get-tuple-element.43), channel_id=1, source_target_pairs={{0,64},{8,72},{16,80},{24,88},{32,96},{40,104},{48,112},{56,120},{... | collective-permute-start | bytes 98312 | tf_op jit(solution)/shard_map/ppermute | solution.py:15
  20.1 0.0 collective-permute-done.1
  20.2 10.2 %collective-permute-done = bf16[1,8,32,64]{3,2,1,0:T(8,128)(2,1)S(1)} collective-permute-done((bf16[1,8,32,64]{3,2,1,0:T(8,128)(2,1)S(1)}, bf16[1,8,32,64]{3,2,1,0:T(8,128)(2,1)S(1)}, u32[]{:S(2)}, u32[]{:S(2)}) %collective-permute-start) | collective-permute-done | bytes 32800 | tf_op jit(solution)/shard_map/ppermute | solution.py:15
  30.3 9.6 %collective-permute-start.3 = (bf16[4,1,32,64]{3,2,1,0:T(8,128)(2,1)S(1)}, bf16[4,1,32,64]{3,2,1,0:T(8,128)(2,1)S(1)}, u32[]{:S(2)}, u32[]{:S(2)}) collective-permute-start(bf16[4,1,32,64]{3,2,1,0:T(8,128)(2,1)S(1)} %get-tuple-element.42), channel_id=1, source_target_pairs={{0,504},{8,0},{16,8},{24,16},{32,24},{40,32},{48,40},{56,48},{64,5... | collective-permute-start | bytes 49160 | tf_op jit(solution)/shard_map/ppermute | solution.py:15
  40.0 1.9 %collective-permute-start.2 = (bf16[4,1,32,64]{3,2,1,0:T(8,128)(2,1)S(1)}, bf16[4,1,32,64]{3,2,1,0:T(8,128)(2,1)S(1)}, u32[]{:S(2)}, u32[]{:S(2)}) collective-permute-start(bf16[4,1,32,64]{3,2,1,0:T(8,128)(2,1)S(1)} %get-tuple-element.41), channel_id=1, source_target_pairs={{0,8},{8,16},{16,24},{24,32},{32,40},{40,48},{48,56},{56,64},{64,7... | collective-permute-start | bytes 49160 | tf_op jit(solution)/shard_map/ppermute | solution.py:15
  41.9 0.0 collective-permute-done.3
  42.0 11.2 %collective-permute-done.2 = bf16[4,1,32,64]{3,2,1,0:T(8,128)(2,1)S(1)} collective-permute-done((bf16[4,1,32,64]{3,2,1,0:T(8,128)(2,1)S(1)}, bf16[4,1,32,64]{3,2,1,0:T(8,128)(2,1)S(1)}, u32[]{:S(2)}, u32[]{:S(2)}) %collective-permute-start.2) | collective-permute-done | bytes 16416 | tf_op jit(solution)/shard_map/ppermute | solution.py:15
  53.2 0.1 pad_maximum_fusion.9
  53.3 1.2 copy.18
  54.4 0.0 all-gather.2.cloned.1.call-update
  54.5 0.0 copy-done
  54.5 0.1 fusion.1
  54.6 0.2 copy.21
  54.8 0.2 copy.23
  55.1 0.2 copy.25
  55.3 0.2 copy.27
  55.5 0.2 copy.29
  55.8 0.2 copy.31
  56.0 0.2 copy.33
  56.2 0.2 copy.35
  56.5 0.2 copy.37
  56.7 56.6 %all-gather.2.cloned.1.call-done = bf16[4,10,32,512]{2,0,1,3:T(4,128)(2,1)} async-done(((bf16[4,10,32,64]{2,0,1,3:T(4,128)(2,1)}), bf16[4,10,32,512]{2,0,1,3:T(4,128)(2,1)}) %all-gather.2.cloned.1.call-update) | async-done | bytes 1310736 | tf_op jit(solution)/shard_map/all_gather | solution.py:74
  113.3 6.2 %copy.19 = bf16[4,10,32,512]{3,2,1,0:T(8,128)(2,1)S(1)} copy(bf16[4,10,32,512]{2,0,1,3:T(4,128)(2,1)} %all-gather.2.cloned.1.call-done) | data formatting | bytes 2621440 | tf_op jit(solution)/shard_map/all_gather | solution.py:74
  119.5 5.4 %pad_slice_fusion.1 = (bf16[2,8,32,512]{3,2,1,0:T(8,128)(2,1)S(1)}, bf16[2,8,32,512]{3,2,1,0:T(8,128)(2,1)S(1)}, bf16[2,8,32,512]{3,2,1,0:T(8,128)(2,1)S(1)}, bf...) fusion(bf16[4,10,32,512]{3,2,1,0:T(8,128)(2,1)S(1)} %copy.19), kind=kLoop, calls=%fused_computation.19 | loop fusion | bytes 12320768 | tf_op jit(solution)/shard_map/slice | solution.py:44
  124.9 0.5 fusion.2
  125.4 0.3 pad_maximum_fusion
  125.8 0.6 fusion.4
  126.4 0.6 convolution_add_fusion.7
  127.0 0.3 pad_maximum_fusion.2
  127.3 0.6 convolution_add_fusion.6
  127.9 0.6 convolution_add_fusion.5
  128.5 0.3 pad_maximum_fusion.4
  128.9 0.6 convolution_add_fusion.4
  129.5 0.6 convolution_add_fusion.3
  130.1 0.3 pad_maximum_fusion.6
  130.4 0.6 convolution_add_fusion.2
  131.0 0.6 convolution_add_fusion.1
  131.6 0.0 copy-start.1
  131.6 0.1 pad_maximum_fusion.8
  131.7 0.5 copy-done.1
  132.3 0.6 multiply_maximum_fusion
  132.9 0.1 copy.38
  133.0 0.8 copy.39
  (13 shorter events, 0.5 us)
Async XLA Ops:
  6.5 106.8 %all-gather.2.cloned.1.call-start = ((), (), s32[]{:S(2)}) async-start(), calls=%async_computation | async-start | bytes 5898240 | tf_op jit(solution)/shard_map/all_gather | solution.py:74
  7.6 46.9 %copy-start = (bf16[3,3,3,64,512]{4,3,2,1,0:T(8,128)(2,1)S(1)}, bf16[3,3,3,64,512]{4,3,2,1,0:T(8,128)(2,1)}, u32[]{:S(2)}) copy-start(bf16[3,3,3,64,512]{4,3,2,1,0:T(8,128)(2,1)} %param.4) | copy-start | bytes 5308420
  7.6 12.5 %collective-permute-start.1 = (bf16[1,8,32,64]{3,2,1,0:T(8,128)(2,1)S(1)}, bf16[1,8,32,64]{3,2,1,0:T(8,128)(2,1)S(1)}, u32[]{:S(2)}, u32[]{:S(2)}) collective-permute-start(bf16[1,8,32,64]{3,2,1,0:T(8,128)(2,1)S(1)} %get-tuple-element.44), channel_id=1, source_target_pairs={{0,448},{8,456},{16,464},{24,472},{32,480},{40,488},{48,496},{56,5... | collective-permute-start | bytes 98312 | tf_op jit(solution)/shard_map/ppermute | solution.py:15
  18.2 12.1 %collective-permute-start = (bf16[1,8,32,64]{3,2,1,0:T(8,128)(2,1)S(1)}, bf16[1,8,32,64]{3,2,1,0:T(8,128)(2,1)S(1)}, u32[]{:S(2)}, u32[]{:S(2)}) collective-permute-start(bf16[1,8,32,64]{3,2,1,0:T(8,128)(2,1)S(1)} %get-tuple-element.43), channel_id=1, source_target_pairs={{0,64},{8,72},{16,80},{24,88},{32,96},{40,104},{48,112},{56,120},{... | collective-permute-start | bytes 98312 | tf_op jit(solution)/shard_map/ppermute | solution.py:15
  30.3 11.6 %collective-permute-start.3 = (bf16[4,1,32,64]{3,2,1,0:T(8,128)(2,1)S(1)}, bf16[4,1,32,64]{3,2,1,0:T(8,128)(2,1)S(1)}, u32[]{:S(2)}, u32[]{:S(2)}) collective-permute-start(bf16[4,1,32,64]{3,2,1,0:T(8,128)(2,1)S(1)} %get-tuple-element.42), channel_id=1, source_target_pairs={{0,504},{8,0},{16,8},{24,16},{32,24},{40,32},{48,40},{56,48},{64,5... | collective-permute-start | bytes 49160 | tf_op jit(solution)/shard_map/ppermute | solution.py:15
  40.0 13.1 %collective-permute-start.2 = (bf16[4,1,32,64]{3,2,1,0:T(8,128)(2,1)S(1)}, bf16[4,1,32,64]{3,2,1,0:T(8,128)(2,1)S(1)}, u32[]{:S(2)}, u32[]{:S(2)}) collective-permute-start(bf16[4,1,32,64]{3,2,1,0:T(8,128)(2,1)S(1)} %get-tuple-element.41), channel_id=1, source_target_pairs={{0,8},{8,16},{16,24},{24,32},{32,40},{40,48},{48,56},{56,64},{64,7... | collective-permute-start | bytes 49160 | tf_op jit(solution)/shard_map/ppermute | solution.py:15
  131.6 0.7 copy-start.1
Sparse Core Ops, SparseCore 0:
  54.6 58.6 all-gather.1

commit v3 on v0

--- a/solution.py
+++ b/solution.py
@@ -11,8 +11,17 @@
 
 def shifted(value, axis, steps):
     count = lax.axis_size(axis)
-    pairs = [(source, (source + steps) % count) for source in range(count)]
-    return lax.ppermute(value, axis, pairs)
+    width = lax.axis_size("chan")
+    run_y = width // 2
+    pairs = []
+    for source in range(count):
+        target = (source + steps) % count
+        crosses = (source // CY) % 2 != (target // CY) % 2
+        for lane in range(width):
+            place, core = divmod(lane, 2)
+            moved = ((place + run_y // 2) % run_y) * 2 + core if crosses else lane
+            pairs.append((source * width + lane, target * width + moved))
+    return lax.ppermute(value, (axis, "chan"), pairs)
 
 
 def haloed(own_block):

time: 94.7 us -> 91 us (0.961)
  waiting for transfers between devices: 19.6 us -> 17.2 us
    ppermute x4, waiting for transfers between devices: 19.6 us -> 17.2 us  [shifted(): return lax.ppermute(value, (axis, 'chan'), pairs)]
  transfers between devices with their start and end apart: 4 -> 4, of which waited for: 4 -> 3; matrix products, arithmetic and copies ran while one was open for 2% -> 2% of each run, Pallas kernels for 0% -> 0%
where the time goes in v3:
time: 91 us; the launch traced here: 90.8 us
  starting transfers between devices  28.4 us (31%)
  blocking collectives  27.3 us (30%)
  waiting for transfers between devices  17.2 us (19%)
  local copies, waits for them, and re-layouts  9.53 us (10%)
  matrix products  5.38 us (6%)
  other arithmetic  2.59 us (3%)
    ppermute x4, starting transfers between devices, shifted(): return lax.ppermute(value, (axis, 'chan'), pairs)  28.4 us
    all_gather x1, blocking collectives, body(): gathered = lax.all_gather(own_block, 'chan', axis=3, tiled=True)  27.3 us
    ppermute x4, waiting for transfers between devices, shifted(): return lax.ppermute(value, (axis, 'chan'), pairs)  17.2 us
    dot_general x9, matrix products, tap_sum(): jnp.dot(columns, kernel[tap_x, tap_y].reshape(3 * width_in, -1), preferre...  5.38 us
    slice x3, local copies, waits for them, and re-layouts, tap_sum(): padded[tap_x:tap_x + size_x, tap_y:tap_y + size_y, tap_z:tap_z + size_z, :]  3.58 us
  transfers between devices with their start and end apart: 4, of which 3 were waited for; matrix products, arithmetic and copies ran while one was open for 2% of the time, Pallas kernels for 0%

profile of v3, /device:TPU:1, one launch (start us, length us, event | category | flops | bytes accessed | tf_op | source)
XLA Modules:
  0.0 90.8 jit_solution(7168739187300909789)
XLA Ops:
  0.0 1.0 %copy.17 = bf16[1,2,64,256]{2,3,1,0:T(8,128)(2,1)S(1)} copy(f32[1,2,64,256]{3,2,1,0:T(8,128)} %param.3) | data formatting | bytes 196608 | tf_op args[0]
  1.0 0.3 copy.18
  1.3 27.3 %all_gather.3 = bf16[2,8,32,512]{2,1,0,3:T(8,128)(2,1)S(1)} all-gather(bf16[2,8,32,64]{2,1,0,3:T(8,128)(2,1)S(1)} %copy.18), channel_id=1, replica_groups=mesh['space'=64,'chan'=8] {'chan'}, dimensions={3}, use_global_device_ids=true | all-gather | bytes 589824 | tf_op jit(solution)/shard_map/all_gather | solution.py:83
  28.6 1.6 %copy.19 = bf16[2,8,32,512]{3,2,1,0:T(8,128)(2,1)S(1)} copy(bf16[2,8,32,512]{2,1,0,3:T(8,128)(2,1)S(1)} %all_gather.3) | data formatting | bytes 1048576 | tf_op jit(solution)/shard_map/all_gather | solution.py:83
  30.3 0.0 copy-start
  30.3 2.4 %collective-permute-start = (bf16[1,8,32,512]{3,2,1,0:T(8,128)(2,1)S(1)}, bf16[1,8,32,512]{3,2,1,0:T(8,128)(2,1)S(1)}, u32[]{:S(2)}, u32[]{:S(2)}) collective-permute-start(bf16[1,8,32,512]{3,2,1,0:T(8,128)(2,1)S(1)} %get-tuple-element.45), channel_id=1, source_target_pairs={{0,68},{1,69},{2,70},{3,71},{4,64},{5,65},{6,66},{7,67},{8,76},{9,... | collective-permute-start | bytes 786440 | tf_op jit(solution)/shard_map/ppermute | solution.py:24
  32.7 7.2 %collective-permute-start.1 = (bf16[1,8,32,512]{3,2,1,0:T(8,128)(2,1)S(1)}, bf16[1,8,32,512]{3,2,1,0:T(8,128)(2,1)S(1)}, u32[]{:S(2)}, u32[]{:S(2)}) collective-permute-start(bf16[1,8,32,512]{3,2,1,0:T(8,128)(2,1)S(1)} %get-tuple-element.46), channel_id=1, source_target_pairs={{0,452},{1,453},{2,454},{3,455},{4,448},{5,449},{6,450},{7,451},{8... | collective-permute-start | bytes 786440 | tf_op jit(solution)/shard_map/ppermute | solution.py:24
  40.0 9.7 %collective-permute-done = bf16[1,8,32,512]{3,2,1,0:T(8,128)(2,1)S(1)} collective-permute-done((bf16[1,8,32,512]{3,2,1,0:T(8,128)(2,1)S(1)}, bf16[1,8,32,512]{3,2,1,0:T(8,128)(2,1)S(1)}, u32[]{:S(2)}, u32[]{:S(2)}) %collective-permute-start) | collective-permute-done | bytes 262176 | tf_op jit(solution)/shard_map/ppermute | solution.py:24
  49.6 5.6 %collective-permute-done.1 = bf16[1,8,32,512]{3,2,1,0:T(8,128)(2,1)S(1)} collective-permute-done((bf16[1,8,32,512]{3,2,1,0:T(8,128)(2,1)S(1)}, bf16[1,8,32,512]{3,2,1,0:T(8,128)(2,1)S(1)}, u32[]{:S(2)}, u32[]{:S(2)}) %collective-permute-start.1) | collective-permute-done | bytes 262176 | tf_op jit(solution)/shard_map/ppermute | solution.py:24
  55.3 4.0 %collective-permute-start.2 = (bf16[4,1,32,512]{3,2,1,0:T(8,128)(2,1)S(1)}, bf16[4,1,32,512]{3,2,1,0:T(8,128)(2,1)S(1)}, u32[]{:S(2)}, u32[]{:S(2)}) collective-permute-start(bf16[4,1,32,512]{3,2,1,0:T(8,128)(2,1)S(1)} %get-tuple-element.40), channel_id=1, source_target_pairs={{0,8},{1,9},{2,10},{3,11},{4,12},{5,13},{6,14},{7,15},{8,16},{9,17... | collective-permute-start | bytes 393224 | tf_op jit(solution)/shard_map/ppermute | solution.py:24
  59.3 0.0 copy-done
  59.3 0.1 fusion.12
  59.5 0.2 copy.24
  59.7 0.2 copy.22
  59.9 0.2 copy.25
  60.2 0.2 copy.26
  60.4 0.2 copy.28
  60.6 0.2 copy.29
  60.9 0.2 copy.30
  61.1 0.2 copy.33
  61.3 0.2 copy.32
  61.6 14.7 %collective-permute-start.3 = (bf16[4,1,32,512]{3,2,1,0:T(8,128)(2,1)S(1)}, bf16[4,1,32,512]{3,2,1,0:T(8,128)(2,1)S(1)}, u32[]{:S(2)}, u32[]{:S(2)}) collective-permute-start(bf16[4,1,32,512]{3,2,1,0:T(8,128)(2,1)S(1)} %get-tuple-element.41), channel_id=1, source_target_pairs={{0,508},{1,509},{2,510},{3,511},{4,504},{5,505},{6,506},{7,507},{8... | collective-permute-start | bytes 393224 | tf_op jit(solution)/shard_map/ppermute | solution.py:24
  76.3 0.0 collective-permute-done.2
  76.3 1.9 %collective-permute-done.3 = bf16[4,1,32,512]{3,2,1,0:T(8,128)(2,1)S(1)} collective-permute-done((bf16[4,1,32,512]{3,2,1,0:T(8,128)(2,1)S(1)}, bf16[4,1,32,512]{3,2,1,0:T(8,128)(2,1)S(1)}, u32[]{:S(2)}, u32[]{:S(2)}) %collective-permute-start.3) | collective-permute-done | bytes 131104 | tf_op jit(solution)/shard_map/ppermute | solution.py:24
  78.2 0.2 maximum_maximum_fusion
  78.5 0.2 fusion.14
  78.6 0.2 fusion.15
  78.8 1.0 %select_maximum_fusion = bf16[4,10,34,512]{3,2,1,0:T(8,128)(2,1)S(1)} fusion(bf16[4,1,32,512]{3,2,1,0:T(8,128)(2,1)S(1)} %broadcast_select_fusion, bf16[4,1,32,512]{3,2,1,0:T(8,128)(2,1)S(1)} %broadcast_select_fusion.1, bf16[1,8,32,512]{3,2,1,0:T(8,128)(2,1)S(1)} %collective-permute-done.1, bf16[2,8,32,512]{3,2,1,0:T(8,128)(2,1)S(1)} %copy.19, ...), kind=kLoop, calls=%fused_computation.3 | loop fusion | flops 12533760 | bytes 2703360 | tf_op jit(solution)/shard_map/concatenate | solution.py:36
  79.8 3.2 %fusion.13 = (bf16[2,8,32,512]{3,2,1,0:T(8,128)(2,1)S(1)}, bf16[2,8,32,512]{3,2,1,0:T(8,128)(2,1)S(1)}, bf16[2,8,32,512]{3,2,1,0:T(8,128)(2,1)S(1)}, bf16[2,8,32...) fusion(bf16[4,10,34,512]{3,2,1,0:T(8,128)(2,1)S(1)} %select_max, ...), kind=kLoop, calls=%fused_computation.41 | loop fusion | bytes 18874368 | tf_op jit(solution)/shard_map/slice | solution.py:53
  83.0 0.5 fusion.7
  83.5 0.6 fusion.17
  84.1 0.3 pad_maximum_fusion.7
  84.4 0.6 fusion.18
  85.0 0.3 pad_maximum_fusion.2
  85.3 0.6 convolution_add_fusion.6
  85.9 0.6 convolution_add_fusion.5
  86.5 0.3 pad_maximum_fusion.4
  86.8 0.6 convolution_add_fusion.4
  87.4 0.6 convolution_add_fusion.3
  88.0 0.0 copy-start.1
  88.0 0.6 convolution_add_fusion.2
  88.6 0.6 convolution_add_fusion.1
  89.2 0.0 copy-done.1
  89.2 0.6 multiply_maximum_fusion
  89.9 0.1 copy.34
  90.0 0.8 copy.35
  (13 shorter events, 0.5 us)
Async XLA Ops:
  30.3 29.1 %copy-start = (bf16[3,3,3,64,512]{4,3,2,1,0:T(8,128)(2,1)S(1)}, bf16[3,3,3,64,512]{4,3,2,1,0:T(8,128)(2,1)}, u32[]{:S(2)}) copy-start(bf16[3,3,3,64,512]{4,3,2,1,0:T(8,128)(2,1)} %param.4) | copy-start | bytes 5308420
  30.3 19.3 %collective-permute-start = (bf16[1,8,32,512]{3,2,1,0:T(8,128)(2,1)S(1)}, bf16[1,8,32,512]{3,2,1,0:T(8,128)(2,1)S(1)}, u32[]{:S(2)}, u32[]{:S(2)}) collective-permute-start(bf16[1,8,32,512]{3,2,1,0:T(8,128)(2,1)S(1)} %get-tuple-element.45), channel_id=1, source_target_pairs={{0,68},{1,69},{2,70},{3,71},{4,64},{5,65},{6,66},{7,67},{8,76},{9,... | collective-permute-start | bytes 786440 | tf_op jit(solution)/shard_map/ppermute | solution.py:24
  32.7 22.5 %collective-permute-start.1 = (bf16[1,8,32,512]{3,2,1,0:T(8,128)(2,1)S(1)}, bf16[1,8,32,512]{3,2,1,0:T(8,128)(2,1)S(1)}, u32[]{:S(2)}, u32[]{:S(2)}) collective-permute-start(bf16[1,8,32,512]{3,2,1,0:T(8,128)(2,1)S(1)} %get-tuple-element.46), channel_id=1, source_target_pairs={{0,452},{1,453},{2,454},{3,455},{4,448},{5,449},{6,450},{7,451},{8... | collective-permute-start | bytes 786440 | tf_op jit(solution)/shard_map/ppermute | solution.py:24
  55.3 21.0 %collective-permute-start.2 = (bf16[4,1,32,512]{3,2,1,0:T(8,128)(2,1)S(1)}, bf16[4,1,32,512]{3,2,1,0:T(8,128)(2,1)S(1)}, u32[]{:S(2)}, u32[]{:S(2)}) collective-permute-start(bf16[4,1,32,512]{3,2,1,0:T(8,128)(2,1)S(1)} %get-tuple-element.40), channel_id=1, source_target_pairs={{0,8},{1,9},{2,10},{3,11},{4,12},{5,13},{6,14},{7,15},{8,16},{9,17... | collective-permute-start | bytes 393224 | tf_op jit(solution)/shard_map/ppermute | solution.py:24
  61.6 16.7 %collective-permute-start.3 = (bf16[4,1,32,512]{3,2,1,0:T(8,128)(2,1)S(1)}, bf16[4,1,32,512]{3,2,1,0:T(8,128)(2,1)S(1)}, u32[]{:S(2)}, u32[]{:S(2)}) collective-permute-start(bf16[4,1,32,512]{3,2,1,0:T(8,128)(2,1)S(1)} %get-tuple-element.41), channel_id=1, source_target_pairs={{0,508},{1,509},{2,510},{3,511},{4,504},{5,505},{6,506},{7,507},{8... | collective-permute-start | bytes 393224 | tf_op jit(solution)/shard_map/ppermute | solution.py:24
  88.0 1.2 %copy-start.1 = (f32[64]{0:T(128)S(1)}, f32[64]{0:T(128)}, u32[]{:S(2)}) copy-start(f32[64]{0:T(128)} %param.5) | copy-start | bytes 772

commit v4 on v3

v4 whole, which is shorter than its diff:
```python
import jax
import jax.numpy as jnp
from jax import lax
from jax.sharding import PartitionSpec as P

CY = 8


negative_slope = 0.3


def shifted(value, axis, steps):
    count = lax.axis_size(axis)
    width = lax.axis_size("chan")
    run_y = width // 2
    pairs = []
    for source in range(count):
        target = (source + steps) % count
        crosses = (source // CY) % 2 != (target // CY) % 2
        for lane in range(width):
            place, core = divmod(lane, 2)
            moved = ((place + run_y // 2) % run_y) * 2 + core if crosses else lane
            pairs.append((source * width + lane, target * width + moved))
    return lax.ppermute(value, (axis, "chan"), pairs)


def haloed(own_block):
    below = shifted(own_block[:, -1:], "space", 8)
    above = shifted(own_block[:, :1], "space", -8)
    widened = jnp.concatenate([below, own_block, above], axis=1)
    lower_from = shifted(widened[:, :, -1:], "space", 1)
    upper_from = shifted(widened[:, :, :1], "space", -1)
    place_y = (lax.axis_index("space") + 4) % 8
    lower_rim = jnp.where(place_y > 0, lower_from, jnp.zeros_like(lower_from))
    upper_rim = jnp.where(place_y < 7, upper_from, jnp.zeros_like(upper_from))
    return jnp.concatenate([lower_rim, widened, upper_rim], axis=2)


def tap_sum(padded, weight):
    size_x = padded.shape[1] - 2
    size_y = padded.shape[2] - 2
    size_z = padded.shape[3] - 2
    width_in = padded.shape[0]
    total = None
    for tap_x in range(3):
        for tap_y in range(3):
            columns = jnp.concatenate(
                [
                    padded[
                        :, tap_x : tap_x + size_x, tap_y : tap_y + size_y, tap_z : tap_z + size_z
                    ]
                    for tap_z in range(3)
                ],
                axis=0,
            )
            columns = columns.reshape(3 * width_in, -1)
            taps = weight[tap_x, tap_y].transpose(1, 0, 2).reshape(-1, 3 * width_in)
            product = jnp.dot(taps, columns, preferred_element_type=jnp.float32)
            total = product if total is None else total + product
    return total


def body(activation, weight, conv_bias):
    size_x = activation.shape[1]
    width_in = activation.shape[2]
    size_y = CY
    size_z = activation.shape[3] // size_y
    own_block = activation[0].astype(jnp.bfloat16).transpose(1, 0, 2)
    gathered = lax.all_gather(own_block, "chan", axis=0, tiled=True)
    gathered = gathered.reshape(-1, size_x, size_y, size_z)
    padded = jnp.pad(haloed(gathered), ((0, 0), (0, 0), (0, 0), (1, 1)))
    total = tap_sum(padded, weight)
    width_out = total.shape[0]
    before = total + conv_bias[:, None]
    result = jnp.maximum(before, negative_slope * before)
    result = result.reshape(width_out, size_x, size_y * size_z).transpose(1, 0, 2)
    return result[None]


def solution(mesh):
    placed = (P("space", None, "chan", None), P(None, None, None, "chan", None), P("chan"))
    return jax.shard_map(
        body, mesh=mesh, in_specs=placed, out_specs=P("space", None, "chan", None), check_vma=False
    )
```

time: 91 us -> 85.3 us (0.937)
  blocking collectives: 27.3 us -> 21.7 us
  waiting for transfers between devices: 17.2 us -> 15 us
  other arithmetic: 2.59 us -> 4.71 us
    all_gather x1, blocking collectives: 27.3 us -> 21.7 us  [body(): gathered = lax.all_gather(own_block, 'chan', axis=0, tiled=True)]
    reshape x1 -> x10, local copies, waits for them, and re-layouts: 0.78 us -> 4.55 us  [the longest x9 3.89 us: tap_sum(): taps = weight[tap_x, tap_y].transpose(1, 0, 2).reshape(-1, 3 * width_in)]
    ppermute x4, waiting for transfers between devices: 17.2 us -> 15 us  [shifted(): return lax.ppermute(value, (axis, 'chan'), pairs)]
    slice x14 -> x3, local copies, waits for them, and re-layouts: 5.28 us -> 3.61 us  [the longest x2 3.58 us: tap_sum(): padded[:, tap_x:tap_x + size_x, tap_y:tap_y + size_y, tap_z:tap_z + size_z]]
    convert_element_type x0 -> x1, other arithmetic: none -> 0.91 us  [body(): own_block = activation[0].astype(jnp.bfloat16).transpose(1, 0, 2)]
    select_n x1, other arithmetic: 0.02 us -> 0.93 us  [haloed(): lower_rim = jnp.where(place_y > 0, lower_from, jnp.zeros_like(lower_from))]
    concatenate x6 -> x9, other arithmetic: 2.53 us -> 2.17 us  [the longest x2 1.17 us: haloed(): return jnp.concatenate([lower_rim, widened, upper_rim], axis=2)]
  transfers between devices with their start and end apart: 4 -> 4, of which waited for: 3 -> 3; matrix products, arithmetic and copies ran while one was open for 2% -> 7% of each run, Pallas kernels for 0% -> 0%
where the time goes in v4:
time: 85.3 us; the launch traced here: 84.9 us
  starting transfers between devices  27.8 us (33%)
  blocking collectives  21.7 us (25%)
  waiting for transfers between devices  15 us (18%)
  local copies, waits for them, and re-layouts  10 us (12%)
  matrix products  5.34 us (6%)
  other arithmetic  4.71 us (6%)
    ppermute x4, starting transfers between devices, shifted(): return lax.ppermute(value, (axis, 'chan'), pairs)  27.8 us
    all_gather x1, blocking collectives, body(): gathered = lax.all_gather(own_block, 'chan', axis=0, tiled=True)  21.7 us
    ppermute x4, waiting for transfers between devices, shifted(): return lax.ppermute(value, (axis, 'chan'), pairs)  15 us
    dot_general x9, matrix products, tap_sum(): product = jnp.dot(taps, columns, preferred_element_type=jnp.float32)  5.34 us
    reshape x9, local copies, waits for them, and re-layouts, tap_sum(): taps = weight[tap_x, tap_y].transpose(1, 0, 2).reshape(-1, 3 * width_in)  3.89 us
    slice x2, local copies, waits for them, and re-layouts, tap_sum(): padded[:, tap_x:tap_x + size_x, tap_y:tap_y + size_y, tap_z:tap_z + size_z]  3.58 us
  transfers between devices with their start and end apart: 4, of which 3 were waited for; matrix products, arithmetic and copies ran while one was open for 7% of the time, Pallas kernels for 0%

profile of v4, /device:TPU:1, one launch (start us, length us, event | category | flops | bytes accessed | tf_op | source)
XLA Modules:
  0.0 84.9 jit_solution(10094547412967534462)
XLA Ops:
  0.0 0.9 %convert_element_type.10 = bf16[1,2,64,256]{3,2,1,0:T(8,128)(2,1)S(1)} convert(f32[1,2,64,256]{3,2,1,0:T(8,128)} %param.3) | non-fusion elementwise | flops 32768 | bytes 196608 | tf_op jit(solution)/shard_map/convert_element_type | solution.py:68
  0.9 0.1 copy.43
  1.0 21.7 %all_gather.3 = bf16[512,2,256]{2,1,0:T(2,128)(2,1)S(1)} all-gather(bf16[64,2,256]{2,1,0:T(2,128)(2,1)S(1)} %bitcast.125), channel_id=1, replica_groups=mesh['space'=64,'chan'=8] {'chan'}, dimensions={0}, use_global_device_ids=true | all-gather | bytes 589824 | tf_op jit(solution)/shard_map/all_gather | solution.py:69
  22.7 0.0 copy-start
  22.7 0.7 copy.17
  23.5 1.9 %collective-permute-start = (bf16[512,1,8,32]{0,3,2,1:T(8,128)(2,1)S(1)}, bf16[512,1,8,32]{0,3,2,1:T(8,128)(2,1)S(1)}, u32[]{:S(2)}, u32[]{:S(2)}) collective-permute-start(bf16[512,1,8,32]{0,3,2,1:T(8,128)(2,1)S(1)} %get-tuple-element.44), channel_id=1, source_target_pairs={{0,68},{1,69},{2,70},{3,71},{4,64},{5,65},{6,66},{7,67},{8,76},{9,... | collective-permute-start | bytes 786440 | tf_op jit(solution)/shard_map/ppermute | solution.py:24
  25.4 7.6 %collective-permute-start.1 = (bf16[512,1,8,32]{0,3,2,1:T(8,128)(2,1)S(1)}, bf16[512,1,8,32]{0,3,2,1:T(8,128)(2,1)S(1)}, u32[]{:S(2)}, u32[]{:S(2)}) collective-permute-start(bf16[512,1,8,32]{0,3,2,1:T(8,128)(2,1)S(1)} %get-tuple-element.45), channel_id=1, source_target_pairs={{0,452},{1,453},{2,454},{3,455},{4,448},{5,449},{6,450},{7,451},{8... | collective-permute-start | bytes 786440 | tf_op jit(solution)/shard_map/ppermute | solution.py:24
  33.0 8.2 %collective-permute-done = bf16[512,1,8,32]{0,3,2,1:T(8,128)(2,1)S(1)} collective-permute-done((bf16[512,1,8,32]{0,3,2,1:T(8,128)(2,1)S(1)}, bf16[512,1,8,32]{0,3,2,1:T(8,128)(2,1)S(1)}, u32[]{:S(2)}, u32[]{:S(2)}) %collective-permute-start) | collective-permute-done | bytes 262176 | tf_op jit(solution)/shard_map/ppermute | solution.py:24
  41.2 5.6 %collective-permute-done.1 = bf16[512,1,8,32]{0,3,2,1:T(8,128)(2,1)S(1)} collective-permute-done((bf16[512,1,8,32]{0,3,2,1:T(8,128)(2,1)S(1)}, bf16[512,1,8,32]{0,3,2,1:T(8,128)(2,1)S(1)}, u32[]{:S(2)}, u32[]{:S(2)}) %collective-permute-start.1) | collective-permute-done | bytes 262176 | tf_op jit(solution)/shard_map/ppermute | solution.py:24
  46.8 0.7 pad_maximum_fusion.11
  47.5 3.5 %collective-permute-start.2 = (bf16[512,4,1,32]{0,3,2,1:T(8,128)(2,1)}, bf16[512,4,1,32]{0,3,2,1:T(8,128)(2,1)}, u32[]{:S(2)}, u32[]{:S(2)}) collective-permute-start(bf16[512,4,1,32]{0,3,2,1:T(8,128)(2,1)} %get-tuple-element.40), channel_id=1, source_target_pairs={{0,8},{1,9},{2,10},{3,11},{4,12},{5,13},{6,14},{7,15},{8,16},{9,17... | collective-permute-start | bytes 393224 | tf_op jit(solution)/shard_map/ppermute | solution.py:24
  51.1 0.0 copy-done
  51.1 1.1 %slice_bitcast_fusion.4 = (bf16[3,8,8,512]{3,2,1,0:T(8,128)(2,1)S(1)}, bf16[3,8,8,512]{3,2,1,0:T(8,128)(2,1)}, bf16[3,8,8,512]{3,2,1,0:T(8,128)(2,1)}, bf16[3,8,...) fusion(bf16[3,3,3,64,512]{4,3,2,1,0:T(8,128)(2,1)S(1)} %copy-done), kind=kLoop, calls=%fused_computation.45 | loop fusion | bytes 3538944
  52.1 0.0 copy-start.2
  52.2 0.0 copy-start.1
  52.2 1.0 %copy.31 = bf16[3,8,8,512]{3,2,0,1:T(8,128)(2,1)S(1)} copy(bf16[3,8,8,512]{3,2,1,0:T(8,128)(2,1)} %get-tuple-element.10) | data formatting | bytes 393216 | tf_op jit(solution)/shard_map/reshape | solution.py:57
  53.1 0.9 %copy.30 = bf16[3,8,8,512]{3,2,0,1:T(8,128)(2,1)S(1)} copy(bf16[3,8,8,512]{3,2,1,0:T(8,128)(2,1)} %get-tuple-element.11) | data formatting | bytes 393216 | tf_op jit(solution)/shard_map/reshape | solution.py:57
  54.1 0.9 %copy.32 = bf16[3,8,8,512]{3,2,0,1:T(8,128)(2,1)S(1)} copy(bf16[3,8,8,512]{3,2,1,0:T(8,128)(2,1)} %get-tuple-element.9) | data formatting | bytes 393216 | tf_op jit(solution)/shard_map/reshape | solution.py:57
  55.0 0.9 %copy.33 = bf16[3,8,8,512]{3,2,0,1:T(8,128)(2,1)S(1)} copy(bf16[3,8,8,512]{3,2,1,0:T(8,128)(2,1)} %get-tuple-element.8) | data formatting | bytes 393216 | tf_op jit(solution)/shard_map/reshape | solution.py:57
  56.0 0.0 copy-done.2
  56.0 0.0 copy-done.1
  56.1 14.7 %collective-permute-start.3 = (bf16[512,4,1,32]{0,3,2,1:T(8,128)(2,1)S(1)}, bf16[512,4,1,32]{0,3,2,1:T(8,128)(2,1)S(1)}, u32[]{:S(2)}, u32[]{:S(2)}) collective-permute-start(bf16[512,4,1,32]{0,3,2,1:T(8,128)(2,1)S(1)} %get-tuple-element.41), channel_id=1, source_target_pairs={{0,508},{1,509},{2,510},{3,511},{4,504},{5,505},{6,506},{7,507},{8... | collective-permute-start | bytes 393224 | tf_op jit(solution)/shard_map/ppermute | solution.py:24
  70.9 0.0 collective-permute-done.2
  70.9 0.9 %broadcast_select_fusion.1 = bf16[512,4,1,32]{0,3,2,1:T(8,128)(2,1)S(1)} fusion(bf16[512,4,1,32]{0,3,2,1:T(8,128)(2,1)} %collective-permute-done.2, pred[]{:T(512)S(6)} %gt.3), kind=kLoop, calls=%fused_computation.55 | loop fusion | flops 65536 | bytes 262145 | tf_op jit(solution)/shard_map/jit(_where)/select_n | solution.py:34
  71.8 1.2 %collective-permute-done.3 = bf16[512,4,1,32]{0,3,2,1:T(8,128)(2,1)S(1)} collective-permute-done((bf16[512,4,1,32]{0,3,2,1:T(8,128)(2,1)S(1)}, bf16[512,4,1,32]{0,3,2,1:T(8,128)(2,1)S(1)}, u32[]{:S(2)}, u32[]{:S(2)}) %collective-permute-start.3) | collective-permute-done | bytes 131104 | tf_op jit(solution)/shard_map/ppermute | solution.py:24
  73.0 1.0 %select_maximum_fusion = bf16[512,4,10,34]{0,3,2,1:T(8,128)(2,1)S(1)} fusion(bf16[512,4,1,32]{0,3,2,1:T(8,128)(2,1)S(1)} %broadcast_select_fusion, bf16[512,4,1,32]{0,3,2,1:T(8,128)(2,1)S(1)} %broadcast_select_fusion.1, bf16[512,1,8,32]{0,3,2,1:T(8,128)(2,1)S(1)} %collective-permute-done.1, bf16[512,2,8,32]{0,3,2,1:T(8,128)(2,1)S(1)} %bitcast.103, ...), kind=kLoop, calls=%fused_computation.3 | loop fusion | flops 12533760 | bytes 2703360 | tf_op jit(solution)/shard_map/concatenate | solution.py:36
  74.0 3.1 %fusion.40 = (bf16[512,2,8,32]{0,3,2,1:T(8,128)(2,1)S(1)}, bf16[512,2,8,32]{0,3,2,1:T(8,128)(2,1)S(1)}, bf16[512,2,8,32]{0,3,2,1:T(8,128)(2,1)S(1)}, bf16[512,2,...) fusion(bf16[512,4,10,34]{0,3,2,1:T(8,128)(2,1)S(1)} %select_max, ...), kind=kLoop, calls=%fused_computation.58 | loop fusion | bytes 18874368 | tf_op jit(solution)/shard_map/slice | solution.py:49
  77.1 0.2 maximum_maximum_fusion
  77.4 0.4 fusion.41
  77.8 0.3 fusion.9
  78.1 0.6 fusion.44
  78.7 0.1 pad_maximum_fusion.5
  78.8 0.6 fusion.45
  79.4 0.1 pad_maximum_fusion.6
  79.5 0.6 fusion.46
  80.1 0.6 fusion.47
  80.7 0.1 pad_maximum_fusion.7
  80.8 0.6 fusion.48
  81.4 0.1 pad_maximum_fusion.4
  81.5 0.1 pad_maximum_fusion.3
  81.7 0.1 pad_maximum_fusion.2
  81.8 0.6 convolution_add_fusion.2
  82.4 0.0 copy-start.3
  82.4 0.6 convolution_add_fusion.1
  83.0 0.6 convolution_add_fusion
  83.6 0.0 copy-done.3
  83.6 0.6 multiply_maximum_fusion
  84.3 0.7 copy.42
  (7 shorter events, 0.1 us)
Async XLA Ops:
  22.7 28.4 %copy-start = (bf16[3,3,3,64,512]{4,3,2,1,0:T(8,128)(2,1)S(1)}, bf16[3,3,3,64,512]{4,3,2,1,0:T(8,128)(2,1)}, u32[]{:S(2)}) copy-start(bf16[3,3,3,64,512]{4,3,2,1,0:T(8,128)(2,1)} %param.4) | copy-start | bytes 5308420
  23.5 17.7 %collective-permute-start = (bf16[512,1,8,32]{0,3,2,1:T(8,128)(2,1)S(1)}, bf16[512,1,8,32]{0,3,2,1:T(8,128)(2,1)S(1)}, u32[]{:S(2)}, u32[]{:S(2)}) collective-permute-start(bf16[512,1,8,32]{0,3,2,1:T(8,128)(2,1)S(1)} %get-tuple-element.44), channel_id=1, source_target_pairs={{0,68},{1,69},{2,70},{3,71},{4,64},{5,65},{6,66},{7,67},{8,76},{9,... | collective-permute-start | bytes 786440 | tf_op jit(solution)/shard_map/ppermute | solution.py:24
  25.4 21.4 %collective-permute-start.1 = (bf16[512,1,8,32]{0,3,2,1:T(8,128)(2,1)S(1)}, bf16[512,1,8,32]{0,3,2,1:T(8,128)(2,1)S(1)}, u32[]{:S(2)}, u32[]{:S(2)}) collective-permute-start(bf16[512,1,8,32]{0,3,2,1:T(8,128)(2,1)S(1)} %get-tuple-element.45), channel_id=1, source_target_pairs={{0,452},{1,453},{2,454},{3,455},{4,448},{5,449},{6,450},{7,451},{8... | collective-permute-start | bytes 786440 | tf_op jit(solution)/shard_map/ppermute | solution.py:24
  47.5 23.3 %collective-permute-start.2 = (bf16[512,4,1,32]{0,3,2,1:T(8,128)(2,1)}, bf16[512,4,1,32]{0,3,2,1:T(8,128)(2,1)}, u32[]{:S(2)}, u32[]{:S(2)}) collective-permute-start(bf16[512,4,1,32]{0,3,2,1:T(8,128)(2,1)} %get-tuple-element.40), channel_id=1, source_target_pairs={{0,8},{1,9},{2,10},{3,11},{4,12},{5,13},{6,14},{7,15},{8,16},{9,17... | collective-permute-start | bytes 393224 | tf_op jit(solution)/shard_map/ppermute | solution.py:24
  52.1 3.8 %copy-start.2 = (bf16[3,8,8,512]{3,2,1,0:T(8,128)(2,1)S(1)}, bf16[3,8,8,512]{3,2,1,0:T(8,128)(2,1)}, u32[]{:S(2)}) copy-start(bf16[3,8,8,512]{3,2,1,0:T(8,128)(2,1)} %get-tuple-element.7) | copy-start | bytes 589828
  52.2 3.9 %copy-start.1 = (bf16[3,8,8,512]{3,2,1,0:T(8,128)(2,1)S(1)}, bf16[3,8,8,512]{3,2,1,0:T(8,128)(2,1)}, u32[]{:S(2)}) copy-start(bf16[3,8,8,512]{3,2,1,0:T(8,128)(2,1)} %get-tuple-element.6) | copy-start | bytes 589828
  56.1 16.9 %collective-permute-start.3 = (bf16[512,4,1,32]{0,3,2,1:T(8,128)(2,1)S(1)}, bf16[512,4,1,32]{0,3,2,1:T(8,128)(2,1)S(1)}, u32[]{:S(2)}, u32[]{:S(2)}) collective-permute-start(bf16[512,4,1,32]{0,3,2,1:T(8,128)(2,1)S(1)} %get-tuple-element.41), channel_id=1, source_target_pairs={{0,508},{1,509},{2,510},{3,511},{4,504},{5,505},{6,506},{7,507},{8... | collective-permute-start | bytes 393224 | tf_op jit(solution)/shard_map/ppermute | solution.py:24
  82.4 1.2 %copy-start.3 = (f32[64]{0:T(128)S(1)}, f32[64]{0:T(128)}, u32[]{:S(2)}) copy-start(f32[64]{0:T(128)} %param.5) | copy-start | bytes 772

commit v5 on v4

--- a/solution.py
+++ b/solution.py
@@ -24,10 +24,18 @@
     return lax.ppermute(value, (axis, "chan"), pairs)
 
 
-def haloed(own_block):
-    below = shifted(own_block[:, -1:], "space", 8)
-    above = shifted(own_block[:, :1], "space", -8)
-    widened = jnp.concatenate([below, own_block, above], axis=1)
+def plain_shift(value, axis, steps):
+    count = lax.axis_size(axis)
+    return lax.ppermute(value, axis, [(source, (source + steps) % count) for source in range(count)])
+
+
+def haloed(own_block, size_y):
+    below = plain_shift(own_block[:, -1:], "space", 8)
+    above = plain_shift(own_block[:, :1], "space", -8)
+    gathered = lax.all_gather(own_block, "chan", axis=0, tiled=True)
+    faces = lax.all_gather(jnp.concatenate([below, above], axis=1), "chan", axis=0, tiled=True)
+    widened = jnp.concatenate([faces[:, :1], gathered, faces[:, 1:]], axis=1)
+    widened = widened.reshape(widened.shape[0], widened.shape[1], size_y, -1)
     lower_from = shifted(widened[:, :, -1:], "space", 1)
     upper_from = shifted(widened[:, :, :1], "space", -1)
     place_y = (lax.axis_index("space") + 4) % 8
@@ -66,9 +74,7 @@
     size_y = CY
     size_z = activation.shape[3] // size_y
     own_block = activation[0].astype(jnp.bfloat16).transpose(1, 0, 2)
-    gathered = lax.all_gather(own_block, "chan", axis=0, tiled=True)
-    gathered = gathered.reshape(-1, size_x, size_y, size_z)
-    padded = jnp.pad(haloed(gathered), ((0, 0), (0, 0), (0, 0), (1, 1)))
+    padded = jnp.pad(haloed(own_block, size_y), ((0, 0), (0, 0), (0, 0), (1, 1)))
     total = tap_sum(padded, weight)
     width_out = total.shape[0]
     before = total + conv_bias[:, None]

time: 85.3 us -> 90.3 us (1.059)
  blocking collectives: 21.7 us -> 36.1 us
  waiting for transfers between devices: 15 us -> 4.69 us
  local copies, waits for them, and re-layouts: 10 us -> 13.9 us
  starting transfers between devices: 27.8 us -> 24 us
    ppermute x4 -> x2, starting transfers between devices: 27.8 us -> 11.6 us  [shifted(): return lax.ppermute(value, (axis, 'chan'), pairs)]
    all_gather x1 -> x2, blocking collectives: 21.7 us -> 36.1 us  [the longest x1 21.2 us: haloed(): gathered = lax.all_gather(own_block, 'chan', axis=0, tiled=True)]
    ppermute x0 -> x2, starting transfers between devices: none -> 12.4 us  [plain_shift(): lax.ppermute(value, axis, [(source, (source + steps) % count) for source...]
    ppermute x4 -> x2, waiting for transfers between devices: 15 us -> 4.69 us  [shifted(): return lax.ppermute(value, (axis, 'chan'), pairs)]
    unnamed x10 -> x14, local copies, waits for them, and re-layouts: 1.14 us -> 3.83 us
    slice x1 -> x3, local copies, waits for them, and re-layouts: 0.04 us -> 1.52 us  [the longest x1 0.73 us: haloed(): widened = jnp.concatenate([faces[:, :1], gathered, faces[:, 1:]], axis=1)]
    concatenate x0 -> x2, other arithmetic: none -> 1.3 us  [the longest x1 1.15 us: haloed(): widened = jnp.concatenate([faces[:, :1], gathered, faces[:, 1:]], axis=1)]
    slice x2 -> x1, local copies, waits for them, and re-layouts: 3.58 us -> 3.21 us  [tap_sum(): padded[:, tap_x:tap_x + size_x, tap_y:tap_y + size_y, tap_z:tap_z + size_z]]
  transfers between devices with their start and end apart: 4 -> 4, of which waited for: 3 -> 1; matrix products, arithmetic and copies ran while one was open for 7% -> 7% of each run, Pallas kernels for 0% -> 0%
where the time goes in v5:
time: 90.3 us; the launch traced here: 89.9 us
  blocking collectives  36.1 us (40%)
  starting transfers between devices  24 us (27%)
  local copies, waits for them, and re-layouts  13.9 us (15%)
  other arithmetic  5.55 us (6%)
  matrix products  5.36 us (6%)
  waiting for transfers between devices  4.69 us (5%)
    all_gather x1, blocking collectives, haloed(): gathered = lax.all_gather(own_block, 'chan', axis=0, tiled=True)  21.2 us
    all_gather x1, blocking collectives, haloed(): lax.all_gather(jnp.concatenate([below, above], axis=1), 'chan', axis=0, t...  15 us
    ppermute x2, starting transfers between devices, plain_shift(): lax.ppermute(value, axis, [(source, (source + steps) % count) for source...  12.4 us
    ppermute x2, starting transfers between devices, shifted(): return lax.ppermute(value, (axis, 'chan'), pairs)  11.6 us
    dot_general x9, matrix products, tap_sum(): product = jnp.dot(taps, columns, preferred_element_type=jnp.float32)  5.36 us
    ppermute x2, waiting for transfers between devices, shifted(): return lax.ppermute(value, (axis, 'chan'), pairs)  4.69 us
    reshape x9, local copies, waits for them, and re-layouts, tap_sum(): taps = weight[tap_x, tap_y].transpose(1, 0, 2).reshape(-1, 3 * width_in)  3.92 us
    unnamed x14, local copies, waits for them, and re-layouts  3.83 us
  transfers between devices with their start and end apart: 4, of which 1 were waited for; matrix products, arithmetic and copies ran while one was open for 7% of the time, Pallas kernels for 0%

profile of v5, /device:TPU:1, one launch (start us, length us, event | category | flops | bytes accessed | tf_op | source)
XLA Modules:
  0.0 89.9 jit_solution(7793121754984302458)
XLA Ops:
  0.0 0.9 %convert_element_type.10 = bf16[1,2,64,256]{3,2,1,0:T(8,128)(2,1)S(1)} convert(f32[1,2,64,256]{3,2,1,0:T(8,128)} %param.3) | non-fusion elementwise | flops 32768 | bytes 196608 | tf_op jit(solution)/shard_map/convert_element_type | solution.py:76
  0.9 0.1 copy.46
  1.0 0.1 fusion.20
  1.1 8.3 %collective-permute-start = (bf16[64,1,256]{2,1,0:T(2,128)(2,1)S(1)}, bf16[64,1,256]{2,1,0:T(2,128)(2,1)S(1)}, u32[]{:S(2)}, u32[]{:S(2)}) collective-permute-start(bf16[64,1,256]{2,1,0:T(2,128)(2,1)S(1)} %get-tuple-element.47), channel_id=1, source_target_pairs={{0,64},{8,72},{16,80},{24,88},{32,96},{40,104},{48,112},{56,120},{... | collective-permute-start | bytes 98312 | tf_op jit(solution)/shard_map/ppermute | solution.py:29
  9.4 4.1 %collective-permute-start.1 = (bf16[64,1,256]{2,1,0:T(2,128)(2,1)S(1)}, bf16[64,1,256]{2,1,0:T(2,128)(2,1)S(1)}, u32[]{:S(2)}, u32[]{:S(2)}) collective-permute-start(bf16[64,1,256]{2,1,0:T(2,128)(2,1)S(1)} %get-tuple-element.48), channel_id=1, source_target_pairs={{0,448},{8,456},{16,464},{24,472},{32,480},{40,488},{48,496},{56,5... | collective-permute-start | bytes 98312 | tf_op jit(solution)/shard_map/ppermute | solution.py:29
  13.5 21.2 %all_gather.7 = bf16[512,2,256]{2,1,0:T(2,128)(2,1)S(1)} all-gather(bf16[64,2,256]{2,1,0:T(2,128)(2,1)S(1)} %bitcast.114), channel_id=1, replica_groups=mesh['space'=64,'chan'=8] {'chan'}, dimensions={0}, use_global_device_ids=true | all-gather | bytes 589824 | tf_op jit(solution)/shard_map/all_gather | solution.py:35
  34.7 0.7 copy.19
  35.4 0.0 collective-permute-done
  35.4 0.0 collective-permute-done.1
  35.4 0.2 pad_maximum_fusion.10
  35.6 15.0 %all_gather.6 = bf16[512,2,256]{2,1,0:T(2,128)(2,1)S(1)} all-gather(bf16[64,2,256]{2,1,0:T(2,128)(2,1)S(1)} %pad_maximum_fusion.10), channel_id=1, replica_groups=mesh['space'=64,'chan'=8] {'chan'}, dimensions={0}, use_global_device_ids=true | all-gather | bytes 589824 | tf_op jit(solution)/shard_map/all_gather | solution.py:36
  50.6 0.7 fusion.19
  51.3 1.3 %copy.30 = bf16[512,1,256]{0,2,1:T(8,128)(2,1)} copy(bf16[512,1,256]{2,1,0:T(2,128)(2,1)S(1)} %get-tuple-element.45) | data formatting | bytes 524288
  52.6 0.0 copy-start
  52.6 1.3 %copy.31 = bf16[512,1,256]{0,2,1:T(8,128)(2,1)} copy(bf16[512,1,256]{2,1,0:T(2,128)(2,1)S(1)} %get-tuple-element.46) | data formatting | bytes 524288
  53.9 1.1 %pad_maximum_fusion.9 = bf16[512,4,256]{0,2,1:T(8,128)(2,1)S(1)} fusion(bf16[512,1,256]{0,2,1:T(8,128)(2,1)} %copy.31, bf16[512,2,256]{0,2,1:T(8,128)(2,1)S(1)} %copy.19, bf16[512,1,256]{0,2,1:T(8,128)(2,1)} %copy.30), kind=kLoop, calls=%fused_computation.39 | loop fusion | flops 1048576 | bytes 2097152 | tf_op jit(solution)/shard_map/concatenate | solution.py:37
  55.1 0.7 fusion.18
  55.8 1.9 %collective-permute-start.2 = (bf16[512,4,1,32]{0,3,2,1:T(8,128)(2,1)}, bf16[512,4,1,32]{0,3,2,1:T(8,128)(2,1)}, u32[]{:S(2)}, u32[]{:S(2)}) collective-permute-start(bf16[512,4,1,32]{0,3,2,1:T(8,128)(2,1)} %get-tuple-element.43), channel_id=1, source_target_pairs={{0,8},{1,9},{2,10},{3,11},{4,12},{5,13},{6,14},{7,15},{8,16},{9,17... | collective-permute-start | bytes 393224 | tf_op jit(solution)/shard_map/ppermute | solution.py:24
  57.7 0.0 copy-done
  57.7 1.1 %slice_bitcast_fusion = (bf16[3,8,8,512]{3,2,1,0:T(8,128)(2,1)S(1)}, bf16[3,8,8,512]{3,2,1,0:T(8,128)(2,1)S(1)}, bf16[3,8,8,512]{3,2,1,0:T(8,128)(2,1)}, bf16[3,...) fusion(bf16[3,3,3,64,512]{4,3,2,1,0:T(8,128)(2,1)S(1)} %copy-done), kind=kLoop, calls=%fused_computation.45 | loop fusion | bytes 3538944
  58.8 0.0 copy-start.2
  58.8 0.0 copy-start.1
  58.8 1.0 %copy.33 = bf16[3,8,8,512]{3,2,0,1:T(8,128)(2,1)S(1)} copy(bf16[3,8,8,512]{3,2,1,0:T(8,128)(2,1)} %get-tuple-element.12) | data formatting | bytes 393216 | tf_op jit(solution)/shard_map/reshape | solution.py:65
  59.8 0.0 copy-start.3
  59.8 1.0 %copy.34 = bf16[3,8,8,512]{3,2,0,1:T(8,128)(2,1)S(1)} copy(bf16[3,8,8,512]{3,2,1,0:T(8,128)(2,1)} %get-tuple-element.11) | data formatting | bytes 393216 | tf_op jit(solution)/shard_map/reshape | solution.py:65
  60.8 0.9 %copy.35 = bf16[3,8,8,512]{3,2,0,1:T(8,128)(2,1)S(1)} copy(bf16[3,8,8,512]{3,2,1,0:T(8,128)(2,1)} %get-tuple-element.10) | data formatting | bytes 393216 | tf_op jit(solution)/shard_map/reshape | solution.py:65
  61.7 0.9 %copy.36 = bf16[3,8,8,512]{3,2,0,1:T(8,128)(2,1)S(1)} copy(bf16[3,8,8,512]{3,2,1,0:T(8,128)(2,1)} %get-tuple-element.9) | data formatting | bytes 393216 | tf_op jit(solution)/shard_map/reshape | solution.py:65
  62.7 0.0 copy-done.2
  62.7 0.0 copy-done.1
  62.8 0.0 copy-done.3
  62.8 9.7 %collective-permute-start.3 = (bf16[512,4,1,32]{0,3,2,1:T(8,128)(2,1)S(1)}, bf16[512,4,1,32]{0,3,2,1:T(8,128)(2,1)S(1)}, u32[]{:S(2)}, u32[]{:S(2)}) collective-permute-start(bf16[512,4,1,32]{0,3,2,1:T(8,128)(2,1)S(1)} %copy-done.3), channel_id=1, source_target_pairs={{0,508},{1,509},{2,510},{3,511},{4,504},{5,505},{6,506},{7,507},{8... | collective-permute-start | bytes 393224 | tf_op jit(solution)/shard_map/ppermute | solution.py:24
  72.5 0.0 collective-permute-done.2
  72.5 0.9 %broadcast_select_fusion.1 = bf16[512,4,1,32]{0,3,2,1:T(8,128)(2,1)S(1)} fusion(bf16[512,4,1,32]{0,3,2,1:T(8,128)(2,1)} %collective-permute-done.2, pred[]{:T(512)S(6)} %gt.3), kind=kLoop, calls=%fused_computation.56 | loop fusion | flops 65536 | bytes 262145 | tf_op jit(solution)/shard_map/jit(_where)/select_n | solution.py:42
  73.4 4.7 %collective-permute-done.3 = bf16[512,4,1,32]{0,3,2,1:T(8,128)(2,1)S(1)} collective-permute-done((bf16[512,4,1,32]{0,3,2,1:T(8,128)(2,1)S(1)}, bf16[512,4,1,32]{0,3,2,1:T(8,128)(2,1)S(1)}, u32[]{:S(2)}, u32[]{:S(2)}) %collective-permute-start.3) | collective-permute-done | bytes 131104 | tf_op jit(solution)/shard_map/ppermute | solution.py:24
  78.1 0.9 fusion.5
  79.0 0.3 fusion.13
  79.3 3.2 %fusion.17 = (bf16[512,2,8,32]{0,3,2,1:T(8,128)(2,1)S(1)}, bf16[512,2,8,32]{0,3,2,1:T(8,128)(2,1)S(1)}, bf16[512,2,8,32]{0,3,2,1:T(8,128)(2,1)S(1)}, bf16[512,2,...) fusion(bf16[512,4,10,34]{0,3,2,1:T(8,128)(2,1)S(1)} %fusion.5), kind=kLoop, calls=%fused_computation.59 | loop fusion | bytes 18874368 | tf_op jit(solution)/shard_map/slice | solution.py:57
  82.5 0.3 pad_maximum_fusion.2
  82.8 0.6 fusion.21
  83.4 0.1 pad_maximum_fusion.8
  83.5 0.6 fusion.22
  84.1 0.6 convolution_add_fusion.6
  84.7 0.3 pad_maximum_fusion.4
  85.0 0.6 convolution_add_fusion.5
  85.6 0.6 convolution_add_fusion.4
  86.2 0.3 pad_maximum_fusion.6
  86.5 0.6 convolution_add_fusion.3
  87.1 0.6 convolution_add_fusion.2
  87.7 0.3 fusion.7
  88.0 0.0 copy-start.4
  88.0 0.6 fusion.12
  88.6 0.0 copy-done.4
  88.6 0.6 multiply_maximum_fusion
  89.2 0.7 copy.45
  (6 shorter events, 0.1 us)
Async XLA Ops:
  1.1 34.3 %collective-permute-start = (bf16[64,1,256]{2,1,0:T(2,128)(2,1)S(1)}, bf16[64,1,256]{2,1,0:T(2,128)(2,1)S(1)}, u32[]{:S(2)}, u32[]{:S(2)}) collective-permute-start(bf16[64,1,256]{2,1,0:T(2,128)(2,1)S(1)} %get-tuple-element.47), channel_id=1, source_target_pairs={{0,64},{8,72},{16,80},{24,88},{32,96},{40,104},{48,112},{56,120},{... | collective-permute-start | bytes 98312 | tf_op jit(solution)/shard_map/ppermute | solution.py:29
  9.4 26.1 %collective-permute-start.1 = (bf16[64,1,256]{2,1,0:T(2,128)(2,1)S(1)}, bf16[64,1,256]{2,1,0:T(2,128)(2,1)S(1)}, u32[]{:S(2)}, u32[]{:S(2)}) collective-permute-start(bf16[64,1,256]{2,1,0:T(2,128)(2,1)S(1)} %get-tuple-element.48), channel_id=1, source_target_pairs={{0,448},{8,456},{16,464},{24,472},{32,480},{40,488},{48,496},{56,5... | collective-permute-start | bytes 98312 | tf_op jit(solution)/shard_map/ppermute | solution.py:29
  52.6 5.1 %copy-start = (bf16[3,3,3,64,512]{4,3,2,1,0:T(8,128)(2,1)S(1)}, bf16[3,3,3,64,512]{4,3,2,1,0:T(8,128)(2,1)}, u32[]{:S(2)}) copy-start(bf16[3,3,3,64,512]{4,3,2,1,0:T(8,128)(2,1)} %param.4) | copy-start | bytes 5308420
  55.8 16.7 %collective-permute-start.2 = (bf16[512,4,1,32]{0,3,2,1:T(8,128)(2,1)}, bf16[512,4,1,32]{0,3,2,1:T(8,128)(2,1)}, u32[]{:S(2)}, u32[]{:S(2)}) collective-permute-start(bf16[512,4,1,32]{0,3,2,1:T(8,128)(2,1)} %get-tuple-element.43), channel_id=1, source_target_pairs={{0,8},{1,9},{2,10},{3,11},{4,12},{5,13},{6,14},{7,15},{8,16},{9,17... | collective-permute-start | bytes 393224 | tf_op jit(solution)/shard_map/ppermute | solution.py:24
  58.8 3.9 %copy-start.2 = (bf16[3,8,8,512]{3,2,1,0:T(8,128)(2,1)S(1)}, bf16[3,8,8,512]{3,2,1,0:T(8,128)(2,1)}, u32[]{:S(2)}) copy-start(bf16[3,8,8,512]{3,2,1,0:T(8,128)(2,1)} %get-tuple-element.8) | copy-start | bytes 589828
  58.8 3.9 %copy-start.1 = (bf16[3,8,8,512]{3,2,1,0:T(8,128)(2,1)S(1)}, bf16[3,8,8,512]{3,2,1,0:T(8,128)(2,1)}, u32[]{:S(2)}) copy-start(bf16[3,8,8,512]{3,2,1,0:T(8,128)(2,1)} %get-tuple-element.7) | copy-start | bytes 589828
  59.8 3.0 %copy-start.3 = (bf16[512,4,1,32]{0,3,2,1:T(8,128)(2,1)S(1)}, bf16[512,4,1,32]{0,3,2,1:T(8,128)(2,1)}, u32[]{:S(2)}) copy-start(bf16[512,4,1,32]{0,3,2,1:T(8,128)(2,1)} %get-tuple-element.44) | copy-start | bytes 393220
  62.8 15.3 %collective-permute-start.3 = (bf16[512,4,1,32]{0,3,2,1:T(8,128)(2,1)S(1)}, bf16[512,4,1,32]{0,3,2,1:T(8,128)(2,1)S(1)}, u32[]{:S(2)}, u32[]{:S(2)}) collective-permute-start(bf16[512,4,1,32]{0,3,2,1:T(8,128)(2,1)S(1)} %copy-done.3), channel_id=1, source_target_pairs={{0,508},{1,509},{2,510},{3,511},{4,504},{5,505},{6,506},{7,507},{8... | collective-permute-start | bytes 393224 | tf_op jit(solution)/shard_map/ppermute | solution.py:24
  88.0 0.7 copy-start.4

commit v6 on v4

--- a/solution.py
+++ b/solution.py
@@ -68,9 +68,16 @@
     own_block = activation[0].astype(jnp.bfloat16).transpose(1, 0, 2)
     gathered = lax.all_gather(own_block, "chan", axis=0, tiled=True)
     gathered = gathered.reshape(-1, size_x, size_y, size_z)
-    padded = jnp.pad(haloed(gathered), ((0, 0), (0, 0), (0, 0), (1, 1)))
-    total = tap_sum(padded, weight)
+    total = lax.conv_general_dilated(
+        haloed(gathered)[None],
+        weight,
+        window_strides=(1, 1, 1),
+        padding=((0, 0), (0, 0), (1, 1)),
+        dimension_numbers=("NCDHW", "DHWOI", "NCDHW"),
+        preferred_element_type=jnp.float32,
+    )[0]
     width_out = total.shape[0]
+    total = total.reshape(width_out, -1)
     before = total + conv_bias[:, None]
     result = jnp.maximum(before, negative_slope * before)
     result = result.reshape(width_out, size_x, size_y * size_z).transpose(1, 0, 2)

time: 85.3 us -> 76.5 us (0.90)
  local copies, waits for them, and re-layouts: 10 us -> 4.57 us
  other arithmetic: 4.71 us -> 1.36 us
  waiting for transfers between devices: 15 us -> 15.9 us
    dot_general x9 -> x0, matrix products: 5.34 us -> none  [tap_sum(): product = jnp.dot(taps, columns, preferred_element_type=jnp.float32)]
    conv_general_dilated x0 -> x1, matrix products: none -> 4.72 us  [body(): lax.conv_general_dilated(haloed(gathered)[None], weight, window_strides=(...]
    reshape x10 -> x0, local copies, waits for them, and re-layouts: 4.55 us -> none  [the longest x9 3.89 us: tap_sum(): taps = weight[tap_x, tap_y].transpose(1, 0, 2).reshape(-1, 3 * width_in)]
    slice x2 -> x0, local copies, waits for them, and re-layouts: 3.58 us -> none  [tap_sum(): padded[:, tap_x:tap_x + size_x, tap_y:tap_y + size_y, tap_z:tap_z + size_z]]
    concatenate x9 -> x0, other arithmetic: 2.17 us -> none  [the longest x2 1.17 us: haloed(): return jnp.concatenate([lower_rim, widened, upper_rim], axis=2)]
    broadcast_in_dim x0 -> x2, local copies, waits for them, and re-layouts: none -> 1.42 us  [the longest x1 0.77 us: body(): return result[None]]
    ppermute x4, waiting for transfers between devices: 15 us -> 15.9 us  [shifted(): return lax.ppermute(value, (axis, 'chan'), pairs)]
    select_n x1, other arithmetic: 0.93 us -> 0.01 us  [haloed(): lower_rim = jnp.where(place_y > 0, lower_from, jnp.zeros_like(lower_from))]
  transfers between devices with their start and end apart: 4 -> 4, of which waited for: 3 -> 4; matrix products, arithmetic and copies ran while one was open for 7% -> 0% of each run, Pallas kernels for 0% -> 0%
where the time goes in v6:
time: 76.5 us; the launch traced here: 76.3 us
  starting transfers between devices  27.8 us (36%)
  blocking collectives  21.7 us (28%)
  waiting for transfers between devices  15.9 us (21%)
  matrix products  4.72 us (6%)
  local copies, waits for them, and re-layouts  4.57 us (6%)
  other arithmetic  1.36 us (2%)
    ppermute x4, starting transfers between devices, shifted(): return lax.ppermute(value, (axis, 'chan'), pairs)  27.8 us
    all_gather x1, blocking collectives, body(): gathered = lax.all_gather(own_block, 'chan', axis=0, tiled=True)  21.7 us
    ppermute x4, waiting for transfers between devices, shifted(): return lax.ppermute(value, (axis, 'chan'), pairs)  15.9 us
    conv_general_dilated x1, matrix products, body(): lax.conv_general_dilated(haloed(gathered)[None], weight, window_strides=(...  4.72 us
    unnamed x8, local copies, waits for them, and re-layouts  1.76 us
  transfers between devices with their start and end apart: 4, of which 4 were waited for; matrix products, arithmetic and copies ran while one was open for 0% of the time, Pallas kernels for 0%

profile of v6, /device:TPU:1, one launch (start us, length us, event | category | flops | bytes accessed | tf_op | source)
XLA Modules:
  0.0 76.3 jit_solution(4816351810197598926)
XLA Ops:
  0.0 0.0 copy-start
  0.0 1.0 %convert_element_type.8 = bf16[1,2,64,256]{3,2,1,0:T(8,128)(2,1)S(1)} convert(f32[1,2,64,256]{3,2,1,0:T(8,128)} %param.3) | non-fusion elementwise | flops 32768 | bytes 196608 | tf_op jit(solution)/shard_map/convert_element_type | solution.py:68
  1.0 0.1 copy.22
  1.1 21.7 %all_gather.3 = bf16[512,2,256]{2,1,0:T(2,128)(2,1)S(1)} all-gather(bf16[64,2,256]{2,1,0:T(2,128)(2,1)S(1)} %bitcast.29), channel_id=1, replica_groups=mesh['space'=64,'chan'=8] {'chan'}, dimensions={0}, use_global_device_ids=true | all-gather | bytes 589824 | tf_op jit(solution)/shard_map/all_gather | solution.py:69
  22.9 0.7 copy.12
  23.6 1.9 %collective-permute-start = (bf16[512,1,8,32]{0,3,2,1:T(8,128)(2,1)S(1)}, bf16[512,1,8,32]{0,3,2,1:T(8,128)(2,1)S(1)}, u32[]{:S(2)}, u32[]{:S(2)}) collective-permute-start(bf16[512,1,8,32]{0,3,2,1:T(8,128)(2,1)S(1)} %get-tuple-element.7), channel_id=1, source_target_pairs={{0,68},{1,69},{2,70},{3,71},{4,64},{5,65},{6,66},{7,67},{8,76},{9,... | collective-permute-start | bytes 786440 | tf_op jit(solution)/shard_map/ppermute | solution.py:24
  25.6 7.6 %collective-permute-start.1 = (bf16[512,1,8,32]{0,3,2,1:T(8,128)(2,1)S(1)}, bf16[512,1,8,32]{0,3,2,1:T(8,128)(2,1)S(1)}, u32[]{:S(2)}, u32[]{:S(2)}) collective-permute-start(bf16[512,1,8,32]{0,3,2,1:T(8,128)(2,1)S(1)} %get-tuple-element.8), channel_id=1, source_target_pairs={{0,452},{1,453},{2,454},{3,455},{4,448},{5,449},{6,450},{7,451},{8... | collective-permute-start | bytes 786440 | tf_op jit(solution)/shard_map/ppermute | solution.py:24
  33.2 8.2 %collective-permute-done = bf16[512,1,8,32]{0,3,2,1:T(8,128)(2,1)S(1)} collective-permute-done((bf16[512,1,8,32]{0,3,2,1:T(8,128)(2,1)S(1)}, bf16[512,1,8,32]{0,3,2,1:T(8,128)(2,1)S(1)}, u32[]{:S(2)}, u32[]{:S(2)}) %collective-permute-start) | collective-permute-done | bytes 262176 | tf_op jit(solution)/shard_map/ppermute | solution.py:24
  41.4 5.6 %collective-permute-done.1 = bf16[512,1,8,32]{0,3,2,1:T(8,128)(2,1)S(1)} collective-permute-done((bf16[512,1,8,32]{0,3,2,1:T(8,128)(2,1)S(1)}, bf16[512,1,8,32]{0,3,2,1:T(8,128)(2,1)S(1)}, u32[]{:S(2)}, u32[]{:S(2)}) %collective-permute-start.1) | collective-permute-done | bytes 262176 | tf_op jit(solution)/shard_map/ppermute | solution.py:24
  47.0 3.6 %collective-permute-start.2 = (bf16[512,4,1,32]{0,3,2,1:T(8,128)(2,1)S(1)}, bf16[512,4,1,32]{0,3,2,1:T(8,128)(2,1)S(1)}, u32[]{:S(2)}, u32[]{:S(2)}) collective-permute-start(bf16[512,4,1,32]{0,3,2,1:T(8,128)(2,1)S(1)} %get-tuple-element.5), channel_id=1, source_target_pairs={{0,8},{1,9},{2,10},{3,11},{4,12},{5,13},{6,14},{7,15},{8,16},{9,17... | collective-permute-start | bytes 393224 | tf_op jit(solution)/shard_map/ppermute | solution.py:24
  50.6 14.7 %collective-permute-start.3 = (bf16[512,4,1,32]{0,3,2,1:T(8,128)(2,1)S(1)}, bf16[512,4,1,32]{0,3,2,1:T(8,128)(2,1)S(1)}, u32[]{:S(2)}, u32[]{:S(2)}) collective-permute-start(bf16[512,4,1,32]{0,3,2,1:T(8,128)(2,1)S(1)} %get-tuple-element.6), channel_id=1, source_target_pairs={{0,508},{1,509},{2,510},{3,511},{4,504},{5,505},{6,506},{7,507},{8... | collective-permute-start | bytes 393224 | tf_op jit(solution)/shard_map/ppermute | solution.py:24
  65.3 1.3 %collective-permute-done.2 = bf16[512,4,1,32]{0,3,2,1:T(8,128)(2,1)S(1)} collective-permute-done((bf16[512,4,1,32]{0,3,2,1:T(8,128)(2,1)S(1)}, bf16[512,4,1,32]{0,3,2,1:T(8,128)(2,1)S(1)}, u32[]{:S(2)}, u32[]{:S(2)}) %collective-permute-start.2) | collective-permute-done | bytes 131104 | tf_op jit(solution)/shard_map/ppermute | solution.py:24
  66.6 0.9 %collective-permute-done.3 = bf16[512,4,1,32]{0,3,2,1:T(8,128)(2,1)S(1)} collective-permute-done((bf16[512,4,1,32]{0,3,2,1:T(8,128)(2,1)S(1)}, bf16[512,4,1,32]{0,3,2,1:T(8,128)(2,1)S(1)}, u32[]{:S(2)}, u32[]{:S(2)}) %collective-permute-start.3) | collective-permute-done | bytes 131104 | tf_op jit(solution)/shard_map/ppermute | solution.py:24
  67.5 0.2 maximum_bitcast_fusion
  67.7 1.0 %copy.19 = bf16[512,4,10,1,32]{0,1,4,2,3:T(4,128)(2,1)S(1)} copy(bf16[512,4,10,1,32]{0,4,2,1,3:T(8,128)(2,1)S(1)} %maximum_bitcast_fusion) | data formatting | bytes 2621440
  68.8 0.7 pad.clone
  69.4 0.0 copy-start.2
  69.4 0.3 copy.15
  69.8 0.2 slice.20
  69.9 0.0 copy-done
  69.9 0.2 copy-done.2
  70.1 4.7 %fusion.8 = f32[2,8,8,5,64]{4,2,3,1,0:T(8,128)S(1)} fusion(bf16[3,3,3,64,512]{4,3,2,1,0:T(8,128)(2,1)S(1)} %copy-done, bf16[512,4,10,1,7,2]{0,4,5,2,1,3:T(8,128)(2,1)S(1)} %slice.20, bf16[512,4,10,1,8,5]{0,4,5,2,1,3:T(8,128)(2,1)S(1)} %copy.15, pred[8,5]{0,1:T(8,128)(4,1)S(1)} %copy-done.2), kind=kOutput, calls=%fused_computation.9 | convolution fusion | flops 1139384320 | bytes 4145192 | tf_op jit(solution)/shard_map/conv_general_dilated | solution.py:71
  74.8 0.0 copy-start.1
  74.8 0.1 copy.16
  74.9 0.1 copy.17
  75.0 0.5 copy-done.1
  75.5 0.8 %copy.18 = f32[1,2,64,256]{3,2,1,0:T(8,128)} copy(f32[1,2,64,256]{2,3,1,0:T(8,128)S(1)} %fusion.12) | data formatting | bytes 262144 | tf_op jit(solution)/shard_map/broadcast_in_dim | solution.py:84
  (6 shorter events, 0.1 us)
Async XLA Ops:
  0.0 69.9 %copy-start = (bf16[3,3,3,64,512]{4,3,2,1,0:T(8,128)(2,1)S(1)}, bf16[3,3,3,64,512]{4,3,2,1,0:T(8,128)(2,1)}, u32[]{:S(2)}) copy-start(bf16[3,3,3,64,512]{4,3,2,1,0:T(8,128)(2,1)} %param.4) | copy-start | bytes 5308420
  23.6 17.7 %collective-permute-start = (bf16[512,1,8,32]{0,3,2,1:T(8,128)(2,1)S(1)}, bf16[512,1,8,32]{0,3,2,1:T(8,128)(2,1)S(1)}, u32[]{:S(2)}, u32[]{:S(2)}) collective-permute-start(bf16[512,1,8,32]{0,3,2,1:T(8,128)(2,1)S(1)} %get-tuple-element.7), channel_id=1, source_target_pairs={{0,68},{1,69},{2,70},{3,71},{4,64},{5,65},{6,66},{7,67},{8,76},{9,... | collective-permute-start | bytes 786440 | tf_op jit(solution)/shard_map/ppermute | solution.py:24
  25.6 21.4 %collective-permute-start.1 = (bf16[512,1,8,32]{0,3,2,1:T(8,128)(2,1)S(1)}, bf16[512,1,8,32]{0,3,2,1:T(8,128)(2,1)S(1)}, u32[]{:S(2)}, u32[]{:S(2)}) collective-permute-start(bf16[512,1,8,32]{0,3,2,1:T(8,128)(2,1)S(1)} %get-tuple-element.8), channel_id=1, source_target_pairs={{0,452},{1,453},{2,454},{3,455},{4,448},{5,449},{6,450},{7,451},{8... | collective-permute-start | bytes 786440 | tf_op jit(solution)/shard_map/ppermute | solution.py:24
  47.0 19.6 %collective-permute-start.2 = (bf16[512,4,1,32]{0,3,2,1:T(8,128)(2,1)S(1)}, bf16[512,4,1,32]{0,3,2,1:T(8,128)(2,1)S(1)}, u32[]{:S(2)}, u32[]{:S(2)}) collective-permute-start(bf16[512,4,1,32]{0,3,2,1:T(8,128)(2,1)S(1)} %get-tuple-element.5), channel_id=1, source_target_pairs={{0,8},{1,9},{2,10},{3,11},{4,12},{5,13},{6,14},{7,15},{8,16},{9,17... | collective-permute-start | bytes 393224 | tf_op jit(solution)/shard_map/ppermute | solution.py:24
  50.6 16.9 %collective-permute-start.3 = (bf16[512,4,1,32]{0,3,2,1:T(8,128)(2,1)S(1)}, bf16[512,4,1,32]{0,3,2,1:T(8,128)(2,1)S(1)}, u32[]{:S(2)}, u32[]{:S(2)}) collective-permute-start(bf16[512,4,1,32]{0,3,2,1:T(8,128)(2,1)S(1)} %get-tuple-element.6), channel_id=1, source_target_pairs={{0,508},{1,509},{2,510},{3,511},{4,504},{5,505},{6,506},{7,507},{8... | collective-permute-start | bytes 393224 | tf_op jit(solution)/shard_map/ppermute | solution.py:24
  69.4 0.7 copy-start.2
  74.8 0.7 copy-start.1

commit v7 on v4

v7 whole, which is shorter than its diff:
```python
import jax
import jax.numpy as jnp
from jax import lax
from jax.sharding import PartitionSpec as P

CY = 8


negative_slope = 0.3


def shifted(value, axis, steps):
    count = lax.axis_size(axis)
    width = lax.axis_size("chan")
    run_y = width // 2
    pairs = []
    for source in range(count):
        target = (source + steps) % count
        crosses = (source // CY) % 2 != (target // CY) % 2
        for lane in range(width):
            place, core = divmod(lane, 2)
            moved = ((place + run_y // 2) % run_y) * 2 + core if crosses else lane
            pairs.append((source * width + lane, target * width + moved))
    return lax.ppermute(value, (axis, "chan"), pairs)


def conv(field, taps, padding):
    return lax.conv_general_dilated(
        field[None],
        taps,
        window_strides=(1, 1, 1),
        padding=padding,
        dimension_numbers=("NCDHW", "DHWOI", "NCDHW"),
        preferred_element_type=jnp.float32,
    )[0]


def body(activation, weight, conv_bias):
    size_x = activation.shape[1]
    size_y = CY
    size_z = activation.shape[3] // size_y
    own_block = activation[0].astype(jnp.bfloat16).transpose(1, 0, 2)
    gathered = lax.all_gather(own_block, "chan", axis=0, tiled=True)
    gathered = gathered.reshape(-1, size_x, size_y, size_z)
    below = shifted(gathered[:, -1:], "space", 8)
    above = shifted(gathered[:, :1], "space", -8)
    own_part = conv(gathered, weight, ((1, 1), (1, 1), (1, 1)))
    face_part = jnp.concatenate(
        [
            conv(below, weight[:1], ((0, 0), (1, 1), (1, 1))),
            conv(above, weight[2:], ((0, 0), (1, 1), (1, 1))),
        ],
        axis=1,
    )
    widened = jnp.concatenate([below, gathered, above], axis=1)
    lower_from = shifted(widened[:, :, -1:], "space", 1)
    upper_from = shifted(widened[:, :, :1], "space", -1)
    place_y = (lax.axis_index("space") + 4) % 8
    lower_rim = jnp.where(place_y > 0, lower_from, jnp.zeros_like(lower_from))
    upper_rim = jnp.where(place_y < 7, upper_from, jnp.zeros_like(upper_from))
    lower_part = conv(lower_rim, weight[:, :1], ((0, 0), (0, 0), (1, 1)))
    upper_part = conv(upper_rim, weight[:, 2:], ((0, 0), (0, 0), (1, 1)))
    width_out = own_part.shape[0]
    middle = jnp.zeros((width_out, size_x, size_y - 2, size_z), jnp.float32)
    rim_part = jnp.concatenate([lower_part, middle, upper_part], axis=2)
    total = (own_part + face_part + rim_part).reshape(width_out, -1)
    before = total + conv_bias[:, None]
    result = jnp.maximum(before, negative_slope * before)
    result = result.reshape(width_out, size_x, size_y * size_z).transpose(1, 0, 2)
    return result[None]


def solution(mesh):
    placed = (P("space", None, "chan", None), P(None, None, None, "chan", None), P("chan"))
    return jax.shard_map(
        body, mesh=mesh, in_specs=placed, out_specs=P("space", None, "chan", None), check_vma=False
    )
```

time: 85.3 us -> 70.5 us (0.83)
  waiting for transfers between devices: 15 us -> 7.04 us
  local copies, waits for them, and re-layouts: 10 us -> 4.83 us
  other arithmetic: 4.71 us -> 1.14 us
  matrix products: 5.34 us -> 7.24 us
    ppermute x4, waiting for transfers between devices: 15 us -> 7.04 us  [shifted(): return lax.ppermute(value, (axis, 'chan'), pairs)]
    conv_general_dilated x0 -> x5, matrix products: none -> 7.24 us  [conv(): lax.conv_general_dilated(field[None], taps, window_strides=(1, 1, 1), pad...]
    dot_general x9 -> x0, matrix products: 5.34 us -> none  [tap_sum(): product = jnp.dot(taps, columns, preferred_element_type=jnp.float32)]
    reshape x10 -> x0, local copies, waits for them, and re-layouts: 4.55 us -> none  [the longest x9 3.89 us: tap_sum(): taps = weight[tap_x, tap_y].transpose(1, 0, 2).reshape(-1, 3 * width_in)]
    slice x3 -> x1, local copies, waits for them, and re-layouts: 3.61 us -> 0.04 us  [body(): below = shifted(gathered[:, -1:], 'space', 8)]
    concatenate x9 -> x1, other arithmetic: 2.17 us -> 0.09 us  [body(): rim_part = jnp.concatenate([lower_part, middle, upper_part], axis=2)]
    conv_general_dilated x0 -> x21, local copies, waits for them, and re-layouts: none -> 0.95 us  [conv(): lax.conv_general_dilated(field[None], taps, window_strides=(1, 1, 1), pad...]
    select_n x2 -> x0, other arithmetic: 0.94 us -> none  [the longest x1 0.93 us: haloed(): lower_rim = jnp.where(place_y > 0, lower_from, jnp.zeros_like(lower_from))]
  transfers between devices with their start and end apart: 4 -> 4, of which waited for: 3 -> 2; matrix products, arithmetic and copies ran while one was open for 7% -> 12% of each run, Pallas kernels for 0% -> 0%
where the time goes in v7:
time: 70.5 us; the launch traced here: 70.3 us
  starting transfers between devices  27.8 us (39%)
  blocking collectives  21.7 us (31%)
  matrix products  7.24 us (10%)
  waiting for transfers between devices  7.04 us (10%)
  local copies, waits for them, and re-layouts  4.83 us (7%)
  other arithmetic  1.14 us (2%)
    ppermute x4, starting transfers between devices, shifted(): return lax.ppermute(value, (axis, 'chan'), pairs)  27.8 us
    all_gather x1, blocking collectives, body(): gathered = lax.all_gather(own_block, 'chan', axis=0, tiled=True)  21.7 us
    conv_general_dilated x5, matrix products, conv(): lax.conv_general_dilated(field[None], taps, window_strides=(1, 1, 1), pad...  7.24 us
    ppermute x4, waiting for transfers between devices, shifted(): return lax.ppermute(value, (axis, 'chan'), pairs)  7.04 us
    unnamed x14, local copies, waits for them, and re-layouts  2.03 us
  transfers between devices with their start and end apart: 4, of which 2 were waited for; matrix products, arithmetic and copies ran while one was open for 12% of the time, Pallas kernels for 0%

profile of v7, /device:TPU:1, one launch (start us, length us, event | category | flops | bytes accessed | tf_op | source)
XLA Modules:
  0.0 70.3 jit_solution(6176775314418931451)
XLA Ops:
  0.0 0.9 %convert_element_type.8 = bf16[1,2,64,256]{3,2,1,0:T(8,128)(2,1)S(1)} convert(f32[1,2,64,256]{3,2,1,0:T(8,128)} %param.3) | non-fusion elementwise | flops 32768 | bytes 196608 | tf_op jit(solution)/shard_map/convert_element_type | solution.py:42
  0.9 0.1 copy.67
  1.0 21.7 %all_gather.3 = bf16[512,2,256]{2,1,0:T(2,128)(2,1)S(1)} all-gather(bf16[64,2,256]{2,1,0:T(2,128)(2,1)S(1)} %bitcast.78), channel_id=1, replica_groups=mesh['space'=64,'chan'=8] {'chan'}, dimensions={0}, use_global_device_ids=true | all-gather | bytes 589824 | tf_op jit(solution)/shard_map/all_gather | solution.py:43
  22.7 0.7 %copy.32 = bf16[512,2,256]{0,2,1:T(8,128)(2,1)S(1)} copy(bf16[512,2,256]{2,1,0:T(2,128)(2,1)S(1)} %all_gather.3) | data formatting | bytes 1048576 | tf_op jit(solution)/shard_map/all_gather | solution.py:43
  23.5 1.9 %collective-permute-start = (bf16[512,1,8,32]{0,3,2,1:T(8,128)(2,1)S(1)}, bf16[512,1,8,32]{0,3,2,1:T(8,128)(2,1)S(1)}, u32[]{:S(2)}, u32[]{:S(2)}) collective-permute-start(bf16[512,1,8,32]{0,3,2,1:T(8,128)(2,1)S(1)} %get-tuple-element.7), channel_id=1, source_target_pairs={{0,68},{1,69},{2,70},{3,71},{4,64},{5,65},{6,66},{7,67},{8,76},{9,... | collective-permute-start | bytes 786440 | tf_op jit(solution)/shard_map/ppermute | solution.py:24
  25.4 7.6 %collective-permute-start.1 = (bf16[512,1,8,32]{0,3,2,1:T(8,128)(2,1)S(1)}, bf16[512,1,8,32]{0,3,2,1:T(8,128)(2,1)S(1)}, u32[]{:S(2)}, u32[]{:S(2)}) collective-permute-start(bf16[512,1,8,32]{0,3,2,1:T(8,128)(2,1)S(1)} %get-tuple-element.8), channel_id=1, source_target_pairs={{0,452},{1,453},{2,454},{3,455},{4,448},{5,449},{6,450},{7,451},{8... | collective-permute-start | bytes 786440 | tf_op jit(solution)/shard_map/ppermute | solution.py:24
  33.0 0.3 copy.60
  33.3 0.0 copy-start.1
  33.3 0.0 copy-start.3
  33.4 0.2 copy.35
  33.6 0.1 slice.42
  33.7 1.1 %copy-done.1 = bf16[3,3,3,64,512]{4,3,2,1,0:T(8,128)(2,1)S(1)} copy-done((bf16[3,3,3,64,512]{4,3,2,1,0:T(8,128)(2,1)S(1)}, bf16[3,3,3,64,512]{4,3,2,1,0:T(8,128)(2,1)}, u32[]{:S(2)}) %copy-start.1) | copy-done | bytes 1769496
  34.8 0.0 copy-done.3
  34.8 4.7 %convolution_select_fusion = f32[2,8,8,5,64]{4,2,3,1,0:T(8,128)S(1)} fusion(bf16[3,3,3,64,512]{4,3,2,1,0:T(8,128)(2,1)S(1)} %copy-done.1, bf16[512,2,8,1,7,2]{0,4,5,2,1,3:T(8,128)(2,1)S(1)} %slice.42, bf16[512,2,8,1,8,5]{0,4,5,2,1,3:T(8,128)(2,1)S(1)} %copy.35, pred[8,5]{0,1:T(8,128)(4,1)S(1)} %copy-done.3), kind=kOutput, calls=%fused_computation.2 | convolution fusion | flops 694853632 | bytes 2818088 | tf_op jit(solution)/shard_map/conv_general_dilated | solution.py:28
  39.6 0.1 copy.36
  39.6 0.1 copy.37
  39.7 0.0 copy-start.2
  39.7 0.1 pad.11.clone
  39.8 1.4 %collective-permute-done = bf16[512,1,8,32]{0,3,2,1:T(8,128)(2,1)S(1)} collective-permute-done((bf16[512,1,8,32]{0,3,2,1:T(8,128)(2,1)S(1)}, bf16[512,1,8,32]{0,3,2,1:T(8,128)(2,1)S(1)}, u32[]{:S(2)}, u32[]{:S(2)}) %collective-permute-start) | collective-permute-done | bytes 262176 | tf_op jit(solution)/shard_map/ppermute | solution.py:24
  41.2 5.6 %collective-permute-done.1 = bf16[512,1,8,32]{0,3,2,1:T(8,128)(2,1)S(1)} collective-permute-done((bf16[512,1,8,32]{0,3,2,1:T(8,128)(2,1)S(1)}, bf16[512,1,8,32]{0,3,2,1:T(8,128)(2,1)S(1)}, u32[]{:S(2)}, u32[]{:S(2)}) %collective-permute-start.1) | collective-permute-done | bytes 262176 | tf_op jit(solution)/shard_map/ppermute | solution.py:24
  46.9 3.6 %collective-permute-start.2 = (bf16[512,4,1,32]{0,3,2,1:T(8,128)(2,1)S(1)}, bf16[512,4,1,32]{0,3,2,1:T(8,128)(2,1)S(1)}, u32[]{:S(2)}, u32[]{:S(2)}) collective-permute-start(bf16[512,4,1,32]{0,3,2,1:T(8,128)(2,1)S(1)} %get-tuple-element.5), channel_id=1, source_target_pairs={{0,8},{1,9},{2,10},{3,11},{4,12},{5,13},{6,14},{7,15},{8,16},{9,17... | collective-permute-start | bytes 393224 | tf_op jit(solution)/shard_map/ppermute | solution.py:24
  50.4 14.7 %collective-permute-start.3 = (bf16[512,4,1,32]{0,3,2,1:T(8,128)(2,1)S(1)}, bf16[512,4,1,32]{0,3,2,1:T(8,128)(2,1)S(1)}, u32[]{:S(2)}, u32[]{:S(2)}) collective-permute-start(bf16[512,4,1,32]{0,3,2,1:T(8,128)(2,1)S(1)} %get-tuple-element.6), channel_id=1, source_target_pairs={{0,508},{1,509},{2,510},{3,511},{4,504},{5,505},{6,506},{7,507},{8... | collective-permute-start | bytes 393224 | tf_op jit(solution)/shard_map/ppermute | solution.py:24
  65.2 0.2 copy.61
  65.4 0.1 copy.41
  65.5 0.0 copy-done.2
  65.5 0.9 %convolution_select_fusion.2 = f32[1,8,8,5,64]{4,2,3,1,0:T(8,128)S(1)} fusion(bf16[3,3,3,64,512]{4,3,2,1,0:T(8,128)(2,1)S(1)} %copy-done.2, bf16[512,1,8,1,7,2]{0,4,5,2,3,1:T(8,128)(2,1)S(1)} %slice.45, bf16[512,1,8,1,8,5]{0,4,5,2,3,1:T(8,128)(2,1)S(1)} %copy.41, pred[8,5]{0,1:T(8,128)(4,1)S(1)} %copy-done.3), kind=kOutput, calls=%fused_computation.4 | convolution fusion | flops 174411776 | bytes 1131520 | tf_op jit(solution)/shard_map/conv_general_dilated | solution.py:28
  66.6 0.2 copy.62
  66.8 0.1 copy.46
  66.9 0.9 %convolution_select_fusion.1 = f32[1,8,8,5,64]{4,2,3,1,0:T(8,128)S(1)} fusion(bf16[3,3,3,64,512]{4,3,2,1,0:T(8,128)(2,1)S(1)} %copy-done.2, bf16[512,1,8,1,7,2]{0,4,5,2,3,1:T(8,128)(2,1)S(1)} %slice.48, bf16[512,1,8,1,8,5]{0,4,5,2,3,1:T(8,128)(2,1)S(1)} %copy.46, pred[8,5]{0,1:T(8,128)(4,1)S(1)} %copy-done.3), kind=kOutput, calls=%fused_computation.3 | convolution fusion | flops 174411776 | bytes 1131520 | tf_op jit(solution)/shard_map/conv_general_dilated | solution.py:28
  67.9 0.0 collective-permute-done.2
  68.0 0.1 copy.63
  68.1 0.1 pad.6.clone
  68.2 0.3 convolution_select_fusion.4
  68.6 0.0 copy-start
  68.6 0.0 collective-permute-done.3
  68.6 0.1 copy.64
  68.8 0.1 pad.8.clone
  68.9 0.3 convolution_select_fusion.3
  69.3 0.1 pad_maximum_fusion
  69.4 0.0 copy-done
  69.4 0.1 fusion.28
  69.5 0.8 %copy.59 = f32[1,2,64,256]{3,2,1,0:T(8,128)} copy(f32[1,2,64,256]{2,3,1,0:T(8,128)S(1)} %fusion.28) | data formatting | bytes 262144 | tf_op jit(solution)/shard_map/broadcast_in_dim | solution.py:70
  (27 shorter events, 0.6 us)
Async XLA Ops:
  23.5 17.7 %collective-permute-start = (bf16[512,1,8,32]{0,3,2,1:T(8,128)(2,1)S(1)}, bf16[512,1,8,32]{0,3,2,1:T(8,128)(2,1)S(1)}, u32[]{:S(2)}, u32[]{:S(2)}) collective-permute-start(bf16[512,1,8,32]{0,3,2,1:T(8,128)(2,1)S(1)} %get-tuple-element.7), channel_id=1, source_target_pairs={{0,68},{1,69},{2,70},{3,71},{4,64},{5,65},{6,66},{7,67},{8,76},{9,... | collective-permute-start | bytes 786440 | tf_op jit(solution)/shard_map/ppermute | solution.py:24
  25.4 21.4 %collective-permute-start.1 = (bf16[512,1,8,32]{0,3,2,1:T(8,128)(2,1)S(1)}, bf16[512,1,8,32]{0,3,2,1:T(8,128)(2,1)S(1)}, u32[]{:S(2)}, u32[]{:S(2)}) collective-permute-start(bf16[512,1,8,32]{0,3,2,1:T(8,128)(2,1)S(1)} %get-tuple-element.8), channel_id=1, source_target_pairs={{0,452},{1,453},{2,454},{3,455},{4,448},{5,449},{6,450},{7,451},{8... | collective-permute-start | bytes 786440 | tf_op jit(solution)/shard_map/ppermute | solution.py:24
  33.3 1.5 %copy-start.1 = (bf16[3,3,3,64,512]{4,3,2,1,0:T(8,128)(2,1)S(1)}, bf16[3,3,3,64,512]{4,3,2,1,0:T(8,128)(2,1)}, u32[]{:S(2)}) copy-start(bf16[3,3,3,64,512]{4,3,2,1,0:T(8,128)(2,1)} %param.4) | copy-start | bytes 5308420
  33.3 1.5 %copy-start.3 = (pred[8,5]{0,1:T(8,128)(4,1)S(1)}, pred[8,5]{0,1:T(8,128)(4,1)}, u32[]{:S(2)}) copy-start(pred[8,5]{0,1:T(8,128)(4,1)} %constant.50) | copy-start | bytes 124
  39.7 25.8 %copy-start.2 = (bf16[3,3,3,64,512]{4,3,2,1,0:T(8,128)(2,1)S(1)}, bf16[3,3,3,64,512]{4,3,2,1,0:T(8,128)(2,1)}, u32[]{:S(2)}) copy-start(bf16[3,3,3,64,512]{4,3,2,1,0:T(8,128)(2,1)} %param.4) | copy-start | bytes 5308420
  46.9 21.0 %collective-permute-start.2 = (bf16[512,4,1,32]{0,3,2,1:T(8,128)(2,1)S(1)}, bf16[512,4,1,32]{0,3,2,1:T(8,128)(2,1)S(1)}, u32[]{:S(2)}, u32[]{:S(2)}) collective-permute-start(bf16[512,4,1,32]{0,3,2,1:T(8,128)(2,1)S(1)} %get-tuple-element.5), channel_id=1, source_target_pairs={{0,8},{1,9},{2,10},{3,11},{4,12},{5,13},{6,14},{7,15},{8,16},{9,17... | collective-permute-start | bytes 393224 | tf_op jit(solution)/shard_map/ppermute | solution.py:24
  50.4 18.2 %collective-permute-start.3 = (bf16[512,4,1,32]{0,3,2,1:T(8,128)(2,1)S(1)}, bf16[512,4,1,32]{0,3,2,1:T(8,128)(2,1)S(1)}, u32[]{:S(2)}, u32[]{:S(2)}) collective-permute-start(bf16[512,4,1,32]{0,3,2,1:T(8,128)(2,1)S(1)} %get-tuple-element.6), channel_id=1, source_target_pairs={{0,508},{1,509},{2,510},{3,511},{4,504},{5,505},{6,506},{7,507},{8... | collective-permute-start | bytes 393224 | tf_op jit(solution)/shard_map/ppermute | solution.py:24
  68.6 0.8 %copy-start = (f32[64]{0:T(128)S(1)}, f32[64]{0:T(128)}, u32[]{:S(2)}) copy-start(f32[64]{0:T(128)} %param.5) | copy-start | bytes 772

commit v8 on v7

--- a/solution.py
+++ b/solution.py
@@ -9,19 +9,23 @@
 negative_slope = 0.3
 
 
-def shifted(value, axis, steps):
+def faces_from(lower_source, upper_source, axis, steps):
     count = lax.axis_size(axis)
     width = lax.axis_size("chan")
     run_y = width // 2
     pairs = []
     for source in range(count):
-        target = (source + steps) % count
-        crosses = (source // CY) % 2 != (target // CY) % 2
         for lane in range(width):
             place, core = divmod(lane, 2)
+            target = (source + (steps if core == 0 else -steps)) % count
+            crosses = (source // CY) % 2 != (target // CY) % 2
             moved = ((place + run_y // 2) % run_y) * 2 + core if crosses else lane
             pairs.append((source * width + lane, target * width + moved))
-    return lax.ppermute(value, (axis, "chan"), pairs)
+    on_first = lax.axis_index("chan") % 2 == 0
+    sent = jnp.where(on_first, lower_source, upper_source)
+    got = lax.ppermute(sent, (axis, "chan"), pairs)
+    swapped = lax.ppermute(got, "chan", [(lane, lane ^ 1) for lane in range(width)])
+    return jnp.where(on_first, got, swapped), jnp.where(on_first, swapped, got)
 
 
 def conv(field, taps, padding):
@@ -42,8 +46,7 @@
     own_block = activation[0].astype(jnp.bfloat16).transpose(1, 0, 2)
     gathered = lax.all_gather(own_block, "chan", axis=0, tiled=True)
     gathered = gathered.reshape(-1, size_x, size_y, size_z)
-    below = shifted(gathered[:, -1:], "space", 8)
-    above = shifted(gathered[:, :1], "space", -8)
+    below, above = faces_from(gathered[:, -1:], gathered[:, :1], "space", 8)
     own_part = conv(gathered, weight, ((1, 1), (1, 1), (1, 1)))
     face_part = jnp.concatenate(
         [
@@ -53,8 +56,7 @@
         axis=1,
     )
     widened = jnp.concatenate([below, gathered, above], axis=1)
-    lower_from = shifted(widened[:, :, -1:], "space", 1)
-    upper_from = shifted(widened[:, :, :1], "space", -1)
+    lower_from, upper_from = faces_from(widened[:, :, -1:], widened[:, :, :1], "space", 1)
     place_y = (lax.axis_index("space") + 4) % 8
     lower_rim = jnp.where(place_y > 0, lower_from, jnp.zeros_like(lower_from))
     upper_rim = jnp.where(place_y < 7, upper_from, jnp.zeros_like(upper_from))

time: 70.5 us -> 68.7 us (0.974)
  starting transfers between devices: 27.8 us -> 23.6 us
  waiting for transfers between devices: 7.04 us -> 10.6 us
  local copies, waits for them, and re-layouts: 4.83 us -> 3.66 us
    ppermute x4, starting transfers between devices: 27.8 us -> 23.6 us  [the longest x2 18.8 us: faces_from(): got = lax.ppermute(sent, (axis, 'chan'), pairs)]
    ppermute x4, waiting for transfers between devices: 7.04 us -> 10.6 us  [the longest x2 9.7 us: faces_from(): got = lax.ppermute(sent, (axis, 'chan'), pairs)]
    unnamed x14 -> x12, local copies, waits for them, and re-layouts: 2.03 us -> 0.89 us
where the time goes in v8:
time: 68.7 us; the launch traced here: 68.5 us
  starting transfers between devices  23.6 us (34%)
  blocking collectives  21.7 us (32%)
  waiting for transfers between devices  10.6 us (15%)
  matrix products  7.22 us (11%)
  local copies, waits for them, and re-layouts  3.66 us (5%)
  other arithmetic  1.2 us (2%)
    all_gather x1, blocking collectives, body(): gathered = lax.all_gather(own_block, 'chan', axis=0, tiled=True)  21.7 us
    ppermute x2, starting transfers between devices, faces_from(): got = lax.ppermute(sent, (axis, 'chan'), pairs)  18.8 us
    ppermute x2, waiting for transfers between devices, faces_from(): got = lax.ppermute(sent, (axis, 'chan'), pairs)  9.7 us
    conv_general_dilated x5, matrix products, conv(): lax.conv_general_dilated(field[None], taps, window_strides=(1, 1, 1), pad...  7.22 us
    ppermute x2, starting transfers between devices, faces_from(): lax.ppermute(got, 'chan', [(lane, lane ^ 1) for lane in range(width)])  4.81 us
  transfers between devices with their start and end apart: 4, of which 2 were waited for; matrix products, arithmetic and copies ran while one was open for 12% of the time, Pallas kernels for 0%

profile of v8, /device:TPU:1, one launch (start us, length us, event | category | flops | bytes accessed | tf_op | source)
XLA Modules:
  0.0 68.5 jit_solution(16030516771388805333)
XLA Ops:
  0.0 0.9 %convert_element_type.8 = bf16[1,2,64,256]{3,2,1,0:T(8,128)(2,1)S(1)} convert(f32[1,2,64,256]{3,2,1,0:T(8,128)} %param.3) | non-fusion elementwise | flops 32768 | bytes 196608 | tf_op jit(solution)/shard_map/convert_element_type | solution.py:46
  0.9 0.1 copy.67
  1.0 21.7 %all_gather.3 = bf16[512,2,256]{2,1,0:T(2,128)(2,1)S(1)} all-gather(bf16[64,2,256]{2,1,0:T(2,128)(2,1)S(1)} %bitcast.78), channel_id=1, replica_groups=mesh['space'=64,'chan'=8] {'chan'}, dimensions={0}, use_global_device_ids=true | all-gather | bytes 589824 | tf_op jit(solution)/shard_map/all_gather | solution.py:47
  22.7 0.7 %copy.32 = bf16[512,2,256]{0,2,1:T(8,128)(2,1)S(1)} copy(bf16[512,2,256]{2,1,0:T(2,128)(2,1)S(1)} %all_gather.3) | data formatting | bytes 1048576 | tf_op jit(solution)/shard_map/all_gather | solution.py:47
  23.5 2.4 %collective-permute-start = (bf16[512,1,8,32]{0,3,2,1:T(8,128)(2,1)S(1)}, bf16[512,1,8,32]{0,3,2,1:T(8,128)(2,1)S(1)}, u32[]{:S(2)}, u32[]{:S(2)}) collective-permute-start(bf16[512,1,8,32]{0,3,2,1:T(8,128)(2,1)S(1)} %slice_select_fusion), channel_id=1, source_target_pairs={{0,68},{1,453},{2,70},{3,455},{4,64},{5,449},{6,66},{7,451},{8,76}... | collective-permute-start | bytes 786440 | tf_op jit(solution)/shard_map/ppermute | solution.py:26
  25.9 0.3 copy.60
  26.2 0.0 copy-start.1
  26.2 0.0 copy-start.2
  26.3 0.2 copy.35
  26.5 0.1 slice.42
  26.6 9.7 %collective-permute-done = bf16[512,1,8,32]{0,3,2,1:T(8,128)(2,1)S(1)} collective-permute-done((bf16[512,1,8,32]{0,3,2,1:T(8,128)(2,1)S(1)}, bf16[512,1,8,32]{0,3,2,1:T(8,128)(2,1)S(1)}, u32[]{:S(2)}, u32[]{:S(2)}) %collective-permute-start) | collective-permute-done | bytes 262176 | tf_op jit(solution)/shard_map/ppermute | solution.py:26
  36.3 2.3 %collective-permute-start.1 = (bf16[512,1,8,32]{0,3,2,1:T(8,128)(2,1)S(1)}, bf16[512,1,8,32]{0,3,2,1:T(8,128)(2,1)S(1)}, u32[]{:S(2)}, u32[]{:S(2)}) collective-permute-start(bf16[512,1,8,32]{0,3,2,1:T(8,128)(2,1)S(1)} %collective-permute-done), channel_id=1, source_target_pairs={{0,1},{1,0},{2,3},{3,2},{4,5},{5,4},{6,7},{7,6},{8,9},{9,8},{10,11... | collective-permute-start | bytes 786440 | tf_op jit(solution)/shard_map/ppermute | solution.py:27
  38.5 0.0 copy-done.1
  38.6 0.0 copy-done.2
  38.6 4.7 %convolution_select_fusion = f32[2,8,8,5,64]{4,2,3,1,0:T(8,128)S(1)} fusion(bf16[3,3,3,64,512]{4,3,2,1,0:T(8,128)(2,1)S(1)} %copy-done.1, bf16[512,2,8,1,7,2]{0,4,5,2,1,3:T(8,128)(2,1)S(1)} %slice.42, bf16[512,2,8,1,8,5]{0,4,5,2,1,3:T(8,128)(2,1)S(1)} %copy.35, pred[8,5]{0,1:T(8,128)(4,1)S(1)} %copy-done.2), kind=kOutput, calls=%fused_computation.2 | convolution fusion | flops 694853632 | bytes 2818088 | tf_op jit(solution)/shard_map/conv_general_dilated | solution.py:32
  43.3 0.1 copy.36
  43.4 0.1 copy.37
  43.5 0.1 pad.11.clone
  43.5 0.0 collective-permute-done.1
  43.6 16.4 %collective-permute-start.2 = (bf16[512,4,1,32]{0,3,2,1:T(8,128)(2,1)S(1)}, bf16[512,4,1,32]{0,3,2,1:T(8,128)(2,1)S(1)}, u32[]{:S(2)}, u32[]{:S(2)}) collective-permute-start(bf16[512,4,1,32]{0,3,2,1:T(8,128)(2,1)S(1)} %fusion.45), channel_id=1, source_target_pairs={{0,8},{1,509},{2,10},{3,511},{4,12},{5,505},{6,14},{7,507},{8,16},... | collective-permute-start | bytes 393224 | tf_op jit(solution)/shard_map/ppermute | solution.py:26
  60.0 0.2 copy.62
  60.2 0.1 copy.46
  60.3 0.9 %convolution_select_fusion.1 = f32[1,8,8,5,64]{4,2,3,1,0:T(8,128)S(1)} fusion(bf16[3,3,3,64,512]{4,3,2,1,0:T(8,128)(2,1)S(1)} %copy-done.1, bf16[512,1,8,1,7,2]{0,4,5,2,3,1:T(8,128)(2,1)S(1)} %slice.48, bf16[512,1,8,1,8,5]{0,4,5,2,3,1:T(8,128)(2,1)S(1)} %copy.46, pred[8,5]{0,1:T(8,128)(4,1)S(1)} %copy-done.2), kind=kOutput, calls=%fused_computation.3 | convolution fusion | flops 174411776 | bytes 1131520 | tf_op jit(solution)/shard_map/conv_general_dilated | solution.py:32
  61.3 0.2 copy.61
  61.5 0.1 copy.41
  61.7 0.9 %convolution_select_fusion.2 = f32[1,8,8,5,64]{4,2,3,1,0:T(8,128)S(1)} fusion(bf16[3,3,3,64,512]{4,3,2,1,0:T(8,128)(2,1)S(1)} %copy-done.1, bf16[512,1,8,1,7,2]{0,4,5,2,3,1:T(8,128)(2,1)S(1)} %slice.46, bf16[512,1,8,1,8,5]{0,4,5,2,3,1:T(8,128)(2,1)S(1)} %copy.41, pred[8,5]{0,1:T(8,128)(4,1)S(1)} %copy-done.2), kind=kOutput, calls=%fused_computation.4 | convolution fusion | flops 174411776 | bytes 1131520 | tf_op jit(solution)/shard_map/conv_general_dilated | solution.py:32
  62.6 0.0 collective-permute-done.2
  62.7 2.5 %collective-permute-start.3 = (bf16[512,4,1,32]{0,3,2,1:T(8,128)(2,1)S(1)}, bf16[512,4,1,32]{0,3,2,1:T(8,128)(2,1)S(1)}, u32[]{:S(2)}, u32[]{:S(2)}) collective-permute-start(bf16[512,4,1,32]{0,3,2,1:T(8,128)(2,1)S(1)} %collective-permute-done.2), channel_id=1, source_target_pairs={{0,1},{1,0},{2,3},{3,2},{4,5},{5,4},{6,7},{7,6},{8,9},{9,8},{10,11... | collective-permute-start | bytes 393224 | tf_op jit(solution)/shard_map/ppermute | solution.py:27
  65.3 0.9 %collective-permute-done.3 = bf16[512,4,1,32]{0,3,2,1:T(8,128)(2,1)S(1)} collective-permute-done((bf16[512,4,1,32]{0,3,2,1:T(8,128)(2,1)S(1)}, bf16[512,4,1,32]{0,3,2,1:T(8,128)(2,1)S(1)}, u32[]{:S(2)}, u32[]{:S(2)}) %collective-permute-start.3) | collective-permute-done | bytes 131104 | tf_op jit(solution)/shard_map/ppermute | solution.py:27
  66.2 0.1 copy.63
  66.3 0.1 pad.6.clone
  66.4 0.3 convolution_select_fusion.4
  66.8 0.0 copy-start
  66.9 0.1 copy.64
  67.0 0.1 pad.8.clone
  67.1 0.3 convolution_select_fusion.3
  67.5 0.1 pad_maximum_fusion
  67.6 0.0 copy-done
  67.6 0.1 fusion.28
  67.7 0.8 %copy.59 = f32[1,2,64,256]{3,2,1,0:T(8,128)} copy(f32[1,2,64,256]{2,3,1,0:T(8,128)S(1)} %fusion.28) | data formatting | bytes 262144 | tf_op jit(solution)/shard_map/broadcast_in_dim | solution.py:72
  (27 shorter events, 0.6 us)
Async XLA Ops:
  23.5 12.8 %collective-permute-start = (bf16[512,1,8,32]{0,3,2,1:T(8,128)(2,1)S(1)}, bf16[512,1,8,32]{0,3,2,1:T(8,128)(2,1)S(1)}, u32[]{:S(2)}, u32[]{:S(2)}) collective-permute-start(bf16[512,1,8,32]{0,3,2,1:T(8,128)(2,1)S(1)} %slice_select_fusion), channel_id=1, source_target_pairs={{0,68},{1,453},{2,70},{3,455},{4,64},{5,449},{6,66},{7,451},{8,76}... | collective-permute-start | bytes 786440 | tf_op jit(solution)/shard_map/ppermute | solution.py:26
  26.2 12.3 %copy-start.1 = (bf16[3,3,3,64,512]{4,3,2,1,0:T(8,128)(2,1)S(1)}, bf16[3,3,3,64,512]{4,3,2,1,0:T(8,128)(2,1)}, u32[]{:S(2)}) copy-start(bf16[3,3,3,64,512]{4,3,2,1,0:T(8,128)(2,1)} %param.4) | copy-start | bytes 5308420
  26.2 12.3 %copy-start.2 = (pred[8,5]{0,1:T(8,128)(4,1)S(1)}, pred[8,5]{0,1:T(8,128)(4,1)}, u32[]{:S(2)}) copy-start(pred[8,5]{0,1:T(8,128)(4,1)} %constant.65) | copy-start | bytes 124
  36.3 7.3 %collective-permute-start.1 = (bf16[512,1,8,32]{0,3,2,1:T(8,128)(2,1)S(1)}, bf16[512,1,8,32]{0,3,2,1:T(8,128)(2,1)S(1)}, u32[]{:S(2)}, u32[]{:S(2)}) collective-permute-start(bf16[512,1,8,32]{0,3,2,1:T(8,128)(2,1)S(1)} %collective-permute-done), channel_id=1, source_target_pairs={{0,1},{1,0},{2,3},{3,2},{4,5},{5,4},{6,7},{7,6},{8,9},{9,8},{10,11... | collective-permute-start | bytes 786440 | tf_op jit(solution)/shard_map/ppermute | solution.py:27
  43.6 19.0 %collective-permute-start.2 = (bf16[512,4,1,32]{0,3,2,1:T(8,128)(2,1)S(1)}, bf16[512,4,1,32]{0,3,2,1:T(8,128)(2,1)S(1)}, u32[]{:S(2)}, u32[]{:S(2)}) collective-permute-start(bf16[512,4,1,32]{0,3,2,1:T(8,128)(2,1)S(1)} %fusion.45), channel_id=1, source_target_pairs={{0,8},{1,509},{2,10},{3,511},{4,12},{5,505},{6,14},{7,507},{8,16},... | collective-permute-start | bytes 393224 | tf_op jit(solution)/shard_map/ppermute | solution.py:26
  62.7 3.5 %collective-permute-start.3 = (bf16[512,4,1,32]{0,3,2,1:T(8,128)(2,1)S(1)}, bf16[512,4,1,32]{0,3,2,1:T(8,128)(2,1)S(1)}, u32[]{:S(2)}, u32[]{:S(2)}) collective-permute-start(bf16[512,4,1,32]{0,3,2,1:T(8,128)(2,1)S(1)} %collective-permute-done.2), channel_id=1, source_target_pairs={{0,1},{1,0},{2,3},{3,2},{4,5},{5,4},{6,7},{7,6},{8,9},{9,8},{10,11... | collective-permute-start | bytes 393224 | tf_op jit(solution)/shard_map/ppermute | solution.py:27
  66.8 0.8 %copy-start = (f32[64]{0:T(128)S(1)}, f32[64]{0:T(128)}, u32[]{:S(2)}) copy-start(f32[64]{0:T(128)} %param.5) | copy-start | bytes 772

commit v9 on v8

--- a/solution.py
+++ b/solution.py
@@ -9,7 +9,7 @@
 negative_slope = 0.3
 
 
-def faces_from(lower_source, upper_source, axis, steps):
+def faces_from(lower_source, upper_source, axis, steps, cover=None):
     count = lax.axis_size(axis)
     width = lax.axis_size("chan")
     run_y = width // 2
@@ -24,8 +24,10 @@
     on_first = lax.axis_index("chan") % 2 == 0
     sent = jnp.where(on_first, lower_source, upper_source)
     got = lax.ppermute(sent, (axis, "chan"), pairs)
+    if cover is not None:
+        got, cover = lax.optimization_barrier((got, cover))
     swapped = lax.ppermute(got, "chan", [(lane, lane ^ 1) for lane in range(width)])
-    return jnp.where(on_first, got, swapped), jnp.where(on_first, swapped, got)
+    return jnp.where(on_first, got, swapped), jnp.where(on_first, swapped, got), cover
 
 
 def conv(field, taps, padding):
@@ -46,8 +48,8 @@
     own_block = activation[0].astype(jnp.bfloat16).transpose(1, 0, 2)
     gathered = lax.all_gather(own_block, "chan", axis=0, tiled=True)
     gathered = gathered.reshape(-1, size_x, size_y, size_z)
-    below, above = faces_from(gathered[:, -1:], gathered[:, :1], "space", 8)
     own_part = conv(gathered, weight, ((1, 1), (1, 1), (1, 1)))
+    below, above, own_part = faces_from(gathered[:, -1:], gathered[:, :1], "space", 8, own_part)
     face_part = jnp.concatenate(
         [
             conv(below, weight[:1], ((0, 0), (1, 1), (1, 1))),
@@ -56,7 +58,7 @@
         axis=1,
     )
     widened = jnp.concatenate([below, gathered, above], axis=1)
-    lower_from, upper_from = faces_from(widened[:, :, -1:], widened[:, :, :1], "space", 1)
+    lower_from, upper_from, _ = faces_from(widened[:, :, -1:], widened[:, :, :1], "space", 1)
     place_y = (lax.axis_index("space") + 4) % 8
     lower_rim = jnp.where(place_y > 0, lower_from, jnp.zeros_like(lower_from))
     upper_rim = jnp.where(place_y < 7, upper_from, jnp.zeros_like(upper_from))

time: 68.7 us -> 65.2 us (0.949)
  waiting for transfers between devices: 10.6 us -> 5.74 us
  local copies, waits for them, and re-layouts: 3.66 us -> 4.73 us
    ppermute x2, waiting for transfers between devices: 9.7 us -> 3.76 us  [faces_from(): got = lax.ppermute(sent, (axis, 'chan'), pairs)]
    unnamed x12 -> x14, local copies, waits for them, and re-layouts: 0.89 us -> 2.03 us
    ppermute x2, waiting for transfers between devices: 0.91 us -> 1.97 us  [faces_from(): lax.ppermute(got, 'chan', [(lane, lane ^ 1) for lane in range(width)])]
  transfers between devices with their start and end apart: 4 -> 4, of which waited for: 2 -> 3; matrix products, arithmetic and copies ran while one was open for 12% -> 12% of each run, Pallas kernels for 0% -> 0%
where the time goes in v9:
time: 65.2 us; the launch traced here: 64.9 us
  starting transfers between devices  23.9 us (37%)
  blocking collectives  21.7 us (33%)
  matrix products  7.23 us (11%)
  waiting for transfers between devices  5.74 us (9%)
  local copies, waits for them, and re-layouts  4.73 us (7%)
  other arithmetic  1.21 us (2%)
    all_gather x1, blocking collectives, body(): gathered = lax.all_gather(own_block, 'chan', axis=0, tiled=True)  21.7 us
    ppermute x2, starting transfers between devices, faces_from(): got = lax.ppermute(sent, (axis, 'chan'), pairs)  18.8 us
    conv_general_dilated x5, matrix products, conv(): lax.conv_general_dilated(field[None], taps, window_strides=(1, 1, 1), pad...  7.23 us
    ppermute x2, starting transfers between devices, faces_from(): lax.ppermute(got, 'chan', [(lane, lane ^ 1) for lane in range(width)])  5.13 us
    ppermute x2, waiting for transfers between devices, faces_from(): got = lax.ppermute(sent, (axis, 'chan'), pairs)  3.76 us
    unnamed x14, local copies, waits for them, and re-layouts  2.03 us
    ppermute x2, waiting for transfers between devices, faces_from(): lax.ppermute(got, 'chan', [(lane, lane ^ 1) for lane in range(width)])  1.97 us
  transfers between devices with their start and end apart: 4, of which 3 were waited for; matrix products, arithmetic and copies ran while one was open for 12% of the time, Pallas kernels for 0%

profile of v9, /device:TPU:1, one launch (start us, length us, event | category | flops | bytes accessed | tf_op | source)
XLA Modules:
  0.0 64.9 jit_solution(4104297345924153059)
XLA Ops:
  0.0 0.9 %convert_element_type.8 = bf16[1,2,64,256]{3,2,1,0:T(8,128)(2,1)S(1)} convert(f32[1,2,64,256]{3,2,1,0:T(8,128)} %param.3) | non-fusion elementwise | flops 32768 | bytes 196608 | tf_op jit(solution)/shard_map/convert_element_type | solution.py:48
  0.9 0.1 copy.69
  1.0 21.7 %all_gather.3 = bf16[512,2,256]{2,1,0:T(2,128)(2,1)S(1)} all-gather(bf16[64,2,256]{2,1,0:T(2,128)(2,1)S(1)} %bitcast.82), channel_id=1, replica_groups=mesh['space'=64,'chan'=8] {'chan'}, dimensions={0}, use_global_device_ids=true | all-gather | bytes 589824 | tf_op jit(solution)/shard_map/all_gather | solution.py:49
  22.7 0.7 %copy.32 = bf16[512,2,256]{0,2,1:T(8,128)(2,1)S(1)} copy(bf16[512,2,256]{2,1,0:T(2,128)(2,1)S(1)} %all_gather.3) | data formatting | bytes 1048576 | tf_op jit(solution)/shard_map/all_gather | solution.py:49
  23.5 2.4 %collective-permute-start = (bf16[512,1,8,32]{0,3,2,1:T(8,128)(2,1)S(1)}, bf16[512,1,8,32]{0,3,2,1:T(8,128)(2,1)S(1)}, u32[]{:S(2)}, u32[]{:S(2)}) collective-permute-start(bf16[512,1,8,32]{0,3,2,1:T(8,128)(2,1)S(1)} %slice_select_fusion), channel_id=1, source_target_pairs={{0,68},{1,453},{2,70},{3,455},{4,64},{5,449},{6,66},{7,451},{8,76}... | collective-permute-start | bytes 786440 | tf_op jit(solution)/shard_map/ppermute | solution.py:26
  25.9 0.3 copy.62
  26.2 0.0 copy-start.1
  26.2 0.0 copy-start.2
  26.3 0.2 copy.36
  26.5 0.1 slice.44
  26.6 1.1 %copy-done.1 = bf16[3,3,3,64,512]{4,3,2,1,0:T(8,128)(2,1)S(1)} copy-done((bf16[3,3,3,64,512]{4,3,2,1,0:T(8,128)(2,1)S(1)}, bf16[3,3,3,64,512]{4,3,2,1,0:T(8,128)(2,1)}, u32[]{:S(2)}) %copy-start.1) | copy-done | bytes 1769496
  27.7 0.0 copy-done.2
  27.7 4.7 %convolution_select_fusion = f32[2,8,8,5,64]{4,2,3,1,0:T(8,128)S(1)} fusion(bf16[3,3,3,64,512]{4,3,2,1,0:T(8,128)(2,1)S(1)} %copy-done.1, bf16[512,2,8,1,7,2]{0,4,5,2,1,3:T(8,128)(2,1)S(1)} %slice.44, bf16[512,2,8,1,8,5]{0,4,5,2,1,3:T(8,128)(2,1)S(1)} %copy.36, pred[8,5]{0,1:T(8,128)(4,1)S(1)} %copy-done.2), kind=kOutput, calls=%fused_computation.2 | convolution fusion | flops 694853632 | bytes 2818088 | tf_op jit(solution)/shard_map/conv_general_dilated | solution.py:34
  32.4 0.1 copy.37
  32.5 3.8 %collective-permute-done = bf16[512,1,8,32]{0,3,2,1:T(8,128)(2,1)S(1)} collective-permute-done((bf16[512,1,8,32]{0,3,2,1:T(8,128)(2,1)S(1)}, bf16[512,1,8,32]{0,3,2,1:T(8,128)(2,1)S(1)}, u32[]{:S(2)}, u32[]{:S(2)}) %collective-permute-start) | collective-permute-done | bytes 262176 | tf_op jit(solution)/shard_map/ppermute | solution.py:26
  36.3 2.3 %collective-permute-start.1 = (bf16[512,1,8,32]{0,3,2,1:T(8,128)(2,1)S(1)}, bf16[512,1,8,32]{0,3,2,1:T(8,128)(2,1)S(1)}, u32[]{:S(2)}, u32[]{:S(2)}) collective-permute-start(bf16[512,1,8,32]{0,3,2,1:T(8,128)(2,1)S(1)} %collective-permute-done), channel_id=1, source_target_pairs={{0,1},{1,0},{2,3},{3,2},{4,5},{5,4},{6,7},{7,6},{8,9},{9,8},{10,11... | collective-permute-start | bytes 786440 | tf_op jit(solution)/shard_map/ppermute | solution.py:29
  38.6 0.1 pad.11.clone
  38.6 1.0 %collective-permute-done.1 = bf16[512,1,8,32]{0,3,2,1:T(8,128)(2,1)S(1)} collective-permute-done((bf16[512,1,8,32]{0,3,2,1:T(8,128)(2,1)S(1)}, bf16[512,1,8,32]{0,3,2,1:T(8,128)(2,1)S(1)}, u32[]{:S(2)}, u32[]{:S(2)}) %collective-permute-start.1) | collective-permute-done | bytes 262176 | tf_op jit(solution)/shard_map/ppermute | solution.py:29
  39.8 16.4 %collective-permute-start.2 = (bf16[512,4,1,32]{0,3,2,1:T(8,128)(2,1)S(1)}, bf16[512,4,1,32]{0,3,2,1:T(8,128)(2,1)S(1)}, u32[]{:S(2)}, u32[]{:S(2)}) collective-permute-start(bf16[512,4,1,32]{0,3,2,1:T(8,128)(2,1)S(1)} %fusion.44), channel_id=1, source_target_pairs={{0,8},{1,509},{2,10},{3,511},{4,12},{5,505},{6,14},{7,507},{8,16},... | collective-permute-start | bytes 393224 | tf_op jit(solution)/shard_map/ppermute | solution.py:26
  56.1 0.2 copy.65
  56.3 0.1 copy.40
  56.5 0.9 %convolution_select_fusion.2 = f32[1,8,8,5,64]{4,2,3,1,0:T(8,128)S(1)} fusion(bf16[3,3,3,64,512]{4,3,2,1,0:T(8,128)(2,1)S(1)} %copy-done.1, bf16[512,1,8,1,7,2]{0,4,5,2,3,1:T(8,128)(2,1)S(1)} %slice.46, bf16[512,1,8,1,8,5]{0,4,5,2,3,1:T(8,128)(2,1)S(1)} %copy.40, pred[8,5]{0,1:T(8,128)(4,1)S(1)} %copy-done.2), kind=kOutput, calls=%fused_computation.4 | convolution fusion | flops 174411776 | bytes 1131520 | tf_op jit(solution)/shard_map/conv_general_dilated | solution.py:34
  57.4 0.2 copy.66
  57.6 0.1 copy.45
  57.8 0.9 %convolution_select_fusion.1 = f32[1,8,8,5,64]{4,2,3,1,0:T(8,128)S(1)} fusion(bf16[3,3,3,64,512]{4,3,2,1,0:T(8,128)(2,1)S(1)} %copy-done.1, bf16[512,1,8,1,7,2]{0,4,5,2,3,1:T(8,128)(2,1)S(1)} %slice.48, bf16[512,1,8,1,8,5]{0,4,5,2,3,1:T(8,128)(2,1)S(1)} %copy.45, pred[8,5]{0,1:T(8,128)(4,1)S(1)} %copy-done.2), kind=kOutput, calls=%fused_computation.3 | convolution fusion | flops 174411776 | bytes 1131520 | tf_op jit(solution)/shard_map/conv_general_dilated | solution.py:34
  58.7 0.0 collective-permute-done.2
  58.7 2.9 %collective-permute-start.3 = (bf16[512,4,1,32]{0,3,2,1:T(8,128)(2,1)S(1)}, bf16[512,4,1,32]{0,3,2,1:T(8,128)(2,1)S(1)}, u32[]{:S(2)}, u32[]{:S(2)}) collective-permute-start(bf16[512,4,1,32]{0,3,2,1:T(8,128)(2,1)S(1)} %collective-permute-done.2), channel_id=1, source_target_pairs={{0,1},{1,0},{2,3},{3,2},{4,5},{5,4},{6,7},{7,6},{8,9},{9,8},{10,11... | collective-permute-start | bytes 393224 | tf_op jit(solution)/shard_map/ppermute | solution.py:29
  61.6 0.9 %collective-permute-done.3 = bf16[512,4,1,32]{0,3,2,1:T(8,128)(2,1)S(1)} collective-permute-done((bf16[512,4,1,32]{0,3,2,1:T(8,128)(2,1)S(1)}, bf16[512,4,1,32]{0,3,2,1:T(8,128)(2,1)S(1)}, u32[]{:S(2)}, u32[]{:S(2)}) %collective-permute-start.3) | collective-permute-done | bytes 131104 | tf_op jit(solution)/shard_map/ppermute | solution.py:29
  62.6 0.1 copy.63
  62.7 0.1 pad.6.clone
  62.9 0.3 convolution_select_fusion.4
  63.3 0.1 copy.64
  63.4 0.1 pad.8.clone
  63.4 0.0 copy-start
  63.5 0.3 convolution_select_fusion.3
  63.9 0.1 fusion.29
  64.1 0.1 copy.58
  64.1 0.0 copy-done
  64.2 0.8 %copy.59 = f32[1,2,64,256]{3,2,1,0:T(8,128)} copy(f32[1,2,64,256]{2,3,1,0:T(8,128)S(1)} %fusion.28) | data formatting | bytes 262144 | tf_op jit(solution)/shard_map/broadcast_in_dim | solution.py:74
  (25 shorter events, 0.6 us)
Async XLA Ops:
  23.5 12.8 %collective-permute-start = (bf16[512,1,8,32]{0,3,2,1:T(8,128)(2,1)S(1)}, bf16[512,1,8,32]{0,3,2,1:T(8,128)(2,1)S(1)}, u32[]{:S(2)}, u32[]{:S(2)}) collective-permute-start(bf16[512,1,8,32]{0,3,2,1:T(8,128)(2,1)S(1)} %slice_select_fusion), channel_id=1, source_target_pairs={{0,68},{1,453},{2,70},{3,455},{4,64},{5,449},{6,66},{7,451},{8,76}... | collective-permute-start | bytes 786440 | tf_op jit(solution)/shard_map/ppermute | solution.py:26
  26.2 1.5 %copy-start.1 = (bf16[3,3,3,64,512]{4,3,2,1,0:T(8,128)(2,1)S(1)}, bf16[3,3,3,64,512]{4,3,2,1,0:T(8,128)(2,1)}, u32[]{:S(2)}) copy-start(bf16[3,3,3,64,512]{4,3,2,1,0:T(8,128)(2,1)} %param.4) | copy-start | bytes 5308420
  26.2 1.5 %copy-start.2 = (pred[8,5]{0,1:T(8,128)(4,1)S(1)}, pred[8,5]{0,1:T(8,128)(4,1)}, u32[]{:S(2)}) copy-start(pred[8,5]{0,1:T(8,128)(4,1)} %constant.65) | copy-start | bytes 124
  36.3 3.4 %collective-permute-start.1 = (bf16[512,1,8,32]{0,3,2,1:T(8,128)(2,1)S(1)}, bf16[512,1,8,32]{0,3,2,1:T(8,128)(2,1)S(1)}, u32[]{:S(2)}, u32[]{:S(2)}) collective-permute-start(bf16[512,1,8,32]{0,3,2,1:T(8,128)(2,1)S(1)} %collective-permute-done), channel_id=1, source_target_pairs={{0,1},{1,0},{2,3},{3,2},{4,5},{5,4},{6,7},{7,6},{8,9},{9,8},{10,11... | collective-permute-start | bytes 786440 | tf_op jit(solution)/shard_map/ppermute | solution.py:29
  39.8 19.0 %collective-permute-start.2 = (bf16[512,4,1,32]{0,3,2,1:T(8,128)(2,1)S(1)}, bf16[512,4,1,32]{0,3,2,1:T(8,128)(2,1)S(1)}, u32[]{:S(2)}, u32[]{:S(2)}) collective-permute-start(bf16[512,4,1,32]{0,3,2,1:T(8,128)(2,1)S(1)} %fusion.44), channel_id=1, source_target_pairs={{0,8},{1,509},{2,10},{3,511},{4,12},{5,505},{6,14},{7,507},{8,16},... | collective-permute-start | bytes 393224 | tf_op jit(solution)/shard_map/ppermute | solution.py:26
  58.7 3.8 %collective-permute-start.3 = (bf16[512,4,1,32]{0,3,2,1:T(8,128)(2,1)S(1)}, bf16[512,4,1,32]{0,3,2,1:T(8,128)(2,1)S(1)}, u32[]{:S(2)}, u32[]{:S(2)}) collective-permute-start(bf16[512,4,1,32]{0,3,2,1:T(8,128)(2,1)S(1)} %collective-permute-done.2), channel_id=1, source_target_pairs={{0,1},{1,0},{2,3},{3,2},{4,5},{5,4},{6,7},{7,6},{8,9},{9,8},{10,11... | collective-permute-start | bytes 393224 | tf_op jit(solution)/shard_map/ppermute | solution.py:29
  63.4 0.7 %copy-start = (f32[64]{0:T(128)S(1)}, f32[64]{0:T(128)}, u32[]{:S(2)}) copy-start(f32[64]{0:T(128)} %param.5) | copy-start | bytes 772

commit v10 on v8

--- a/solution.py
+++ b/solution.py
@@ -9,7 +9,7 @@
 negative_slope = 0.3
 
 
-def faces_from(lower_source, upper_source, axis, steps):
+def cross(lower_source, upper_source, axis, steps):
     count = lax.axis_size(axis)
     width = lax.axis_size("chan")
     run_y = width // 2
@@ -23,7 +23,12 @@
             pairs.append((source * width + lane, target * width + moved))
     on_first = lax.axis_index("chan") % 2 == 0
     sent = jnp.where(on_first, lower_source, upper_source)
-    got = lax.ppermute(sent, (axis, "chan"), pairs)
+    return lax.ppermute(sent, (axis, "chan"), pairs)
+
+
+def swap(got):
+    width = lax.axis_size("chan")
+    on_first = lax.axis_index("chan") % 2 == 0
     swapped = lax.ppermute(got, "chan", [(lane, lane ^ 1) for lane in range(width)])
     return jnp.where(on_first, got, swapped), jnp.where(on_first, swapped, got)
 
@@ -46,8 +51,21 @@
     own_block = activation[0].astype(jnp.bfloat16).transpose(1, 0, 2)
     gathered = lax.all_gather(own_block, "chan", axis=0, tiled=True)
     gathered = gathered.reshape(-1, size_x, size_y, size_z)
-    below, above = faces_from(gathered[:, -1:], gathered[:, :1], "space", 8)
     own_part = conv(gathered, weight, ((1, 1), (1, 1), (1, 1)))
+    got_x = cross(gathered[:, -1:], gathered[:, :1], "space", 8)
+    got_y = cross(gathered[:, :, -1:], gathered[:, :, :1], "space", 1)
+    got_x, got_y, own_part = lax.optimization_barrier((got_x, got_y, own_part))
+    below, above = swap(got_x)
+    lower_row, upper_row = swap(got_y)
+    place_y = (lax.axis_index("space") + 4) % 8
+    lower_row = jnp.where(place_y > 0, lower_row, jnp.zeros_like(lower_row))
+    upper_row = jnp.where(place_y < 7, upper_row, jnp.zeros_like(upper_row))
+    got_corners = cross(
+        jnp.concatenate([lower_row[:, -1:], upper_row[:, -1:]], axis=2),
+        jnp.concatenate([lower_row[:, :1], upper_row[:, :1]], axis=2),
+        "space",
+        8,
+    )
     face_part = jnp.concatenate(
         [
             conv(below, weight[:1], ((0, 0), (1, 1), (1, 1))),
@@ -55,11 +73,10 @@
         ],
         axis=1,
     )
-    widened = jnp.concatenate([below, gathered, above], axis=1)
-    lower_from, upper_from = faces_from(widened[:, :, -1:], widened[:, :, :1], "space", 1)
-    place_y = (lax.axis_index("space") + 4) % 8
-    lower_rim = jnp.where(place_y > 0, lower_from, jnp.zeros_like(lower_from))
-    upper_rim = jnp.where(place_y < 7, upper_from, jnp.zeros_like(upper_from))
+    got_corners, face_part = lax.optimization_barrier((got_corners, face_part))
+    corner_lo, corner_hi = swap(got_corners)
+    lower_rim = jnp.concatenate([corner_lo[:, :, :1], lower_row, corner_hi[:, :, :1]], axis=1)
+    upper_rim = jnp.concatenate([corner_lo[:, :, 1:], upper_row, corner_hi[:, :, 1:]], axis=1)
     lower_part = conv(lower_rim, weight[:, :1], ((0, 0), (0, 0), (1, 1)))
     upper_part = conv(upper_rim, weight[:, 2:], ((0, 0), (0, 0), (1, 1)))
     width_out = own_part.shape[0]

time: 68.7 us -> 68.1 us (level)
  the two profiles are of different devices: /device:TPU:1 before, /device:TPU:9 now
where the time goes in v10:
time: 68.1 us; the launch traced here: 67.7 us
  starting transfers between devices  32.3 us (47%)
  blocking collectives  17.9 us (26%)
  matrix products  7.22 us (11%)
  local copies, waits for them, and re-layouts  4.76 us (7%)
  waiting for transfers between devices  3.81 us (6%)
  other arithmetic  1.26 us (2%)
    all_gather x1, blocking collectives, body(): gathered = lax.all_gather(own_block, 'chan', axis=0, tiled=True)  17.9 us
    ppermute x3, starting transfers between devices, cross(): return lax.ppermute(sent, (axis, 'chan'), pairs)  17.6 us
    ppermute x3, starting transfers between devices, swap(): lax.ppermute(got, 'chan', [(lane, lane ^ 1) for lane in range(width)])  14.6 us
    conv_general_dilated x5, matrix products, conv(): lax.conv_general_dilated(field[None], taps, window_strides=(1, 1, 1), pad...  7.22 us
    ppermute x3, waiting for transfers between devices, cross(): return lax.ppermute(sent, (axis, 'chan'), pairs)  3.01 us
    unnamed x14, local copies, waits for them, and re-layouts  2.03 us
  transfers between devices with their start and end apart: 6, of which 2 were waited for; matrix products, arithmetic and copies ran while one was open for 12% of the time, Pallas kernels for 0%

profile of v10, /device:TPU:9, one launch (start us, length us, event | category | flops | bytes accessed | tf_op | source)
XLA Modules:
  0.0 67.7 jit_solution(10134600512956832862)
XLA Ops:
  0.0 0.9 %convert_element_type.8 = bf16[1,2,64,256]{3,2,1,0:T(8,128)(2,1)S(1)} convert(f32[1,2,64,256]{3,2,1,0:T(8,128)} %param.3) | non-fusion elementwise | flops 32768 | bytes 196608 | tf_op jit(solution)/shard_map/convert_element_type | solution.py:51
  0.9 0.1 copy.69
  1.0 17.9 %all_gather.3 = bf16[512,2,256]{2,1,0:T(2,128)(2,1)S(1)} all-gather(bf16[64,2,256]{2,1,0:T(2,128)(2,1)S(1)} %bitcast.82), channel_id=1, replica_groups=mesh['space'=64,'chan'=8] {'chan'}, dimensions={0}, use_global_device_ids=true | all-gather | bytes 589824 | tf_op jit(solution)/shard_map/all_gather | solution.py:52
  18.9 0.7 %copy.32 = bf16[512,2,256]{0,2,1:T(8,128)(2,1)S(1)} copy(bf16[512,2,256]{2,1,0:T(2,128)(2,1)S(1)} %all_gather.3) | data formatting | bytes 1048576 | tf_op jit(solution)/shard_map/all_gather | solution.py:52
  19.7 4.6 %collective-permute-start = (bf16[512,1,8,32]{0,3,2,1:T(8,128)(2,1)S(1)}, bf16[512,1,8,32]{0,3,2,1:T(8,128)(2,1)S(1)}, u32[]{:S(2)}, u32[]{:S(2)}) collective-permute-start(bf16[512,1,8,32]{0,3,2,1:T(8,128)(2,1)S(1)} %slice_select_fusion), channel_id=1, source_target_pairs={{0,68},{1,453},{2,70},{3,455},{4,64},{5,449},{6,66},{7,451},{8,76}... | collective-permute-start | bytes 786440 | tf_op jit(solution)/shard_map/ppermute | solution.py:26
  24.3 11.1 %collective-permute-start.1 = (bf16[512,2,1,32]{0,3,2,1:T(8,128)(2,1)S(1)}, bf16[512,2,1,32]{0,3,2,1:T(8,128)(2,1)S(1)}, u32[]{:S(2)}, u32[]{:S(2)}) collective-permute-start(bf16[512,2,1,32]{0,3,2,1:T(8,128)(2,1)S(1)} %slice_select_fusion.1), channel_id=1, source_target_pairs={{0,8},{1,509},{2,10},{3,511},{4,12},{5,505},{6,14},{7,507},{8,16},... | collective-permute-start | bytes 196616 | tf_op jit(solution)/shard_map/ppermute | solution.py:26
  35.4 0.3 copy.62
  35.7 0.0 copy-start.1
  35.7 0.0 copy-start.2
  35.8 0.2 copy.36
  36.0 0.1 slice.78
  36.1 1.1 %copy-done.1 = bf16[3,3,3,64,512]{4,3,2,1,0:T(8,128)(2,1)S(1)} copy-done((bf16[3,3,3,64,512]{4,3,2,1,0:T(8,128)(2,1)S(1)}, bf16[3,3,3,64,512]{4,3,2,1,0:T(8,128)(2,1)}, u32[]{:S(2)}) %copy-start.1) | copy-done | bytes 1769496
  37.2 0.0 copy-done.2
  37.2 4.7 %convolution_select_fusion = f32[2,8,8,5,64]{4,2,3,1,0:T(8,128)S(1)} fusion(bf16[3,3,3,64,512]{4,3,2,1,0:T(8,128)(2,1)S(1)} %copy-done.1, bf16[512,2,8,1,7,2]{0,4,5,2,1,3:T(8,128)(2,1)S(1)} %slice.78, bf16[512,2,8,1,8,5]{0,4,5,2,1,3:T(8,128)(2,1)S(1)} %copy.36, pred[8,5]{0,1:T(8,128)(4,1)S(1)} %copy-done.2), kind=kOutput, calls=%fused_computation.2 | convolution fusion | flops 694853632 | bytes 2818088 | tf_op jit(solution)/shard_map/conv_general_dilated | solution.py:37
  41.9 0.1 copy.37
  42.0 0.0 collective-permute-done.1
  42.0 0.0 collective-permute-done
  42.0 7.6 %collective-permute-start.2 = (bf16[512,2,1,32]{0,3,2,1:T(8,128)(2,1)S(1)}, bf16[512,2,1,32]{0,3,2,1:T(8,128)(2,1)S(1)}, u32[]{:S(2)}, u32[]{:S(2)}) collective-permute-start(bf16[512,2,1,32]{0,3,2,1:T(8,128)(2,1)S(1)} %collective-permute-done.1), channel_id=1, source_target_pairs={{0,1},{1,0},{2,3},{3,2},{4,5},{5,4},{6,7},{7,6},{8,9},{9,8},{10,11... | collective-permute-start | bytes 196616 | tf_op jit(solution)/shard_map/ppermute | solution.py:32
  49.6 1.9 %collective-permute-start.4 = (bf16[512,1,8,32]{0,3,2,1:T(8,128)(2,1)S(1)}, bf16[512,1,8,32]{0,3,2,1:T(8,128)(2,1)S(1)}, u32[]{:S(2)}, u32[]{:S(2)}) collective-permute-start(bf16[512,1,8,32]{0,3,2,1:T(8,128)(2,1)S(1)} %collective-permute-done), channel_id=1, source_target_pairs={{0,1},{1,0},{2,3},{3,2},{4,5},{5,4},{6,7},{7,6},{8,9},{9,8},{10,11... | collective-permute-start | bytes 786440 | tf_op jit(solution)/shard_map/ppermute | solution.py:32
  51.6 0.0 collective-permute-done.2
  51.7 1.9 %collective-permute-start.3 = (bf16[512,1,2,32]{0,3,2,1:T(8,128)(2,1)S(1)}, bf16[512,1,2,32]{0,3,2,1:T(8,128)(2,1)S(1)}, u32[]{:S(2)}, u32[]{:S(2)}) collective-permute-start(bf16[512,1,2,32]{0,3,2,1:T(8,128)(2,1)S(1)} %maximum_select_fusion), channel_id=1, source_target_pairs={{0,68},{1,453},{2,70},{3,455},{4,64},{5,449},{6,66},{7,451},{8,76}... | collective-permute-start | bytes 196616 | tf_op jit(solution)/shard_map/ppermute | solution.py:26
  53.6 0.0 collective-permute-done.4
  53.6 0.2 copy.63
  53.8 0.1 copy.40
  54.0 0.9 %convolution_select_fusion.2 = f32[1,8,8,5,64]{4,2,3,1,0:T(8,128)S(1)} fusion(bf16[3,3,3,64,512]{4,3,2,1,0:T(8,128)(2,1)S(1)} %copy-done.1, bf16[512,1,8,1,7,2]{0,4,5,2,3,1:T(8,128)(2,1)S(1)} %slice.84, bf16[512,1,8,1,8,5]{0,4,5,2,3,1:T(8,128)(2,1)S(1)} %copy.40, pred[8,5]{0,1:T(8,128)(4,1)S(1)} %copy-done.2), kind=kOutput, calls=%fused_computation.4 | convolution fusion | flops 174411776 | bytes 1131520 | tf_op jit(solution)/shard_map/conv_general_dilated | solution.py:37
  55.0 0.2 copy.64
  55.2 0.1 copy.45
  55.3 0.9 %convolution_select_fusion.1 = f32[1,8,8,5,64]{4,2,3,1,0:T(8,128)S(1)} fusion(bf16[3,3,3,64,512]{4,3,2,1,0:T(8,128)(2,1)S(1)} %copy-done.1, bf16[512,1,8,1,7,2]{0,4,5,2,3,1:T(8,128)(2,1)S(1)} %slice.86, bf16[512,1,8,1,8,5]{0,4,5,2,3,1:T(8,128)(2,1)S(1)} %copy.45, pred[8,5]{0,1:T(8,128)(4,1)S(1)} %copy-done.2), kind=kOutput, calls=%fused_computation.3 | convolution fusion | flops 174411776 | bytes 1131520 | tf_op jit(solution)/shard_map/conv_general_dilated | solution.py:37
  56.3 3.0 %collective-permute-done.3 = bf16[512,1,2,32]{0,3,2,1:T(8,128)(2,1)S(1)} collective-permute-done((bf16[512,1,2,32]{0,3,2,1:T(8,128)(2,1)S(1)}, bf16[512,1,2,32]{0,3,2,1:T(8,128)(2,1)S(1)}, u32[]{:S(2)}, u32[]{:S(2)}) %collective-permute-start.3) | collective-permute-done | bytes 65568 | tf_op jit(solution)/shard_map/ppermute | solution.py:26
  59.3 5.1 %collective-permute-start.5 = (bf16[512,1,2,32]{0,3,2,1:T(8,128)(2,1)S(1)}, bf16[512,1,2,32]{0,3,2,1:T(8,128)(2,1)S(1)}, u32[]{:S(2)}, u32[]{:S(2)}) collective-permute-start(bf16[512,1,2,32]{0,3,2,1:T(8,128)(2,1)S(1)} %collective-permute-done.3), channel_id=1, source_target_pairs={{0,1},{1,0},{2,3},{3,2},{4,5},{5,4},{6,7},{7,6},{8,9},{9,8},{10,11... | collective-permute-start | bytes 196616 | tf_op jit(solution)/shard_map/ppermute | solution.py:32
  64.5 0.1 pad.11.clone
  64.5 0.8 %collective-permute-done.5 = bf16[512,1,2,32]{0,3,2,1:T(8,128)(2,1)S(1)} collective-permute-done((bf16[512,1,2,32]{0,3,2,1:T(8,128)(2,1)S(1)}, bf16[512,1,2,32]{0,3,2,1:T(8,128)(2,1)S(1)}, u32[]{:S(2)}, u32[]{:S(2)}) %collective-permute-start.5) | collective-permute-done | bytes 65568 | tf_op jit(solution)/shard_map/ppermute | solution.py:32
  65.4 0.1 copy.65
  65.5 0.1 pad.6.clone
  65.7 0.3 convolution_select_fusion.4
  66.1 0.1 copy.66
  66.2 0.1 pad.8.clone
  66.2 0.0 copy-start
  66.3 0.3 convolution_select_fusion.3
  66.7 0.1 maximum_add_fusion
  66.9 0.1 copy.58
  66.9 0.0 copy-done
  67.0 0.8 %copy.59 = f32[1,2,64,256]{3,2,1,0:T(8,128)} copy(f32[1,2,64,256]{2,3,1,0:T(8,128)S(1)} %fusion.28) | data formatting | bytes 262144 | tf_op jit(solution)/shard_map/broadcast_in_dim | solution.py:89
  (34 shorter events, 0.7 us)
Async XLA Ops:
  19.7 22.4 %collective-permute-start = (bf16[512,1,8,32]{0,3,2,1:T(8,128)(2,1)S(1)}, bf16[512,1,8,32]{0,3,2,1:T(8,128)(2,1)S(1)}, u32[]{:S(2)}, u32[]{:S(2)}) collective-permute-start(bf16[512,1,8,32]{0,3,2,1:T(8,128)(2,1)S(1)} %slice_select_fusion), channel_id=1, source_target_pairs={{0,68},{1,453},{2,70},{3,455},{4,64},{5,449},{6,66},{7,451},{8,76}... | collective-permute-start | bytes 786440 | tf_op jit(solution)/shard_map/ppermute | solution.py:26
  24.3 17.7 %collective-permute-start.1 = (bf16[512,2,1,32]{0,3,2,1:T(8,128)(2,1)S(1)}, bf16[512,2,1,32]{0,3,2,1:T(8,128)(2,1)S(1)}, u32[]{:S(2)}, u32[]{:S(2)}) collective-permute-start(bf16[512,2,1,32]{0,3,2,1:T(8,128)(2,1)S(1)} %slice_select_fusion.1), channel_id=1, source_target_pairs={{0,8},{1,509},{2,10},{3,511},{4,12},{5,505},{6,14},{7,507},{8,16},... | collective-permute-start | bytes 196616 | tf_op jit(solution)/shard_map/ppermute | solution.py:26
  35.7 1.5 %copy-start.1 = (bf16[3,3,3,64,512]{4,3,2,1,0:T(8,128)(2,1)S(1)}, bf16[3,3,3,64,512]{4,3,2,1,0:T(8,128)(2,1)}, u32[]{:S(2)}) copy-start(bf16[3,3,3,64,512]{4,3,2,1,0:T(8,128)(2,1)} %param.4) | copy-start | bytes 5308420
  35.7 1.5 %copy-start.2 = (pred[8,5]{0,1:T(8,128)(4,1)S(1)}, pred[8,5]{0,1:T(8,128)(4,1)}, u32[]{:S(2)}) copy-start(pred[8,5]{0,1:T(8,128)(4,1)} %constant.73) | copy-start | bytes 124
  42.0 9.6 %collective-permute-start.2 = (bf16[512,2,1,32]{0,3,2,1:T(8,128)(2,1)S(1)}, bf16[512,2,1,32]{0,3,2,1:T(8,128)(2,1)S(1)}, u32[]{:S(2)}, u32[]{:S(2)}) collective-permute-start(bf16[512,2,1,32]{0,3,2,1:T(8,128)(2,1)S(1)} %collective-permute-done.1), channel_id=1, source_target_pairs={{0,1},{1,0},{2,3},{3,2},{4,5},{5,4},{6,7},{7,6},{8,9},{9,8},{10,11... | collective-permute-start | bytes 196616 | tf_op jit(solution)/shard_map/ppermute | solution.py:32
  49.6 3.9 %collective-permute-start.4 = (bf16[512,1,8,32]{0,3,2,1:T(8,128)(2,1)S(1)}, bf16[512,1,8,32]{0,3,2,1:T(8,128)(2,1)S(1)}, u32[]{:S(2)}, u32[]{:S(2)}) collective-permute-start(bf16[512,1,8,32]{0,3,2,1:T(8,128)(2,1)S(1)} %collective-permute-done), channel_id=1, source_target_pairs={{0,1},{1,0},{2,3},{3,2},{4,5},{5,4},{6,7},{7,6},{8,9},{9,8},{10,11... | collective-permute-start | bytes 786440 | tf_op jit(solution)/shard_map/ppermute | solution.py:32
  51.7 7.7 %collective-permute-start.3 = (bf16[512,1,2,32]{0,3,2,1:T(8,128)(2,1)S(1)}, bf16[512,1,2,32]{0,3,2,1:T(8,128)(2,1)S(1)}, u32[]{:S(2)}, u32[]{:S(2)}) collective-permute-start(bf16[512,1,2,32]{0,3,2,1:T(8,128)(2,1)S(1)} %maximum_select_fusion), channel_id=1, source_target_pairs={{0,68},{1,453},{2,70},{3,455},{4,64},{5,449},{6,66},{7,451},{8,76}... | collective-permute-start | bytes 196616 | tf_op jit(solution)/shard_map/ppermute | solution.py:26
  59.3 6.0 %collective-permute-start.5 = (bf16[512,1,2,32]{0,3,2,1:T(8,128)(2,1)S(1)}, bf16[512,1,2,32]{0,3,2,1:T(8,128)(2,1)S(1)}, u32[]{:S(2)}, u32[]{:S(2)}) collective-permute-start(bf16[512,1,2,32]{0,3,2,1:T(8,128)(2,1)S(1)} %collective-permute-done.3), channel_id=1, source_target_pairs={{0,1},{1,0},{2,3},{3,2},{4,5},{5,4},{6,7},{7,6},{8,9},{9,8},{10,11... | collective-permute-start | bytes 196616 | tf_op jit(solution)/shard_map/ppermute | solution.py:32
  66.2 0.7 %copy-start = (f32[64]{0:T(128)S(1)}, f32[64]{0:T(128)}, u32[]{:S(2)}) copy-start(f32[64]{0:T(128)} %param.5) | copy-start | bytes 772

commit v11 on v8

--- a/solution.py
+++ b/solution.py
@@ -9,7 +9,7 @@
 negative_slope = 0.3
 
 
-def faces_from(lower_source, upper_source, axis, steps):
+def cross(lower_source, upper_source, axis, steps):
     count = lax.axis_size(axis)
     width = lax.axis_size("chan")
     run_y = width // 2
@@ -23,7 +23,12 @@
             pairs.append((source * width + lane, target * width + moved))
     on_first = lax.axis_index("chan") % 2 == 0
     sent = jnp.where(on_first, lower_source, upper_source)
-    got = lax.ppermute(sent, (axis, "chan"), pairs)
+    return lax.ppermute(sent, (axis, "chan"), pairs)
+
+
+def swap(got):
+    width = lax.axis_size("chan")
+    on_first = lax.axis_index("chan") % 2 == 0
     swapped = lax.ppermute(got, "chan", [(lane, lane ^ 1) for lane in range(width)])
     return jnp.where(on_first, got, swapped), jnp.where(on_first, swapped, got)
 
@@ -46,8 +51,27 @@
     own_block = activation[0].astype(jnp.bfloat16).transpose(1, 0, 2)
     gathered = lax.all_gather(own_block, "chan", axis=0, tiled=True)
     gathered = gathered.reshape(-1, size_x, size_y, size_z)
-    below, above = faces_from(gathered[:, -1:], gathered[:, :1], "space", 8)
     own_part = conv(gathered, weight, ((1, 1), (1, 1), (1, 1)))
+    width_in = gathered.shape[0]
+    got = [
+        cross(gathered[:, -1:], gathered[:, :1], "space", CY),
+        cross(gathered[:, :, -1:], gathered[:, :, :1], "space", 1),
+        cross(gathered[:, -1:, -1:], gathered[:, :1, :1], "space", CY + 1),
+        cross(gathered[:, -1:, :1], gathered[:, :1, -1:], "space", CY - 1),
+    ]
+    got, own_part = lax.optimization_barrier((got, own_part))
+    sizes = [piece[0].size for piece in got]
+    joined = jnp.concatenate([piece.reshape(width_in, -1) for piece in got], axis=1)
+    lower_all, upper_all = swap(joined)
+    offsets = [sum(sizes[:k]) for k in range(len(sizes) + 1)]
+
+    def piece(joined_half, k):
+        return joined_half[:, offsets[k] : offsets[k + 1]].reshape(got[k].shape)
+
+    below, above = piece(lower_all, 0), piece(upper_all, 0)
+    lower_row, upper_row = piece(lower_all, 1), piece(upper_all, 1)
+    corner_ll, corner_hh = piece(lower_all, 2), piece(upper_all, 2)
+    corner_lh, corner_hl = piece(lower_all, 3), piece(upper_all, 3)
     face_part = jnp.concatenate(
         [
             conv(below, weight[:1], ((0, 0), (1, 1), (1, 1))),
@@ -55,11 +79,11 @@
         ],
         axis=1,
     )
-    widened = jnp.concatenate([below, gathered, above], axis=1)
-    lower_from, upper_from = faces_from(widened[:, :, -1:], widened[:, :, :1], "space", 1)
     place_y = (lax.axis_index("space") + 4) % 8
-    lower_rim = jnp.where(place_y > 0, lower_from, jnp.zeros_like(lower_from))
-    upper_rim = jnp.where(place_y < 7, upper_from, jnp.zeros_like(upper_from))
+    lower_rim = jnp.concatenate([corner_ll, lower_row, corner_hl], axis=1)
+    upper_rim = jnp.concatenate([corner_lh, upper_row, corner_hh], axis=1)
+    lower_rim = jnp.where(place_y > 0, lower_rim, jnp.zeros_like(lower_rim))
+    upper_rim = jnp.where(place_y < 7, upper_rim, jnp.zeros_like(upper_rim))
     lower_part = conv(lower_rim, weight[:, :1], ((0, 0), (0, 0), (1, 1)))
     upper_part = conv(upper_rim, weight[:, 2:], ((0, 0), (0, 0), (1, 1)))
     width_out = own_part.shape[0]

time: 68.7 us -> 64.4 us (0.937)
  the two profiles are of different devices: /device:TPU:1 before, /device:TPU:17 now
where the time goes in v11:
time: 64.4 us; the launch traced here: 64.1 us
  starting transfers between devices  29.7 us (46%)
  blocking collectives  19 us (30%)
  matrix products  7.22 us (11%)
  local copies, waits for them, and re-layouts  5.17 us (8%)
  other arithmetic  1.34 us (2%)
  waiting for transfers between devices  1.24 us (2%)
    ppermute x4, starting transfers between devices, cross(): return lax.ppermute(sent, (axis, 'chan'), pairs)  22.1 us
    all_gather x1, blocking collectives, body(): gathered = lax.all_gather(own_block, 'chan', axis=0, tiled=True)  19 us
    ppermute x1, starting transfers between devices, swap(): lax.ppermute(got, 'chan', [(lane, lane ^ 1) for lane in range(width)])  7.6 us
    conv_general_dilated x5, matrix products, conv(): lax.conv_general_dilated(field[None], taps, window_strides=(1, 1, 1), pad...  7.22 us
    unnamed x14, local copies, waits for them, and re-layouts  2.41 us
  transfers between devices with their start and end apart: 5, of which 1 were waited for; matrix products, arithmetic and copies ran while one was open for 9% of the time, Pallas kernels for 0%

profile of v11, /device:TPU:17, one launch (start us, length us, event | category | flops | bytes accessed | tf_op | source)
XLA Modules:
  0.0 64.1 jit_solution(7139663115717700669)
XLA Ops:
  0.0 0.9 %convert_element_type.8 = bf16[1,2,64,256]{3,2,1,0:T(8,128)(2,1)S(1)} convert(f32[1,2,64,256]{3,2,1,0:T(8,128)} %param.3) | non-fusion elementwise | flops 32768 | bytes 196608 | tf_op jit(solution)/shard_map/convert_element_type | solution.py:51
  0.9 0.1 copy.81
  1.0 19.0 %all_gather.3 = bf16[512,2,256]{2,1,0:T(2,128)(2,1)S(1)} all-gather(bf16[64,2,256]{2,1,0:T(2,128)(2,1)S(1)} %bitcast.109), channel_id=1, replica_groups=mesh['space'=64,'chan'=8] {'chan'}, dimensions={0}, use_global_device_ids=true | all-gather | bytes 589824 | tf_op jit(solution)/shard_map/all_gather | solution.py:52
  20.0 0.7 %copy.40 = bf16[512,2,256]{0,2,1:T(8,128)(2,1)S(1)} copy(bf16[512,2,256]{2,1,0:T(2,128)(2,1)S(1)} %all_gather.3) | data formatting | bytes 1048576 | tf_op jit(solution)/shard_map/all_gather | solution.py:52
  20.7 7.6 %collective-permute-start.2 = (bf16[512,1,1,32]{0,3,2,1:T(8,128)(2,1)S(1)}, bf16[512,1,1,32]{0,3,2,1:T(8,128)(2,1)S(1)}, u32[]{:S(2)}, u32[]{:S(2)}) collective-permute-start(bf16[512,1,1,32]{0,3,2,1:T(8,128)(2,1)S(1)} %get-tuple-element.18), channel_id=1, source_target_pairs={{0,76},{1,441},{2,78},{3,443},{4,72},{5,445},{6,74},{7,447},{8,84}... | collective-permute-start | bytes 98312 | tf_op jit(solution)/shard_map/ppermute | solution.py:26
  28.3 1.9 %collective-permute-start.3 = (bf16[512,1,1,32]{0,3,2,1:T(8,128)(2,1)S(1)}, bf16[512,1,1,32]{0,3,2,1:T(8,128)(2,1)S(1)}, u32[]{:S(2)}, u32[]{:S(2)}) collective-permute-start(bf16[512,1,1,32]{0,3,2,1:T(8,128)(2,1)S(1)} %get-tuple-element.17), channel_id=1, source_target_pairs={{0,56},{1,461},{2,58},{3,463},{4,60},{5,457},{6,62},{7,459},{8,68}... | collective-permute-start | bytes 98312 | tf_op jit(solution)/shard_map/ppermute | solution.py:26
  30.3 7.4 %collective-permute-start = (bf16[512,1,8,32]{0,3,2,1:T(8,128)(2,1)S(1)}, bf16[512,1,8,32]{0,3,2,1:T(8,128)(2,1)S(1)}, u32[]{:S(2)}, u32[]{:S(2)}) collective-permute-start(bf16[512,1,8,32]{0,3,2,1:T(8,128)(2,1)S(1)} %slice_select_fusion), channel_id=1, source_target_pairs={{0,68},{1,453},{2,70},{3,455},{4,64},{5,449},{6,66},{7,451},{8,76}... | collective-permute-start | bytes 786440 | tf_op jit(solution)/shard_map/ppermute | solution.py:26
  37.7 5.2 %collective-permute-start.1 = (bf16[512,2,1,32]{0,3,2,1:T(8,128)(2,1)S(1)}, bf16[512,2,1,32]{0,3,2,1:T(8,128)(2,1)S(1)}, u32[]{:S(2)}, u32[]{:S(2)}) collective-permute-start(bf16[512,2,1,32]{0,3,2,1:T(8,128)(2,1)S(1)} %slice_select_fusion.1), channel_id=1, source_target_pairs={{0,8},{1,509},{2,10},{3,511},{4,12},{5,505},{6,14},{7,507},{8,16},... | collective-permute-start | bytes 196616 | tf_op jit(solution)/shard_map/ppermute | solution.py:26
  42.9 0.3 copy.74
  43.2 0.0 copy-start.1
  43.2 0.0 copy-start.2
  43.3 0.2 copy.44
  43.5 0.1 slice.98
  43.5 1.1 %copy-done.1 = bf16[3,3,3,64,512]{4,3,2,1,0:T(8,128)(2,1)S(1)} copy-done((bf16[3,3,3,64,512]{4,3,2,1,0:T(8,128)(2,1)S(1)}, bf16[3,3,3,64,512]{4,3,2,1,0:T(8,128)(2,1)}, u32[]{:S(2)}) %copy-start.1) | copy-done | bytes 1769496
  44.7 0.0 copy-done.2
  44.7 4.7 %convolution_select_fusion = f32[2,8,8,5,64]{4,2,3,1,0:T(8,128)S(1)} fusion(bf16[3,3,3,64,512]{4,3,2,1,0:T(8,128)(2,1)S(1)} %copy-done.1, bf16[512,2,8,1,7,2]{0,4,5,2,1,3:T(8,128)(2,1)S(1)} %slice.98, bf16[512,2,8,1,8,5]{0,4,5,2,1,3:T(8,128)(2,1)S(1)} %copy.44, pred[8,5]{0,1:T(8,128)(4,1)S(1)} %copy-done.2), kind=kOutput, calls=%fused_computation.2 | convolution fusion | flops 694853632 | bytes 2818088 | tf_op jit(solution)/shard_map/conv_general_dilated | solution.py:37
  49.4 0.1 copy.45
  49.5 0.0 collective-permute-done.2
  49.5 0.0 collective-permute-done.3
  49.5 0.0 collective-permute-done.1
  49.5 0.0 collective-permute-done
  49.5 7.6 %collective-permute-start.4 = (bf16[512,384]{0,1:T(8,128)(2,1)S(1)}, bf16[512,384]{0,1:T(8,128)(2,1)S(1)}, u32[]{:S(2)}, u32[]{:S(2)}) collective-permute-start(bf16[512,384]{0,1:T(8,128)(2,1)S(1)} %pad_maximum_fusion), channel_id=1, source_target_pairs={{0,1},{1,0},{2,3},{3,2},{4,5},{5,4},{6,7},{7,6},{8,9},{9,8},{10,11... | collective-permute-start | bytes 1179656 | tf_op jit(solution)/shard_map/ppermute | solution.py:32
  57.2 0.1 pad.11.clone
  57.2 1.2 %collective-permute-done.4 = bf16[512,384]{0,1:T(8,128)(2,1)S(1)} collective-permute-done((bf16[512,384]{0,1:T(8,128)(2,1)S(1)}, bf16[512,384]{0,1:T(8,128)(2,1)S(1)}, u32[]{:S(2)}, u32[]{:S(2)}) %collective-permute-start.4) | collective-permute-done | bytes 393248 | tf_op jit(solution)/shard_map/ppermute | solution.py:32
  58.5 0.1 broadcast_select_fusion.1
  58.8 0.1 copy.75
  58.9 0.1 pad.6.clone
  59.0 0.3 convolution_select_fusion.4
  59.4 0.1 copy.76
  59.5 0.1 pad.8.clone
  59.7 0.3 convolution_select_fusion.3
  60.1 0.2 copy.77
  60.3 0.1 copy.48
  60.4 0.9 %convolution_select_fusion.2 = f32[1,8,8,5,64]{4,2,3,1,0:T(8,128)S(1)} fusion(bf16[3,3,3,64,512]{4,3,2,1,0:T(8,128)(2,1)S(1)} %copy-done.1, bf16[512,1,8,1,7,2]{0,4,5,2,3,1:T(8,128)(2,1)S(1)} %slice.101, bf16[512,1,8,1,8,5]{0,4,5,2,3,1:T(8,128)(2,1)S(1)} %copy.48, pred[8,5]{0,1:T(8,128)(4,1)S(1)} %copy-done.2), kind=kOutput, calls=%fused_computation.4 | convolution fusion | flops 174411776 | bytes 1131520 | tf_op jit(solution)/shard_map/conv_general_dilated | solution.py:37
  61.4 0.2 copy.78
  61.6 0.1 copy.53
  61.7 0.9 %convolution_select_fusion.1 = f32[1,8,8,5,64]{4,2,3,1,0:T(8,128)S(1)} fusion(bf16[3,3,3,64,512]{4,3,2,1,0:T(8,128)(2,1)S(1)} %copy-done.1, bf16[512,1,8,1,7,2]{0,4,5,2,3,1:T(8,128)(2,1)S(1)} %slice.104, bf16[512,1,8,1,8,5]{0,4,5,2,3,1:T(8,128)(2,1)S(1)} %copy.53, pred[8,5]{0,1:T(8,128)(4,1)S(1)} %copy-done.2), kind=kOutput, calls=%fused_computation.3 | convolution fusion | flops 174411776 | bytes 1131520 | tf_op jit(solution)/shard_map/conv_general_dilated | solution.py:37
  62.7 0.0 copy-start
  62.7 0.1 fusion.29
  62.9 0.1 copy.70
  62.9 0.4 copy-done
  63.3 0.8 %copy.71 = f32[1,2,64,256]{3,2,1,0:T(8,128)} copy(f32[1,2,64,256]{2,3,1,0:T(8,128)S(1)} %fusion.28) | data formatting | bytes 262144 | tf_op jit(solution)/shard_map/broadcast_in_dim | solution.py:96
  (32 shorter events, 0.6 us)
Async XLA Ops:
  20.7 28.7 %collective-permute-start.2 = (bf16[512,1,1,32]{0,3,2,1:T(8,128)(2,1)S(1)}, bf16[512,1,1,32]{0,3,2,1:T(8,128)(2,1)S(1)}, u32[]{:S(2)}, u32[]{:S(2)}) collective-permute-start(bf16[512,1,1,32]{0,3,2,1:T(8,128)(2,1)S(1)} %get-tuple-element.18), channel_id=1, source_target_pairs={{0,76},{1,441},{2,78},{3,443},{4,72},{5,445},{6,74},{7,447},{8,84}... | collective-permute-start | bytes 98312 | tf_op jit(solution)/shard_map/ppermute | solution.py:26
  28.3 21.1 %collective-permute-start.3 = (bf16[512,1,1,32]{0,3,2,1:T(8,128)(2,1)S(1)}, bf16[512,1,1,32]{0,3,2,1:T(8,128)(2,1)S(1)}, u32[]{:S(2)}, u32[]{:S(2)}) collective-permute-start(bf16[512,1,1,32]{0,3,2,1:T(8,128)(2,1)S(1)} %get-tuple-element.17), channel_id=1, source_target_pairs={{0,56},{1,461},{2,58},{3,463},{4,60},{5,457},{6,62},{7,459},{8,68}... | collective-permute-start | bytes 98312 | tf_op jit(solution)/shard_map/ppermute | solution.py:26
  30.3 19.2 %collective-permute-start = (bf16[512,1,8,32]{0,3,2,1:T(8,128)(2,1)S(1)}, bf16[512,1,8,32]{0,3,2,1:T(8,128)(2,1)S(1)}, u32[]{:S(2)}, u32[]{:S(2)}) collective-permute-start(bf16[512,1,8,32]{0,3,2,1:T(8,128)(2,1)S(1)} %slice_select_fusion), channel_id=1, source_target_pairs={{0,68},{1,453},{2,70},{3,455},{4,64},{5,449},{6,66},{7,451},{8,76}... | collective-permute-start | bytes 786440 | tf_op jit(solution)/shard_map/ppermute | solution.py:26
  37.7 11.8 %collective-permute-start.1 = (bf16[512,2,1,32]{0,3,2,1:T(8,128)(2,1)S(1)}, bf16[512,2,1,32]{0,3,2,1:T(8,128)(2,1)S(1)}, u32[]{:S(2)}, u32[]{:S(2)}) collective-permute-start(bf16[512,2,1,32]{0,3,2,1:T(8,128)(2,1)S(1)} %slice_select_fusion.1), channel_id=1, source_target_pairs={{0,8},{1,509},{2,10},{3,511},{4,12},{5,505},{6,14},{7,507},{8,16},... | collective-permute-start | bytes 196616 | tf_op jit(solution)/shard_map/ppermute | solution.py:26
  43.2 1.5 %copy-start.1 = (bf16[3,3,3,64,512]{4,3,2,1,0:T(8,128)(2,1)S(1)}, bf16[3,3,3,64,512]{4,3,2,1,0:T(8,128)(2,1)}, u32[]{:S(2)}) copy-start(bf16[3,3,3,64,512]{4,3,2,1,0:T(8,128)(2,1)} %param.4) | copy-start | bytes 5308420
  43.2 1.5 %copy-start.2 = (pred[8,5]{0,1:T(8,128)(4,1)S(1)}, pred[8,5]{0,1:T(8,128)(4,1)}, u32[]{:S(2)}) copy-start(pred[8,5]{0,1:T(8,128)(4,1)} %constant.71) | copy-start | bytes 124
  49.5 8.9 %collective-permute-start.4 = (bf16[512,384]{0,1:T(8,128)(2,1)S(1)}, bf16[512,384]{0,1:T(8,128)(2,1)S(1)}, u32[]{:S(2)}, u32[]{:S(2)}) collective-permute-start(bf16[512,384]{0,1:T(8,128)(2,1)S(1)} %pad_maximum_fusion), channel_id=1, source_target_pairs={{0,1},{1,0},{2,3},{3,2},{4,5},{5,4},{6,7},{7,6},{8,9},{9,8},{10,11... | collective-permute-start | bytes 1179656 | tf_op jit(solution)/shard_map/ppermute | solution.py:32
  62.7 0.7 %copy-start = (f32[64]{0:T(128)S(1)}, f32[64]{0:T(128)}, u32[]{:S(2)}) copy-start(f32[64]{0:T(128)} %param.5) | copy-start | bytes 772

commit v12 on v11

--- a/solution.py
+++ b/solution.py
@@ -56,8 +56,11 @@
     got = [
         cross(gathered[:, -1:], gathered[:, :1], "space", CY),
         cross(gathered[:, :, -1:], gathered[:, :, :1], "space", 1),
-        cross(gathered[:, -1:, -1:], gathered[:, :1, :1], "space", CY + 1),
-        cross(gathered[:, -1:, :1], gathered[:, :1, -1:], "space", CY - 1),
+    ]
+    corners_from, own_part = lax.optimization_barrier((gathered[:, ::size_x - 1, ::size_y - 1], own_part))
+    got += [
+        cross(corners_from[:, 1:, 1:], corners_from[:, :1, :1], "space", CY + 1),
+        cross(corners_from[:, 1:, :1], corners_from[:, :1, 1:], "space", CY - 1),
     ]
     got, own_part = lax.optimization_barrier((got, own_part))
     sizes = [piece[0].size for piece in got]

time: 64.4 us -> 64.2 us (level)
  the two profiles are of different devices: /device:TPU:17 before, /device:TPU:65 now
where the time goes in v12:
time: 64.2 us; the launch traced here: 63.9 us
  starting transfers between devices  26.7 us (42%)
  blocking collectives  15.6 us (24%)
  waiting for transfers between devices  7.32 us (11%)
  matrix products  7.22 us (11%)
  local copies, waits for them, and re-layouts  5.18 us (8%)
  other arithmetic  1.34 us (2%)
    ppermute x4, starting transfers between devices, cross(): return lax.ppermute(sent, (axis, 'chan'), pairs)  24.8 us
    all_gather x1, blocking collectives, body(): gathered = lax.all_gather(own_block, 'chan', axis=0, tiled=True)  15.6 us
    conv_general_dilated x5, matrix products, conv(): lax.conv_general_dilated(field[None], taps, window_strides=(1, 1, 1), pad...  7.22 us
    ppermute x4, waiting for transfers between devices, cross(): return lax.ppermute(sent, (axis, 'chan'), pairs)  5.74 us
    unnamed x14, local copies, waits for them, and re-layouts  2.41 us
    ppermute x1, starting transfers between devices, swap(): lax.ppermute(got, 'chan', [(lane, lane ^ 1) for lane in range(width)])  1.92 us
    ppermute x1, waiting for transfers between devices, swap(): lax.ppermute(got, 'chan', [(lane, lane ^ 1) for lane in range(width)])  1.59 us
  transfers between devices with their start and end apart: 5, of which 2 were waited for; matrix products, arithmetic and copies ran while one was open for 9% of the time, Pallas kernels for 0%

profile of v12, /device:TPU:65, one launch (start us, length us, event | category | flops | bytes accessed | tf_op | source)
XLA Modules:
  0.0 63.9 jit_solution(6020378528566479765)
XLA Ops:
  0.0 0.9 %convert_element_type.8 = bf16[1,2,64,256]{3,2,1,0:T(8,128)(2,1)S(1)} convert(f32[1,2,64,256]{3,2,1,0:T(8,128)} %param.3) | non-fusion elementwise | flops 32768 | bytes 196608 | tf_op jit(solution)/shard_map/convert_element_type | solution.py:51
  0.9 0.1 copy.81
  1.0 15.6 %all_gather.3 = bf16[512,2,256]{2,1,0:T(2,128)(2,1)S(1)} all-gather(bf16[64,2,256]{2,1,0:T(2,128)(2,1)S(1)} %bitcast.109), channel_id=1, replica_groups=mesh['space'=64,'chan'=8] {'chan'}, dimensions={0}, use_global_device_ids=true | all-gather | bytes 589824 | tf_op jit(solution)/shard_map/all_gather | solution.py:52
  16.6 0.7 %copy.40 = bf16[512,2,256]{0,2,1:T(8,128)(2,1)S(1)} copy(bf16[512,2,256]{2,1,0:T(2,128)(2,1)S(1)} %all_gather.3) | data formatting | bytes 1048576 | tf_op jit(solution)/shard_map/all_gather | solution.py:52
  17.4 7.7 %collective-permute-start = (bf16[512,1,8,32]{0,3,2,1:T(8,128)(2,1)S(1)}, bf16[512,1,8,32]{0,3,2,1:T(8,128)(2,1)S(1)}, u32[]{:S(2)}, u32[]{:S(2)}) collective-permute-start(bf16[512,1,8,32]{0,3,2,1:T(8,128)(2,1)S(1)} %slice_select_fusion), channel_id=1, source_target_pairs={{0,68},{1,453},{2,70},{3,455},{4,64},{5,449},{6,66},{7,451},{8,76}... | collective-permute-start | bytes 786440 | tf_op jit(solution)/shard_map/ppermute | solution.py:26
  25.1 1.9 %collective-permute-start.1 = (bf16[512,2,1,32]{0,3,2,1:T(8,128)(2,1)S(1)}, bf16[512,2,1,32]{0,3,2,1:T(8,128)(2,1)S(1)}, u32[]{:S(2)}, u32[]{:S(2)}) collective-permute-start(bf16[512,2,1,32]{0,3,2,1:T(8,128)(2,1)S(1)} %slice_select_fusion.1), channel_id=1, source_target_pairs={{0,8},{1,509},{2,10},{3,511},{4,12},{5,505},{6,14},{7,507},{8,16},... | collective-permute-start | bytes 196616 | tf_op jit(solution)/shard_map/ppermute | solution.py:26
  27.0 0.3 copy.74
  27.3 0.0 copy-start.1
  27.3 0.0 copy-start.2
  27.4 0.2 copy.44
  27.6 0.1 slice.98
  27.7 1.1 %copy-done.1 = bf16[3,3,3,64,512]{4,3,2,1,0:T(8,128)(2,1)S(1)} copy-done((bf16[3,3,3,64,512]{4,3,2,1,0:T(8,128)(2,1)S(1)}, bf16[3,3,3,64,512]{4,3,2,1,0:T(8,128)(2,1)}, u32[]{:S(2)}) %copy-start.1) | copy-done | bytes 1769496
  28.8 0.0 copy-done.2
  28.8 4.7 %convolution_select_fusion = f32[2,8,8,5,64]{4,2,3,1,0:T(8,128)S(1)} fusion(bf16[3,3,3,64,512]{4,3,2,1,0:T(8,128)(2,1)S(1)} %copy-done.1, bf16[512,2,8,1,7,2]{0,4,5,2,1,3:T(8,128)(2,1)S(1)} %slice.98, bf16[512,2,8,1,8,5]{0,4,5,2,1,3:T(8,128)(2,1)S(1)} %copy.44, pred[8,5]{0,1:T(8,128)(4,1)S(1)} %copy-done.2), kind=kOutput, calls=%fused_computation.2 | convolution fusion | flops 694853632 | bytes 2818088 | tf_op jit(solution)/shard_map/conv_general_dilated | solution.py:37
  33.5 0.1 copy.45
  33.7 13.3 %collective-permute-start.2 = (bf16[512,1,1,32]{0,3,2,1:T(8,128)(2,1)S(1)}, bf16[512,1,1,32]{0,3,2,1:T(8,128)(2,1)S(1)}, u32[]{:S(2)}, u32[]{:S(2)}) collective-permute-start(bf16[512,1,1,32]{0,3,2,1:T(8,128)(2,1)S(1)} %get-tuple-element.26), channel_id=1, source_target_pairs={{0,76},{1,441},{2,78},{3,443},{4,72},{5,445},{6,74},{7,447},{8,84}... | collective-permute-start | bytes 98312 | tf_op jit(solution)/shard_map/ppermute | solution.py:26
  47.0 1.9 %collective-permute-start.3 = (bf16[512,1,1,32]{0,3,2,1:T(8,128)(2,1)S(1)}, bf16[512,1,1,32]{0,3,2,1:T(8,128)(2,1)S(1)}, u32[]{:S(2)}, u32[]{:S(2)}) collective-permute-start(bf16[512,1,1,32]{0,3,2,1:T(8,128)(2,1)S(1)} %get-tuple-element.25), channel_id=1, source_target_pairs={{0,56},{1,461},{2,58},{3,463},{4,60},{5,457},{6,62},{7,459},{8,68}... | collective-permute-start | bytes 98312 | tf_op jit(solution)/shard_map/ppermute | solution.py:26
  48.9 0.0 collective-permute-done.2
  48.9 5.7 %collective-permute-done.3 = bf16[512,1,1,32]{0,3,2,1:T(8,128)(2,1)S(1)} collective-permute-done((bf16[512,1,1,32]{0,3,2,1:T(8,128)(2,1)S(1)}, bf16[512,1,1,32]{0,3,2,1:T(8,128)(2,1)S(1)}, u32[]{:S(2)}, u32[]{:S(2)}) %collective-permute-start.3) | collective-permute-done | bytes 32800 | tf_op jit(solution)/shard_map/ppermute | solution.py:26
  54.6 0.0 collective-permute-done.1
  54.6 0.0 collective-permute-done
  54.7 1.9 %collective-permute-start.4 = (bf16[512,384]{0,1:T(8,128)(2,1)S(1)}, bf16[512,384]{0,1:T(8,128)(2,1)S(1)}, u32[]{:S(2)}, u32[]{:S(2)}) collective-permute-start(bf16[512,384]{0,1:T(8,128)(2,1)S(1)} %pad_maximum_fusion), channel_id=1, source_target_pairs={{0,1},{1,0},{2,3},{3,2},{4,5},{5,4},{6,7},{7,6},{8,9},{9,8},{10,11... | collective-permute-start | bytes 1179656 | tf_op jit(solution)/shard_map/ppermute | solution.py:32
  56.6 0.1 pad.11.clone
  56.7 1.6 %collective-permute-done.4 = bf16[512,384]{0,1:T(8,128)(2,1)S(1)} collective-permute-done((bf16[512,384]{0,1:T(8,128)(2,1)S(1)}, bf16[512,384]{0,1:T(8,128)(2,1)S(1)}, u32[]{:S(2)}, u32[]{:S(2)}) %collective-permute-start.4) | collective-permute-done | bytes 393248 | tf_op jit(solution)/shard_map/ppermute | solution.py:32
  58.3 0.1 broadcast_select_fusion.1
  58.6 0.1 copy.75
  58.7 0.1 pad.6.clone
  58.8 0.3 convolution_select_fusion.4
  59.3 0.1 copy.76
  59.4 0.1 pad.8.clone
  59.5 0.3 convolution_select_fusion.3
  59.9 0.2 copy.77
  60.1 0.1 copy.48
  60.2 0.9 %convolution_select_fusion.2 = f32[1,8,8,5,64]{4,2,3,1,0:T(8,128)S(1)} fusion(bf16[3,3,3,64,512]{4,3,2,1,0:T(8,128)(2,1)S(1)} %copy-done.1, bf16[512,1,8,1,7,2]{0,4,5,2,3,1:T(8,128)(2,1)S(1)} %slice.101, bf16[512,1,8,1,8,5]{0,4,5,2,3,1:T(8,128)(2,1)S(1)} %copy.48, pred[8,5]{0,1:T(8,128)(4,1)S(1)} %copy-done.2), kind=kOutput, calls=%fused_computation.4 | convolution fusion | flops 174411776 | bytes 1131520 | tf_op jit(solution)/shard_map/conv_general_dilated | solution.py:37
  61.2 0.2 copy.78
  61.4 0.1 copy.53
  61.5 0.9 %convolution_select_fusion.1 = f32[1,8,8,5,64]{4,2,3,1,0:T(8,128)S(1)} fusion(bf16[3,3,3,64,512]{4,3,2,1,0:T(8,128)(2,1)S(1)} %copy-done.1, bf16[512,1,8,1,7,2]{0,4,5,2,3,1:T(8,128)(2,1)S(1)} %slice.104, bf16[512,1,8,1,8,5]{0,4,5,2,3,1:T(8,128)(2,1)S(1)} %copy.53, pred[8,5]{0,1:T(8,128)(4,1)S(1)} %copy-done.2), kind=kOutput, calls=%fused_computation.3 | convolution fusion | flops 174411776 | bytes 1131520 | tf_op jit(solution)/shard_map/conv_general_dilated | solution.py:37
  62.5 0.0 copy-start
  62.6 0.1 fusion.29
  62.7 0.1 copy.70
  62.7 0.4 copy-done
  63.2 0.8 %copy.71 = f32[1,2,64,256]{3,2,1,0:T(8,128)} copy(f32[1,2,64,256]{2,3,1,0:T(8,128)S(1)} %fusion.28) | data formatting | bytes 262144 | tf_op jit(solution)/shard_map/broadcast_in_dim | solution.py:99
  (33 shorter events, 0.7 us)
Async XLA Ops:
  17.4 37.2 %collective-permute-start = (bf16[512,1,8,32]{0,3,2,1:T(8,128)(2,1)S(1)}, bf16[512,1,8,32]{0,3,2,1:T(8,128)(2,1)S(1)}, u32[]{:S(2)}, u32[]{:S(2)}) collective-permute-start(bf16[512,1,8,32]{0,3,2,1:T(8,128)(2,1)S(1)} %slice_select_fusion), channel_id=1, source_target_pairs={{0,68},{1,453},{2,70},{3,455},{4,64},{5,449},{6,66},{7,451},{8,76}... | collective-permute-start | bytes 786440 | tf_op jit(solution)/shard_map/ppermute | solution.py:26
  25.1 29.5 %collective-permute-start.1 = (bf16[512,2,1,32]{0,3,2,1:T(8,128)(2,1)S(1)}, bf16[512,2,1,32]{0,3,2,1:T(8,128)(2,1)S(1)}, u32[]{:S(2)}, u32[]{:S(2)}) collective-permute-start(bf16[512,2,1,32]{0,3,2,1:T(8,128)(2,1)S(1)} %slice_select_fusion.1), channel_id=1, source_target_pairs={{0,8},{1,509},{2,10},{3,511},{4,12},{5,505},{6,14},{7,507},{8,16},... | collective-permute-start | bytes 196616 | tf_op jit(solution)/shard_map/ppermute | solution.py:26
  27.3 1.5 %copy-start.1 = (bf16[3,3,3,64,512]{4,3,2,1,0:T(8,128)(2,1)S(1)}, bf16[3,3,3,64,512]{4,3,2,1,0:T(8,128)(2,1)}, u32[]{:S(2)}) copy-start(bf16[3,3,3,64,512]{4,3,2,1,0:T(8,128)(2,1)} %param.4) | copy-start | bytes 5308420
  27.3 1.5 %copy-start.2 = (pred[8,5]{0,1:T(8,128)(4,1)S(1)}, pred[8,5]{0,1:T(8,128)(4,1)}, u32[]{:S(2)}) copy-start(pred[8,5]{0,1:T(8,128)(4,1)} %constant.71) | copy-start | bytes 124
  33.7 15.2 %collective-permute-start.2 = (bf16[512,1,1,32]{0,3,2,1:T(8,128)(2,1)S(1)}, bf16[512,1,1,32]{0,3,2,1:T(8,128)(2,1)S(1)}, u32[]{:S(2)}, u32[]{:S(2)}) collective-permute-start(bf16[512,1,1,32]{0,3,2,1:T(8,128)(2,1)S(1)} %get-tuple-element.26), channel_id=1, source_target_pairs={{0,76},{1,441},{2,78},{3,443},{4,72},{5,445},{6,74},{7,447},{8,84}... | collective-permute-start | bytes 98312 | tf_op jit(solution)/shard_map/ppermute | solution.py:26
  47.0 7.7 %collective-permute-start.3 = (bf16[512,1,1,32]{0,3,2,1:T(8,128)(2,1)S(1)}, bf16[512,1,1,32]{0,3,2,1:T(8,128)(2,1)S(1)}, u32[]{:S(2)}, u32[]{:S(2)}) collective-permute-start(bf16[512,1,1,32]{0,3,2,1:T(8,128)(2,1)S(1)} %get-tuple-element.25), channel_id=1, source_target_pairs={{0,56},{1,461},{2,58},{3,463},{4,60},{5,457},{6,62},{7,459},{8,68}... | collective-permute-start | bytes 98312 | tf_op jit(solution)/shard_map/ppermute | solution.py:26
  54.7 3.6 %collective-permute-start.4 = (bf16[512,384]{0,1:T(8,128)(2,1)S(1)}, bf16[512,384]{0,1:T(8,128)(2,1)S(1)}, u32[]{:S(2)}, u32[]{:S(2)}) collective-permute-start(bf16[512,384]{0,1:T(8,128)(2,1)S(1)} %pad_maximum_fusion), channel_id=1, source_target_pairs={{0,1},{1,0},{2,3},{3,2},{4,5},{5,4},{6,7},{7,6},{8,9},{9,8},{10,11... | collective-permute-start | bytes 1179656 | tf_op jit(solution)/shard_map/ppermute | solution.py:32
  62.5 0.7 %copy-start = (f32[64]{0:T(128)S(1)}, f32[64]{0:T(128)}, u32[]{:S(2)}) copy-start(f32[64]{0:T(128)} %param.5) | copy-start | bytes 772

commit v13 on v12

--- a/solution.py
+++ b/solution.py
@@ -64,35 +64,42 @@
     ]
     got, own_part = lax.optimization_barrier((got, own_part))
     sizes = [piece[0].size for piece in got]
-    joined = jnp.concatenate([piece.reshape(width_in, -1) for piece in got], axis=1)
-    lower_all, upper_all = swap(joined)
     offsets = [sum(sizes[:k]) for k in range(len(sizes) + 1)]
+    mine = jnp.concatenate([piece.reshape(width_in, -1) for piece in got], axis=1)
+    width = lax.axis_size("chan")
+    parity = lax.axis_index("chan") % 2
+    place_y = (lax.axis_index("space") + 4) % 8
 
-    def piece(joined_half, k):
-        return joined_half[:, offsets[k] : offsets[k + 1]].reshape(got[k].shape)
+    def halo_part(joined, side):
+        face, row, corner_a, corner_b = (
+            joined[:, offsets[k] : offsets[k + 1]].reshape(got[k].shape) for k in range(4)
+        )
+        width_out = weight.shape[3]
+        zeros_rim = jnp.zeros((width_in, size_x + 2, 1, size_z), joined.dtype)
+        row_rim = lax.dynamic_update_slice(zeros_rim, row, (0, 1, 0, 0))
+        row_rim = lax.dynamic_update_slice(row_rim, corner_a, (0, 3 * side, 0, 0))
+        corner_rim = lax.dynamic_update_slice(zeros_rim, corner_b, (0, 3 * side, 0, 0))
+        face_taps = lax.dynamic_slice_in_dim(weight, 2 * side, 1, axis=0)
+        row_taps = lax.dynamic_slice_in_dim(weight, 2 * side, 1, axis=1)
+        corner_taps = lax.dynamic_slice_in_dim(weight, 2 - 2 * side, 1, axis=1)
+        face_out = conv(face, face_taps, ((0, 0), (1, 1), (1, 1)))
+        row_out = conv(row_rim, row_taps, ((0, 0), (0, 0), (1, 1)))
+        corner_out = conv(corner_rim, corner_taps, ((0, 0), (0, 0), (1, 1)))
+        row_valid = jnp.where(side == 0, place_y > 0, place_y < 7)
+        corner_valid = jnp.where(side == 0, place_y < 7, place_y > 0)
+        row_out = jnp.where(row_valid, row_out, jnp.zeros_like(row_out))
+        corner_out = jnp.where(corner_valid, corner_out, jnp.zeros_like(corner_out))
+        zeros_out = jnp.zeros((width_out, size_x, size_y, size_z), jnp.float32)
+        part = lax.dynamic_update_slice(zeros_out, face_out, (0, side, 0, 0))
+        part = part + lax.dynamic_update_slice(zeros_out, row_out, (0, 0, (size_y - 1) * side, 0))
+        return part + lax.dynamic_update_slice(zeros_out, corner_out, (0, 0, (size_y - 1) * (1 - side), 0))
 
-    below, above = piece(lower_all, 0), piece(upper_all, 0)
-    lower_row, upper_row = piece(lower_all, 1), piece(upper_all, 1)
-    corner_ll, corner_hh = piece(lower_all, 2), piece(upper_all, 2)
-    corner_lh, corner_hl = piece(lower_all, 3), piece(upper_all, 3)
-    face_part = jnp.concatenate(
-        [
-            conv(below, weight[:1], ((0, 0), (1, 1), (1, 1))),
-            conv(above, weight[2:], ((0, 0), (1, 1), (1, 1))),
-        ],
-        axis=1,
-    )
-    place_y = (lax.axis_index("space") + 4) % 8
-    lower_rim = jnp.concatenate([corner_ll, lower_row, corner_hl], axis=1)
-    upper_rim = jnp.concatenate([corner_lh, upper_row, corner_hh], axis=1)
-    lower_rim = jnp.where(place_y > 0, lower_rim, jnp.zeros_like(lower_rim))
-    upper_rim = jnp.where(place_y < 7, upper_rim, jnp.zeros_like(upper_rim))
-    lower_part = conv(lower_rim, weight[:, :1], ((0, 0), (0, 0), (1, 1)))
-    upper_part = conv(upper_rim, weight[:, 2:], ((0, 0), (0, 0), (1, 1)))
+    other = lax.ppermute(mine, "chan", [(lane, lane ^ 1) for lane in range(width)])
+    mine_part = halo_part(mine, parity)
+    other, mine_part = lax.optimization_barrier((other, mine_part))
+    own_part = own_part + mine_part + halo_part(other, 1 - parity)
     width_out = own_part.shape[0]
-    middle = jnp.zeros((width_out, size_x, size_y - 2, size_z), jnp.float32)
-    rim_part = jnp.concatenate([lower_part, middle, upper_part], axis=2)
-    total = (own_part + face_part + rim_part).reshape(width_out, -1)
+    total = own_part.reshape(width_out, -1)
     before = total + conv_bias[:, None]
     result = jnp.maximum(before, negative_slope * before)
     result = result.reshape(width_out, size_x, size_y * size_z).transpose(1, 0, 2)

time: 64.2 us -> 66.2 us (1.031)
  local copies, waits for them, and re-layouts: 5.18 us -> 6.53 us
  matrix products: 7.22 us -> 7.94 us
    dynamic_update_slice x0 -> x17, local copies, waits for them, and re-layouts: none -> 1.66 us  [the longest x9 1.47 us: halo_part(): lax.dynamic_update_slice(zeros_rim, corner_b, (0, 3 * side, 0, 0))]
    unnamed x14 -> x18, local copies, waits for them, and re-layouts: 2.41 us -> 1.27 us
    conv_general_dilated x5 -> x7, matrix products: 7.22 us -> 7.94 us  [conv(): lax.conv_general_dilated(field[None], taps, window_strides=(1, 1, 1), pad...]
where the time goes in v13:
time: 66.2 us; the launch traced here: 65.9 us
  starting transfers between devices  26.7 us (40%)
  blocking collectives  15.6 us (24%)
  matrix products  7.94 us (12%)
  waiting for transfers between devices  6.87 us (10%)
  local copies, waits for them, and re-layouts  6.53 us (10%)
  other arithmetic  1.36 us (2%)
  between operations  0.78 us (1%)
    ppermute x4, starting transfers between devices, cross(): return lax.ppermute(sent, (axis, 'chan'), pairs)  24.8 us
    all_gather x1, blocking collectives, body(): gathered = lax.all_gather(own_block, 'chan', axis=0, tiled=True)  15.6 us
    conv_general_dilated x7, matrix products, conv(): lax.conv_general_dilated(field[None], taps, window_strides=(1, 1, 1), pad...  7.94 us
    ppermute x4, waiting for transfers between devices, cross(): return lax.ppermute(sent, (axis, 'chan'), pairs)  5.65 us
    ppermute x1, starting transfers between devices, body(): lax.ppermute(mine, 'chan', [(lane, lane ^ 1) for lane in range(width)])  1.92 us
    dynamic_update_slice x9, local copies, waits for them, and re-layouts, halo_part(): lax.dynamic_update_slice(zeros_rim, corner_b, (0, 3 * side, 0, 0))  1.47 us
  transfers between devices with their start and end apart: 5, of which 2 were waited for; matrix products, arithmetic and copies ran while one was open for 9% of the time, Pallas kernels for 0%

profile of v13, /device:TPU:65, one launch (start us, length us, event | category | flops | bytes accessed | tf_op | source)
XLA Modules:
  0.0 65.9 jit_solution(10951742384851707662)
XLA Ops:
  0.0 0.0 copy-start
  0.0 1.0 %convert_element_type.8 = bf16[1,2,64,256]{3,2,1,0:T(8,128)(2,1)S(1)} convert(f32[1,2,64,256]{3,2,1,0:T(8,128)} %param.3) | non-fusion elementwise | flops 32768 | bytes 196608 | tf_op jit(solution)/shard_map/convert_element_type | solution.py:51
  1.0 0.1 copy.96
  1.1 15.6 %all_gather.3 = bf16[512,2,256]{2,1,0:T(2,128)(2,1)S(1)} all-gather(bf16[64,2,256]{2,1,0:T(2,128)(2,1)S(1)} %bitcast.122), channel_id=1, replica_groups=mesh['space'=64,'chan'=8] {'chan'}, dimensions={0}, use_global_device_ids=true | all-gather | bytes 589824 | tf_op jit(solution)/shard_map/all_gather | solution.py:52
  16.8 0.7 %copy.46 = bf16[512,2,256]{0,2,1:T(8,128)(2,1)S(1)} copy(bf16[512,2,256]{2,1,0:T(2,128)(2,1)S(1)} %all_gather.3) | data formatting | bytes 1048576 | tf_op jit(solution)/shard_map/all_gather | solution.py:52
  17.5 7.7 %collective-permute-start = (bf16[512,1,8,32]{0,3,2,1:T(8,128)(2,1)S(1)}, bf16[512,1,8,32]{0,3,2,1:T(8,128)(2,1)S(1)}, u32[]{:S(2)}, u32[]{:S(2)}) collective-permute-start(bf16[512,1,8,32]{0,3,2,1:T(8,128)(2,1)S(1)} %slice_select_fusion), channel_id=1, source_target_pairs={{0,68},{1,453},{2,70},{3,455},{4,64},{5,449},{6,66},{7,451},{8,76}... | collective-permute-start | bytes 786440 | tf_op jit(solution)/shard_map/ppermute | solution.py:26
  25.2 1.9 %collective-permute-start.1 = (bf16[512,2,1,32]{0,3,2,1:T(8,128)(2,1)S(1)}, bf16[512,2,1,32]{0,3,2,1:T(8,128)(2,1)S(1)}, u32[]{:S(2)}, u32[]{:S(2)}) collective-permute-start(bf16[512,2,1,32]{0,3,2,1:T(8,128)(2,1)S(1)} %slice_select_fusion.1), channel_id=1, source_target_pairs={{0,8},{1,509},{2,10},{3,511},{4,12},{5,505},{6,14},{7,507},{8,16},... | collective-permute-start | bytes 196616 | tf_op jit(solution)/shard_map/ppermute | solution.py:26
  27.2 0.3 copy.89
  27.5 0.0 copy-start.3
  27.5 0.2 copy.50
  27.7 0.1 slice.70
  27.8 0.0 copy-done
  27.8 0.3 copy-done.3
  28.1 4.7 %convolution_select_fusion = f32[2,8,8,5,64]{4,2,3,1,0:T(8,128)S(1)} fusion(bf16[3,3,3,64,512]{4,3,2,1,0:T(8,128)(2,1)S(1)} %copy-done, bf16[512,2,8,1,7,2]{0,4,5,2,1,3:T(8,128)(2,1)S(1)} %slice.70, bf16[512,2,8,1,8,5]{0,4,5,2,1,3:T(8,128)(2,1)S(1)} %copy.50, pred[8,5]{0,1:T(8,128)(4,1)S(1)} %copy-done.3), kind=kOutput, calls=%fused_computation.2 | convolution fusion | flops 694853632 | bytes 2818088 | tf_op jit(solution)/shard_map/conv_general_dilated | solution.py:37
  32.9 0.1 copy.51
  33.0 13.3 %collective-permute-start.2 = (bf16[512,1,1,32]{0,3,2,1:T(8,128)(2,1)S(1)}, bf16[512,1,1,32]{0,3,2,1:T(8,128)(2,1)S(1)}, u32[]{:S(2)}, u32[]{:S(2)}) collective-permute-start(bf16[512,1,1,32]{0,3,2,1:T(8,128)(2,1)S(1)} %get-tuple-element.24), channel_id=1, source_target_pairs={{0,76},{1,441},{2,78},{3,443},{4,72},{5,445},{6,74},{7,447},{8,84}... | collective-permute-start | bytes 98312 | tf_op jit(solution)/shard_map/ppermute | solution.py:26
  46.3 1.9 %collective-permute-start.3 = (bf16[512,1,1,32]{0,3,2,1:T(8,128)(2,1)S(1)}, bf16[512,1,1,32]{0,3,2,1:T(8,128)(2,1)S(1)}, u32[]{:S(2)}, u32[]{:S(2)}) collective-permute-start(bf16[512,1,1,32]{0,3,2,1:T(8,128)(2,1)S(1)} %get-tuple-element.23), channel_id=1, source_target_pairs={{0,56},{1,461},{2,58},{3,463},{4,60},{5,457},{6,62},{7,459},{8,68}... | collective-permute-start | bytes 98312 | tf_op jit(solution)/shard_map/ppermute | solution.py:26
  48.3 0.0 collective-permute-done.2
  48.3 5.6 %collective-permute-done.3 = bf16[512,1,1,32]{0,3,2,1:T(8,128)(2,1)S(1)} collective-permute-done((bf16[512,1,1,32]{0,3,2,1:T(8,128)(2,1)S(1)}, bf16[512,1,1,32]{0,3,2,1:T(8,128)(2,1)S(1)}, u32[]{:S(2)}, u32[]{:S(2)}) %collective-permute-start.3) | collective-permute-done | bytes 32800 | tf_op jit(solution)/shard_map/ppermute | solution.py:26
  54.0 0.0 collective-permute-done.1
  54.0 0.0 collective-permute-done
  54.0 0.1 copy.62
  54.1 0.6 dynamic_update_slice.59
  54.7 0.1 pad.8
  54.8 0.4 fusion.3
  55.3 0.1 copy.90
  55.4 0.1 pad.6.clone
  55.5 0.4 fusion.4
  55.9 0.2 copy.91
  56.1 0.1 copy.54
  56.3 0.9 %convolution_select_fusion.2 = f32[1,8,8,5,64]{4,2,3,1,0:T(8,128)S(1)} fusion(bf16[3,3,3,64,512]{4,3,2,1,0:T(8,128)(2,1)S(1)} %copy-done, s32[]{:T(128)S(6)} %select_n.174, bf16[512,1,8,1,7,2]{0,4,5,2,3,1:T(8,128)(2,1)S(1)} %slice.72, bf16[512,1,8,1,8,5]{0,4,5,2,3,1:T(8,128)(2,1)S(1)} %copy.54, pred[8,5]{0,1:T(8,128)(4,1)S(1)} %copy-done.3), kind=kOutput, calls=%fused_computation.4 | convolution fusion | flops 174411776 | bytes 1131524 | tf_op jit(solution)/shard_map/conv_general_dilated | solution.py:37
  57.3 1.9 %collective-permute-start.4 = (bf16[512,384]{0,1:T(8,128)(2,1)S(1)}, bf16[512,384]{0,1:T(8,128)(2,1)S(1)}, u32[]{:S(2)}, u32[]{:S(2)}) collective-permute-start(bf16[512,384]{0,1:T(8,128)(2,1)S(1)} %pad_maximum_fusion), channel_id=1, source_target_pairs={{0,1},{1,0},{2,3},{3,2},{4,5},{5,4},{6,7},{7,6},{8,9},{9,8},{10,11... | collective-permute-start | bytes 1179656 | tf_op jit(solution)/shard_map/ppermute | solution.py:97
  59.3 0.2 add.99
  59.5 0.2 add.103
  59.7 1.2 %collective-permute-done.4 = bf16[512,384]{0,1:T(8,128)(2,1)S(1)} collective-permute-done((bf16[512,384]{0,1:T(8,128)(2,1)S(1)}, bf16[512,384]{0,1:T(8,128)(2,1)S(1)}, u32[]{:S(2)}, u32[]{:S(2)}) %collective-permute-start.4) | collective-permute-done | bytes 393248 | tf_op jit(solution)/shard_map/ppermute | solution.py:97
  60.9 0.0 copy-start.1
  60.9 0.1 copy.78
  61.0 0.6 dynamic_update_slice.61
  61.6 0.1 pad.14
  61.7 0.3 fusion.1
  62.1 0.0 copy-done.1
  62.2 0.0 slice-start
  62.2 0.1 copy.92
  62.3 0.1 pad.12.clone
  62.4 0.4 fusion.2
  62.8 0.3 slice-done
  63.1 0.1 copy.93
  63.3 0.1 copy.69
  63.5 0.9 %convolution_select_fusion.1 = f32[1,8,8,5,64]{4,2,3,1,0:T(8,128)S(1)} fusion(bf16[3,3,3,64,512]{4,3,2,1,0:T(8,128)(2,1)S(1)} %copy-done, s32[]{:T(128)S(6)} %select_n.189, bf16[512,1,8,1,7,2]{0,4,5,2,3,1:T(8,128)(2,1)S(1)} %slice.78, bf16[512,1,8,1,8,5]{0,4,5,2,3,1:T(8,128)(2,1)S(1)} %copy.69, pred[8,5]{0,1:T(8,128)(4,1)S(1)} %copy-done.3), kind=kOutput, calls=%fused_computation.3 | convolution fusion | flops 174411776 | bytes 1131524 | tf_op jit(solution)/shard_map/conv_general_dilated | solution.py:37
  64.4 0.0 copy-start.2
  64.5 0.2 add.108
  64.8 0.2 add.111
  65.0 0.1 copy.83
  65.0 0.0 copy-done.2
  65.1 0.8 %copy.84 = f32[1,2,64,256]{3,2,1,0:T(8,128)} copy(f32[1,2,64,256]{2,3,1,0:T(8,128)S(1)} %fusion.36) | data formatting | bytes 262144 | tf_op jit(solution)/shard_map/broadcast_in_dim | solution.py:106
  (51 shorter events, 1.1 us)
Async XLA Ops:
  0.0 27.8 %copy-start = (bf16[3,3,3,64,512]{4,3,2,1,0:T(8,128)(2,1)S(1)}, bf16[3,3,3,64,512]{4,3,2,1,0:T(8,128)(2,1)}, u32[]{:S(2)}) copy-start(bf16[3,3,3,64,512]{4,3,2,1,0:T(8,128)(2,1)} %param.4) | copy-start | bytes 5308420
  17.5 36.4 %collective-permute-start = (bf16[512,1,8,32]{0,3,2,1:T(8,128)(2,1)S(1)}, bf16[512,1,8,32]{0,3,2,1:T(8,128)(2,1)S(1)}, u32[]{:S(2)}, u32[]{:S(2)}) collective-permute-start(bf16[512,1,8,32]{0,3,2,1:T(8,128)(2,1)S(1)} %slice_select_fusion), channel_id=1, source_target_pairs={{0,68},{1,453},{2,70},{3,455},{4,64},{5,449},{6,66},{7,451},{8,76}... | collective-permute-start | bytes 786440 | tf_op jit(solution)/shard_map/ppermute | solution.py:26
  25.2 28.7 %collective-permute-start.1 = (bf16[512,2,1,32]{0,3,2,1:T(8,128)(2,1)S(1)}, bf16[512,2,1,32]{0,3,2,1:T(8,128)(2,1)S(1)}, u32[]{:S(2)}, u32[]{:S(2)}) collective-permute-start(bf16[512,2,1,32]{0,3,2,1:T(8,128)(2,1)S(1)} %slice_select_fusion.1), channel_id=1, source_target_pairs={{0,8},{1,509},{2,10},{3,511},{4,12},{5,505},{6,14},{7,507},{8,16},... | collective-permute-start | bytes 196616 | tf_op jit(solution)/shard_map/ppermute | solution.py:26
  27.5 0.7 %copy-start.3 = (pred[8,5]{0,1:T(8,128)(4,1)S(1)}, pred[8,5]{0,1:T(8,128)(4,1)}, u32[]{:S(2)}) copy-start(pred[8,5]{0,1:T(8,128)(4,1)} %constant.95) | copy-start | bytes 124
  33.0 15.3 %collective-permute-start.2 = (bf16[512,1,1,32]{0,3,2,1:T(8,128)(2,1)S(1)}, bf16[512,1,1,32]{0,3,2,1:T(8,128)(2,1)S(1)}, u32[]{:S(2)}, u32[]{:S(2)}) collective-permute-start(bf16[512,1,1,32]{0,3,2,1:T(8,128)(2,1)S(1)} %get-tuple-element.24), channel_id=1, source_target_pairs={{0,76},{1,441},{2,78},{3,443},{4,72},{5,445},{6,74},{7,447},{8,84}... | collective-permute-start | bytes 98312 | tf_op jit(solution)/shard_map/ppermute | solution.py:26
  46.3 7.7 %collective-permute-start.3 = (bf16[512,1,1,32]{0,3,2,1:T(8,128)(2,1)S(1)}, bf16[512,1,1,32]{0,3,2,1:T(8,128)(2,1)S(1)}, u32[]{:S(2)}, u32[]{:S(2)}) collective-permute-start(bf16[512,1,1,32]{0,3,2,1:T(8,128)(2,1)S(1)} %get-tuple-element.23), channel_id=1, source_target_pairs={{0,56},{1,461},{2,58},{3,463},{4,60},{5,457},{6,62},{7,459},{8,68}... | collective-permute-start | bytes 98312 | tf_op jit(solution)/shard_map/ppermute | solution.py:26
  57.3 3.6 %collective-permute-start.4 = (bf16[512,384]{0,1:T(8,128)(2,1)S(1)}, bf16[512,384]{0,1:T(8,128)(2,1)S(1)}, u32[]{:S(2)}, u32[]{:S(2)}) collective-permute-start(bf16[512,384]{0,1:T(8,128)(2,1)S(1)} %pad_maximum_fusion), channel_id=1, source_target_pairs={{0,1},{1,0},{2,3},{3,2},{4,5},{5,4},{6,7},{7,6},{8,9},{9,8},{10,11... | collective-permute-start | bytes 1179656 | tf_op jit(solution)/shard_map/ppermute | solution.py:97
  60.9 1.3 %copy-start.1 = (bf16[512,384]{0,1:T(8,128)(2,1)}, bf16[512,384]{0,1:T(8,128)(2,1)S(1)}, u32[]{:S(2)}) copy-start(bf16[512,384]{0,1:T(8,128)(2,1)S(1)} %collective-permute-done.4) | copy-start | bytes 1179652
  62.2 1.0 %slice-start = ((bf16[512,384]{0,1:T(8,128)(2,1)}), bf16[512,256]{0,1:T(8,128)(2,1)S(1)}, s32[]{:S(2)}) async-start(bf16[512,384]{0,1:T(8,128)(2,1)} %copy-done.1), calls=%async_computation | async-start | bytes 524288 | tf_op jit(solution)/shard_map/slice | solution.py:75
  64.4 0.7 copy-start.2

commit v14 on v12

--- a/solution.py
+++ b/solution.py
@@ -48,8 +48,10 @@
     size_x = activation.shape[1]
     size_y = CY
     size_z = activation.shape[3] // size_y
-    own_block = activation[0].astype(jnp.bfloat16).transpose(1, 0, 2)
+    width = lax.axis_size("chan")
+    own_block = activation[0].astype(jnp.bfloat16).reshape(-1, activation.shape[3])
     gathered = lax.all_gather(own_block, "chan", axis=0, tiled=True)
+    gathered = gathered.reshape(width, size_x, -1, activation.shape[3]).transpose(0, 2, 1, 3)
     gathered = gathered.reshape(-1, size_x, size_y, size_z)
     own_part = conv(gathered, weight, ((1, 1), (1, 1), (1, 1)))
     width_in = gathered.shape[0]

time: 64.2 us -> 63.9 us (level)
  the two profiles are of different devices: /device:TPU:65 before, /device:TPU:1 now
where the time goes in v14:
time: 63.9 us; the launch traced here: 63.5 us
  blocking collectives  21.7 us (34%)
  starting transfers between devices  21.7 us (34%)
  matrix products  7.23 us (11%)
  local copies, waits for them, and re-layouts  6.8 us (11%)
  waiting for transfers between devices  4.22 us (7%)
  other arithmetic  1.34 us (2%)
    all_gather x1, blocking collectives, body(): gathered = lax.all_gather(own_block, 'chan', axis=0, tiled=True)  21.7 us
    ppermute x4, starting transfers between devices, cross(): return lax.ppermute(sent, (axis, 'chan'), pairs)  19.6 us
    conv_general_dilated x5, matrix products, conv(): lax.conv_general_dilated(field[None], taps, window_strides=(1, 1, 1), pad...  7.23 us
    unnamed x15, local copies, waits for them, and re-layouts  2.97 us
    ppermute x4, waiting for transfers between devices, cross(): return lax.ppermute(sent, (axis, 'chan'), pairs)  2.85 us
    ppermute x1, starting transfers between devices, swap(): lax.ppermute(got, 'chan', [(lane, lane ^ 1) for lane in range(width)])  2.14 us
    ppermute x1, waiting for transfers between devices, swap(): lax.ppermute(got, 'chan', [(lane, lane ^ 1) for lane in range(width)])  1.37 us
  transfers between devices with their start and end apart: 5, of which 2 were waited for; matrix products, arithmetic and copies ran while one was open for 10% of the time, Pallas kernels for 0%

profile of v14, /device:TPU:1, one launch (start us, length us, event | category | flops | bytes accessed | tf_op | source)
XLA Modules:
  0.0 63.5 jit_solution(17501144632801136437)
XLA Ops:
  0.0 0.9 %convert_element_type.7 = bf16[1,2,64,256]{3,2,1,0:T(8,128)(2,1)S(1)} convert(f32[1,2,64,256]{3,2,1,0:T(8,128)} %param.3) | non-fusion elementwise | flops 32768 | bytes 196608 | tf_op jit(solution)/shard_map/convert_element_type | solution.py:52
  0.9 21.7 %all_gather.3 = bf16[1024,256]{1,0:T(8,128)(2,1)S(1)} all-gather(bf16[128,256]{1,0:T(8,128)(2,1)S(1)} %bitcast.111), channel_id=1, replica_groups=mesh['space'=64,'chan'=8] {'chan'}, dimensions={0}, use_global_device_ids=true | all-gather | bytes 589824 | tf_op jit(solution)/shard_map/all_gather | solution.py:53
  22.6 0.6 copy.38
  23.2 0.6 reshape.155
  23.9 10.9 %collective-permute-start.1 = (bf16[512,2,1,32]{0,3,2,1:T(8,128)(2,1)S(1)}, bf16[512,2,1,32]{0,3,2,1:T(8,128)(2,1)S(1)}, u32[]{:S(2)}, u32[]{:S(2)}) collective-permute-start(bf16[512,2,1,32]{0,3,2,1:T(8,128)(2,1)S(1)} %slice_select_fusion.1), channel_id=1, source_target_pairs={{0,8},{1,509},{2,10},{3,511},{4,12},{5,505},{6,14},{7,507},{8,16},... | collective-permute-start | bytes 196616 | tf_op jit(solution)/shard_map/ppermute | solution.py:26
  34.8 1.9 %collective-permute-start = (bf16[512,1,8,32]{0,3,2,1:T(8,128)(2,1)S(1)}, bf16[512,1,8,32]{0,3,2,1:T(8,128)(2,1)S(1)}, u32[]{:S(2)}, u32[]{:S(2)}) collective-permute-start(bf16[512,1,8,32]{0,3,2,1:T(8,128)(2,1)S(1)} %slice_select_fusion), channel_id=1, source_target_pairs={{0,68},{1,453},{2,70},{3,455},{4,64},{5,449},{6,66},{7,451},{8,76}... | collective-permute-start | bytes 786440 | tf_op jit(solution)/shard_map/ppermute | solution.py:26
  36.7 0.6 reshape.196
  37.3 0.3 copy.72
  37.6 0.0 copy-start.1
  37.6 0.0 copy-start.3
  37.7 0.2 copy.42
  37.9 0.1 slice.98
  38.0 1.1 %copy-done.1 = bf16[3,3,3,64,512]{4,3,2,1,0:T(8,128)(2,1)S(1)} copy-done((bf16[3,3,3,64,512]{4,3,2,1,0:T(8,128)(2,1)S(1)}, bf16[3,3,3,64,512]{4,3,2,1,0:T(8,128)(2,1)}, u32[]{:S(2)}) %copy-start.1) | copy-done | bytes 1769496
  39.1 0.0 copy-done.3
  39.1 4.7 %convolution_select_fusion = f32[2,8,8,5,64]{4,2,3,1,0:T(8,128)S(1)} fusion(bf16[3,3,3,64,512]{4,3,2,1,0:T(8,128)(2,1)S(1)} %copy-done.1, bf16[512,2,8,1,7,2]{0,4,5,2,1,3:T(8,128)(2,1)S(1)} %slice.98, bf16[512,2,8,1,8,5]{0,4,5,2,1,3:T(8,128)(2,1)S(1)} %copy.42, pred[8,5]{0,1:T(8,128)(4,1)S(1)} %copy-done.3), kind=kOutput, calls=%fused_computation.2 | convolution fusion | flops 694853632 | bytes 2818088 | tf_op jit(solution)/shard_map/conv_general_dilated | solution.py:37
  43.8 0.1 copy.43
  44.0 1.9 %collective-permute-start.3 = (bf16[512,1,1,32]{0,3,2,1:T(8,128)(2,1)S(1)}, bf16[512,1,1,32]{0,3,2,1:T(8,128)(2,1)S(1)}, u32[]{:S(2)}, u32[]{:S(2)}) collective-permute-start(bf16[512,1,1,32]{0,3,2,1:T(8,128)(2,1)S(1)} %get-tuple-element.25), channel_id=1, source_target_pairs={{0,56},{1,461},{2,58},{3,463},{4,60},{5,457},{6,62},{7,459},{8,68}... | collective-permute-start | bytes 98312 | tf_op jit(solution)/shard_map/ppermute | solution.py:26
  45.9 4.8 %collective-permute-start.2 = (bf16[512,1,1,32]{0,3,2,1:T(8,128)(2,1)S(1)}, bf16[512,1,1,32]{0,3,2,1:T(8,128)(2,1)S(1)}, u32[]{:S(2)}, u32[]{:S(2)}) collective-permute-start(bf16[512,1,1,32]{0,3,2,1:T(8,128)(2,1)S(1)} %get-tuple-element.26), channel_id=1, source_target_pairs={{0,76},{1,441},{2,78},{3,443},{4,72},{5,445},{6,74},{7,447},{8,84}... | collective-permute-start | bytes 98312 | tf_op jit(solution)/shard_map/ppermute | solution.py:26
  50.7 0.0 collective-permute-done.3
  50.8 2.8 %collective-permute-done.2 = bf16[512,1,1,32]{0,3,2,1:T(8,128)(2,1)S(1)} collective-permute-done((bf16[512,1,1,32]{0,3,2,1:T(8,128)(2,1)S(1)}, bf16[512,1,1,32]{0,3,2,1:T(8,128)(2,1)S(1)}, u32[]{:S(2)}, u32[]{:S(2)}) %collective-permute-start.2) | collective-permute-done | bytes 32800 | tf_op jit(solution)/shard_map/ppermute | solution.py:26
  53.6 0.0 collective-permute-done.1
  53.6 0.0 collective-permute-done
  53.6 2.1 %collective-permute-start.4 = (bf16[512,384]{0,1:T(8,128)(2,1)S(1)}, bf16[512,384]{0,1:T(8,128)(2,1)S(1)}, u32[]{:S(2)}, u32[]{:S(2)}) collective-permute-start(bf16[512,384]{0,1:T(8,128)(2,1)S(1)} %pad_maximum_fusion), channel_id=1, source_target_pairs={{0,1},{1,0},{2,3},{3,2},{4,5},{5,4},{6,7},{7,6},{8,9},{9,8},{10,11... | collective-permute-start | bytes 1179656 | tf_op jit(solution)/shard_map/ppermute | solution.py:32
  55.8 0.1 pad.11.clone
  55.9 1.4 %collective-permute-done.4 = bf16[512,384]{0,1:T(8,128)(2,1)S(1)} collective-permute-done((bf16[512,384]{0,1:T(8,128)(2,1)S(1)}, bf16[512,384]{0,1:T(8,128)(2,1)S(1)}, u32[]{:S(2)}, u32[]{:S(2)}) %collective-permute-start.4) | collective-permute-done | bytes 393248 | tf_op jit(solution)/shard_map/ppermute | solution.py:32
  57.3 0.1 broadcast_select_fusion.1
  57.5 0.0 copy-start.2
  57.5 0.2 copy.76
  57.7 0.2 copy.75
  57.9 0.1 copy.73
  58.0 0.1 pad.6.clone
  58.1 0.1 copy.74
  58.2 0.1 pad.8.clone
  58.3 0.6 copy-done.2
  59.0 0.3 convolution_select_fusion.3
  59.4 0.3 convolution_select_fusion.4
  59.9 0.1 copy.46
  60.0 0.1 copy.51
  60.1 0.9 %convolution_select_fusion.1 = f32[1,8,8,5,64]{4,2,3,1,0:T(8,128)S(1)} fusion(bf16[3,3,3,64,512]{4,3,2,1,0:T(8,128)(2,1)S(1)} %copy-done.2, bf16[512,1,8,1,7,2]{0,4,5,2,3,1:T(8,128)(2,1)S(1)} %slice.104, bf16[512,1,8,1,8,5]{0,4,5,2,3,1:T(8,128)(2,1)S(1)} %copy.51, pred[8,5]{0,1:T(8,128)(4,1)S(1)} %copy-done.3), kind=kOutput, calls=%fused_computation.3 | convolution fusion | flops 174411776 | bytes 1131520 | tf_op jit(solution)/shard_map/conv_general_dilated | solution.py:37
  61.1 0.9 %convolution_select_fusion.2 = f32[1,8,8,5,64]{4,2,3,1,0:T(8,128)S(1)} fusion(bf16[3,3,3,64,512]{4,3,2,1,0:T(8,128)(2,1)S(1)} %copy-done.2, bf16[512,1,8,1,7,2]{0,4,5,2,3,1:T(8,128)(2,1)S(1)} %slice.101, bf16[512,1,8,1,8,5]{0,4,5,2,3,1:T(8,128)(2,1)S(1)} %copy.46, pred[8,5]{0,1:T(8,128)(4,1)S(1)} %copy-done.3), kind=kOutput, calls=%fused_computation.4 | convolution fusion | flops 174411776 | bytes 1131520 | tf_op jit(solution)/shard_map/conv_general_dilated | solution.py:37
  62.1 0.0 copy-start
  62.2 0.1 fusion.29
  62.3 0.1 copy.68
  62.3 0.4 copy-done
  62.8 0.8 %copy.69 = f32[1,2,64,256]{3,2,1,0:T(8,128)} copy(f32[1,2,64,256]{2,3,1,0:T(8,128)S(1)} %fusion.28) | data formatting | bytes 262144 | tf_op jit(solution)/shard_map/broadcast_in_dim | solution.py:101
  (33 shorter events, 0.7 us)
Async XLA Ops:
  23.9 29.7 %collective-permute-start.1 = (bf16[512,2,1,32]{0,3,2,1:T(8,128)(2,1)S(1)}, bf16[512,2,1,32]{0,3,2,1:T(8,128)(2,1)S(1)}, u32[]{:S(2)}, u32[]{:S(2)}) collective-permute-start(bf16[512,2,1,32]{0,3,2,1:T(8,128)(2,1)S(1)} %slice_select_fusion.1), channel_id=1, source_target_pairs={{0,8},{1,509},{2,10},{3,511},{4,12},{5,505},{6,14},{7,507},{8,16},... | collective-permute-start | bytes 196616 | tf_op jit(solution)/shard_map/ppermute | solution.py:26
  34.8 18.8 %collective-permute-start = (bf16[512,1,8,32]{0,3,2,1:T(8,128)(2,1)S(1)}, bf16[512,1,8,32]{0,3,2,1:T(8,128)(2,1)S(1)}, u32[]{:S(2)}, u32[]{:S(2)}) collective-permute-start(bf16[512,1,8,32]{0,3,2,1:T(8,128)(2,1)S(1)} %slice_select_fusion), channel_id=1, source_target_pairs={{0,68},{1,453},{2,70},{3,455},{4,64},{5,449},{6,66},{7,451},{8,76}... | collective-permute-start | bytes 786440 | tf_op jit(solution)/shard_map/ppermute | solution.py:26
  37.6 1.5 %copy-start.1 = (bf16[3,3,3,64,512]{4,3,2,1,0:T(8,128)(2,1)S(1)}, bf16[3,3,3,64,512]{4,3,2,1,0:T(8,128)(2,1)}, u32[]{:S(2)}) copy-start(bf16[3,3,3,64,512]{4,3,2,1,0:T(8,128)(2,1)} %param.4) | copy-start | bytes 5308420
  37.6 1.5 %copy-start.3 = (pred[8,5]{0,1:T(8,128)(4,1)S(1)}, pred[8,5]{0,1:T(8,128)(4,1)}, u32[]{:S(2)}) copy-start(pred[8,5]{0,1:T(8,128)(4,1)} %constant.71) | copy-start | bytes 124
  44.0 6.8 %collective-permute-start.3 = (bf16[512,1,1,32]{0,3,2,1:T(8,128)(2,1)S(1)}, bf16[512,1,1,32]{0,3,2,1:T(8,128)(2,1)S(1)}, u32[]{:S(2)}, u32[]{:S(2)}) collective-permute-start(bf16[512,1,1,32]{0,3,2,1:T(8,128)(2,1)S(1)} %get-tuple-element.25), channel_id=1, source_target_pairs={{0,56},{1,461},{2,58},{3,463},{4,60},{5,457},{6,62},{7,459},{8,68}... | collective-permute-start | bytes 98312 | tf_op jit(solution)/shard_map/ppermute | solution.py:26
  45.9 7.7 %collective-permute-start.2 = (bf16[512,1,1,32]{0,3,2,1:T(8,128)(2,1)S(1)}, bf16[512,1,1,32]{0,3,2,1:T(8,128)(2,1)S(1)}, u32[]{:S(2)}, u32[]{:S(2)}) collective-permute-start(bf16[512,1,1,32]{0,3,2,1:T(8,128)(2,1)S(1)} %get-tuple-element.26), channel_id=1, source_target_pairs={{0,76},{1,441},{2,78},{3,443},{4,72},{5,445},{6,74},{7,447},{8,84}... | collective-permute-start | bytes 98312 | tf_op jit(solution)/shard_map/ppermute | solution.py:26
  53.6 3.6 %collective-permute-start.4 = (bf16[512,384]{0,1:T(8,128)(2,1)S(1)}, bf16[512,384]{0,1:T(8,128)(2,1)S(1)}, u32[]{:S(2)}, u32[]{:S(2)}) collective-permute-start(bf16[512,384]{0,1:T(8,128)(2,1)S(1)} %pad_maximum_fusion), channel_id=1, source_target_pairs={{0,1},{1,0},{2,3},{3,2},{4,5},{5,4},{6,7},{7,6},{8,9},{9,8},{10,11... | collective-permute-start | bytes 1179656 | tf_op jit(solution)/shard_map/ppermute | solution.py:32
  57.5 1.5 %copy-start.2 = (bf16[3,3,3,64,512]{4,3,2,1,0:T(8,128)(2,1)S(1)}, bf16[3,3,3,64,512]{4,3,2,1,0:T(8,128)(2,1)}, u32[]{:S(2)}) copy-start(bf16[3,3,3,64,512]{4,3,2,1,0:T(8,128)(2,1)} %param.4) | copy-start | bytes 5308420
  62.1 0.7 %copy-start = (f32[64]{0:T(128)S(1)}, f32[64]{0:T(128)}, u32[]{:S(2)}) copy-start(f32[64]{0:T(128)} %param.5) | copy-start | bytes 772

commit v15 on v8

v15 whole, which is shorter than its diff:
```python
import jax
import jax.numpy as jnp
from jax import lax
from jax.sharding import PartitionSpec as P

CY = 8


negative_slope = 0.3


def plain_shift(value, axis, steps):
    count = lax.axis_size(axis)
    return lax.ppermute(value, axis, [(source, (source + steps) % count) for source in range(count)])


def cross(lower_source, upper_source, axis, steps):
    count = lax.axis_size(axis)
    width = lax.axis_size("chan")
    run_y = width // 2
    pairs = []
    for source in range(count):
        for lane in range(width):
            place, core = divmod(lane, 2)
            target = (source + (steps if core == 0 else -steps)) % count
            crosses = (source // CY) % 2 != (target // CY) % 2
            moved = ((place + run_y // 2) % run_y) * 2 + core if crosses else lane
            pairs.append((source * width + lane, target * width + moved))
    on_first = lax.axis_index("chan") % 2 == 0
    sent = jnp.where(on_first, lower_source, upper_source)
    return lax.ppermute(sent, (axis, "chan"), pairs)


def swap(got):
    width = lax.axis_size("chan")
    on_first = lax.axis_index("chan") % 2 == 0
    swapped = lax.ppermute(got, "chan", [(lane, lane ^ 1) for lane in range(width)])
    return jnp.where(on_first, got, swapped), jnp.where(on_first, swapped, got)


def conv(field, taps, padding):
    return lax.conv_general_dilated(
        field[None],
        taps,
        window_strides=(1, 1, 1),
        padding=padding,
        dimension_numbers=("NCDHW", "DHWOI", "NCDHW"),
        preferred_element_type=jnp.float32,
    )[0]


def body(activation, weight, conv_bias):
    size_x = activation.shape[1]
    size_y = CY
    size_z = activation.shape[3] // size_y
    width = lax.axis_size("chan")
    own_block = activation[0].astype(jnp.bfloat16).reshape(-1, activation.shape[3])
    gathered = lax.all_gather(own_block, "chan", axis=0, tiled=True)
    gathered = gathered.reshape(width, size_x, -1, activation.shape[3]).transpose(0, 2, 1, 3)
    gathered = gathered.reshape(-1, size_x, size_y, size_z)
    own_part = conv(gathered, weight, ((1, 1), (1, 1), (1, 1)))
    spill_lo = conv(gathered[:, :1], weight[2:], ((0, 0), (2, 2), (1, 1)))
    spill_hi = conv(gathered[:, -1:], weight[:1], ((0, 0), (2, 2), (1, 1)))
    from_lo = plain_shift(spill_hi, "space", CY)
    from_hi = plain_shift(spill_lo, "space", -CY)
    row_lo = conv(gathered[:, :, :1], weight[:, 2:], ((1, 1), (0, 0), (1, 1)))
    row_hi = conv(gathered[:, :, -1:], weight[:, :1], ((1, 1), (0, 0), (1, 1)))
    from_lo, from_hi, own_part, row_lo, row_hi = lax.optimization_barrier((from_lo, from_hi, own_part, row_lo, row_hi))
    row_lo = row_lo + jnp.concatenate([from_lo[:, :, :1], from_hi[:, :, :1]], axis=1)
    row_hi = row_hi + jnp.concatenate([from_lo[:, :, -1:], from_hi[:, :, -1:]], axis=1)
    from_below = plain_shift(row_hi, "space", 1)
    from_above = plain_shift(row_lo, "space", -1)
    place_y = (lax.axis_index("space") + 4) % 8
    from_below = jnp.where(place_y > 0, from_below, jnp.zeros_like(from_below))
    from_above = jnp.where(place_y < 7, from_above, jnp.zeros_like(from_above))
    width_out = own_part.shape[0]
    x_part = jnp.concatenate([from_lo[:, :, 1:-1], from_hi[:, :, 1:-1]], axis=1)
    middle = jnp.zeros((width_out, size_x, size_y - 2, size_z), jnp.float32)
    y_part = jnp.concatenate([from_below, middle, from_above], axis=2)
    total = (own_part + x_part + y_part).reshape(width_out, -1)
    before = total + conv_bias[:, None]
    result = jnp.maximum(before, negative_slope * before)
    result = result.reshape(width_out, size_x, size_y * size_z).transpose(1, 0, 2)
    return result[None]


def solution(mesh):
    placed = (P("space", None, "chan", None), P(None, None, None, "chan", None), P("chan"))
    return jax.shard_map(
        body, mesh=mesh, in_specs=placed, out_specs=P("space", None, "chan", None), check_vma=False
    )
```

time: 68.7 us -> 64.6 us (0.940)
  waiting for transfers between devices: 10.6 us -> 0.98 us
  local copies, waits for them, and re-layouts: 3.66 us -> 6.69 us
  starting transfers between devices: 23.6 us -> 25.8 us
    ppermute x4, waiting for transfers between devices: 10.6 us -> 0.98 us  [plain_shift(): lax.ppermute(value, axis, [(source, (source + steps) % count) for source...]
    ppermute x4, starting transfers between devices: 23.6 us -> 25.8 us  [plain_shift(): lax.ppermute(value, axis, [(source, (source + steps) % count) for source...]
    unnamed x12 -> x14, local copies, waits for them, and re-layouts: 0.89 us -> 2.61 us
    all_gather x1 -> x0, local copies, waits for them, and re-layouts: 0.74 us -> none  [body(): gathered = lax.all_gather(own_block, 'chan', axis=0, tiled=True)]
  transfers between devices with their start and end apart: 4 -> 4, of which waited for: 2 -> 1; matrix products, arithmetic and copies ran while one was open for 12% -> 14% of each run, Pallas kernels for 0% -> 0%
where the time goes in v15:
time: 64.6 us; the launch traced here: 64.4 us
  starting transfers between devices  25.8 us (40%)
  blocking collectives  21.7 us (34%)
  matrix products  7.61 us (12%)
  local copies, waits for them, and re-layouts  6.69 us (10%)
  other arithmetic  1.06 us (2%)
  waiting for transfers between devices  0.98 us (2%)
    ppermute x4, starting transfers between devices, plain_shift(): lax.ppermute(value, axis, [(source, (source + steps) % count) for source...  25.8 us
    all_gather x1, blocking collectives, body(): gathered = lax.all_gather(own_block, 'chan', axis=0, tiled=True)  21.7 us
    conv_general_dilated x5, matrix products, conv(): lax.conv_general_dilated(field[None], taps, window_strides=(1, 1, 1), pad...  7.61 us
    unnamed x14, local copies, waits for them, and re-layouts  2.61 us
  transfers between devices with their start and end apart: 4, of which 1 were waited for; matrix products, arithmetic and copies ran while one was open for 14% of the time, Pallas kernels for 0%

profile of v15, /device:TPU:1, one launch (start us, length us, event | category | flops | bytes accessed | tf_op | source)
XLA Modules:
  0.0 64.4 jit_solution(3158021699686189956)
XLA Ops:
  0.0 0.9 %convert_element_type.7 = bf16[1,2,64,256]{3,2,1,0:T(8,128)(2,1)S(1)} convert(f32[1,2,64,256]{3,2,1,0:T(8,128)} %param.3) | non-fusion elementwise | flops 32768 | bytes 196608 | tf_op jit(solution)/shard_map/convert_element_type | solution.py:57
  0.9 21.7 %all_gather.3 = bf16[1024,256]{1,0:T(8,128)(2,1)S(1)} all-gather(bf16[128,256]{1,0:T(8,128)(2,1)S(1)} %bitcast.86), channel_id=1, replica_groups=mesh['space'=64,'chan'=8] {'chan'}, dimensions={0}, use_global_device_ids=true | all-gather | bytes 589824 | tf_op jit(solution)/shard_map/all_gather | solution.py:58
  22.6 0.6 copy.29
  23.2 0.6 reshape.21
  23.8 0.0 copy-start.1
  23.8 0.0 copy-start.3
  23.9 0.2 copy.63
  24.1 0.1 copy.36
  24.2 1.1 %copy-done.1 = bf16[3,3,3,64,512]{4,3,2,1,0:T(8,128)(2,1)S(1)} copy-done((bf16[3,3,3,64,512]{4,3,2,1,0:T(8,128)(2,1)S(1)}, bf16[3,3,3,64,512]{4,3,2,1,0:T(8,128)(2,1)}, u32[]{:S(2)}) %copy-start.1) | copy-done | bytes 1769496
  25.3 0.0 copy-done.3
  25.3 1.1 %convolution_select_fusion.1 = f32[1,10,8,5,64]{4,2,3,1,0:T(8,128)S(1)} fusion(bf16[3,3,3,64,512]{4,3,2,1,0:T(8,128)(2,1)S(1)} %copy-done.1, bf16[512,1,8,1,7,2]{0,4,5,2,3,1:T(8,128)(2,1)S(1)} %slice.70, bf16[512,1,8,1,8,5]{0,4,5,2,3,1:T(8,128)(2,1)S(1)} %copy.36, pred[8,5]{0,1:T(8,128)(4,1)S(1)} %copy-done.3), kind=kOutput, calls=%fused_computation.3 | convolution fusion | flops 190145536 | bytes 1152000 | tf_op jit(solution)/shard_map/conv_general_dilated | solution.py:42
  26.4 0.2 copy.37
  26.7 4.1 %collective-permute-start.1 = (f32[64,1,10,32]{0,3,2,1:T(8,128)S(1)}, f32[64,1,10,32]{0,3,2,1:T(8,128)S(1)}, u32[]{:S(2)}, u32[]{:S(2)}) collective-permute-start(f32[64,1,10,32]{0,3,2,1:T(8,128)S(1)} %slice_bitcast_fusion.2), channel_id=1, source_target_pairs={{0,448},{8,456},{16,464},{24,472},{32,480},{40,488},{48,496},{56,5... | collective-permute-start | bytes 245768 | tf_op jit(solution)/shard_map/ppermute | solution.py:14
  30.8 0.2 copy.62
  31.0 0.1 copy.32
  31.1 1.1 %convolution_select_fusion.2 = f32[1,10,8,5,64]{4,2,3,1,0:T(8,128)S(1)} fusion(bf16[3,3,3,64,512]{4,3,2,1,0:T(8,128)(2,1)S(1)} %copy-done.1, bf16[512,1,8,1,7,2]{0,4,5,2,3,1:T(8,128)(2,1)S(1)} %slice.67, bf16[512,1,8,1,8,5]{0,4,5,2,3,1:T(8,128)(2,1)S(1)} %copy.32, pred[8,5]{0,1:T(8,128)(4,1)S(1)} %copy-done.3), kind=kOutput, calls=%fused_computation.4 | convolution fusion | flops 190145536 | bytes 1152000 | tf_op jit(solution)/shard_map/conv_general_dilated | solution.py:42
  32.2 0.2 copy.33
  32.5 5.1 %collective-permute-start = (f32[64,1,10,32]{0,3,2,1:T(8,128)S(1)}, f32[64,1,10,32]{0,3,2,1:T(8,128)S(1)}, u32[]{:S(2)}, u32[]{:S(2)}) collective-permute-start(f32[64,1,10,32]{0,3,2,1:T(8,128)S(1)} %bitcast.87), channel_id=1, source_target_pairs={{0,64},{8,72},{16,80},{24,88},{32,96},{40,104},{48,112},{56,120},{... | collective-permute-start | bytes 245768 | tf_op jit(solution)/shard_map/ppermute | solution.py:14
  37.6 0.6 reshape.66
  38.2 0.0 copy-start.2
  38.2 0.3 copy.59
  38.6 0.2 copy.42
  38.8 0.1 copy.61
  38.8 0.1 pad.8.clone
  38.9 0.7 %copy-done.2 = bf16[3,3,3,64,512]{4,3,2,1,0:T(8,128)(2,1)S(1)} copy-done((bf16[3,3,3,64,512]{4,3,2,1,0:T(8,128)(2,1)S(1)}, bf16[3,3,3,64,512]{4,3,2,1,0:T(8,128)(2,1)}, u32[]{:S(2)}) %copy-start.2) | copy-done | bytes 1769496
  39.7 0.3 convolution_select_fusion.3
  40.1 0.1 copy.60
  40.1 0.1 pad.6.clone
  40.2 0.3 convolution_select_fusion.4
  40.6 0.1 slice.72
  40.7 4.7 %convolution_select_fusion = f32[2,8,8,5,64]{4,2,3,1,0:T(8,128)S(1)} fusion(bf16[3,3,3,64,512]{4,3,2,1,0:T(8,128)(2,1)S(1)} %copy-done.2, bf16[512,2,8,1,7,2]{0,4,5,2,1,3:T(8,128)(2,1)S(1)} %slice.72, bf16[512,2,8,1,8,5]{0,4,5,2,1,3:T(8,128)(2,1)S(1)} %copy.42, pred[8,5]{0,1:T(8,128)(4,1)S(1)} %copy-done.3), kind=kOutput, calls=%fused_computation.2 | convolution fusion | flops 694853632 | bytes 2818088 | tf_op jit(solution)/shard_map/conv_general_dilated | solution.py:42
  45.5 0.0 copy-start
  45.5 0.1 copy.43
  45.6 0.1 copy.67
  45.6 0.1 pad.11.clone
  45.7 0.0 collective-permute-done.1
  45.7 0.0 collective-permute-done
  45.8 3.9 %collective-permute-start.2 = (f32[64,2,1,32]{0,3,2,1:T(8,128)S(1)}, f32[64,2,1,32]{0,3,2,1:T(8,128)S(1)}, u32[]{:S(2)}, u32[]{:S(2)}) collective-permute-start(f32[64,2,1,32]{0,3,2,1:T(8,128)S(1)} %maximum_add_fusion.1), channel_id=1, source_target_pairs={{0,8},{8,16},{16,24},{24,32},{32,40},{40,48},{48,56},{56,64},{64,7... | collective-permute-start | bytes 49160 | tf_op jit(solution)/shard_map/ppermute | solution.py:14
  49.8 12.7 %collective-permute-start.3 = (f32[64,2,1,32]{0,3,2,1:T(8,128)S(1)}, f32[64,2,1,32]{0,3,2,1:T(8,128)S(1)}, u32[]{:S(2)}, u32[]{:S(2)}) collective-permute-start(f32[64,2,1,32]{0,3,2,1:T(8,128)S(1)} %maximum_add_fusion.2), channel_id=1, source_target_pairs={{0,504},{8,0},{16,8},{24,16},{32,24},{40,32},{48,40},{56,48},{64,5... | collective-permute-start | bytes 49160 | tf_op jit(solution)/shard_map/ppermute | solution.py:14
  62.4 0.0 collective-permute-done.2
  62.5 1.0 %collective-permute-done.3 = f32[64,2,1,32]{0,3,2,1:T(8,128)S(1)} collective-permute-done((f32[64,2,1,32]{0,3,2,1:T(8,128)S(1)}, f32[64,2,1,32]{0,3,2,1:T(8,128)S(1)}, u32[]{:S(2)}, u32[]{:S(2)}) %collective-permute-start.3) | collective-permute-done | bytes 16416 | tf_op jit(solution)/shard_map/ppermute | solution.py:14
  63.4 0.1 fusion.27
  63.5 0.0 copy-done
  63.6 0.8 %copy.55 = f32[1,2,64,256]{3,2,1,0:T(8,128)} copy(f32[1,2,64,256]{2,3,1,0:T(8,128)S(1)} %fusion.26) | data formatting | bytes 262144 | tf_op jit(solution)/shard_map/broadcast_in_dim | solution.py:84
  (29 shorter events, 0.5 us)
Async XLA Ops:
  23.8 1.5 %copy-start.1 = (bf16[3,3,3,64,512]{4,3,2,1,0:T(8,128)(2,1)S(1)}, bf16[3,3,3,64,512]{4,3,2,1,0:T(8,128)(2,1)}, u32[]{:S(2)}) copy-start(bf16[3,3,3,64,512]{4,3,2,1,0:T(8,128)(2,1)} %param.4) | copy-start | bytes 5308420
  23.8 1.5 %copy-start.3 = (pred[8,5]{0,1:T(8,128)(4,1)S(1)}, pred[8,5]{0,1:T(8,128)(4,1)}, u32[]{:S(2)}) copy-start(pred[8,5]{0,1:T(8,128)(4,1)} %constant.49) | copy-start | bytes 124
  26.7 19.1 %collective-permute-start.1 = (f32[64,1,10,32]{0,3,2,1:T(8,128)S(1)}, f32[64,1,10,32]{0,3,2,1:T(8,128)S(1)}, u32[]{:S(2)}, u32[]{:S(2)}) collective-permute-start(f32[64,1,10,32]{0,3,2,1:T(8,128)S(1)} %slice_bitcast_fusion.2), channel_id=1, source_target_pairs={{0,448},{8,456},{16,464},{24,472},{32,480},{40,488},{48,496},{56,5... | collective-permute-start | bytes 245768 | tf_op jit(solution)/shard_map/ppermute | solution.py:14
  32.5 13.3 %collective-permute-start = (f32[64,1,10,32]{0,3,2,1:T(8,128)S(1)}, f32[64,1,10,32]{0,3,2,1:T(8,128)S(1)}, u32[]{:S(2)}, u32[]{:S(2)}) collective-permute-start(f32[64,1,10,32]{0,3,2,1:T(8,128)S(1)} %bitcast.87), channel_id=1, source_target_pairs={{0,64},{8,72},{16,80},{24,88},{32,96},{40,104},{48,112},{56,120},{... | collective-permute-start | bytes 245768 | tf_op jit(solution)/shard_map/ppermute | solution.py:14
  38.2 1.5 %copy-start.2 = (bf16[3,3,3,64,512]{4,3,2,1,0:T(8,128)(2,1)S(1)}, bf16[3,3,3,64,512]{4,3,2,1,0:T(8,128)(2,1)}, u32[]{:S(2)}) copy-start(bf16[3,3,3,64,512]{4,3,2,1,0:T(8,128)(2,1)} %param.4) | copy-start | bytes 5308420
  45.5 18.1 %copy-start = (f32[64]{0:T(128)S(1)}, f32[64]{0:T(128)}, u32[]{:S(2)}) copy-start(f32[64]{0:T(128)} %param.5) | copy-start | bytes 772
  45.8 16.7 %collective-permute-start.2 = (f32[64,2,1,32]{0,3,2,1:T(8,128)S(1)}, f32[64,2,1,32]{0,3,2,1:T(8,128)S(1)}, u32[]{:S(2)}, u32[]{:S(2)}) collective-permute-start(f32[64,2,1,32]{0,3,2,1:T(8,128)S(1)} %maximum_add_fusion.1), channel_id=1, source_target_pairs={{0,8},{8,16},{16,24},{24,32},{32,40},{40,48},{48,56},{56,64},{64,7... | collective-permute-start | bytes 49160 | tf_op jit(solution)/shard_map/ppermute | solution.py:14
  49.8 13.7 %collective-permute-start.3 = (f32[64,2,1,32]{0,3,2,1:T(8,128)S(1)}, f32[64,2,1,32]{0,3,2,1:T(8,128)S(1)}, u32[]{:S(2)}, u32[]{:S(2)}) collective-permute-start(f32[64,2,1,32]{0,3,2,1:T(8,128)S(1)} %maximum_add_fusion.2), channel_id=1, source_target_pairs={{0,504},{8,0},{16,8},{24,16},{32,24},{40,32},{48,40},{56,48},{64,5... | collective-permute-start | bytes 49160 | tf_op jit(solution)/shard_map/ppermute | solution.py:14

commit v16 on v15

--- a/solution.py
+++ b/solution.py
@@ -59,24 +59,27 @@
     gathered = gathered.reshape(width, size_x, -1, activation.shape[3]).transpose(0, 2, 1, 3)
     gathered = gathered.reshape(-1, size_x, size_y, size_z)
     own_part = conv(gathered, weight, ((1, 1), (1, 1), (1, 1)))
-    spill_lo = conv(gathered[:, :1], weight[2:], ((0, 0), (2, 2), (1, 1)))
-    spill_hi = conv(gathered[:, -1:], weight[:1], ((0, 0), (2, 2), (1, 1)))
-    from_lo = plain_shift(spill_hi, "space", CY)
-    from_hi = plain_shift(spill_lo, "space", -CY)
-    row_lo = conv(gathered[:, :, :1], weight[:, 2:], ((1, 1), (0, 0), (1, 1)))
-    row_hi = conv(gathered[:, :, -1:], weight[:, :1], ((1, 1), (0, 0), (1, 1)))
-    from_lo, from_hi, own_part, row_lo, row_hi = lax.optimization_barrier((from_lo, from_hi, own_part, row_lo, row_hi))
-    row_lo = row_lo + jnp.concatenate([from_lo[:, :, :1], from_hi[:, :, :1]], axis=1)
-    row_hi = row_hi + jnp.concatenate([from_lo[:, :, -1:], from_hi[:, :, -1:]], axis=1)
+    row_lo = conv(gathered[:, :, :1], weight[:, 2:], ((2, 2), (0, 0), (1, 1)))
+    row_hi = conv(gathered[:, :, -1:], weight[:, :1], ((2, 2), (0, 0), (1, 1)))
     from_below = plain_shift(row_hi, "space", 1)
     from_above = plain_shift(row_lo, "space", -1)
+    spill_lo = conv(gathered[:, :1], weight[2:], ((0, 0), (1, 1), (1, 1)))
+    spill_hi = conv(gathered[:, -1:], weight[:1], ((0, 0), (1, 1), (1, 1)))
+    from_below, from_above, own_part, spill_lo, spill_hi = lax.optimization_barrier(
+        (from_below, from_above, own_part, spill_lo, spill_hi)
+    )
     place_y = (lax.axis_index("space") + 4) % 8
     from_below = jnp.where(place_y > 0, from_below, jnp.zeros_like(from_below))
     from_above = jnp.where(place_y < 7, from_above, jnp.zeros_like(from_above))
     width_out = own_part.shape[0]
-    x_part = jnp.concatenate([from_lo[:, :, 1:-1], from_hi[:, :, 1:-1]], axis=1)
+    middle = jnp.zeros((width_out, 1, size_y - 2, size_z), jnp.float32)
+    spill_lo = spill_lo + jnp.concatenate([from_below[:, :1], middle, from_above[:, :1]], axis=2)
+    spill_hi = spill_hi + jnp.concatenate([from_below[:, -1:], middle, from_above[:, -1:]], axis=2)
+    from_lo = plain_shift(spill_hi, "space", CY)
+    from_hi = plain_shift(spill_lo, "space", -CY)
+    x_part = jnp.concatenate([from_lo, from_hi], axis=1)
     middle = jnp.zeros((width_out, size_x, size_y - 2, size_z), jnp.float32)
-    y_part = jnp.concatenate([from_below, middle, from_above], axis=2)
+    y_part = jnp.concatenate([from_below[:, 1:-1], middle, from_above[:, 1:-1]], axis=2)
     total = (own_part + x_part + y_part).reshape(width_out, -1)
     before = total + conv_bias[:, None]
     result = jnp.maximum(before, negative_slope * before)

time: 64.6 us -> 70.1 us (1.085)
  the two profiles are of different devices: /device:TPU:1 before, /device:TPU:6 now
where the time goes in v16:
time: 70.1 us; the launch traced here: 69.8 us
  starting transfers between devices  28.8 us (41%)
  blocking collectives  15.1 us (22%)
  matrix products  9.75 us (14%)
  waiting for transfers between devices  8.85 us (13%)
  local copies, waits for them, and re-layouts  5.58 us (8%)
  other arithmetic  1.22 us (2%)
    ppermute x4, starting transfers between devices, plain_shift(): lax.ppermute(value, axis, [(source, (source + steps) % count) for source...  28.8 us
    all_gather x1, blocking collectives, body(): gathered = lax.all_gather(own_block, 'chan', axis=0, tiled=True)  15.1 us
    conv_general_dilated x5, matrix products, conv(): lax.conv_general_dilated(field[None], taps, window_strides=(1, 1, 1), pad...  9.75 us
    ppermute x4, waiting for transfers between devices, plain_shift(): lax.ppermute(value, axis, [(source, (source + steps) % count) for source...  8.85 us
    unnamed x11, local copies, waits for them, and re-layouts  1.67 us
  transfers between devices with their start and end apart: 4, of which 2 were waited for; matrix products, arithmetic and copies ran while one was open for 15% of the time, Pallas kernels for 0%

profile of v16, /device:TPU:6, one launch (start us, length us, event | category | flops | bytes accessed | tf_op | source)
XLA Modules:
  0.0 69.8 jit_solution(12884036837396748057)
XLA Ops:
  0.0 0.9 %convert_element_type.7 = bf16[1,2,64,256]{3,2,1,0:T(8,128)(2,1)S(1)} convert(f32[1,2,64,256]{3,2,1,0:T(8,128)} %param.3) | non-fusion elementwise | flops 32768 | bytes 196608 | tf_op jit(solution)/shard_map/convert_element_type | solution.py:57
  0.9 15.1 %all_gather.3 = bf16[1024,256]{1,0:T(8,128)(2,1)S(1)} all-gather(bf16[128,256]{1,0:T(8,128)(2,1)S(1)} %bitcast.99), channel_id=1, replica_groups=mesh['space'=64,'chan'=8] {'chan'}, dimensions={0}, use_global_device_ids=true | all-gather | bytes 589824 | tf_op jit(solution)/shard_map/all_gather | solution.py:58
  16.0 0.0 copy-start.2
  16.0 0.6 copy.35
  16.6 0.6 reshape.21
  17.2 0.1 copy.68
  17.3 0.1 pad.clone
  17.4 0.0 copy-done.2
  17.4 1.6 %convolution_select_fusion.4 = f32[4,1,8,5,64]{4,2,3,1,0:T(8,128)S(1)} fusion(bf16[3,3,3,64,512]{4,3,2,1,0:T(8,128)(2,1)} %param.4, bf16[512,2,1,1,7,2]{0,4,5,1,3,2:T(8,128)(2,1)S(1)} %slice.67, bf16[512,2,1,1,8,5]{0,4,5,1,3,2:T(8,128)(2,1)S(1)} %copy.38, pred[8,5]{0,1:T(8,128)(4,1)S(1)} %copy-done.2), kind=kOutput, calls=%fused_computation.6 | convolution fusion | flops 47540224 | bytes 741416 | tf_op jit(solution)/shard_map/conv_general_dilated | solution.py:42
  19.1 4.3 %collective-permute-start = (f32[64,4,1,32]{0,1,3,2:T(4,128)S(1)}, f32[64,4,1,32]{0,1,3,2:T(4,128)S(1)}, u32[]{:S(2)}, u32[]{:S(2)}) collective-permute-start(f32[64,4,1,32]{0,1,3,2:T(4,128)S(1)} %slice_bitcast_fusion.7), channel_id=1, source_target_pairs={{0,8},{8,16},{16,24},{24,32},{32,40},{40,48},{48,56},{56,64},{64,7... | collective-permute-start | bytes 98312 | tf_op jit(solution)/shard_map/ppermute | solution.py:14
  23.4 0.1 copy.69
  23.5 0.1 pad.2.clone
  23.6 1.6 %convolution_select_fusion.3 = f32[4,1,8,5,64]{4,2,3,1,0:T(8,128)S(1)} fusion(bf16[3,3,3,64,512]{4,3,2,1,0:T(8,128)(2,1)} %param.4, bf16[512,2,1,1,7,2]{0,4,5,1,3,2:T(8,128)(2,1)S(1)} %slice.70, bf16[512,2,1,1,8,5]{0,4,5,1,3,2:T(8,128)(2,1)S(1)} %copy.42, pred[8,5]{0,1:T(8,128)(4,1)S(1)} %copy-done.2), kind=kOutput, calls=%fused_computation.5 | convolution fusion | flops 47540224 | bytes 741416 | tf_op jit(solution)/shard_map/conv_general_dilated | solution.py:42
  25.2 13.8 %collective-permute-start.1 = (f32[64,4,1,32]{0,1,3,2:T(4,128)S(1)}, f32[64,4,1,32]{0,1,3,2:T(4,128)S(1)}, u32[]{:S(2)}, u32[]{:S(2)}) collective-permute-start(f32[64,4,1,32]{0,1,3,2:T(4,128)S(1)} %slice_bitcast_fusion.5), channel_id=1, source_target_pairs={{0,504},{8,0},{16,8},{24,16},{32,24},{40,32},{48,40},{56,48},{64,5... | collective-permute-start | bytes 98312 | tf_op jit(solution)/shard_map/ppermute | solution.py:14
  39.1 0.6 reshape.66
  39.7 0.3 copy.70
  40.1 0.0 copy-start.1
  40.1 0.2 copy.48
  40.3 0.2 copy.72
  40.5 0.1 copy.57
  40.6 0.9 %copy-done.1 = bf16[3,3,3,64,512]{4,3,2,1,0:T(8,128)(2,1)S(1)} copy-done((bf16[3,3,3,64,512]{4,3,2,1,0:T(8,128)(2,1)S(1)}, bf16[3,3,3,64,512]{4,3,2,1,0:T(8,128)(2,1)}, u32[]{:S(2)}) %copy-start.1) | copy-done | bytes 1769496
  41.6 0.9 %convolution_select_fusion.1 = f32[1,8,8,5,64]{4,2,3,1,0:T(8,128)S(1)} fusion(bf16[3,3,3,64,512]{4,3,2,1,0:T(8,128)(2,1)S(1)} %copy-done.1, bf16[512,1,8,1,7,2]{0,4,5,2,3,1:T(8,128)(2,1)S(1)} %slice.78, bf16[512,1,8,1,8,5]{0,4,5,2,3,1:T(8,128)(2,1)S(1)} %copy.57, pred[8,5]{0,1:T(8,128)(4,1)S(1)} %copy-done.2), kind=kOutput, calls=%fused_computation.3 | convolution fusion | flops 174411776 | bytes 1131520 | tf_op jit(solution)/shard_map/conv_general_dilated | solution.py:42
  42.5 0.2 copy.71
  42.7 0.1 copy.52
  42.9 0.9 %convolution_select_fusion.2 = f32[1,8,8,5,64]{4,2,3,1,0:T(8,128)S(1)} fusion(bf16[3,3,3,64,512]{4,3,2,1,0:T(8,128)(2,1)S(1)} %copy-done.1, bf16[512,1,8,1,7,2]{0,4,5,2,3,1:T(8,128)(2,1)S(1)} %slice.75, bf16[512,1,8,1,8,5]{0,4,5,2,3,1:T(8,128)(2,1)S(1)} %copy.52, pred[8,5]{0,1:T(8,128)(4,1)S(1)} %copy-done.2), kind=kOutput, calls=%fused_computation.4 | convolution fusion | flops 174411776 | bytes 1131520 | tf_op jit(solution)/shard_map/conv_general_dilated | solution.py:42
  43.8 0.1 slice.72
  43.9 4.7 %convolution_select_fusion = f32[2,8,8,5,64]{4,2,3,1,0:T(8,128)S(1)} fusion(bf16[3,3,3,64,512]{4,3,2,1,0:T(8,128)(2,1)S(1)} %copy-done.1, bf16[512,2,8,1,7,2]{0,4,5,2,1,3:T(8,128)(2,1)S(1)} %slice.72, bf16[512,2,8,1,8,5]{0,4,5,2,1,3:T(8,128)(2,1)S(1)} %copy.48, pred[8,5]{0,1:T(8,128)(4,1)S(1)} %copy-done.2), kind=kOutput, calls=%fused_computation.2 | convolution fusion | flops 694853632 | bytes 2818088 | tf_op jit(solution)/shard_map/conv_general_dilated | solution.py:42
  48.6 0.1 copy.49
  48.7 0.0 copy-start
  48.8 0.1 pad.19.clone
  48.9 0.0 collective-permute-done
  48.9 0.0 collective-permute-done.1
  49.0 0.1 maximum_add_fusion.1
  49.1 2.0 %collective-permute-start.2 = (f32[64,1,8,32]{0,2,3,1:T(8,128)S(1)}, f32[64,1,8,32]{0,2,3,1:T(8,128)S(1)}, u32[]{:S(2)}, u32[]{:S(2)}) collective-permute-start(f32[64,1,8,32]{0,2,3,1:T(8,128)S(1)} %get-tuple-element.23), channel_id=1, source_target_pairs={{0,64},{8,72},{16,80},{24,88},{32,96},{40,104},{48,112},{56,120},{... | collective-permute-start | bytes 196616 | tf_op jit(solution)/shard_map/ppermute | solution.py:14
  51.1 8.6 %collective-permute-start.3 = (f32[64,1,8,32]{0,2,3,1:T(8,128)S(1)}, f32[64,1,8,32]{0,2,3,1:T(8,128)S(1)}, u32[]{:S(2)}, u32[]{:S(2)}) collective-permute-start(f32[64,1,8,32]{0,2,3,1:T(8,128)S(1)} %get-tuple-element.24), channel_id=1, source_target_pairs={{0,448},{8,456},{16,464},{24,472},{32,480},{40,488},{48,496},{56,5... | collective-permute-start | bytes 196616 | tf_op jit(solution)/shard_map/ppermute | solution.py:14
  59.9 3.4 %collective-permute-done.2 = f32[64,1,8,32]{0,2,3,1:T(8,128)S(1)} collective-permute-done((f32[64,1,8,32]{0,2,3,1:T(8,128)S(1)}, f32[64,1,8,32]{0,2,3,1:T(8,128)S(1)}, u32[]{:S(2)}, u32[]{:S(2)}) %collective-permute-start.2) | collective-permute-done | bytes 65568 | tf_op jit(solution)/shard_map/ppermute | solution.py:14
  63.3 5.5 %collective-permute-done.3 = f32[64,1,8,32]{0,2,3,1:T(8,128)S(1)} collective-permute-done((f32[64,1,8,32]{0,2,3,1:T(8,128)S(1)}, f32[64,1,8,32]{0,2,3,1:T(8,128)S(1)}, u32[]{:S(2)}, u32[]{:S(2)}) %collective-permute-start.3) | collective-permute-done | bytes 65568 | tf_op jit(solution)/shard_map/ppermute | solution.py:14
  68.8 0.1 fusion.27
  68.9 0.1 copy.66
  69.0 0.0 copy-done
  69.0 0.8 %copy.67 = f32[1,2,64,256]{3,2,1,0:T(8,128)} copy(f32[1,2,64,256]{2,3,1,0:T(8,128)S(1)} %fusion.26) | data formatting | bytes 262144 | tf_op jit(solution)/shard_map/broadcast_in_dim | solution.py:87
  (29 shorter events, 0.7 us)
Async XLA Ops:
  16.0 1.4 %copy-start.2 = (pred[8,5]{0,1:T(8,128)(4,1)S(1)}, pred[8,5]{0,1:T(8,128)(4,1)}, u32[]{:S(2)}) copy-start(pred[8,5]{0,1:T(8,128)(4,1)} %constant.50) | copy-start | bytes 124
  19.1 29.8 %collective-permute-start = (f32[64,4,1,32]{0,1,3,2:T(4,128)S(1)}, f32[64,4,1,32]{0,1,3,2:T(4,128)S(1)}, u32[]{:S(2)}, u32[]{:S(2)}) collective-permute-start(f32[64,4,1,32]{0,1,3,2:T(4,128)S(1)} %slice_bitcast_fusion.7), channel_id=1, source_target_pairs={{0,8},{8,16},{16,24},{24,32},{32,40},{40,48},{48,56},{56,64},{64,7... | collective-permute-start | bytes 98312 | tf_op jit(solution)/shard_map/ppermute | solution.py:14
  25.2 23.7 %collective-permute-start.1 = (f32[64,4,1,32]{0,1,3,2:T(4,128)S(1)}, f32[64,4,1,32]{0,1,3,2:T(4,128)S(1)}, u32[]{:S(2)}, u32[]{:S(2)}) collective-permute-start(f32[64,4,1,32]{0,1,3,2:T(4,128)S(1)} %slice_bitcast_fusion.5), channel_id=1, source_target_pairs={{0,504},{8,0},{16,8},{24,16},{32,24},{40,32},{48,40},{56,48},{64,5... | collective-permute-start | bytes 98312 | tf_op jit(solution)/shard_map/ppermute | solution.py:14
  40.1 1.5 %copy-start.1 = (bf16[3,3,3,64,512]{4,3,2,1,0:T(8,128)(2,1)S(1)}, bf16[3,3,3,64,512]{4,3,2,1,0:T(8,128)(2,1)}, u32[]{:S(2)}) copy-start(bf16[3,3,3,64,512]{4,3,2,1,0:T(8,128)(2,1)} %param.4) | copy-start | bytes 5308420
  48.7 20.3 %copy-start = (f32[64]{0:T(128)S(1)}, f32[64]{0:T(128)}, u32[]{:S(2)}) copy-start(f32[64]{0:T(128)} %param.5) | copy-start | bytes 772
  49.1 14.2 %collective-permute-start.2 = (f32[64,1,8,32]{0,2,3,1:T(8,128)S(1)}, f32[64,1,8,32]{0,2,3,1:T(8,128)S(1)}, u32[]{:S(2)}, u32[]{:S(2)}) collective-permute-start(f32[64,1,8,32]{0,2,3,1:T(8,128)S(1)} %get-tuple-element.23), channel_id=1, source_target_pairs={{0,64},{8,72},{16,80},{24,88},{32,96},{40,104},{48,112},{56,120},{... | collective-permute-start | bytes 196616 | tf_op jit(solution)/shard_map/ppermute | solution.py:14
  51.1 17.6 %collective-permute-start.3 = (f32[64,1,8,32]{0,2,3,1:T(8,128)S(1)}, f32[64,1,8,32]{0,2,3,1:T(8,128)S(1)}, u32[]{:S(2)}, u32[]{:S(2)}) collective-permute-start(f32[64,1,8,32]{0,2,3,1:T(8,128)S(1)} %get-tuple-element.24), channel_id=1, source_target_pairs={{0,448},{8,456},{16,464},{24,472},{32,480},{40,488},{48,496},{56,5... | collective-permute-start | bytes 196616 | tf_op jit(solution)/shard_map/ppermute | solution.py:14

commit v17 on v14

--- a/solution.py
+++ b/solution.py
@@ -64,7 +64,11 @@
         cross(corners_from[:, 1:, 1:], corners_from[:, :1, :1], "space", CY + 1),
         cross(corners_from[:, 1:, :1], corners_from[:, :1, 1:], "space", CY - 1),
     ]
-    got, own_part = lax.optimization_barrier((got, own_part))
+    parity = lax.axis_index("chan") % 2
+    mine_face = conv(
+        got[0], lax.dynamic_slice_in_dim(weight, 2 * parity, 1, axis=0), ((0, 0), (1, 1), (1, 1))
+    )
+    got, own_part, mine_face = lax.optimization_barrier((got, own_part, mine_face))
     sizes = [piece[0].size for piece in got]
     joined = jnp.concatenate([piece.reshape(width_in, -1) for piece in got], axis=1)
     lower_all, upper_all = swap(joined)
@@ -77,12 +81,16 @@
     lower_row, upper_row = piece(lower_all, 1), piece(upper_all, 1)
     corner_ll, corner_hh = piece(lower_all, 2), piece(upper_all, 2)
     corner_lh, corner_hl = piece(lower_all, 3), piece(upper_all, 3)
-    face_part = jnp.concatenate(
-        [
-            conv(below, weight[:1], ((0, 0), (1, 1), (1, 1))),
-            conv(above, weight[2:], ((0, 0), (1, 1), (1, 1))),
-        ],
-        axis=1,
+    on_first = parity == 0
+    other_face = conv(
+        jnp.where(on_first, above, below),
+        lax.dynamic_slice_in_dim(weight, 2 - 2 * parity, 1, axis=0),
+        ((0, 0), (1, 1), (1, 1)),
+    )
+    face_part = jnp.where(
+        on_first,
+        jnp.concatenate([mine_face, other_face], axis=1),
+        jnp.concatenate([other_face, mine_face], axis=1),
     )
     place_y = (lax.axis_index("space") + 4) % 8
     lower_rim = jnp.concatenate([corner_ll, lower_row, corner_hl], axis=1)

time: 63.9 us -> 62 us (0.970)
  waiting for transfers between devices: 4.22 us -> 2.85 us
  local copies, waits for them, and re-layouts: 6.8 us -> 6.14 us
    ppermute x4, waiting for transfers between devices: 2.85 us -> 1.49 us  [cross(): return lax.ppermute(sent, (axis, 'chan'), pairs)]
  transfers between devices with their start and end apart: 5 -> 5, of which waited for: 2 -> 2; matrix products, arithmetic and copies ran while one was open for 10% -> 12% of each run, Pallas kernels for 0% -> 0%
where the time goes in v17:
time: 62 us; the launch traced here: 61.7 us
  starting transfers between devices  21.8 us (35%)
  blocking collectives  21.7 us (35%)
  matrix products  7.25 us (12%)
  local copies, waits for them, and re-layouts  6.14 us (10%)
  waiting for transfers between devices  2.85 us (5%)
  other arithmetic  1.37 us (2%)
    all_gather x1, blocking collectives, body(): gathered = lax.all_gather(own_block, 'chan', axis=0, tiled=True)  21.7 us
    ppermute x4, starting transfers between devices, cross(): return lax.ppermute(sent, (axis, 'chan'), pairs)  19.7 us
    conv_general_dilated x5, matrix products, conv(): lax.conv_general_dilated(field[None], taps, window_strides=(1, 1, 1), pad...  7.25 us
    unnamed x15, local copies, waits for them, and re-layouts  2.36 us
    ppermute x1, starting transfers between devices, swap(): lax.ppermute(got, 'chan', [(lane, lane ^ 1) for lane in range(width)])  2.14 us
    ppermute x4, waiting for transfers between devices, cross(): return lax.ppermute(sent, (axis, 'chan'), pairs)  1.49 us
    ppermute x1, waiting for transfers between devices, swap(): lax.ppermute(got, 'chan', [(lane, lane ^ 1) for lane in range(width)])  1.36 us
  transfers between devices with their start and end apart: 5, of which 2 were waited for; matrix products, arithmetic and copies ran while one was open for 12% of the time, Pallas kernels for 0%

profile of v17, /device:TPU:1, one launch (start us, length us, event | category | flops | bytes accessed | tf_op | source)
XLA Modules:
  0.0 61.7 jit_solution(16854134503765209461)
XLA Ops:
  0.0 0.9 %convert_element_type.7 = bf16[1,2,64,256]{3,2,1,0:T(8,128)(2,1)S(1)} convert(f32[1,2,64,256]{3,2,1,0:T(8,128)} %param.3) | non-fusion elementwise | flops 32768 | bytes 196608 | tf_op jit(solution)/shard_map/convert_element_type | solution.py:52
  0.9 21.7 %all_gather.3 = bf16[1024,256]{1,0:T(8,128)(2,1)S(1)} all-gather(bf16[128,256]{1,0:T(8,128)(2,1)S(1)} %bitcast.111), channel_id=1, replica_groups=mesh['space'=64,'chan'=8] {'chan'}, dimensions={0}, use_global_device_ids=true | all-gather | bytes 589824 | tf_op jit(solution)/shard_map/all_gather | solution.py:53
  22.6 0.6 copy.38
  23.2 0.6 reshape.181
  23.9 10.9 %collective-permute-start.1 = (bf16[512,2,1,32]{0,3,2,1:T(8,128)(2,1)S(1)}, bf16[512,2,1,32]{0,3,2,1:T(8,128)(2,1)S(1)}, u32[]{:S(2)}, u32[]{:S(2)}) collective-permute-start(bf16[512,2,1,32]{0,3,2,1:T(8,128)(2,1)S(1)} %slice_select_fusion.2), channel_id=1, source_target_pairs={{0,8},{1,509},{2,10},{3,511},{4,12},{5,505},{6,14},{7,507},{8,16},... | collective-permute-start | bytes 196616 | tf_op jit(solution)/shard_map/ppermute | solution.py:26
  34.8 1.9 %collective-permute-start = (bf16[512,1,8,32]{0,3,2,1:T(8,128)(2,1)S(1)}, bf16[512,1,8,32]{0,3,2,1:T(8,128)(2,1)S(1)}, u32[]{:S(2)}, u32[]{:S(2)}) collective-permute-start(bf16[512,1,8,32]{0,3,2,1:T(8,128)(2,1)S(1)} %slice_select_fusion.1), channel_id=1, source_target_pairs={{0,68},{1,453},{2,70},{3,455},{4,64},{5,449},{6,66},{7,451},{8,76}... | collective-permute-start | bytes 786440 | tf_op jit(solution)/shard_map/ppermute | solution.py:26
  36.7 0.6 reshape.222
  37.3 0.3 copy.72
  37.6 0.0 copy-start.1
  37.6 0.0 copy-start.3
  37.7 0.2 copy.42
  37.9 0.1 slice.90
  38.0 1.1 %copy-done.1 = bf16[3,3,3,64,512]{4,3,2,1,0:T(8,128)(2,1)S(1)} copy-done((bf16[3,3,3,64,512]{4,3,2,1,0:T(8,128)(2,1)S(1)}, bf16[3,3,3,64,512]{4,3,2,1,0:T(8,128)(2,1)}, u32[]{:S(2)}) %copy-start.1) | copy-done | bytes 1769496
  39.1 0.0 copy-done.3
  39.1 4.7 %convolution_select_fusion = f32[2,8,8,5,64]{4,2,3,1,0:T(8,128)S(1)} fusion(bf16[3,3,3,64,512]{4,3,2,1,0:T(8,128)(2,1)S(1)} %copy-done.1, bf16[512,2,8,1,7,2]{0,4,5,2,1,3:T(8,128)(2,1)S(1)} %slice.90, bf16[512,2,8,1,8,5]{0,4,5,2,1,3:T(8,128)(2,1)S(1)} %copy.42, pred[8,5]{0,1:T(8,128)(4,1)S(1)} %copy-done.3), kind=kOutput, calls=%fused_computation.2 | convolution fusion | flops 694853632 | bytes 2818088 | tf_op jit(solution)/shard_map/conv_general_dilated | solution.py:37
  43.8 0.0 copy-start.2
  43.8 0.1 copy.43
  44.0 2.1 %collective-permute-start.3 = (bf16[512,1,1,32]{0,3,2,1:T(8,128)(2,1)S(1)}, bf16[512,1,1,32]{0,3,2,1:T(8,128)(2,1)S(1)}, u32[]{:S(2)}, u32[]{:S(2)}) collective-permute-start(bf16[512,1,1,32]{0,3,2,1:T(8,128)(2,1)S(1)} %get-tuple-element.27), channel_id=1, source_target_pairs={{0,56},{1,461},{2,58},{3,463},{4,60},{5,457},{6,62},{7,459},{8,68}... | collective-permute-start | bytes 98312 | tf_op jit(solution)/shard_map/ppermute | solution.py:26
  46.0 4.8 %collective-permute-start.2 = (bf16[512,1,1,32]{0,3,2,1:T(8,128)(2,1)S(1)}, bf16[512,1,1,32]{0,3,2,1:T(8,128)(2,1)S(1)}, u32[]{:S(2)}, u32[]{:S(2)}) collective-permute-start(bf16[512,1,1,32]{0,3,2,1:T(8,128)(2,1)S(1)} %get-tuple-element.28), channel_id=1, source_target_pairs={{0,76},{1,441},{2,78},{3,443},{4,72},{5,445},{6,74},{7,447},{8,84}... | collective-permute-start | bytes 98312 | tf_op jit(solution)/shard_map/ppermute | solution.py:26
  50.9 0.0 collective-permute-done
  50.9 0.2 copy.73
  51.1 0.1 copy.46
  51.2 0.0 copy-done.2
  51.3 0.9 %convolution_select_fusion.2 = f32[1,8,8,5,64]{4,2,3,1,0:T(8,128)S(1)} fusion(bf16[3,3,3,64,512]{4,3,2,1,0:T(8,128)(2,1)S(1)} %copy-done.2, s32[]{:T(128)S(6)} %select_n.133, bf16[512,1,8,1,7,2]{0,4,5,2,3,1:T(8,128)(2,1)S(1)} %slice.92, bf16[512,1,8,1,8,5]{0,4,5,2,3,1:T(8,128)(2,1)S(1)} %copy.46, pred[8,5]{0,1:T(8,128)(4,1)S(1)} %copy-done.3), kind=kOutput, calls=%fused_computation.4 | convolution fusion | flops 174411776 | bytes 1131524 | tf_op jit(solution)/shard_map/conv_general_dilated | solution.py:37
  52.2 0.0 collective-permute-done.3
  52.3 1.5 %collective-permute-done.2 = bf16[512,1,1,32]{0,3,2,1:T(8,128)(2,1)S(1)} collective-permute-done((bf16[512,1,1,32]{0,3,2,1:T(8,128)(2,1)S(1)}, bf16[512,1,1,32]{0,3,2,1:T(8,128)(2,1)S(1)}, u32[]{:S(2)}, u32[]{:S(2)}) %collective-permute-start.2) | collective-permute-done | bytes 32800 | tf_op jit(solution)/shard_map/ppermute | solution.py:26
  53.7 0.0 collective-permute-done.1
  53.8 2.1 %collective-permute-start.4 = (bf16[512,384]{0,1:T(8,128)(2,1)S(1)}, bf16[512,384]{0,1:T(8,128)(2,1)S(1)}, u32[]{:S(2)}, u32[]{:S(2)}) collective-permute-start(bf16[512,384]{0,1:T(8,128)(2,1)S(1)} %pad_maximum_fusion), channel_id=1, source_target_pairs={{0,1},{1,0},{2,3},{3,2},{4,5},{5,4},{6,7},{7,6},{8,9},{9,8},{10,11... | collective-permute-start | bytes 1179656 | tf_op jit(solution)/shard_map/ppermute | solution.py:32
  56.0 0.1 pad.11.clone
  56.0 1.4 %collective-permute-done.4 = bf16[512,384]{0,1:T(8,128)(2,1)S(1)} collective-permute-done((bf16[512,384]{0,1:T(8,128)(2,1)S(1)}, bf16[512,384]{0,1:T(8,128)(2,1)S(1)}, u32[]{:S(2)}, u32[]{:S(2)}) %collective-permute-start.4) | collective-permute-done | bytes 393248 | tf_op jit(solution)/shard_map/ppermute | solution.py:32
  57.4 0.1 broadcast_select_fusion.1
  57.6 0.2 copy.76
  57.8 0.1 copy.74
  57.9 0.1 pad.6.clone
  58.1 0.1 copy.75
  58.2 0.1 pad.8.clone
  58.3 0.3 convolution_select_fusion.3
  58.7 0.3 convolution_select_fusion.4
  59.2 0.1 copy.51
  59.3 0.9 %convolution_select_fusion.1 = f32[1,8,8,5,64]{4,2,3,1,0:T(8,128)S(1)} fusion(bf16[3,3,3,64,512]{4,3,2,1,0:T(8,128)(2,1)S(1)} %copy-done.2, s32[]{:T(128)S(6)} %select_n.141, bf16[512,1,8,1,7,2]{0,4,5,2,3,1:T(8,128)(2,1)S(1)} %slice.96, bf16[512,1,8,1,8,5]{0,4,5,2,3,1:T(8,128)(2,1)S(1)} %copy.51, pred[8,5]{0,1:T(8,128)(4,1)S(1)} %copy-done.3), kind=kOutput, calls=%fused_computation.3 | convolution fusion | flops 174411776 | bytes 1131524 | tf_op jit(solution)/shard_map/conv_general_dilated | solution.py:37
  60.2 0.0 copy-start
  60.3 0.1 fusion.30
  60.4 0.1 copy.68
  60.5 0.4 copy-done
  60.9 0.8 %copy.69 = f32[1,2,64,256]{3,2,1,0:T(8,128)} copy(f32[1,2,64,256]{2,3,1,0:T(8,128)S(1)} %fusion.28) | data formatting | bytes 262144 | tf_op jit(solution)/shard_map/broadcast_in_dim | solution.py:109
  (33 shorter events, 0.7 us)
Async XLA Ops:
  23.9 29.9 %collective-permute-start.1 = (bf16[512,2,1,32]{0,3,2,1:T(8,128)(2,1)S(1)}, bf16[512,2,1,32]{0,3,2,1:T(8,128)(2,1)S(1)}, u32[]{:S(2)}, u32[]{:S(2)}) collective-permute-start(bf16[512,2,1,32]{0,3,2,1:T(8,128)(2,1)S(1)} %slice_select_fusion.2), channel_id=1, source_target_pairs={{0,8},{1,509},{2,10},{3,511},{4,12},{5,505},{6,14},{7,507},{8,16},... | collective-permute-start | bytes 196616 | tf_op jit(solution)/shard_map/ppermute | solution.py:26
  34.8 16.1 %collective-permute-start = (bf16[512,1,8,32]{0,3,2,1:T(8,128)(2,1)S(1)}, bf16[512,1,8,32]{0,3,2,1:T(8,128)(2,1)S(1)}, u32[]{:S(2)}, u32[]{:S(2)}) collective-permute-start(bf16[512,1,8,32]{0,3,2,1:T(8,128)(2,1)S(1)} %slice_select_fusion.1), channel_id=1, source_target_pairs={{0,68},{1,453},{2,70},{3,455},{4,64},{5,449},{6,66},{7,451},{8,76}... | collective-permute-start | bytes 786440 | tf_op jit(solution)/shard_map/ppermute | solution.py:26
  37.6 1.5 %copy-start.1 = (bf16[3,3,3,64,512]{4,3,2,1,0:T(8,128)(2,1)S(1)}, bf16[3,3,3,64,512]{4,3,2,1,0:T(8,128)(2,1)}, u32[]{:S(2)}) copy-start(bf16[3,3,3,64,512]{4,3,2,1,0:T(8,128)(2,1)} %param.4) | copy-start | bytes 5308420
  37.6 1.5 %copy-start.3 = (pred[8,5]{0,1:T(8,128)(4,1)S(1)}, pred[8,5]{0,1:T(8,128)(4,1)}, u32[]{:S(2)}) copy-start(pred[8,5]{0,1:T(8,128)(4,1)} %constant.77) | copy-start | bytes 124
  43.8 7.4 %copy-start.2 = (bf16[3,3,3,64,512]{4,3,2,1,0:T(8,128)(2,1)S(1)}, bf16[3,3,3,64,512]{4,3,2,1,0:T(8,128)(2,1)}, u32[]{:S(2)}) copy-start(bf16[3,3,3,64,512]{4,3,2,1,0:T(8,128)(2,1)} %param.4) | copy-start | bytes 5308420
  44.0 8.3 %collective-permute-start.3 = (bf16[512,1,1,32]{0,3,2,1:T(8,128)(2,1)S(1)}, bf16[512,1,1,32]{0,3,2,1:T(8,128)(2,1)S(1)}, u32[]{:S(2)}, u32[]{:S(2)}) collective-permute-start(bf16[512,1,1,32]{0,3,2,1:T(8,128)(2,1)S(1)} %get-tuple-element.27), channel_id=1, source_target_pairs={{0,56},{1,461},{2,58},{3,463},{4,60},{5,457},{6,62},{7,459},{8,68}... | collective-permute-start | bytes 98312 | tf_op jit(solution)/shard_map/ppermute | solution.py:26
  46.0 7.7 %collective-permute-start.2 = (bf16[512,1,1,32]{0,3,2,1:T(8,128)(2,1)S(1)}, bf16[512,1,1,32]{0,3,2,1:T(8,128)(2,1)S(1)}, u32[]{:S(2)}, u32[]{:S(2)}) collective-permute-start(bf16[512,1,1,32]{0,3,2,1:T(8,128)(2,1)S(1)} %get-tuple-element.28), channel_id=1, source_target_pairs={{0,76},{1,441},{2,78},{3,443},{4,72},{5,445},{6,74},{7,447},{8,84}... | collective-permute-start | bytes 98312 | tf_op jit(solution)/shard_map/ppermute | solution.py:26
  53.8 3.6 %collective-permute-start.4 = (bf16[512,384]{0,1:T(8,128)(2,1)S(1)}, bf16[512,384]{0,1:T(8,128)(2,1)S(1)}, u32[]{:S(2)}, u32[]{:S(2)}) collective-permute-start(bf16[512,384]{0,1:T(8,128)(2,1)S(1)} %pad_maximum_fusion), channel_id=1, source_target_pairs={{0,1},{1,0},{2,3},{3,2},{4,5},{5,4},{6,7},{7,6},{8,9},{9,8},{10,11... | collective-permute-start | bytes 1179656 | tf_op jit(solution)/shard_map/ppermute | solution.py:32
  60.2 0.7 %copy-start = (f32[64]{0:T(128)S(1)}, f32[64]{0:T(128)}, u32[]{:S(2)}) copy-start(f32[64]{0:T(128)} %param.5) | copy-start | bytes 772

commit v18 on v17

--- a/solution.py
+++ b/solution.py
@@ -65,28 +65,33 @@
         cross(corners_from[:, 1:, :1], corners_from[:, :1, 1:], "space", CY - 1),
     ]
     parity = lax.axis_index("chan") % 2
+    on_first = parity == 0
+    width = lax.axis_size("chan")
+    pairs_core = [(lane, lane ^ 1) for lane in range(width)]
     mine_face = conv(
         got[0], lax.dynamic_slice_in_dim(weight, 2 * parity, 1, axis=0), ((0, 0), (1, 1), (1, 1))
     )
-    got, own_part, mine_face = lax.optimization_barrier((got, own_part, mine_face))
     sizes = [piece[0].size for piece in got]
-    joined = jnp.concatenate([piece.reshape(width_in, -1) for piece in got], axis=1)
-    lower_all, upper_all = swap(joined)
-    offsets = [sum(sizes[:k]) for k in range(len(sizes) + 1)]
-
-    def piece(joined_half, k):
-        return joined_half[:, offsets[k] : offsets[k + 1]].reshape(got[k].shape)
-
-    below, above = piece(lower_all, 0), piece(upper_all, 0)
-    lower_row, upper_row = piece(lower_all, 1), piece(upper_all, 1)
-    corner_ll, corner_hh = piece(lower_all, 2), piece(upper_all, 2)
-    corner_lh, corner_hl = piece(lower_all, 3), piece(upper_all, 3)
-    on_first = parity == 0
+    early = jnp.concatenate([piece.reshape(width_in, -1) for piece in got[:2]], axis=1)
+    early_other = lax.ppermute(early, "chan", pairs_core)
+    face_other = early_other[:, : sizes[0]].reshape(got[0].shape)
+    row_other = early_other[:, sizes[0] :].reshape(got[1].shape)
     other_face = conv(
-        jnp.where(on_first, above, below),
-        lax.dynamic_slice_in_dim(weight, 2 - 2 * parity, 1, axis=0),
-        ((0, 0), (1, 1), (1, 1)),
+        face_other, lax.dynamic_slice_in_dim(weight, 2 - 2 * parity, 1, axis=0), ((0, 0), (1, 1), (1, 1))
     )
+    corners_got, own_part, mine_face, other_face, row_other = lax.optimization_barrier(
+        (got[2:], own_part, mine_face, other_face, row_other)
+    )
+    late = jnp.concatenate([piece.reshape(width_in, -1) for piece in corners_got], axis=1)
+    late_other = lax.ppermute(late, "chan", pairs_core)
+    corner_a_other = late_other[:, : sizes[2]].reshape(got[2].shape)
+    corner_b_other = late_other[:, sizes[2] :].reshape(got[3].shape)
+    lower_row = jnp.where(on_first, got[1], row_other)
+    upper_row = jnp.where(on_first, row_other, got[1])
+    corner_ll = jnp.where(on_first, corners_got[0], corner_a_other)
+    corner_hh = jnp.where(on_first, corner_a_other, corners_got[0])
+    corner_lh = jnp.where(on_first, corners_got[1], corner_b_other)
+    corner_hl = jnp.where(on_first, corner_b_other, corners_got[1])
     face_part = jnp.where(
         on_first,
         jnp.concatenate([mine_face, other_face], axis=1),

time: 62 us -> 62.2 us (level)
  starting transfers between devices: 21.8 us -> 23.7 us
  waiting for transfers between devices: 2.85 us -> 1.66 us
    ppermute x1 -> x2, starting transfers between devices: 2.14 us -> 3.96 us  [the longest x1 2.04 us: body(): late_other = lax.ppermute(late, 'chan', pairs_core)]
    ppermute x4, waiting for transfers between devices: 1.49 us -> 0.01 us  [cross(): return lax.ppermute(sent, (axis, 'chan'), pairs)]
    ppermute x1 -> x2, waiting for transfers between devices: 1.36 us -> 1.65 us  [the longest x1 1.06 us: body(): late_other = lax.ppermute(late, 'chan', pairs_core)]
  transfers between devices with their start and end apart: 5 -> 6, of which waited for: 2 -> 2; matrix products, arithmetic and copies ran while one was open for 12% -> 14% of each run, Pallas kernels for 0% -> 0%
where the time goes in v18:
time: 62.2 us; the launch traced here: 61.9 us
  starting transfers between devices  23.7 us (38%)
  blocking collectives  21.7 us (35%)
  matrix products  7.26 us (12%)
  local copies, waits for them, and re-layouts  5.74 us (9%)
  waiting for transfers between devices  1.66 us (3%)
  other arithmetic  1.24 us (2%)
    all_gather x1, blocking collectives, body(): gathered = lax.all_gather(own_block, 'chan', axis=0, tiled=True)  21.7 us
    ppermute x4, starting transfers between devices, cross(): return lax.ppermute(sent, (axis, 'chan'), pairs)  19.7 us
    conv_general_dilated x5, matrix products, conv(): lax.conv_general_dilated(field[None], taps, window_strides=(1, 1, 1), pad...  7.26 us
    ppermute x1, starting transfers between devices, body(): late_other = lax.ppermute(late, 'chan', pairs_core)  2.04 us
    unnamed x15, local copies, waits for them, and re-layouts  1.97 us
    ppermute x1, starting transfers between devices, body(): early_other = lax.ppermute(early, 'chan', pairs_core)  1.92 us
  transfers between devices with their start and end apart: 6, of which 2 were waited for; matrix products, arithmetic and copies ran while one was open for 14% of the time, Pallas kernels for 0%

profile of v18, /device:TPU:1, one launch (start us, length us, event | category | flops | bytes accessed | tf_op | source)
XLA Modules:
  0.0 61.9 jit_solution(2793025990197342220)
XLA Ops:
  0.0 0.9 %convert_element_type.7 = bf16[1,2,64,256]{3,2,1,0:T(8,128)(2,1)S(1)} convert(f32[1,2,64,256]{3,2,1,0:T(8,128)} %param.3) | non-fusion elementwise | flops 32768 | bytes 196608 | tf_op jit(solution)/shard_map/convert_element_type | solution.py:52
  0.9 21.7 %all_gather.3 = bf16[1024,256]{1,0:T(8,128)(2,1)S(1)} all-gather(bf16[128,256]{1,0:T(8,128)(2,1)S(1)} %bitcast.135), channel_id=1, replica_groups=mesh['space'=64,'chan'=8] {'chan'}, dimensions={0}, use_global_device_ids=true | all-gather | bytes 589824 | tf_op jit(solution)/shard_map/all_gather | solution.py:53
  22.6 0.6 copy.50
  23.2 0.6 reshape.152
  23.9 10.9 %collective-permute-start.3 = (bf16[512,2,1,32]{0,3,2,1:T(8,128)(2,1)S(1)}, bf16[512,2,1,32]{0,3,2,1:T(8,128)(2,1)S(1)}, u32[]{:S(2)}, u32[]{:S(2)}) collective-permute-start(bf16[512,2,1,32]{0,3,2,1:T(8,128)(2,1)S(1)} %bitcast_select_fusion.1), channel_id=1, source_target_pairs={{0,8},{1,509},{2,10},{3,511},{4,12},{5,505},{6,14},{7,507},{8,16},... | collective-permute-start | bytes 196616 | tf_op jit(solution)/shard_map/ppermute | solution.py:26
  34.8 1.9 %collective-permute-start.2 = (bf16[512,1,8,32]{0,3,2,1:T(8,128)(2,1)S(1)}, bf16[512,1,8,32]{0,3,2,1:T(8,128)(2,1)S(1)}, u32[]{:S(2)}, u32[]{:S(2)}) collective-permute-start(bf16[512,1,8,32]{0,3,2,1:T(8,128)(2,1)S(1)} %slice_select_fusion), channel_id=1, source_target_pairs={{0,68},{1,453},{2,70},{3,455},{4,64},{5,449},{6,66},{7,451},{8,76}... | collective-permute-start | bytes 786440 | tf_op jit(solution)/shard_map/ppermute | solution.py:26
  36.7 0.6 reshape.196
  37.3 0.3 copy.87
  37.6 0.0 copy-start.1
  37.6 0.0 copy-start.3
  37.7 0.2 copy.54
  37.9 0.1 slice.70
  38.0 1.1 %copy-done.1 = bf16[3,3,3,64,512]{4,3,2,1,0:T(8,128)(2,1)S(1)} copy-done((bf16[3,3,3,64,512]{4,3,2,1,0:T(8,128)(2,1)S(1)}, bf16[3,3,3,64,512]{4,3,2,1,0:T(8,128)(2,1)}, u32[]{:S(2)}) %copy-start.1) | copy-done | bytes 1769496
  39.1 0.0 copy-done.3
  39.1 4.7 %convolution_select_fusion = f32[2,8,8,5,64]{4,2,3,1,0:T(8,128)S(1)} fusion(bf16[3,3,3,64,512]{4,3,2,1,0:T(8,128)(2,1)S(1)} %copy-done.1, bf16[512,2,8,1,7,2]{0,4,5,2,1,3:T(8,128)(2,1)S(1)} %slice.70, bf16[512,2,8,1,8,5]{0,4,5,2,1,3:T(8,128)(2,1)S(1)} %copy.54, pred[8,5]{0,1:T(8,128)(4,1)S(1)} %copy-done.3), kind=kOutput, calls=%fused_computation.2 | convolution fusion | flops 694853632 | bytes 2818088 | tf_op jit(solution)/shard_map/conv_general_dilated | solution.py:37
  43.8 0.1 copy.55
  43.9 0.0 copy-start.2
  44.0 2.1 %collective-permute-start.1 = (bf16[512,1,1,32]{0,3,2,1:T(8,128)(2,1)S(1)}, bf16[512,1,1,32]{0,3,2,1:T(8,128)(2,1)S(1)}, u32[]{:S(2)}, u32[]{:S(2)}) collective-permute-start(bf16[512,1,1,32]{0,3,2,1:T(8,128)(2,1)S(1)} %get-tuple-element.21), channel_id=1, source_target_pairs={{0,56},{1,461},{2,58},{3,463},{4,60},{5,457},{6,62},{7,459},{8,68}... | collective-permute-start | bytes 98312 | tf_op jit(solution)/shard_map/ppermute | solution.py:26
  46.0 4.8 %collective-permute-start = (bf16[512,1,1,32]{0,3,2,1:T(8,128)(2,1)S(1)}, bf16[512,1,1,32]{0,3,2,1:T(8,128)(2,1)S(1)}, u32[]{:S(2)}, u32[]{:S(2)}) collective-permute-start(bf16[512,1,1,32]{0,3,2,1:T(8,128)(2,1)S(1)} %get-tuple-element.22), channel_id=1, source_target_pairs={{0,76},{1,441},{2,78},{3,443},{4,72},{5,445},{6,74},{7,447},{8,84}... | collective-permute-start | bytes 98312 | tf_op jit(solution)/shard_map/ppermute | solution.py:26
  50.9 0.1 pad.11.clone
  51.0 0.0 collective-permute-done.2
  51.0 0.1 copy.88
  51.2 0.1 copy.58
  51.3 0.0 collective-permute-done.3
  51.4 1.9 %collective-permute-start.4 = (bf16[512,320]{0,1:T(8,128)(2,1)S(1)}, bf16[512,320]{0,1:T(8,128)(2,1)S(1)}, u32[]{:S(2)}, u32[]{:S(2)}) collective-permute-start(bf16[512,320]{0,1:T(8,128)(2,1)S(1)} %pad_maximum_fusion), channel_id=1, source_target_pairs={{0,1},{1,0},{2,3},{3,2},{4,5},{5,4},{6,7},{7,6},{8,9},{9,8},{10,11... | collective-permute-start | bytes 983048 | tf_op jit(solution)/shard_map/ppermute | solution.py:76
  53.3 0.0 copy-done.2
  53.3 0.9 %convolution_select_fusion.2 = f32[1,8,8,5,64]{4,2,3,1,0:T(8,128)S(1)} fusion(bf16[3,3,3,64,512]{4,3,2,1,0:T(8,128)(2,1)S(1)} %copy-done.2, s32[]{:T(128)S(6)} %select_n.123, bf16[512,1,8,1,7,2]{0,4,5,2,3,1:T(8,128)(2,1)S(1)} %slice.74, bf16[512,1,8,1,8,5]{0,4,5,2,3,1:T(8,128)(2,1)S(1)} %copy.58, pred[8,5]{0,1:T(8,128)(4,1)S(1)} %copy-done.3), kind=kOutput, calls=%fused_computation.4 | convolution fusion | flops 174411776 | bytes 1131524 | tf_op jit(solution)/shard_map/conv_general_dilated | solution.py:37
  54.3 0.6 collective-permute-done.4
  54.9 0.2 copy.89
  55.1 0.1 copy.64
  55.3 0.9 %convolution_select_fusion.1 = f32[1,8,8,5,64]{4,2,3,1,0:T(8,128)S(1)} fusion(bf16[3,3,3,64,512]{4,3,2,1,0:T(8,128)(2,1)S(1)} %copy-done.2, s32[]{:T(128)S(6)} %select_n.126, bf16[512,1,8,1,7,2]{0,4,5,2,3,1:T(8,128)(2,1)S(1)} %slice.79, bf16[512,1,8,1,8,5]{0,4,5,2,3,1:T(8,128)(2,1)S(1)} %copy.64, pred[8,5]{0,1:T(8,128)(4,1)S(1)} %copy-done.3), kind=kOutput, calls=%fused_computation.3 | convolution fusion | flops 174411776 | bytes 1131524 | tf_op jit(solution)/shard_map/conv_general_dilated | solution.py:37
  56.3 0.0 collective-permute-done.1
  56.3 0.0 collective-permute-done
  56.3 2.0 %collective-permute-start.5 = (bf16[512,64]{0,1:T(8,128)(2,1)S(1)}, bf16[512,64]{0,1:T(8,128)(2,1)S(1)}, u32[]{:S(2)}, u32[]{:S(2)}) collective-permute-start(bf16[512,64]{0,1:T(8,128)(2,1)S(1)} %pad_maximum_fusion.1), channel_id=1, source_target_pairs={{0,1},{1,0},{2,3},{3,2},{4,5},{5,4},{6,7},{7,6},{8,9},{9,8},{10,11... | collective-permute-start | bytes 196616 | tf_op jit(solution)/shard_map/ppermute | solution.py:86
  58.4 1.1 %collective-permute-done.5 = bf16[512,64]{0,1:T(8,128)(2,1)S(1)} collective-permute-done((bf16[512,64]{0,1:T(8,128)(2,1)S(1)}, bf16[512,64]{0,1:T(8,128)(2,1)S(1)}, u32[]{:S(2)}, u32[]{:S(2)}) %collective-permute-start.5) | collective-permute-done | bytes 65568 | tf_op jit(solution)/shard_map/ppermute | solution.py:86
  59.5 0.1 copy.90
  59.6 0.1 pad.6.clone
  59.8 0.3 convolution_select_fusion.4
  60.2 0.1 copy.91
  60.3 0.1 pad.8.clone
  60.3 0.0 copy-start
  60.4 0.3 convolution_select_fusion.3
  60.8 0.1 fusion.30
  61.0 0.1 copy.83
  61.0 0.0 copy-done
  61.1 0.8 %copy.84 = f32[1,2,64,256]{3,2,1,0:T(8,128)} copy(f32[1,2,64,256]{2,3,1,0:T(8,128)S(1)} %fusion.28) | data formatting | bytes 262144 | tf_op jit(solution)/shard_map/broadcast_in_dim | solution.py:114
  (34 shorter events, 0.7 us)
Async XLA Ops:
  23.9 27.5 %collective-permute-start.3 = (bf16[512,2,1,32]{0,3,2,1:T(8,128)(2,1)S(1)}, bf16[512,2,1,32]{0,3,2,1:T(8,128)(2,1)S(1)}, u32[]{:S(2)}, u32[]{:S(2)}) collective-permute-start(bf16[512,2,1,32]{0,3,2,1:T(8,128)(2,1)S(1)} %bitcast_select_fusion.1), channel_id=1, source_target_pairs={{0,8},{1,509},{2,10},{3,511},{4,12},{5,505},{6,14},{7,507},{8,16},... | collective-permute-start | bytes 196616 | tf_op jit(solution)/shard_map/ppermute | solution.py:26
  34.8 16.2 %collective-permute-start.2 = (bf16[512,1,8,32]{0,3,2,1:T(8,128)(2,1)S(1)}, bf16[512,1,8,32]{0,3,2,1:T(8,128)(2,1)S(1)}, u32[]{:S(2)}, u32[]{:S(2)}) collective-permute-start(bf16[512,1,8,32]{0,3,2,1:T(8,128)(2,1)S(1)} %slice_select_fusion), channel_id=1, source_target_pairs={{0,68},{1,453},{2,70},{3,455},{4,64},{5,449},{6,66},{7,451},{8,76}... | collective-permute-start | bytes 786440 | tf_op jit(solution)/shard_map/ppermute | solution.py:26
  37.6 1.5 %copy-start.1 = (bf16[3,3,3,64,512]{4,3,2,1,0:T(8,128)(2,1)S(1)}, bf16[3,3,3,64,512]{4,3,2,1,0:T(8,128)(2,1)}, u32[]{:S(2)}) copy-start(bf16[3,3,3,64,512]{4,3,2,1,0:T(8,128)(2,1)} %param.4) | copy-start | bytes 5308420
  37.6 1.5 %copy-start.3 = (pred[8,5]{0,1:T(8,128)(4,1)S(1)}, pred[8,5]{0,1:T(8,128)(4,1)}, u32[]{:S(2)}) copy-start(pred[8,5]{0,1:T(8,128)(4,1)} %constant.75) | copy-start | bytes 124
  43.9 9.4 %copy-start.2 = (bf16[3,3,3,64,512]{4,3,2,1,0:T(8,128)(2,1)S(1)}, bf16[3,3,3,64,512]{4,3,2,1,0:T(8,128)(2,1)}, u32[]{:S(2)}) copy-start(bf16[3,3,3,64,512]{4,3,2,1,0:T(8,128)(2,1)} %param.4) | copy-start | bytes 5308420
  44.0 12.3 %collective-permute-start.1 = (bf16[512,1,1,32]{0,3,2,1:T(8,128)(2,1)S(1)}, bf16[512,1,1,32]{0,3,2,1:T(8,128)(2,1)S(1)}, u32[]{:S(2)}, u32[]{:S(2)}) collective-permute-start(bf16[512,1,1,32]{0,3,2,1:T(8,128)(2,1)S(1)} %get-tuple-element.21), channel_id=1, source_target_pairs={{0,56},{1,461},{2,58},{3,463},{4,60},{5,457},{6,62},{7,459},{8,68}... | collective-permute-start | bytes 98312 | tf_op jit(solution)/shard_map/ppermute | solution.py:26
  46.0 10.2 %collective-permute-start = (bf16[512,1,1,32]{0,3,2,1:T(8,128)(2,1)S(1)}, bf16[512,1,1,32]{0,3,2,1:T(8,128)(2,1)S(1)}, u32[]{:S(2)}, u32[]{:S(2)}) collective-permute-start(bf16[512,1,1,32]{0,3,2,1:T(8,128)(2,1)S(1)} %get-tuple-element.22), channel_id=1, source_target_pairs={{0,76},{1,441},{2,78},{3,443},{4,72},{5,445},{6,74},{7,447},{8,84}... | collective-permute-start | bytes 98312 | tf_op jit(solution)/shard_map/ppermute | solution.py:26
  51.4 3.5 %collective-permute-start.4 = (bf16[512,320]{0,1:T(8,128)(2,1)S(1)}, bf16[512,320]{0,1:T(8,128)(2,1)S(1)}, u32[]{:S(2)}, u32[]{:S(2)}) collective-permute-start(bf16[512,320]{0,1:T(8,128)(2,1)S(1)} %pad_maximum_fusion), channel_id=1, source_target_pairs={{0,1},{1,0},{2,3},{3,2},{4,5},{5,4},{6,7},{7,6},{8,9},{9,8},{10,11... | collective-permute-start | bytes 983048 | tf_op jit(solution)/shard_map/ppermute | solution.py:76
  56.3 3.1 %collective-permute-start.5 = (bf16[512,64]{0,1:T(8,128)(2,1)S(1)}, bf16[512,64]{0,1:T(8,128)(2,1)S(1)}, u32[]{:S(2)}, u32[]{:S(2)}) collective-permute-start(bf16[512,64]{0,1:T(8,128)(2,1)S(1)} %pad_maximum_fusion.1), channel_id=1, source_target_pairs={{0,1},{1,0},{2,3},{3,2},{4,5},{5,4},{6,7},{7,6},{8,9},{9,8},{10,11... | collective-permute-start | bytes 196616 | tf_op jit(solution)/shard_map/ppermute | solution.py:86
  60.3 0.7 %copy-start = (f32[64]{0:T(128)S(1)}, f32[64]{0:T(128)}, u32[]{:S(2)}) copy-start(f32[64]{0:T(128)} %param.5) | copy-start | bytes 772

commit v19 on v18

--- a/solution.py
+++ b/solution.py
@@ -59,7 +59,7 @@
         cross(gathered[:, -1:], gathered[:, :1], "space", CY),
         cross(gathered[:, :, -1:], gathered[:, :, :1], "space", 1),
     ]
-    corners_from, own_part = lax.optimization_barrier((gathered[:, ::size_x - 1, ::size_y - 1], own_part))
+    corners_from = gathered[:, ::size_x - 1, ::size_y - 1]
     got += [
         cross(corners_from[:, 1:, 1:], corners_from[:, :1, :1], "space", CY + 1),
         cross(corners_from[:, 1:, :1], corners_from[:, :1, 1:], "space", CY - 1),
@@ -68,6 +68,8 @@
     on_first = parity == 0
     width = lax.axis_size("chan")
     pairs_core = [(lane, lane ^ 1) for lane in range(width)]
+    faces_got, own_part = lax.optimization_barrier((got[:2], own_part))
+    got = faces_got + got[2:]
     mine_face = conv(
         got[0], lax.dynamic_slice_in_dim(weight, 2 * parity, 1, axis=0), ((0, 0), (1, 1), (1, 1))
     )

time: 62.2 us -> 64 us (1.029)
  the two profiles are of different devices: /device:TPU:1 before, /device:TPU:73 now
where the time goes in v19:
time: 64 us; the launch traced here: 63.7 us
  starting transfers between devices  29.5 us (46%)
  blocking collectives  15.5 us (24%)
  matrix products  7.23 us (11%)
  local copies, waits for them, and re-layouts  5.74 us (9%)
  waiting for transfers between devices  3.94 us (6%)
  other arithmetic  1.24 us (2%)
    ppermute x4, starting transfers between devices, cross(): return lax.ppermute(sent, (axis, 'chan'), pairs)  24.1 us
    all_gather x1, blocking collectives, body(): gathered = lax.all_gather(own_block, 'chan', axis=0, tiled=True)  15.5 us
    conv_general_dilated x5, matrix products, conv(): lax.conv_general_dilated(field[None], taps, window_strides=(1, 1, 1), pad...  7.23 us
    ppermute x1, starting transfers between devices, body(): early_other = lax.ppermute(early, 'chan', pairs_core)  3.13 us
    ppermute x4, waiting for transfers between devices, cross(): return lax.ppermute(sent, (axis, 'chan'), pairs)  2.84 us
    ppermute x1, starting transfers between devices, body(): late_other = lax.ppermute(late, 'chan', pairs_core)  2.29 us
    unnamed x13, local copies, waits for them, and re-layouts  1.96 us
  transfers between devices with their start and end apart: 6, of which 3 were waited for; matrix products, arithmetic and copies ran while one was open for 14% of the time, Pallas kernels for 0%

profile of v19, /device:TPU:73, one launch (start us, length us, event | category | flops | bytes accessed | tf_op | source)
XLA Modules:
  0.0 63.7 jit_solution(15713243504304438128)
XLA Ops:
  0.0 0.9 %convert_element_type.7 = bf16[1,2,64,256]{3,2,1,0:T(8,128)(2,1)S(1)} convert(f32[1,2,64,256]{3,2,1,0:T(8,128)} %param.3) | non-fusion elementwise | flops 32768 | bytes 196608 | tf_op jit(solution)/shard_map/convert_element_type | solution.py:52
  0.9 15.5 %all_gather.3 = bf16[1024,256]{1,0:T(8,128)(2,1)S(1)} all-gather(bf16[128,256]{1,0:T(8,128)(2,1)S(1)} %bitcast.135), channel_id=1, replica_groups=mesh['space'=64,'chan'=8] {'chan'}, dimensions={0}, use_global_device_ids=true | all-gather | bytes 589824 | tf_op jit(solution)/shard_map/all_gather | solution.py:53
  16.5 0.6 copy.50
  17.0 0.6 reshape.152
  17.7 3.6 %collective-permute-start.3 = (bf16[512,2,1,32]{0,3,2,1:T(8,128)(2,1)S(1)}, bf16[512,2,1,32]{0,3,2,1:T(8,128)(2,1)S(1)}, u32[]{:S(2)}, u32[]{:S(2)}) collective-permute-start(bf16[512,2,1,32]{0,3,2,1:T(8,128)(2,1)S(1)} %bitcast_select_fusion.1), channel_id=1, source_target_pairs={{0,8},{1,509},{2,10},{3,511},{4,12},{5,505},{6,14},{7,507},{8,16},... | collective-permute-start | bytes 196616 | tf_op jit(solution)/shard_map/ppermute | solution.py:26
  21.3 7.0 %collective-permute-start.1 = (bf16[512,1,1,32]{0,3,2,1:T(8,128)(2,1)S(1)}, bf16[512,1,1,32]{0,3,2,1:T(8,128)(2,1)S(1)}, u32[]{:S(2)}, u32[]{:S(2)}) collective-permute-start(bf16[512,1,1,32]{0,3,2,1:T(8,128)(2,1)S(1)} %get-tuple-element.23), channel_id=1, source_target_pairs={{0,56},{1,461},{2,58},{3,463},{4,60},{5,457},{6,62},{7,459},{8,68}... | collective-permute-start | bytes 98312 | tf_op jit(solution)/shard_map/ppermute | solution.py:26
  28.4 8.4 %collective-permute-start = (bf16[512,1,1,32]{0,3,2,1:T(8,128)(2,1)S(1)}, bf16[512,1,1,32]{0,3,2,1:T(8,128)(2,1)S(1)}, u32[]{:S(2)}, u32[]{:S(2)}) collective-permute-start(bf16[512,1,1,32]{0,3,2,1:T(8,128)(2,1)S(1)} %get-tuple-element.24), channel_id=1, source_target_pairs={{0,76},{1,441},{2,78},{3,443},{4,72},{5,445},{6,74},{7,447},{8,84}... | collective-permute-start | bytes 98312 | tf_op jit(solution)/shard_map/ppermute | solution.py:26
  36.8 5.0 %collective-permute-start.2 = (bf16[512,1,8,32]{0,3,2,1:T(8,128)(2,1)S(1)}, bf16[512,1,8,32]{0,3,2,1:T(8,128)(2,1)S(1)}, u32[]{:S(2)}, u32[]{:S(2)}) collective-permute-start(bf16[512,1,8,32]{0,3,2,1:T(8,128)(2,1)S(1)} %slice_select_fusion), channel_id=1, source_target_pairs={{0,68},{1,453},{2,70},{3,455},{4,64},{5,449},{6,66},{7,451},{8,76}... | collective-permute-start | bytes 786440 | tf_op jit(solution)/shard_map/ppermute | solution.py:26
  41.9 0.6 reshape.196
  42.5 0.3 copy.87
  42.8 0.0 copy-start.1
  42.8 0.0 copy-start.2
  42.9 0.2 copy.55
  43.1 0.1 slice.78
  43.1 1.1 %copy-done.1 = bf16[3,3,3,64,512]{4,3,2,1,0:T(8,128)(2,1)S(1)} copy-done((bf16[3,3,3,64,512]{4,3,2,1,0:T(8,128)(2,1)S(1)}, bf16[3,3,3,64,512]{4,3,2,1,0:T(8,128)(2,1)}, u32[]{:S(2)}) %copy-start.1) | copy-done | bytes 1769496
  44.3 0.0 copy-done.2
  44.3 4.7 %convolution_select_fusion = f32[2,8,8,5,64]{4,2,3,1,0:T(8,128)S(1)} fusion(bf16[3,3,3,64,512]{4,3,2,1,0:T(8,128)(2,1)S(1)} %copy-done.1, bf16[512,2,8,1,7,2]{0,4,5,2,1,3:T(8,128)(2,1)S(1)} %slice.78, bf16[512,2,8,1,8,5]{0,4,5,2,1,3:T(8,128)(2,1)S(1)} %copy.55, pred[8,5]{0,1:T(8,128)(4,1)S(1)} %copy-done.2), kind=kOutput, calls=%fused_computation.2 | convolution fusion | flops 694853632 | bytes 2818088 | tf_op jit(solution)/shard_map/conv_general_dilated | solution.py:37
  49.0 0.1 copy.56
  49.1 0.1 pad.11.clone
  49.2 0.0 collective-permute-done.3
  49.2 2.8 %collective-permute-done.2 = bf16[512,1,8,32]{0,3,2,1:T(8,128)(2,1)S(1)} collective-permute-done((bf16[512,1,8,32]{0,3,2,1:T(8,128)(2,1)S(1)}, bf16[512,1,8,32]{0,3,2,1:T(8,128)(2,1)S(1)}, u32[]{:S(2)}, u32[]{:S(2)}) %collective-permute-start.2) | collective-permute-done | bytes 262176 | tf_op jit(solution)/shard_map/ppermute | solution.py:26
  52.0 0.1 copy.88
  52.2 0.1 copy.59
  52.4 3.1 %collective-permute-start.4 = (bf16[512,320]{0,1:T(8,128)(2,1)S(1)}, bf16[512,320]{0,1:T(8,128)(2,1)S(1)}, u32[]{:S(2)}, u32[]{:S(2)}) collective-permute-start(bf16[512,320]{0,1:T(8,128)(2,1)S(1)} %pad_maximum_fusion), channel_id=1, source_target_pairs={{0,1},{1,0},{2,3},{3,2},{4,5},{5,4},{6,7},{7,6},{8,9},{9,8},{10,11... | collective-permute-start | bytes 983048 | tf_op jit(solution)/shard_map/ppermute | solution.py:78
  55.5 0.9 %convolution_select_fusion.2 = f32[1,8,8,5,64]{4,2,3,1,0:T(8,128)S(1)} fusion(bf16[3,3,3,64,512]{4,3,2,1,0:T(8,128)(2,1)S(1)} %copy-done.1, s32[]{:T(128)S(6)} %select_n.125, bf16[512,1,8,1,7,2]{0,4,5,2,3,1:T(8,128)(2,1)S(1)} %slice.80, bf16[512,1,8,1,8,5]{0,4,5,2,3,1:T(8,128)(2,1)S(1)} %copy.59, pred[8,5]{0,1:T(8,128)(4,1)S(1)} %copy-done.2), kind=kOutput, calls=%fused_computation.4 | convolution fusion | flops 174411776 | bytes 1131524 | tf_op jit(solution)/shard_map/conv_general_dilated | solution.py:37
  56.5 0.2 collective-permute-done.4
  56.8 0.2 copy.89
  57.0 0.1 copy.64
  57.1 0.9 %convolution_select_fusion.1 = f32[1,8,8,5,64]{4,2,3,1,0:T(8,128)S(1)} fusion(bf16[3,3,3,64,512]{4,3,2,1,0:T(8,128)(2,1)S(1)} %copy-done.1, s32[]{:T(128)S(6)} %select_n.126, bf16[512,1,8,1,7,2]{0,4,5,2,3,1:T(8,128)(2,1)S(1)} %slice.83, bf16[512,1,8,1,8,5]{0,4,5,2,3,1:T(8,128)(2,1)S(1)} %copy.64, pred[8,5]{0,1:T(8,128)(4,1)S(1)} %copy-done.2), kind=kOutput, calls=%fused_computation.3 | convolution fusion | flops 174411776 | bytes 1131524 | tf_op jit(solution)/shard_map/conv_general_dilated | solution.py:37
  58.1 0.0 collective-permute-done.1
  58.1 0.0 collective-permute-done
  58.2 2.3 %collective-permute-start.5 = (bf16[512,64]{0,1:T(8,128)(2,1)S(1)}, bf16[512,64]{0,1:T(8,128)(2,1)S(1)}, u32[]{:S(2)}, u32[]{:S(2)}) collective-permute-start(bf16[512,64]{0,1:T(8,128)(2,1)S(1)} %pad_maximum_fusion.1), channel_id=1, source_target_pairs={{0,1},{1,0},{2,3},{3,2},{4,5},{5,4},{6,7},{7,6},{8,9},{9,8},{10,11... | collective-permute-start | bytes 196616 | tf_op jit(solution)/shard_map/ppermute | solution.py:88
  60.5 0.9 %collective-permute-done.5 = bf16[512,64]{0,1:T(8,128)(2,1)S(1)} collective-permute-done((bf16[512,64]{0,1:T(8,128)(2,1)S(1)}, bf16[512,64]{0,1:T(8,128)(2,1)S(1)}, u32[]{:S(2)}, u32[]{:S(2)}) %collective-permute-start.5) | collective-permute-done | bytes 65568 | tf_op jit(solution)/shard_map/ppermute | solution.py:88
  61.4 0.1 copy.90
  61.5 0.1 pad.6.clone
  61.6 0.3 convolution_select_fusion.4
  62.1 0.1 copy.91
  62.2 0.1 pad.8.clone
  62.2 0.0 copy-start
  62.3 0.3 convolution_select_fusion.3
  62.7 0.1 fusion.30
  62.8 0.1 copy.83
  62.9 0.0 copy-done
  63.0 0.8 %copy.84 = f32[1,2,64,256]{3,2,1,0:T(8,128)} copy(f32[1,2,64,256]{2,3,1,0:T(8,128)S(1)} %fusion.28) | data formatting | bytes 262144 | tf_op jit(solution)/shard_map/broadcast_in_dim | solution.py:116
  (34 shorter events, 0.7 us)
Async XLA Ops:
  17.7 31.5 %collective-permute-start.3 = (bf16[512,2,1,32]{0,3,2,1:T(8,128)(2,1)S(1)}, bf16[512,2,1,32]{0,3,2,1:T(8,128)(2,1)S(1)}, u32[]{:S(2)}, u32[]{:S(2)}) collective-permute-start(bf16[512,2,1,32]{0,3,2,1:T(8,128)(2,1)S(1)} %bitcast_select_fusion.1), channel_id=1, source_target_pairs={{0,8},{1,509},{2,10},{3,511},{4,12},{5,505},{6,14},{7,507},{8,16},... | collective-permute-start | bytes 196616 | tf_op jit(solution)/shard_map/ppermute | solution.py:26
  21.3 36.8 %collective-permute-start.1 = (bf16[512,1,1,32]{0,3,2,1:T(8,128)(2,1)S(1)}, bf16[512,1,1,32]{0,3,2,1:T(8,128)(2,1)S(1)}, u32[]{:S(2)}, u32[]{:S(2)}) collective-permute-start(bf16[512,1,1,32]{0,3,2,1:T(8,128)(2,1)S(1)} %get-tuple-element.23), channel_id=1, source_target_pairs={{0,56},{1,461},{2,58},{3,463},{4,60},{5,457},{6,62},{7,459},{8,68}... | collective-permute-start | bytes 98312 | tf_op jit(solution)/shard_map/ppermute | solution.py:26
  28.4 29.7 %collective-permute-start = (bf16[512,1,1,32]{0,3,2,1:T(8,128)(2,1)S(1)}, bf16[512,1,1,32]{0,3,2,1:T(8,128)(2,1)S(1)}, u32[]{:S(2)}, u32[]{:S(2)}) collective-permute-start(bf16[512,1,1,32]{0,3,2,1:T(8,128)(2,1)S(1)} %get-tuple-element.24), channel_id=1, source_target_pairs={{0,76},{1,441},{2,78},{3,443},{4,72},{5,445},{6,74},{7,447},{8,84}... | collective-permute-start | bytes 98312 | tf_op jit(solution)/shard_map/ppermute | solution.py:26
  36.8 15.2 %collective-permute-start.2 = (bf16[512,1,8,32]{0,3,2,1:T(8,128)(2,1)S(1)}, bf16[512,1,8,32]{0,3,2,1:T(8,128)(2,1)S(1)}, u32[]{:S(2)}, u32[]{:S(2)}) collective-permute-start(bf16[512,1,8,32]{0,3,2,1:T(8,128)(2,1)S(1)} %slice_select_fusion), channel_id=1, source_target_pairs={{0,68},{1,453},{2,70},{3,455},{4,64},{5,449},{6,66},{7,451},{8,76}... | collective-permute-start | bytes 786440 | tf_op jit(solution)/shard_map/ppermute | solution.py:26
  42.8 1.5 %copy-start.1 = (bf16[3,3,3,64,512]{4,3,2,1,0:T(8,128)(2,1)S(1)}, bf16[3,3,3,64,512]{4,3,2,1,0:T(8,128)(2,1)}, u32[]{:S(2)}) copy-start(bf16[3,3,3,64,512]{4,3,2,1,0:T(8,128)(2,1)} %param.4) | copy-start | bytes 5308420
  42.8 1.5 %copy-start.2 = (pred[8,5]{0,1:T(8,128)(4,1)S(1)}, pred[8,5]{0,1:T(8,128)(4,1)}, u32[]{:S(2)}) copy-start(pred[8,5]{0,1:T(8,128)(4,1)} %constant.75) | copy-start | bytes 124
  52.4 4.4 %collective-permute-start.4 = (bf16[512,320]{0,1:T(8,128)(2,1)S(1)}, bf16[512,320]{0,1:T(8,128)(2,1)S(1)}, u32[]{:S(2)}, u32[]{:S(2)}) collective-permute-start(bf16[512,320]{0,1:T(8,128)(2,1)S(1)} %pad_maximum_fusion), channel_id=1, source_target_pairs={{0,1},{1,0},{2,3},{3,2},{4,5},{5,4},{6,7},{7,6},{8,9},{9,8},{10,11... | collective-permute-start | bytes 983048 | tf_op jit(solution)/shard_map/ppermute | solution.py:78
  58.2 3.2 %collective-permute-start.5 = (bf16[512,64]{0,1:T(8,128)(2,1)S(1)}, bf16[512,64]{0,1:T(8,128)(2,1)S(1)}, u32[]{:S(2)}, u32[]{:S(2)}) collective-permute-start(bf16[512,64]{0,1:T(8,128)(2,1)S(1)} %pad_maximum_fusion.1), channel_id=1, source_target_pairs={{0,1},{1,0},{2,3},{3,2},{4,5},{5,4},{6,7},{7,6},{8,9},{9,8},{10,11... | collective-permute-start | bytes 196616 | tf_op jit(solution)/shard_map/ppermute | solution.py:88
  62.2 0.7 %copy-start = (f32[64]{0:T(128)S(1)}, f32[64]{0:T(128)}, u32[]{:S(2)}) copy-start(f32[64]{0:T(128)} %param.5) | copy-start | bytes 772

commit v20 on v18

--- a/solution.py
+++ b/solution.py
@@ -48,10 +48,8 @@
     size_x = activation.shape[1]
     size_y = CY
     size_z = activation.shape[3] // size_y
-    width = lax.axis_size("chan")
-    own_block = activation[0].astype(jnp.bfloat16).reshape(-1, activation.shape[3])
+    own_block = activation[0].astype(jnp.bfloat16).transpose(1, 0, 2)
     gathered = lax.all_gather(own_block, "chan", axis=0, tiled=True)
-    gathered = gathered.reshape(width, size_x, -1, activation.shape[3]).transpose(0, 2, 1, 3)
     gathered = gathered.reshape(-1, size_x, size_y, size_z)
     own_part = conv(gathered, weight, ((1, 1), (1, 1), (1, 1)))
     width_in = gathered.shape[0]

time: 62.2 us -> 61 us (0.981)
  local copies, waits for them, and re-layouts: 5.74 us -> 4.76 us
    all_gather x0 -> x1, local copies, waits for them, and re-layouts: none -> 0.74 us  [body(): gathered = lax.all_gather(own_block, 'chan', axis=0, tiled=True)]
    unnamed x15 -> x14, local copies, waits for them, and re-layouts: 1.97 us -> 2.03 us
  transfers between devices with their start and end apart: 6 -> 6, of which waited for: 2 -> 2; matrix products, arithmetic and copies ran while one was open for 14% -> 13% of each run, Pallas kernels for 0% -> 0%
where the time goes in v20:
time: 61 us; the launch traced here: 60.7 us
  starting transfers between devices  23.5 us (39%)
  blocking collectives  21.7 us (36%)
  matrix products  7.23 us (12%)
  local copies, waits for them, and re-layouts  4.76 us (8%)
  waiting for transfers between devices  1.7 us (3%)
  other arithmetic  1.23 us (2%)
    all_gather x1, blocking collectives, body(): gathered = lax.all_gather(own_block, 'chan', axis=0, tiled=True)  21.7 us
    ppermute x4, starting transfers between devices, cross(): return lax.ppermute(sent, (axis, 'chan'), pairs)  19.6 us
    conv_general_dilated x5, matrix products, conv(): lax.conv_general_dilated(field[None], taps, window_strides=(1, 1, 1), pad...  7.23 us
    ppermute x1, starting transfers between devices, body(): late_other = lax.ppermute(late, 'chan', pairs_core)  2.04 us
    unnamed x14, local copies, waits for them, and re-layouts  2.03 us
    ppermute x1, starting transfers between devices, body(): early_other = lax.ppermute(early, 'chan', pairs_core)  1.92 us
  transfers between devices with their start and end apart: 6, of which 2 were waited for; matrix products, arithmetic and copies ran while one was open for 13% of the time, Pallas kernels for 0%

profile of v20, /device:TPU:1, one launch (start us, length us, event | category | flops | bytes accessed | tf_op | source)
XLA Modules:
  0.0 60.7 jit_solution(2263728059174390175)
XLA Ops:
  0.0 0.9 %convert_element_type.8 = bf16[1,2,64,256]{3,2,1,0:T(8,128)(2,1)S(1)} convert(f32[1,2,64,256]{3,2,1,0:T(8,128)} %param.3) | non-fusion elementwise | flops 32768 | bytes 196608 | tf_op jit(solution)/shard_map/convert_element_type | solution.py:51
  0.9 0.1 copy.89
  1.0 21.7 %all_gather.3 = bf16[512,2,256]{2,1,0:T(2,128)(2,1)S(1)} all-gather(bf16[64,2,256]{2,1,0:T(2,128)(2,1)S(1)} %bitcast.128), channel_id=1, replica_groups=mesh['space'=64,'chan'=8] {'chan'}, dimensions={0}, use_global_device_ids=true | all-gather | bytes 589824 | tf_op jit(solution)/shard_map/all_gather | solution.py:52
  22.7 0.7 %copy.46 = bf16[512,2,256]{0,2,1:T(8,128)(2,1)S(1)} copy(bf16[512,2,256]{2,1,0:T(2,128)(2,1)S(1)} %all_gather.3) | data formatting | bytes 1048576 | tf_op jit(solution)/shard_map/all_gather | solution.py:52
  23.5 10.9 %collective-permute-start.3 = (bf16[512,2,1,32]{0,3,2,1:T(8,128)(2,1)S(1)}, bf16[512,2,1,32]{0,3,2,1:T(8,128)(2,1)S(1)}, u32[]{:S(2)}, u32[]{:S(2)}) collective-permute-start(bf16[512,2,1,32]{0,3,2,1:T(8,128)(2,1)S(1)} %slice_select_fusion.1), channel_id=1, source_target_pairs={{0,8},{1,509},{2,10},{3,511},{4,12},{5,505},{6,14},{7,507},{8,16},... | collective-permute-start | bytes 196616 | tf_op jit(solution)/shard_map/ppermute | solution.py:26
  34.4 1.9 %collective-permute-start.2 = (bf16[512,1,8,32]{0,3,2,1:T(8,128)(2,1)S(1)}, bf16[512,1,8,32]{0,3,2,1:T(8,128)(2,1)S(1)}, u32[]{:S(2)}, u32[]{:S(2)}) collective-permute-start(bf16[512,1,8,32]{0,3,2,1:T(8,128)(2,1)S(1)} %slice_select_fusion), channel_id=1, source_target_pairs={{0,68},{1,453},{2,70},{3,455},{4,64},{5,449},{6,66},{7,451},{8,76}... | collective-permute-start | bytes 786440 | tf_op jit(solution)/shard_map/ppermute | solution.py:26
  36.3 0.3 copy.82
  36.6 0.0 copy-start.1
  36.7 0.0 copy-start.2
  36.7 0.2 copy.50
  36.9 0.1 slice.70
  37.0 1.1 %copy-done.1 = bf16[3,3,3,64,512]{4,3,2,1,0:T(8,128)(2,1)S(1)} copy-done((bf16[3,3,3,64,512]{4,3,2,1,0:T(8,128)(2,1)S(1)}, bf16[3,3,3,64,512]{4,3,2,1,0:T(8,128)(2,1)}, u32[]{:S(2)}) %copy-start.1) | copy-done | bytes 1769496
  38.1 0.0 copy-done.2
  38.1 4.7 %convolution_select_fusion = f32[2,8,8,5,64]{4,2,3,1,0:T(8,128)S(1)} fusion(bf16[3,3,3,64,512]{4,3,2,1,0:T(8,128)(2,1)S(1)} %copy-done.1, bf16[512,2,8,1,7,2]{0,4,5,2,1,3:T(8,128)(2,1)S(1)} %slice.70, bf16[512,2,8,1,8,5]{0,4,5,2,1,3:T(8,128)(2,1)S(1)} %copy.50, pred[8,5]{0,1:T(8,128)(4,1)S(1)} %copy-done.2), kind=kOutput, calls=%fused_computation.2 | convolution fusion | flops 694853632 | bytes 2818088 | tf_op jit(solution)/shard_map/conv_general_dilated | solution.py:37
  42.8 0.1 copy.51
  43.0 1.9 %collective-permute-start.1 = (bf16[512,1,1,32]{0,3,2,1:T(8,128)(2,1)S(1)}, bf16[512,1,1,32]{0,3,2,1:T(8,128)(2,1)S(1)}, u32[]{:S(2)}, u32[]{:S(2)}) collective-permute-start(bf16[512,1,1,32]{0,3,2,1:T(8,128)(2,1)S(1)} %get-tuple-element.23), channel_id=1, source_target_pairs={{0,56},{1,461},{2,58},{3,463},{4,60},{5,457},{6,62},{7,459},{8,68}... | collective-permute-start | bytes 98312 | tf_op jit(solution)/shard_map/ppermute | solution.py:26
  44.9 4.8 %collective-permute-start = (bf16[512,1,1,32]{0,3,2,1:T(8,128)(2,1)S(1)}, bf16[512,1,1,32]{0,3,2,1:T(8,128)(2,1)S(1)}, u32[]{:S(2)}, u32[]{:S(2)}) collective-permute-start(bf16[512,1,1,32]{0,3,2,1:T(8,128)(2,1)S(1)} %get-tuple-element.24), channel_id=1, source_target_pairs={{0,76},{1,441},{2,78},{3,443},{4,72},{5,445},{6,74},{7,447},{8,84}... | collective-permute-start | bytes 98312 | tf_op jit(solution)/shard_map/ppermute | solution.py:26
  49.8 0.1 pad.11.clone
  49.9 0.0 collective-permute-done.2
  49.9 0.1 copy.83
  50.0 0.1 copy.54
  50.2 0.0 collective-permute-done.3
  50.2 1.9 %collective-permute-start.4 = (bf16[512,320]{0,1:T(8,128)(2,1)S(1)}, bf16[512,320]{0,1:T(8,128)(2,1)S(1)}, u32[]{:S(2)}, u32[]{:S(2)}) collective-permute-start(bf16[512,320]{0,1:T(8,128)(2,1)S(1)} %pad_maximum_fusion), channel_id=1, source_target_pairs={{0,1},{1,0},{2,3},{3,2},{4,5},{5,4},{6,7},{7,6},{8,9},{9,8},{10,11... | collective-permute-start | bytes 983048 | tf_op jit(solution)/shard_map/ppermute | solution.py:74
  52.2 0.9 %convolution_select_fusion.2 = f32[1,8,8,5,64]{4,2,3,1,0:T(8,128)S(1)} fusion(bf16[3,3,3,64,512]{4,3,2,1,0:T(8,128)(2,1)S(1)} %copy-done.1, s32[]{:T(128)S(6)} %select_n.123, bf16[512,1,8,1,7,2]{0,4,5,2,3,1:T(8,128)(2,1)S(1)} %slice.74, bf16[512,1,8,1,8,5]{0,4,5,2,3,1:T(8,128)(2,1)S(1)} %copy.54, pred[8,5]{0,1:T(8,128)(4,1)S(1)} %copy-done.2), kind=kOutput, calls=%fused_computation.4 | convolution fusion | flops 174411776 | bytes 1131524 | tf_op jit(solution)/shard_map/conv_general_dilated | solution.py:37
  53.1 0.6 %collective-permute-done.4 = bf16[512,320]{0,1:T(8,128)(2,1)S(1)} collective-permute-done((bf16[512,320]{0,1:T(8,128)(2,1)S(1)}, bf16[512,320]{0,1:T(8,128)(2,1)S(1)}, u32[]{:S(2)}, u32[]{:S(2)}) %collective-permute-start.4) | collective-permute-done | bytes 327712 | tf_op jit(solution)/shard_map/ppermute | solution.py:74
  53.8 0.2 copy.84
  54.0 0.1 copy.59
  54.1 0.9 %convolution_select_fusion.1 = f32[1,8,8,5,64]{4,2,3,1,0:T(8,128)S(1)} fusion(bf16[3,3,3,64,512]{4,3,2,1,0:T(8,128)(2,1)S(1)} %copy-done.1, s32[]{:T(128)S(6)} %select_n.126, bf16[512,1,8,1,7,2]{0,4,5,2,3,1:T(8,128)(2,1)S(1)} %slice.79, bf16[512,1,8,1,8,5]{0,4,5,2,3,1:T(8,128)(2,1)S(1)} %copy.59, pred[8,5]{0,1:T(8,128)(4,1)S(1)} %copy-done.2), kind=kOutput, calls=%fused_computation.3 | convolution fusion | flops 174411776 | bytes 1131524 | tf_op jit(solution)/shard_map/conv_general_dilated | solution.py:37
  55.1 0.0 collective-permute-done.1
  55.1 0.0 collective-permute-done
  55.2 2.0 %collective-permute-start.5 = (bf16[512,64]{0,1:T(8,128)(2,1)S(1)}, bf16[512,64]{0,1:T(8,128)(2,1)S(1)}, u32[]{:S(2)}, u32[]{:S(2)}) collective-permute-start(bf16[512,64]{0,1:T(8,128)(2,1)S(1)} %pad_maximum_fusion.1), channel_id=1, source_target_pairs={{0,1},{1,0},{2,3},{3,2},{4,5},{5,4},{6,7},{7,6},{8,9},{9,8},{10,11... | collective-permute-start | bytes 196616 | tf_op jit(solution)/shard_map/ppermute | solution.py:84
  57.2 1.1 %collective-permute-done.5 = bf16[512,64]{0,1:T(8,128)(2,1)S(1)} collective-permute-done((bf16[512,64]{0,1:T(8,128)(2,1)S(1)}, bf16[512,64]{0,1:T(8,128)(2,1)S(1)}, u32[]{:S(2)}, u32[]{:S(2)}) %collective-permute-start.5) | collective-permute-done | bytes 65568 | tf_op jit(solution)/shard_map/ppermute | solution.py:84
  58.4 0.1 copy.85
  58.5 0.1 pad.6.clone
  58.6 0.3 convolution_select_fusion.4
  59.0 0.1 copy.86
  59.1 0.1 pad.8.clone
  59.2 0.0 copy-start
  59.3 0.3 convolution_select_fusion.3
  59.7 0.1 fusion.30
  59.8 0.1 copy.78
  59.9 0.0 copy-done
  59.9 0.8 %copy.79 = f32[1,2,64,256]{3,2,1,0:T(8,128)} copy(f32[1,2,64,256]{2,3,1,0:T(8,128)S(1)} %fusion.28) | data formatting | bytes 262144 | tf_op jit(solution)/shard_map/broadcast_in_dim | solution.py:112
  (33 shorter events, 0.7 us)
Async XLA Ops:
  23.5 26.7 %collective-permute-start.3 = (bf16[512,2,1,32]{0,3,2,1:T(8,128)(2,1)S(1)}, bf16[512,2,1,32]{0,3,2,1:T(8,128)(2,1)S(1)}, u32[]{:S(2)}, u32[]{:S(2)}) collective-permute-start(bf16[512,2,1,32]{0,3,2,1:T(8,128)(2,1)S(1)} %slice_select_fusion.1), channel_id=1, source_target_pairs={{0,8},{1,509},{2,10},{3,511},{4,12},{5,505},{6,14},{7,507},{8,16},... | collective-permute-start | bytes 196616 | tf_op jit(solution)/shard_map/ppermute | solution.py:26
  34.4 15.4 %collective-permute-start.2 = (bf16[512,1,8,32]{0,3,2,1:T(8,128)(2,1)S(1)}, bf16[512,1,8,32]{0,3,2,1:T(8,128)(2,1)S(1)}, u32[]{:S(2)}, u32[]{:S(2)}) collective-permute-start(bf16[512,1,8,32]{0,3,2,1:T(8,128)(2,1)S(1)} %slice_select_fusion), channel_id=1, source_target_pairs={{0,68},{1,453},{2,70},{3,455},{4,64},{5,449},{6,66},{7,451},{8,76}... | collective-permute-start | bytes 786440 | tf_op jit(solution)/shard_map/ppermute | solution.py:26
  36.6 1.5 %copy-start.1 = (bf16[3,3,3,64,512]{4,3,2,1,0:T(8,128)(2,1)S(1)}, bf16[3,3,3,64,512]{4,3,2,1,0:T(8,128)(2,1)}, u32[]{:S(2)}) copy-start(bf16[3,3,3,64,512]{4,3,2,1,0:T(8,128)(2,1)} %param.4) | copy-start | bytes 5308420
  36.7 1.5 %copy-start.2 = (pred[8,5]{0,1:T(8,128)(4,1)S(1)}, pred[8,5]{0,1:T(8,128)(4,1)}, u32[]{:S(2)}) copy-start(pred[8,5]{0,1:T(8,128)(4,1)} %constant.75) | copy-start | bytes 124
  43.0 12.2 %collective-permute-start.1 = (bf16[512,1,1,32]{0,3,2,1:T(8,128)(2,1)S(1)}, bf16[512,1,1,32]{0,3,2,1:T(8,128)(2,1)S(1)}, u32[]{:S(2)}, u32[]{:S(2)}) collective-permute-start(bf16[512,1,1,32]{0,3,2,1:T(8,128)(2,1)S(1)} %get-tuple-element.23), channel_id=1, source_target_pairs={{0,56},{1,461},{2,58},{3,463},{4,60},{5,457},{6,62},{7,459},{8,68}... | collective-permute-start | bytes 98312 | tf_op jit(solution)/shard_map/ppermute | solution.py:26
  44.9 10.3 %collective-permute-start = (bf16[512,1,1,32]{0,3,2,1:T(8,128)(2,1)S(1)}, bf16[512,1,1,32]{0,3,2,1:T(8,128)(2,1)S(1)}, u32[]{:S(2)}, u32[]{:S(2)}) collective-permute-start(bf16[512,1,1,32]{0,3,2,1:T(8,128)(2,1)S(1)} %get-tuple-element.24), channel_id=1, source_target_pairs={{0,76},{1,441},{2,78},{3,443},{4,72},{5,445},{6,74},{7,447},{8,84}... | collective-permute-start | bytes 98312 | tf_op jit(solution)/shard_map/ppermute | solution.py:26
  50.2 3.5 %collective-permute-start.4 = (bf16[512,320]{0,1:T(8,128)(2,1)S(1)}, bf16[512,320]{0,1:T(8,128)(2,1)S(1)}, u32[]{:S(2)}, u32[]{:S(2)}) collective-permute-start(bf16[512,320]{0,1:T(8,128)(2,1)S(1)} %pad_maximum_fusion), channel_id=1, source_target_pairs={{0,1},{1,0},{2,3},{3,2},{4,5},{5,4},{6,7},{7,6},{8,9},{9,8},{10,11... | collective-permute-start | bytes 983048 | tf_op jit(solution)/shard_map/ppermute | solution.py:74
  55.2 3.1 %collective-permute-start.5 = (bf16[512,64]{0,1:T(8,128)(2,1)S(1)}, bf16[512,64]{0,1:T(8,128)(2,1)S(1)}, u32[]{:S(2)}, u32[]{:S(2)}) collective-permute-start(bf16[512,64]{0,1:T(8,128)(2,1)S(1)} %pad_maximum_fusion.1), channel_id=1, source_target_pairs={{0,1},{1,0},{2,3},{3,2},{4,5},{5,4},{6,7},{7,6},{8,9},{9,8},{10,11... | collective-permute-start | bytes 196616 | tf_op jit(solution)/shard_map/ppermute | solution.py:84
  59.2 0.7 %copy-start = (f32[64]{0:T(128)S(1)}, f32[64]{0:T(128)}, u32[]{:S(2)}) copy-start(f32[64]{0:T(128)} %param.5) | copy-start | bytes 772

commit v21 on v17

--- a/solution.py
+++ b/solution.py
@@ -48,10 +48,8 @@
     size_x = activation.shape[1]
     size_y = CY
     size_z = activation.shape[3] // size_y
-    width = lax.axis_size("chan")
-    own_block = activation[0].astype(jnp.bfloat16).reshape(-1, activation.shape[3])
+    own_block = activation[0].astype(jnp.bfloat16).transpose(1, 0, 2)
     gathered = lax.all_gather(own_block, "chan", axis=0, tiled=True)
-    gathered = gathered.reshape(width, size_x, -1, activation.shape[3]).transpose(0, 2, 1, 3)
     gathered = gathered.reshape(-1, size_x, size_y, size_z)
     own_part = conv(gathered, weight, ((1, 1), (1, 1), (1, 1)))
     width_in = gathered.shape[0]

time: 62 us -> 62.5 us (level)
  the two profiles are of different devices: /device:TPU:1 before, /device:TPU:65 now
where the time goes in v21:
time: 62.5 us; the launch traced here: 62.2 us
  starting transfers between devices  26.7 us (43%)
  blocking collectives  15.6 us (25%)
  matrix products  7.22 us (12%)
  waiting for transfers between devices  5.97 us (10%)
  local copies, waits for them, and re-layouts  4.76 us (8%)
  other arithmetic  1.36 us (2%)
    ppermute x4, starting transfers between devices, cross(): return lax.ppermute(sent, (axis, 'chan'), pairs)  24.8 us
    all_gather x1, blocking collectives, body(): gathered = lax.all_gather(own_block, 'chan', axis=0, tiled=True)  15.6 us
    conv_general_dilated x5, matrix products, conv(): lax.conv_general_dilated(field[None], taps, window_strides=(1, 1, 1), pad...  7.22 us
    ppermute x4, waiting for transfers between devices, cross(): return lax.ppermute(sent, (axis, 'chan'), pairs)  4.4 us
    unnamed x14, local copies, waits for them, and re-layouts  2.03 us
    ppermute x1, starting transfers between devices, swap(): lax.ppermute(got, 'chan', [(lane, lane ^ 1) for lane in range(width)])  1.92 us
    ppermute x1, waiting for transfers between devices, swap(): lax.ppermute(got, 'chan', [(lane, lane ^ 1) for lane in range(width)])  1.58 us
  transfers between devices with their start and end apart: 5, of which 2 were waited for; matrix products, arithmetic and copies ran while one was open for 11% of the time, Pallas kernels for 0%

profile of v21, /device:TPU:65, one launch (start us, length us, event | category | flops | bytes accessed | tf_op | source)
XLA Modules:
  0.0 62.2 jit_solution(10491907266677731017)
XLA Ops:
  0.0 0.9 %convert_element_type.8 = bf16[1,2,64,256]{3,2,1,0:T(8,128)(2,1)S(1)} convert(f32[1,2,64,256]{3,2,1,0:T(8,128)} %param.3) | non-fusion elementwise | flops 32768 | bytes 196608 | tf_op jit(solution)/shard_map/convert_element_type | solution.py:51
  0.9 0.1 copy.81
  1.0 15.6 %all_gather.3 = bf16[512,2,256]{2,1,0:T(2,128)(2,1)S(1)} all-gather(bf16[64,2,256]{2,1,0:T(2,128)(2,1)S(1)} %bitcast.109), channel_id=1, replica_groups=mesh['space'=64,'chan'=8] {'chan'}, dimensions={0}, use_global_device_ids=true | all-gather | bytes 589824 | tf_op jit(solution)/shard_map/all_gather | solution.py:52
  16.6 0.7 %copy.40 = bf16[512,2,256]{0,2,1:T(8,128)(2,1)S(1)} copy(bf16[512,2,256]{2,1,0:T(2,128)(2,1)S(1)} %all_gather.3) | data formatting | bytes 1048576 | tf_op jit(solution)/shard_map/all_gather | solution.py:52
  17.4 7.7 %collective-permute-start = (bf16[512,1,8,32]{0,3,2,1:T(8,128)(2,1)S(1)}, bf16[512,1,8,32]{0,3,2,1:T(8,128)(2,1)S(1)}, u32[]{:S(2)}, u32[]{:S(2)}) collective-permute-start(bf16[512,1,8,32]{0,3,2,1:T(8,128)(2,1)S(1)} %slice_select_fusion.1), channel_id=1, source_target_pairs={{0,68},{1,453},{2,70},{3,455},{4,64},{5,449},{6,66},{7,451},{8,76}... | collective-permute-start | bytes 786440 | tf_op jit(solution)/shard_map/ppermute | solution.py:26
  25.1 1.9 %collective-permute-start.1 = (bf16[512,2,1,32]{0,3,2,1:T(8,128)(2,1)S(1)}, bf16[512,2,1,32]{0,3,2,1:T(8,128)(2,1)S(1)}, u32[]{:S(2)}, u32[]{:S(2)}) collective-permute-start(bf16[512,2,1,32]{0,3,2,1:T(8,128)(2,1)S(1)} %slice_select_fusion.2), channel_id=1, source_target_pairs={{0,8},{1,509},{2,10},{3,511},{4,12},{5,505},{6,14},{7,507},{8,16},... | collective-permute-start | bytes 196616 | tf_op jit(solution)/shard_map/ppermute | solution.py:26
  27.0 0.3 copy.74
  27.3 0.0 copy-start.1
  27.4 0.0 copy-start.2
  27.4 0.2 copy.44
  27.6 0.1 slice.90
  27.7 1.1 %copy-done.1 = bf16[3,3,3,64,512]{4,3,2,1,0:T(8,128)(2,1)S(1)} copy-done((bf16[3,3,3,64,512]{4,3,2,1,0:T(8,128)(2,1)S(1)}, bf16[3,3,3,64,512]{4,3,2,1,0:T(8,128)(2,1)}, u32[]{:S(2)}) %copy-start.1) | copy-done | bytes 1769496
  28.8 0.0 copy-done.2
  28.8 4.7 %convolution_select_fusion = f32[2,8,8,5,64]{4,2,3,1,0:T(8,128)S(1)} fusion(bf16[3,3,3,64,512]{4,3,2,1,0:T(8,128)(2,1)S(1)} %copy-done.1, bf16[512,2,8,1,7,2]{0,4,5,2,1,3:T(8,128)(2,1)S(1)} %slice.90, bf16[512,2,8,1,8,5]{0,4,5,2,1,3:T(8,128)(2,1)S(1)} %copy.44, pred[8,5]{0,1:T(8,128)(4,1)S(1)} %copy-done.2), kind=kOutput, calls=%fused_computation.2 | convolution fusion | flops 694853632 | bytes 2818088 | tf_op jit(solution)/shard_map/conv_general_dilated | solution.py:37
  33.5 0.1 copy.45
  33.7 13.3 %collective-permute-start.2 = (bf16[512,1,1,32]{0,3,2,1:T(8,128)(2,1)S(1)}, bf16[512,1,1,32]{0,3,2,1:T(8,128)(2,1)S(1)}, u32[]{:S(2)}, u32[]{:S(2)}) collective-permute-start(bf16[512,1,1,32]{0,3,2,1:T(8,128)(2,1)S(1)} %get-tuple-element.28), channel_id=1, source_target_pairs={{0,76},{1,441},{2,78},{3,443},{4,72},{5,445},{6,74},{7,447},{8,84}... | collective-permute-start | bytes 98312 | tf_op jit(solution)/shard_map/ppermute | solution.py:26
  47.0 1.9 %collective-permute-start.3 = (bf16[512,1,1,32]{0,3,2,1:T(8,128)(2,1)S(1)}, bf16[512,1,1,32]{0,3,2,1:T(8,128)(2,1)S(1)}, u32[]{:S(2)}, u32[]{:S(2)}) collective-permute-start(bf16[512,1,1,32]{0,3,2,1:T(8,128)(2,1)S(1)} %get-tuple-element.27), channel_id=1, source_target_pairs={{0,56},{1,461},{2,58},{3,463},{4,60},{5,457},{6,62},{7,459},{8,68}... | collective-permute-start | bytes 98312 | tf_op jit(solution)/shard_map/ppermute | solution.py:26
  48.9 0.0 collective-permute-done
  48.9 0.2 copy.75
  49.1 0.1 copy.48
  49.3 0.9 %convolution_select_fusion.2 = f32[1,8,8,5,64]{4,2,3,1,0:T(8,128)S(1)} fusion(bf16[3,3,3,64,512]{4,3,2,1,0:T(8,128)(2,1)S(1)} %copy-done.1, s32[]{:T(128)S(6)} %select_n.133, bf16[512,1,8,1,7,2]{0,4,5,2,3,1:T(8,128)(2,1)S(1)} %slice.92, bf16[512,1,8,1,8,5]{0,4,5,2,3,1:T(8,128)(2,1)S(1)} %copy.48, pred[8,5]{0,1:T(8,128)(4,1)S(1)} %copy-done.2), kind=kOutput, calls=%fused_computation.4 | convolution fusion | flops 174411776 | bytes 1131524 | tf_op jit(solution)/shard_map/conv_general_dilated | solution.py:37
  50.2 0.0 collective-permute-done.2
  50.3 4.4 %collective-permute-done.3 = bf16[512,1,1,32]{0,3,2,1:T(8,128)(2,1)S(1)} collective-permute-done((bf16[512,1,1,32]{0,3,2,1:T(8,128)(2,1)S(1)}, bf16[512,1,1,32]{0,3,2,1:T(8,128)(2,1)S(1)}, u32[]{:S(2)}, u32[]{:S(2)}) %collective-permute-start.3) | collective-permute-done | bytes 32800 | tf_op jit(solution)/shard_map/ppermute | solution.py:26
  54.6 0.0 collective-permute-done.1
  54.7 1.9 %collective-permute-start.4 = (bf16[512,384]{0,1:T(8,128)(2,1)S(1)}, bf16[512,384]{0,1:T(8,128)(2,1)S(1)}, u32[]{:S(2)}, u32[]{:S(2)}) collective-permute-start(bf16[512,384]{0,1:T(8,128)(2,1)S(1)} %pad_maximum_fusion), channel_id=1, source_target_pairs={{0,1},{1,0},{2,3},{3,2},{4,5},{5,4},{6,7},{7,6},{8,9},{9,8},{10,11... | collective-permute-start | bytes 1179656 | tf_op jit(solution)/shard_map/ppermute | solution.py:32
  56.6 0.1 pad.11.clone
  56.7 1.6 %collective-permute-done.4 = bf16[512,384]{0,1:T(8,128)(2,1)S(1)} collective-permute-done((bf16[512,384]{0,1:T(8,128)(2,1)S(1)}, bf16[512,384]{0,1:T(8,128)(2,1)S(1)}, u32[]{:S(2)}, u32[]{:S(2)}) %collective-permute-start.4) | collective-permute-done | bytes 393248 | tf_op jit(solution)/shard_map/ppermute | solution.py:32
  58.3 0.1 broadcast_select_fusion.1
  58.5 0.2 copy.78
  58.7 0.1 copy.53
  58.9 0.9 %convolution_select_fusion.1 = f32[1,8,8,5,64]{4,2,3,1,0:T(8,128)S(1)} fusion(bf16[3,3,3,64,512]{4,3,2,1,0:T(8,128)(2,1)S(1)} %copy-done.1, s32[]{:T(128)S(6)} %select_n.141, bf16[512,1,8,1,7,2]{0,4,5,2,3,1:T(8,128)(2,1)S(1)} %slice.96, bf16[512,1,8,1,8,5]{0,4,5,2,3,1:T(8,128)(2,1)S(1)} %copy.53, pred[8,5]{0,1:T(8,128)(4,1)S(1)} %copy-done.2), kind=kOutput, calls=%fused_computation.3 | convolution fusion | flops 174411776 | bytes 1131524 | tf_op jit(solution)/shard_map/conv_general_dilated | solution.py:37
  59.9 0.1 copy.77
  60.0 0.1 pad.8.clone
  60.1 0.3 convolution_select_fusion.3
  60.6 0.1 copy.76
  60.7 0.1 pad.6.clone
  60.8 0.0 copy-start
  60.8 0.3 convolution_select_fusion.4
  61.2 0.1 fusion.30
  61.4 0.1 copy.70
  61.4 0.0 copy-done
  61.5 0.8 %copy.71 = f32[1,2,64,256]{3,2,1,0:T(8,128)} copy(f32[1,2,64,256]{2,3,1,0:T(8,128)S(1)} %fusion.28) | data formatting | bytes 262144 | tf_op jit(solution)/shard_map/broadcast_in_dim | solution.py:107
  (33 shorter events, 0.7 us)
Async XLA Ops:
  17.4 31.5 %collective-permute-start = (bf16[512,1,8,32]{0,3,2,1:T(8,128)(2,1)S(1)}, bf16[512,1,8,32]{0,3,2,1:T(8,128)(2,1)S(1)}, u32[]{:S(2)}, u32[]{:S(2)}) collective-permute-start(bf16[512,1,8,32]{0,3,2,1:T(8,128)(2,1)S(1)} %slice_select_fusion.1), channel_id=1, source_target_pairs={{0,68},{1,453},{2,70},{3,455},{4,64},{5,449},{6,66},{7,451},{8,76}... | collective-permute-start | bytes 786440 | tf_op jit(solution)/shard_map/ppermute | solution.py:26
  25.1 29.5 %collective-permute-start.1 = (bf16[512,2,1,32]{0,3,2,1:T(8,128)(2,1)S(1)}, bf16[512,2,1,32]{0,3,2,1:T(8,128)(2,1)S(1)}, u32[]{:S(2)}, u32[]{:S(2)}) collective-permute-start(bf16[512,2,1,32]{0,3,2,1:T(8,128)(2,1)S(1)} %slice_select_fusion.2), channel_id=1, source_target_pairs={{0,8},{1,509},{2,10},{3,511},{4,12},{5,505},{6,14},{7,507},{8,16},... | collective-permute-start | bytes 196616 | tf_op jit(solution)/shard_map/ppermute | solution.py:26
  27.3 1.5 %copy-start.1 = (bf16[3,3,3,64,512]{4,3,2,1,0:T(8,128)(2,1)S(1)}, bf16[3,3,3,64,512]{4,3,2,1,0:T(8,128)(2,1)}, u32[]{:S(2)}) copy-start(bf16[3,3,3,64,512]{4,3,2,1,0:T(8,128)(2,1)} %param.4) | copy-start | bytes 5308420
  27.4 1.5 %copy-start.2 = (pred[8,5]{0,1:T(8,128)(4,1)S(1)}, pred[8,5]{0,1:T(8,128)(4,1)}, u32[]{:S(2)}) copy-start(pred[8,5]{0,1:T(8,128)(4,1)} %constant.77) | copy-start | bytes 124
  33.7 16.6 %collective-permute-start.2 = (bf16[512,1,1,32]{0,3,2,1:T(8,128)(2,1)S(1)}, bf16[512,1,1,32]{0,3,2,1:T(8,128)(2,1)S(1)}, u32[]{:S(2)}, u32[]{:S(2)}) collective-permute-start(bf16[512,1,1,32]{0,3,2,1:T(8,128)(2,1)S(1)} %get-tuple-element.28), channel_id=1, source_target_pairs={{0,76},{1,441},{2,78},{3,443},{4,72},{5,445},{6,74},{7,447},{8,84}... | collective-permute-start | bytes 98312 | tf_op jit(solution)/shard_map/ppermute | solution.py:26
  47.0 7.7 %collective-permute-start.3 = (bf16[512,1,1,32]{0,3,2,1:T(8,128)(2,1)S(1)}, bf16[512,1,1,32]{0,3,2,1:T(8,128)(2,1)S(1)}, u32[]{:S(2)}, u32[]{:S(2)}) collective-permute-start(bf16[512,1,1,32]{0,3,2,1:T(8,128)(2,1)S(1)} %get-tuple-element.27), channel_id=1, source_target_pairs={{0,56},{1,461},{2,58},{3,463},{4,60},{5,457},{6,62},{7,459},{8,68}... | collective-permute-start | bytes 98312 | tf_op jit(solution)/shard_map/ppermute | solution.py:26
  54.7 3.6 %collective-permute-start.4 = (bf16[512,384]{0,1:T(8,128)(2,1)S(1)}, bf16[512,384]{0,1:T(8,128)(2,1)S(1)}, u32[]{:S(2)}, u32[]{:S(2)}) collective-permute-start(bf16[512,384]{0,1:T(8,128)(2,1)S(1)} %pad_maximum_fusion), channel_id=1, source_target_pairs={{0,1},{1,0},{2,3},{3,2},{4,5},{5,4},{6,7},{7,6},{8,9},{9,8},{10,11... | collective-permute-start | bytes 1179656 | tf_op jit(solution)/shard_map/ppermute | solution.py:32
  60.8 0.7 %copy-start = (f32[64]{0:T(128)S(1)}, f32[64]{0:T(128)}, u32[]{:S(2)}) copy-start(f32[64]{0:T(128)} %param.5) | copy-start | bytes 772

commit v22 on v20

--- a/solution.py
+++ b/solution.py
@@ -39,7 +39,7 @@
         taps,
         window_strides=(1, 1, 1),
         padding=padding,
-        dimension_numbers=("NCDHW", "DHWOI", "NCDHW"),
+        dimension_numbers=("NCDHW", "DHWOI", "NDCHW"),
         preferred_element_type=jnp.float32,
     )[0]
 
@@ -92,8 +92,8 @@
     corner_hl = jnp.where(on_first, corner_b_other, corners_got[1])
     face_part = jnp.where(
         on_first,
-        jnp.concatenate([mine_face, other_face], axis=1),
-        jnp.concatenate([other_face, mine_face], axis=1),
+        jnp.concatenate([mine_face, other_face], axis=0),
+        jnp.concatenate([other_face, mine_face], axis=0),
     )
     place_y = (lax.axis_index("space") + 4) % 8
     lower_rim = jnp.concatenate([corner_ll, lower_row, corner_hl], axis=1)
@@ -102,14 +102,12 @@
     upper_rim = jnp.where(place_y < 7, upper_rim, jnp.zeros_like(upper_rim))
     lower_part = conv(lower_rim, weight[:, :1], ((0, 0), (0, 0), (1, 1)))
     upper_part = conv(upper_rim, weight[:, 2:], ((0, 0), (0, 0), (1, 1)))
-    width_out = own_part.shape[0]
-    middle = jnp.zeros((width_out, size_x, size_y - 2, size_z), jnp.float32)
+    width_out = own_part.shape[1]
+    middle = jnp.zeros((size_x, width_out, size_y - 2, size_z), jnp.float32)
     rim_part = jnp.concatenate([lower_part, middle, upper_part], axis=2)
-    total = (own_part + face_part + rim_part).reshape(width_out, -1)
-    before = total + conv_bias[:, None]
+    before = own_part + face_part + rim_part + conv_bias[None, :, None, None]
     result = jnp.maximum(before, negative_slope * before)
-    result = result.reshape(width_out, size_x, size_y * size_z).transpose(1, 0, 2)
-    return result[None]
+    return result.reshape(1, size_x, width_out, size_y * size_z)
 
 
 def solution(mesh):

time: 61 us -> 61 us (level)
    broadcast_in_dim x2 -> x1, local copies, waits for them, and re-layouts: 0.78 us -> 0.01 us  [body(): middle = jnp.zeros((size_x, width_out, size_y - 2, size_z), jnp.float32)]
    reshape x0 -> x1, local copies, waits for them, and re-layouts: none -> 0.77 us  [body(): return result.reshape(1, size_x, width_out, size_y * size_z)]
where the time goes in v22:
time: 61 us; the launch traced here: 60.7 us
  starting transfers between devices  23.5 us (39%)
  blocking collectives  21.7 us (36%)
  matrix products  7.21 us (12%)
  local copies, waits for them, and re-layouts  4.76 us (8%)
  waiting for transfers between devices  1.69 us (3%)
  other arithmetic  1.23 us (2%)
    all_gather x1, blocking collectives, body(): gathered = lax.all_gather(own_block, 'chan', axis=0, tiled=True)  21.7 us
    ppermute x4, starting transfers between devices, cross(): return lax.ppermute(sent, (axis, 'chan'), pairs)  19.6 us
    conv_general_dilated x5, matrix products, conv(): lax.conv_general_dilated(field[None], taps, window_strides=(1, 1, 1), pad...  7.21 us
    ppermute x1, starting transfers between devices, body(): late_other = lax.ppermute(late, 'chan', pairs_core)  2.06 us
    unnamed x14, local copies, waits for them, and re-layouts  2.03 us
    ppermute x1, starting transfers between devices, body(): early_other = lax.ppermute(early, 'chan', pairs_core)  1.92 us
  transfers between devices with their start and end apart: 6, of which 2 were waited for; matrix products, arithmetic and copies ran while one was open for 13% of the time, Pallas kernels for 0%

profile of v22, /device:TPU:1, one launch (start us, length us, event | category | flops | bytes accessed | tf_op | source)
XLA Modules:
  0.0 60.7 jit_solution(9849114820241428272)
XLA Ops:
  0.0 0.9 %convert_element_type.8 = bf16[1,2,64,256]{3,2,1,0:T(8,128)(2,1)S(1)} convert(f32[1,2,64,256]{3,2,1,0:T(8,128)} %param.3) | non-fusion elementwise | flops 32768 | bytes 196608 | tf_op jit(solution)/shard_map/convert_element_type | solution.py:51
  0.9 0.1 copy.89
  1.0 21.7 %all_gather.3 = bf16[512,2,256]{2,1,0:T(2,128)(2,1)S(1)} all-gather(bf16[64,2,256]{2,1,0:T(2,128)(2,1)S(1)} %bitcast.122), channel_id=1, replica_groups=mesh['space'=64,'chan'=8] {'chan'}, dimensions={0}, use_global_device_ids=true | all-gather | bytes 589824 | tf_op jit(solution)/shard_map/all_gather | solution.py:52
  22.7 0.7 %copy.46 = bf16[512,2,256]{0,2,1:T(8,128)(2,1)S(1)} copy(bf16[512,2,256]{2,1,0:T(2,128)(2,1)S(1)} %all_gather.3) | data formatting | bytes 1048576 | tf_op jit(solution)/shard_map/all_gather | solution.py:52
  23.5 10.9 %collective-permute-start.3 = (bf16[512,2,1,32]{0,3,2,1:T(8,128)(2,1)S(1)}, bf16[512,2,1,32]{0,3,2,1:T(8,128)(2,1)S(1)}, u32[]{:S(2)}, u32[]{:S(2)}) collective-permute-start(bf16[512,2,1,32]{0,3,2,1:T(8,128)(2,1)S(1)} %slice_select_fusion.1), channel_id=1, source_target_pairs={{0,8},{1,509},{2,10},{3,511},{4,12},{5,505},{6,14},{7,507},{8,16},... | collective-permute-start | bytes 196616 | tf_op jit(solution)/shard_map/ppermute | solution.py:26
  34.4 1.9 %collective-permute-start.2 = (bf16[512,1,8,32]{0,3,2,1:T(8,128)(2,1)S(1)}, bf16[512,1,8,32]{0,3,2,1:T(8,128)(2,1)S(1)}, u32[]{:S(2)}, u32[]{:S(2)}) collective-permute-start(bf16[512,1,8,32]{0,3,2,1:T(8,128)(2,1)S(1)} %slice_select_fusion), channel_id=1, source_target_pairs={{0,68},{1,453},{2,70},{3,455},{4,64},{5,449},{6,66},{7,451},{8,76}... | collective-permute-start | bytes 786440 | tf_op jit(solution)/shard_map/ppermute | solution.py:26
  36.3 0.3 copy.82
  36.6 0.0 copy-start.1
  36.7 0.0 copy-start.2
  36.7 0.2 copy.50
  36.9 0.1 slice.70
  37.0 1.1 %copy-done.1 = bf16[3,3,3,64,512]{4,3,2,1,0:T(8,128)(2,1)S(1)} copy-done((bf16[3,3,3,64,512]{4,3,2,1,0:T(8,128)(2,1)S(1)}, bf16[3,3,3,64,512]{4,3,2,1,0:T(8,128)(2,1)}, u32[]{:S(2)}) %copy-start.1) | copy-done | bytes 1769496
  38.1 0.0 copy-done.2
  38.1 4.7 %convolution_select_fusion = f32[2,8,8,5,64]{4,2,3,1,0:T(8,128)S(1)} fusion(bf16[3,3,3,64,512]{4,3,2,1,0:T(8,128)(2,1)S(1)} %copy-done.1, bf16[512,2,8,1,7,2]{0,4,5,2,1,3:T(8,128)(2,1)S(1)} %slice.70, bf16[512,2,8,1,8,5]{0,4,5,2,1,3:T(8,128)(2,1)S(1)} %copy.50, pred[8,5]{0,1:T(8,128)(4,1)S(1)} %copy-done.2), kind=kOutput, calls=%fused_computation.2 | convolution fusion | flops 694853632 | bytes 2818088 | tf_op jit(solution)/shard_map/conv_general_dilated | solution.py:37
  42.8 0.1 copy.51
  43.0 1.9 %collective-permute-start.1 = (bf16[512,1,1,32]{0,3,2,1:T(8,128)(2,1)S(1)}, bf16[512,1,1,32]{0,3,2,1:T(8,128)(2,1)S(1)}, u32[]{:S(2)}, u32[]{:S(2)}) collective-permute-start(bf16[512,1,1,32]{0,3,2,1:T(8,128)(2,1)S(1)} %get-tuple-element.23), channel_id=1, source_target_pairs={{0,56},{1,461},{2,58},{3,463},{4,60},{5,457},{6,62},{7,459},{8,68}... | collective-permute-start | bytes 98312 | tf_op jit(solution)/shard_map/ppermute | solution.py:26
  44.9 4.8 %collective-permute-start = (bf16[512,1,1,32]{0,3,2,1:T(8,128)(2,1)S(1)}, bf16[512,1,1,32]{0,3,2,1:T(8,128)(2,1)S(1)}, u32[]{:S(2)}, u32[]{:S(2)}) collective-permute-start(bf16[512,1,1,32]{0,3,2,1:T(8,128)(2,1)S(1)} %get-tuple-element.24), channel_id=1, source_target_pairs={{0,76},{1,441},{2,78},{3,443},{4,72},{5,445},{6,74},{7,447},{8,84}... | collective-permute-start | bytes 98312 | tf_op jit(solution)/shard_map/ppermute | solution.py:26
  49.8 0.1 pad.11.clone
  49.9 0.0 collective-permute-done.2
  49.9 0.1 copy.83
  50.0 0.1 copy.54
  50.2 0.0 collective-permute-done.3
  50.2 1.9 %collective-permute-start.4 = (bf16[512,320]{0,1:T(8,128)(2,1)S(1)}, bf16[512,320]{0,1:T(8,128)(2,1)S(1)}, u32[]{:S(2)}, u32[]{:S(2)}) collective-permute-start(bf16[512,320]{0,1:T(8,128)(2,1)S(1)} %pad_maximum_fusion), channel_id=1, source_target_pairs={{0,1},{1,0},{2,3},{3,2},{4,5},{5,4},{6,7},{7,6},{8,9},{9,8},{10,11... | collective-permute-start | bytes 983048 | tf_op jit(solution)/shard_map/ppermute | solution.py:74
  52.2 0.9 %convolution_select_fusion.2 = f32[1,8,8,5,64]{4,2,3,1,0:T(8,128)S(1)} fusion(bf16[3,3,3,64,512]{4,3,2,1,0:T(8,128)(2,1)S(1)} %copy-done.1, s32[]{:T(128)S(6)} %select_n.123, bf16[512,1,8,1,7,2]{0,4,5,2,3,1:T(8,128)(2,1)S(1)} %slice.74, bf16[512,1,8,1,8,5]{0,4,5,2,3,1:T(8,128)(2,1)S(1)} %copy.54, pred[8,5]{0,1:T(8,128)(4,1)S(1)} %copy-done.2), kind=kOutput, calls=%fused_computation.4 | convolution fusion | flops 174411776 | bytes 1131524 | tf_op jit(solution)/shard_map/conv_general_dilated | solution.py:37
  53.1 0.6 %collective-permute-done.4 = bf16[512,320]{0,1:T(8,128)(2,1)S(1)} collective-permute-done((bf16[512,320]{0,1:T(8,128)(2,1)S(1)}, bf16[512,320]{0,1:T(8,128)(2,1)S(1)}, u32[]{:S(2)}, u32[]{:S(2)}) %collective-permute-start.4) | collective-permute-done | bytes 327712 | tf_op jit(solution)/shard_map/ppermute | solution.py:74
  53.8 0.2 copy.84
  54.0 0.1 copy.59
  54.1 0.9 %convolution_select_fusion.1 = f32[1,8,8,5,64]{4,2,3,1,0:T(8,128)S(1)} fusion(bf16[3,3,3,64,512]{4,3,2,1,0:T(8,128)(2,1)S(1)} %copy-done.1, s32[]{:T(128)S(6)} %select_n.126, bf16[512,1,8,1,7,2]{0,4,5,2,3,1:T(8,128)(2,1)S(1)} %slice.79, bf16[512,1,8,1,8,5]{0,4,5,2,3,1:T(8,128)(2,1)S(1)} %copy.59, pred[8,5]{0,1:T(8,128)(4,1)S(1)} %copy-done.2), kind=kOutput, calls=%fused_computation.3 | convolution fusion | flops 174411776 | bytes 1131524 | tf_op jit(solution)/shard_map/conv_general_dilated | solution.py:37
  55.1 0.0 collective-permute-done.1
  55.1 0.0 collective-permute-done
  55.2 2.1 %collective-permute-start.5 = (bf16[512,64]{0,1:T(8,128)(2,1)S(1)}, bf16[512,64]{0,1:T(8,128)(2,1)S(1)}, u32[]{:S(2)}, u32[]{:S(2)}) collective-permute-start(bf16[512,64]{0,1:T(8,128)(2,1)S(1)} %pad_maximum_fusion.1), channel_id=1, source_target_pairs={{0,1},{1,0},{2,3},{3,2},{4,5},{5,4},{6,7},{7,6},{8,9},{9,8},{10,11... | collective-permute-start | bytes 196616 | tf_op jit(solution)/shard_map/ppermute | solution.py:84
  57.2 1.1 %collective-permute-done.5 = bf16[512,64]{0,1:T(8,128)(2,1)S(1)} collective-permute-done((bf16[512,64]{0,1:T(8,128)(2,1)S(1)}, bf16[512,64]{0,1:T(8,128)(2,1)S(1)}, u32[]{:S(2)}, u32[]{:S(2)}) %collective-permute-start.5) | collective-permute-done | bytes 65568 | tf_op jit(solution)/shard_map/ppermute | solution.py:84
  58.4 0.1 copy.85
  58.5 0.1 pad.6.clone
  58.6 0.3 convolution_select_fusion.4
  59.0 0.0 copy-start
  59.0 0.1 copy.86
  59.1 0.1 pad.8.clone
  59.3 0.3 convolution_select_fusion.3
  59.7 0.0 copy-done
  59.7 0.2 multiply_maximum_fusion
  59.9 0.1 copy.78
  59.9 0.8 %copy.79 = f32[1,2,64,256]{3,2,1,0:T(8,128)} copy(f32[1,2,64,256]{2,3,1,0:T(8,128)S(1)} %bitcast.116) | data formatting | bytes 262144 | tf_op jit(solution)/shard_map/reshape | solution.py:110
  (32 shorter events, 0.6 us)
Async XLA Ops:
  23.5 26.7 %collective-permute-start.3 = (bf16[512,2,1,32]{0,3,2,1:T(8,128)(2,1)S(1)}, bf16[512,2,1,32]{0,3,2,1:T(8,128)(2,1)S(1)}, u32[]{:S(2)}, u32[]{:S(2)}) collective-permute-start(bf16[512,2,1,32]{0,3,2,1:T(8,128)(2,1)S(1)} %slice_select_fusion.1), channel_id=1, source_target_pairs={{0,8},{1,509},{2,10},{3,511},{4,12},{5,505},{6,14},{7,507},{8,16},... | collective-permute-start | bytes 196616 | tf_op jit(solution)/shard_map/ppermute | solution.py:26
  34.4 15.4 %collective-permute-start.2 = (bf16[512,1,8,32]{0,3,2,1:T(8,128)(2,1)S(1)}, bf16[512,1,8,32]{0,3,2,1:T(8,128)(2,1)S(1)}, u32[]{:S(2)}, u32[]{:S(2)}) collective-permute-start(bf16[512,1,8,32]{0,3,2,1:T(8,128)(2,1)S(1)} %slice_select_fusion), channel_id=1, source_target_pairs={{0,68},{1,453},{2,70},{3,455},{4,64},{5,449},{6,66},{7,451},{8,76}... | collective-permute-start | bytes 786440 | tf_op jit(solution)/shard_map/ppermute | solution.py:26
  36.6 1.5 %copy-start.1 = (bf16[3,3,3,64,512]{4,3,2,1,0:T(8,128)(2,1)S(1)}, bf16[3,3,3,64,512]{4,3,2,1,0:T(8,128)(2,1)}, u32[]{:S(2)}) copy-start(bf16[3,3,3,64,512]{4,3,2,1,0:T(8,128)(2,1)} %param.4) | copy-start | bytes 5308420
  36.7 1.5 %copy-start.2 = (pred[8,5]{0,1:T(8,128)(4,1)S(1)}, pred[8,5]{0,1:T(8,128)(4,1)}, u32[]{:S(2)}) copy-start(pred[8,5]{0,1:T(8,128)(4,1)} %constant.75) | copy-start | bytes 124
  43.0 12.2 %collective-permute-start.1 = (bf16[512,1,1,32]{0,3,2,1:T(8,128)(2,1)S(1)}, bf16[512,1,1,32]{0,3,2,1:T(8,128)(2,1)S(1)}, u32[]{:S(2)}, u32[]{:S(2)}) collective-permute-start(bf16[512,1,1,32]{0,3,2,1:T(8,128)(2,1)S(1)} %get-tuple-element.23), channel_id=1, source_target_pairs={{0,56},{1,461},{2,58},{3,463},{4,60},{5,457},{6,62},{7,459},{8,68}... | collective-permute-start | bytes 98312 | tf_op jit(solution)/shard_map/ppermute | solution.py:26
  44.9 10.2 %collective-permute-start = (bf16[512,1,1,32]{0,3,2,1:T(8,128)(2,1)S(1)}, bf16[512,1,1,32]{0,3,2,1:T(8,128)(2,1)S(1)}, u32[]{:S(2)}, u32[]{:S(2)}) collective-permute-start(bf16[512,1,1,32]{0,3,2,1:T(8,128)(2,1)S(1)} %get-tuple-element.24), channel_id=1, source_target_pairs={{0,76},{1,441},{2,78},{3,443},{4,72},{5,445},{6,74},{7,447},{8,84}... | collective-permute-start | bytes 98312 | tf_op jit(solution)/shard_map/ppermute | solution.py:26
  50.2 3.5 %collective-permute-start.4 = (bf16[512,320]{0,1:T(8,128)(2,1)S(1)}, bf16[512,320]{0,1:T(8,128)(2,1)S(1)}, u32[]{:S(2)}, u32[]{:S(2)}) collective-permute-start(bf16[512,320]{0,1:T(8,128)(2,1)S(1)} %pad_maximum_fusion), channel_id=1, source_target_pairs={{0,1},{1,0},{2,3},{3,2},{4,5},{5,4},{6,7},{7,6},{8,9},{9,8},{10,11... | collective-permute-start | bytes 983048 | tf_op jit(solution)/shard_map/ppermute | solution.py:74
  55.2 3.1 %collective-permute-start.5 = (bf16[512,64]{0,1:T(8,128)(2,1)S(1)}, bf16[512,64]{0,1:T(8,128)(2,1)S(1)}, u32[]{:S(2)}, u32[]{:S(2)}) collective-permute-start(bf16[512,64]{0,1:T(8,128)(2,1)S(1)} %pad_maximum_fusion.1), channel_id=1, source_target_pairs={{0,1},{1,0},{2,3},{3,2},{4,5},{5,4},{6,7},{7,6},{8,9},{9,8},{10,11... | collective-permute-start | bytes 196616 | tf_op jit(solution)/shard_map/ppermute | solution.py:84
  59.0 0.7 %copy-start = (f32[64]{0:T(128)S(1)}, f32[64]{0:T(128)}, u32[]{:S(2)}) copy-start(f32[64]{0:T(128)} %param.5) | copy-start | bytes 772

commit v23 on v22

--- a/solution.py
+++ b/solution.py
@@ -9,7 +9,7 @@
 negative_slope = 0.3
 
 
-def cross(lower_source, upper_source, axis, steps):
+def cross(lower_source, upper_source, axis, steps, route=True):
     count = lax.axis_size(axis)
     width = lax.axis_size("chan")
     run_y = width // 2
@@ -19,7 +19,7 @@
             place, core = divmod(lane, 2)
             target = (source + (steps if core == 0 else -steps)) % count
             crosses = (source // CY) % 2 != (target // CY) % 2
-            moved = ((place + run_y // 2) % run_y) * 2 + core if crosses else lane
+            moved = ((place + run_y // 2) % run_y) * 2 + core if crosses and route else lane
             pairs.append((source * width + lane, target * width + moved))
     on_first = lax.axis_index("chan") % 2 == 0
     sent = jnp.where(on_first, lower_source, upper_source)
@@ -59,8 +59,8 @@
     ]
     corners_from, own_part = lax.optimization_barrier((gathered[:, ::size_x - 1, ::size_y - 1], own_part))
     got += [
-        cross(corners_from[:, 1:, 1:], corners_from[:, :1, :1], "space", CY + 1),
-        cross(corners_from[:, 1:, :1], corners_from[:, :1, 1:], "space", CY - 1),
+        cross(corners_from[:, 1:, 1:], corners_from[:, :1, :1], "space", CY + 1, route=False),
+        cross(corners_from[:, 1:, :1], corners_from[:, :1, 1:], "space", CY - 1, route=False),
     ]
     parity = lax.axis_index("chan") % 2
     on_first = parity == 0

time: 61 us -> 61.9 us (1.015); the launches traced: 60.7 us -> 60.7 us
  no operation moved by 1% of the time
where the time goes in v23:
time: 61.9 us; the launch traced here: 60.7 us
  starting transfers between devices  23.5 us (38%)
  blocking collectives  21.7 us (35%)
  matrix products  7.21 us (12%)
  local copies, waits for them, and re-layouts  4.76 us (8%)
  waiting for transfers between devices  1.69 us (3%)
  other arithmetic  1.23 us (2%)
    all_gather x1, blocking collectives, body(): gathered = lax.all_gather(own_block, 'chan', axis=0, tiled=True)  21.7 us
    ppermute x4, starting transfers between devices, cross(): return lax.ppermute(sent, (axis, 'chan'), pairs)  19.6 us
    conv_general_dilated x5, matrix products, conv(): lax.conv_general_dilated(field[None], taps, window_strides=(1, 1, 1), pad...  7.21 us
    ppermute x1, starting transfers between devices, body(): late_other = lax.ppermute(late, 'chan', pairs_core)  2.06 us
    unnamed x14, local copies, waits for them, and re-layouts  2.03 us
    ppermute x1, starting transfers between devices, body(): early_other = lax.ppermute(early, 'chan', pairs_core)  1.92 us
  transfers between devices with their start and end apart: 6, of which 2 were waited for; matrix products, arithmetic and copies ran while one was open for 13% of the time, Pallas kernels for 0%

profile of v23, /device:TPU:1, one launch (start us, length us, event | category | flops | bytes accessed | tf_op | source)
XLA Modules:
  0.0 60.7 jit_solution(12129858713135847383)
XLA Ops:
  0.0 0.9 %convert_element_type.8 = bf16[1,2,64,256]{3,2,1,0:T(8,128)(2,1)S(1)} convert(f32[1,2,64,256]{3,2,1,0:T(8,128)} %param.3) | non-fusion elementwise | flops 32768 | bytes 196608 | tf_op jit(solution)/shard_map/convert_element_type | solution.py:51
  0.9 0.1 copy.89
  1.0 21.7 %all_gather.3 = bf16[512,2,256]{2,1,0:T(2,128)(2,1)S(1)} all-gather(bf16[64,2,256]{2,1,0:T(2,128)(2,1)S(1)} %bitcast.122), channel_id=1, replica_groups=mesh['space'=64,'chan'=8] {'chan'}, dimensions={0}, use_global_device_ids=true | all-gather | bytes 589824 | tf_op jit(solution)/shard_map/all_gather | solution.py:52
  22.7 0.7 %copy.46 = bf16[512,2,256]{0,2,1:T(8,128)(2,1)S(1)} copy(bf16[512,2,256]{2,1,0:T(2,128)(2,1)S(1)} %all_gather.3) | data formatting | bytes 1048576 | tf_op jit(solution)/shard_map/all_gather | solution.py:52
  23.5 10.9 %collective-permute-start.3 = (bf16[512,2,1,32]{0,3,2,1:T(8,128)(2,1)S(1)}, bf16[512,2,1,32]{0,3,2,1:T(8,128)(2,1)S(1)}, u32[]{:S(2)}, u32[]{:S(2)}) collective-permute-start(bf16[512,2,1,32]{0,3,2,1:T(8,128)(2,1)S(1)} %slice_select_fusion.1), channel_id=1, source_target_pairs={{0,8},{1,509},{2,10},{3,511},{4,12},{5,505},{6,14},{7,507},{8,16},... | collective-permute-start | bytes 196616 | tf_op jit(solution)/shard_map/ppermute | solution.py:26
  34.4 1.9 %collective-permute-start.2 = (bf16[512,1,8,32]{0,3,2,1:T(8,128)(2,1)S(1)}, bf16[512,1,8,32]{0,3,2,1:T(8,128)(2,1)S(1)}, u32[]{:S(2)}, u32[]{:S(2)}) collective-permute-start(bf16[512,1,8,32]{0,3,2,1:T(8,128)(2,1)S(1)} %slice_select_fusion), channel_id=1, source_target_pairs={{0,68},{1,453},{2,70},{3,455},{4,64},{5,449},{6,66},{7,451},{8,76}... | collective-permute-start | bytes 786440 | tf_op jit(solution)/shard_map/ppermute | solution.py:26
  36.3 0.3 copy.82
  36.6 0.0 copy-start.1
  36.7 0.0 copy-start.2
  36.7 0.2 copy.50
  36.9 0.1 slice.70
  37.0 1.1 %copy-done.1 = bf16[3,3,3,64,512]{4,3,2,1,0:T(8,128)(2,1)S(1)} copy-done((bf16[3,3,3,64,512]{4,3,2,1,0:T(8,128)(2,1)S(1)}, bf16[3,3,3,64,512]{4,3,2,1,0:T(8,128)(2,1)}, u32[]{:S(2)}) %copy-start.1) | copy-done | bytes 1769496
  38.1 0.0 copy-done.2
  38.1 4.7 %convolution_select_fusion = f32[2,8,8,5,64]{4,2,3,1,0:T(8,128)S(1)} fusion(bf16[3,3,3,64,512]{4,3,2,1,0:T(8,128)(2,1)S(1)} %copy-done.1, bf16[512,2,8,1,7,2]{0,4,5,2,1,3:T(8,128)(2,1)S(1)} %slice.70, bf16[512,2,8,1,8,5]{0,4,5,2,1,3:T(8,128)(2,1)S(1)} %copy.50, pred[8,5]{0,1:T(8,128)(4,1)S(1)} %copy-done.2), kind=kOutput, calls=%fused_computation.2 | convolution fusion | flops 694853632 | bytes 2818088 | tf_op jit(solution)/shard_map/conv_general_dilated | solution.py:37
  42.8 0.1 copy.51
  43.0 1.9 %collective-permute-start.1 = (bf16[512,1,1,32]{0,3,2,1:T(8,128)(2,1)S(1)}, bf16[512,1,1,32]{0,3,2,1:T(8,128)(2,1)S(1)}, u32[]{:S(2)}, u32[]{:S(2)}) collective-permute-start(bf16[512,1,1,32]{0,3,2,1:T(8,128)(2,1)S(1)} %get-tuple-element.23), channel_id=1, source_target_pairs={{0,56},{1,457},{2,58},{3,459},{4,60},{5,461},{6,62},{7,463},{8,64}... | collective-permute-start | bytes 98312 | tf_op jit(solution)/shard_map/ppermute | solution.py:26
  44.9 4.8 %collective-permute-start = (bf16[512,1,1,32]{0,3,2,1:T(8,128)(2,1)S(1)}, bf16[512,1,1,32]{0,3,2,1:T(8,128)(2,1)S(1)}, u32[]{:S(2)}, u32[]{:S(2)}) collective-permute-start(bf16[512,1,1,32]{0,3,2,1:T(8,128)(2,1)S(1)} %get-tuple-element.24), channel_id=1, source_target_pairs={{0,72},{1,441},{2,74},{3,443},{4,76},{5,445},{6,78},{7,447},{8,80}... | collective-permute-start | bytes 98312 | tf_op jit(solution)/shard_map/ppermute | solution.py:26
  49.8 0.1 pad.11.clone
  49.9 0.0 collective-permute-done.2
  49.9 0.1 copy.83
  50.0 0.1 copy.54
  50.2 0.0 collective-permute-done.3
  50.2 1.9 %collective-permute-start.4 = (bf16[512,320]{0,1:T(8,128)(2,1)S(1)}, bf16[512,320]{0,1:T(8,128)(2,1)S(1)}, u32[]{:S(2)}, u32[]{:S(2)}) collective-permute-start(bf16[512,320]{0,1:T(8,128)(2,1)S(1)} %pad_maximum_fusion), channel_id=1, source_target_pairs={{0,1},{1,0},{2,3},{3,2},{4,5},{5,4},{6,7},{7,6},{8,9},{9,8},{10,11... | collective-permute-start | bytes 983048 | tf_op jit(solution)/shard_map/ppermute | solution.py:74
  52.2 0.9 %convolution_select_fusion.2 = f32[1,8,8,5,64]{4,2,3,1,0:T(8,128)S(1)} fusion(bf16[3,3,3,64,512]{4,3,2,1,0:T(8,128)(2,1)S(1)} %copy-done.1, s32[]{:T(128)S(6)} %select_n.123, bf16[512,1,8,1,7,2]{0,4,5,2,3,1:T(8,128)(2,1)S(1)} %slice.74, bf16[512,1,8,1,8,5]{0,4,5,2,3,1:T(8,128)(2,1)S(1)} %copy.54, pred[8,5]{0,1:T(8,128)(4,1)S(1)} %copy-done.2), kind=kOutput, calls=%fused_computation.4 | convolution fusion | flops 174411776 | bytes 1131524 | tf_op jit(solution)/shard_map/conv_general_dilated | solution.py:37
  53.1 0.6 %collective-permute-done.4 = bf16[512,320]{0,1:T(8,128)(2,1)S(1)} collective-permute-done((bf16[512,320]{0,1:T(8,128)(2,1)S(1)}, bf16[512,320]{0,1:T(8,128)(2,1)S(1)}, u32[]{:S(2)}, u32[]{:S(2)}) %collective-permute-start.4) | collective-permute-done | bytes 327712 | tf_op jit(solution)/shard_map/ppermute | solution.py:74
  53.8 0.2 copy.84
  54.0 0.1 copy.59
  54.1 0.9 %convolution_select_fusion.1 = f32[1,8,8,5,64]{4,2,3,1,0:T(8,128)S(1)} fusion(bf16[3,3,3,64,512]{4,3,2,1,0:T(8,128)(2,1)S(1)} %copy-done.1, s32[]{:T(128)S(6)} %select_n.126, bf16[512,1,8,1,7,2]{0,4,5,2,3,1:T(8,128)(2,1)S(1)} %slice.79, bf16[512,1,8,1,8,5]{0,4,5,2,3,1:T(8,128)(2,1)S(1)} %copy.59, pred[8,5]{0,1:T(8,128)(4,1)S(1)} %copy-done.2), kind=kOutput, calls=%fused_computation.3 | convolution fusion | flops 174411776 | bytes 1131524 | tf_op jit(solution)/shard_map/conv_general_dilated | solution.py:37
  55.1 0.0 collective-permute-done.1
  55.1 0.0 collective-permute-done
  55.2 2.1 %collective-permute-start.5 = (bf16[512,64]{0,1:T(8,128)(2,1)S(1)}, bf16[512,64]{0,1:T(8,128)(2,1)S(1)}, u32[]{:S(2)}, u32[]{:S(2)}) collective-permute-start(bf16[512,64]{0,1:T(8,128)(2,1)S(1)} %pad_maximum_fusion.1), channel_id=1, source_target_pairs={{0,1},{1,0},{2,3},{3,2},{4,5},{5,4},{6,7},{7,6},{8,9},{9,8},{10,11... | collective-permute-start | bytes 196616 | tf_op jit(solution)/shard_map/ppermute | solution.py:84
  57.2 1.1 %collective-permute-done.5 = bf16[512,64]{0,1:T(8,128)(2,1)S(1)} collective-permute-done((bf16[512,64]{0,1:T(8,128)(2,1)S(1)}, bf16[512,64]{0,1:T(8,128)(2,1)S(1)}, u32[]{:S(2)}, u32[]{:S(2)}) %collective-permute-start.5) | collective-permute-done | bytes 65568 | tf_op jit(solution)/shard_map/ppermute | solution.py:84
  58.4 0.1 copy.85
  58.5 0.1 pad.6.clone
  58.6 0.3 convolution_select_fusion.4
  59.0 0.0 copy-start
  59.0 0.1 copy.86
  59.1 0.1 pad.8.clone
  59.3 0.3 convolution_select_fusion.3
  59.7 0.0 copy-done
  59.7 0.2 multiply_maximum_fusion
  59.9 0.1 copy.78
  59.9 0.8 %copy.79 = f32[1,2,64,256]{3,2,1,0:T(8,128)} copy(f32[1,2,64,256]{2,3,1,0:T(8,128)S(1)} %bitcast.116) | data formatting | bytes 262144 | tf_op jit(solution)/shard_map/reshape | solution.py:110
  (32 shorter events, 0.6 us)
Async XLA Ops:
  23.5 26.7 %collective-permute-start.3 = (bf16[512,2,1,32]{0,3,2,1:T(8,128)(2,1)S(1)}, bf16[512,2,1,32]{0,3,2,1:T(8,128)(2,1)S(1)}, u32[]{:S(2)}, u32[]{:S(2)}) collective-permute-start(bf16[512,2,1,32]{0,3,2,1:T(8,128)(2,1)S(1)} %slice_select_fusion.1), channel_id=1, source_target_pairs={{0,8},{1,509},{2,10},{3,511},{4,12},{5,505},{6,14},{7,507},{8,16},... | collective-permute-start | bytes 196616 | tf_op jit(solution)/shard_map/ppermute | solution.py:26
  34.4 15.4 %collective-permute-start.2 = (bf16[512,1,8,32]{0,3,2,1:T(8,128)(2,1)S(1)}, bf16[512,1,8,32]{0,3,2,1:T(8,128)(2,1)S(1)}, u32[]{:S(2)}, u32[]{:S(2)}) collective-permute-start(bf16[512,1,8,32]{0,3,2,1:T(8,128)(2,1)S(1)} %slice_select_fusion), channel_id=1, source_target_pairs={{0,68},{1,453},{2,70},{3,455},{4,64},{5,449},{6,66},{7,451},{8,76}... | collective-permute-start | bytes 786440 | tf_op jit(solution)/shard_map/ppermute | solution.py:26
  36.6 1.5 %copy-start.1 = (bf16[3,3,3,64,512]{4,3,2,1,0:T(8,128)(2,1)S(1)}, bf16[3,3,3,64,512]{4,3,2,1,0:T(8,128)(2,1)}, u32[]{:S(2)}) copy-start(bf16[3,3,3,64,512]{4,3,2,1,0:T(8,128)(2,1)} %param.4) | copy-start | bytes 5308420
  36.7 1.5 %copy-start.2 = (pred[8,5]{0,1:T(8,128)(4,1)S(1)}, pred[8,5]{0,1:T(8,128)(4,1)}, u32[]{:S(2)}) copy-start(pred[8,5]{0,1:T(8,128)(4,1)} %constant.75) | copy-start | bytes 124
  43.0 12.2 %collective-permute-start.1 = (bf16[512,1,1,32]{0,3,2,1:T(8,128)(2,1)S(1)}, bf16[512,1,1,32]{0,3,2,1:T(8,128)(2,1)S(1)}, u32[]{:S(2)}, u32[]{:S(2)}) collective-permute-start(bf16[512,1,1,32]{0,3,2,1:T(8,128)(2,1)S(1)} %get-tuple-element.23), channel_id=1, source_target_pairs={{0,56},{1,457},{2,58},{3,459},{4,60},{5,461},{6,62},{7,463},{8,64}... | collective-permute-start | bytes 98312 | tf_op jit(solution)/shard_map/ppermute | solution.py:26
  44.9 10.2 %collective-permute-start = (bf16[512,1,1,32]{0,3,2,1:T(8,128)(2,1)S(1)}, bf16[512,1,1,32]{0,3,2,1:T(8,128)(2,1)S(1)}, u32[]{:S(2)}, u32[]{:S(2)}) collective-permute-start(bf16[512,1,1,32]{0,3,2,1:T(8,128)(2,1)S(1)} %get-tuple-element.24), channel_id=1, source_target_pairs={{0,72},{1,441},{2,74},{3,443},{4,76},{5,445},{6,78},{7,447},{8,80}... | collective-permute-start | bytes 98312 | tf_op jit(solution)/shard_map/ppermute | solution.py:26
  50.2 3.5 %collective-permute-start.4 = (bf16[512,320]{0,1:T(8,128)(2,1)S(1)}, bf16[512,320]{0,1:T(8,128)(2,1)S(1)}, u32[]{:S(2)}, u32[]{:S(2)}) collective-permute-start(bf16[512,320]{0,1:T(8,128)(2,1)S(1)} %pad_maximum_fusion), channel_id=1, source_target_pairs={{0,1},{1,0},{2,3},{3,2},{4,5},{5,4},{6,7},{7,6},{8,9},{9,8},{10,11... | collective-permute-start | bytes 983048 | tf_op jit(solution)/shard_map/ppermute | solution.py:74
  55.2 3.1 %collective-permute-start.5 = (bf16[512,64]{0,1:T(8,128)(2,1)S(1)}, bf16[512,64]{0,1:T(8,128)(2,1)S(1)}, u32[]{:S(2)}, u32[]{:S(2)}) collective-permute-start(bf16[512,64]{0,1:T(8,128)(2,1)S(1)} %pad_maximum_fusion.1), channel_id=1, source_target_pairs={{0,1},{1,0},{2,3},{3,2},{4,5},{5,4},{6,7},{7,6},{8,9},{9,8},{10,11... | collective-permute-start | bytes 196616 | tf_op jit(solution)/shard_map/ppermute | solution.py:84
  59.0 0.7 %copy-start = (f32[64]{0:T(128)S(1)}, f32[64]{0:T(128)}, u32[]{:S(2)}) copy-start(f32[64]{0:T(128)} %param.5) | copy-start | bytes 772

commit v24 on v22

--- a/solution.py
+++ b/solution.py
@@ -9,7 +9,7 @@
 negative_slope = 0.3
 
 
-def cross(lower_source, upper_source, axis, steps):
+def cross(lower_source, upper_source, axis, steps, shift=None):
     count = lax.axis_size(axis)
     width = lax.axis_size("chan")
     run_y = width // 2
@@ -19,7 +19,8 @@
             place, core = divmod(lane, 2)
             target = (source + (steps if core == 0 else -steps)) % count
             crosses = (source // CY) % 2 != (target // CY) % 2
-            moved = ((place + run_y // 2) % run_y) * 2 + core if crosses else lane
+            step_y = run_y // 2 if shift is None else shift
+            moved = ((place + step_y) % run_y) * 2 + core if crosses else lane
             pairs.append((source * width + lane, target * width + moved))
     on_first = lax.axis_index("chan") % 2 == 0
     sent = jnp.where(on_first, lower_source, upper_source)
@@ -55,7 +56,7 @@
     width_in = gathered.shape[0]
     got = [
         cross(gathered[:, -1:], gathered[:, :1], "space", CY),
-        cross(gathered[:, :, -1:], gathered[:, :, :1], "space", 1),
+        cross(gathered[:, :, -1:], gathered[:, :, :1], "space", 1, shift=1),
     ]
     corners_from, own_part = lax.optimization_barrier((gathered[:, ::size_x - 1, ::size_y - 1], own_part))
     got += [

time: 61 us -> 62.9 us (1.031)
  starting transfers between devices: 23.5 us -> 25.4 us
    ppermute x4, starting transfers between devices: 19.6 us -> 21.5 us  [cross(): return lax.ppermute(sent, (axis, 'chan'), pairs)]
where the time goes in v24:
time: 62.9 us; the launch traced here: 62.6 us
  starting transfers between devices  25.4 us (40%)
  blocking collectives  21.7 us (34%)
  matrix products  7.24 us (12%)
  local copies, waits for them, and re-layouts  4.76 us (8%)
  waiting for transfers between devices  1.69 us (3%)
  other arithmetic  1.23 us (2%)
    all_gather x1, blocking collectives, body(): gathered = lax.all_gather(own_block, 'chan', axis=0, tiled=True)  21.7 us
    ppermute x4, starting transfers between devices, cross(): return lax.ppermute(sent, (axis, 'chan'), pairs)  21.5 us
    conv_general_dilated x5, matrix products, conv(): lax.conv_general_dilated(field[None], taps, window_strides=(1, 1, 1), pad...  7.24 us
    ppermute x1, starting transfers between devices, body(): late_other = lax.ppermute(late, 'chan', pairs_core)  2.04 us
    unnamed x14, local copies, waits for them, and re-layouts  2.03 us
    ppermute x1, starting transfers between devices, body(): early_other = lax.ppermute(early, 'chan', pairs_core)  1.92 us
  transfers between devices with their start and end apart: 6, of which 2 were waited for; matrix products, arithmetic and copies ran while one was open for 13% of the time, Pallas kernels for 0%

profile of v24, /device:TPU:1, one launch (start us, length us, event | category | flops | bytes accessed | tf_op | source)
XLA Modules:
  0.0 62.6 jit_solution(1795000377157166111)
XLA Ops:
  0.0 0.9 %convert_element_type.8 = bf16[1,2,64,256]{3,2,1,0:T(8,128)(2,1)S(1)} convert(f32[1,2,64,256]{3,2,1,0:T(8,128)} %param.3) | non-fusion elementwise | flops 32768 | bytes 196608 | tf_op jit(solution)/shard_map/convert_element_type | solution.py:52
  0.9 0.1 copy.89
  1.0 21.7 %all_gather.3 = bf16[512,2,256]{2,1,0:T(2,128)(2,1)S(1)} all-gather(bf16[64,2,256]{2,1,0:T(2,128)(2,1)S(1)} %bitcast.122), channel_id=1, replica_groups=mesh['space'=64,'chan'=8] {'chan'}, dimensions={0}, use_global_device_ids=true | all-gather | bytes 589824 | tf_op jit(solution)/shard_map/all_gather | solution.py:53
  22.7 0.7 %copy.46 = bf16[512,2,256]{0,2,1:T(8,128)(2,1)S(1)} copy(bf16[512,2,256]{2,1,0:T(2,128)(2,1)S(1)} %all_gather.3) | data formatting | bytes 1048576 | tf_op jit(solution)/shard_map/all_gather | solution.py:53
  23.5 10.1 %collective-permute-start.3 = (bf16[512,2,1,32]{0,3,2,1:T(8,128)(2,1)S(1)}, bf16[512,2,1,32]{0,3,2,1:T(8,128)(2,1)S(1)}, u32[]{:S(2)}, u32[]{:S(2)}) collective-permute-start(bf16[512,2,1,32]{0,3,2,1:T(8,128)(2,1)S(1)} %slice_select_fusion.1), channel_id=1, source_target_pairs={{0,8},{1,507},{2,10},{3,509},{4,12},{5,511},{6,14},{7,505},{8,16},... | collective-permute-start | bytes 196616 | tf_op jit(solution)/shard_map/ppermute | solution.py:27
  33.6 4.6 %collective-permute-start.2 = (bf16[512,1,8,32]{0,3,2,1:T(8,128)(2,1)S(1)}, bf16[512,1,8,32]{0,3,2,1:T(8,128)(2,1)S(1)}, u32[]{:S(2)}, u32[]{:S(2)}) collective-permute-start(bf16[512,1,8,32]{0,3,2,1:T(8,128)(2,1)S(1)} %slice_select_fusion), channel_id=1, source_target_pairs={{0,68},{1,453},{2,70},{3,455},{4,64},{5,449},{6,66},{7,451},{8,76}... | collective-permute-start | bytes 786440 | tf_op jit(solution)/shard_map/ppermute | solution.py:27
  38.2 0.3 copy.82
  38.5 0.0 copy-start.1
  38.6 0.0 copy-start.2
  38.6 0.2 copy.50
  38.8 0.1 slice.70
  38.9 1.1 %copy-done.1 = bf16[3,3,3,64,512]{4,3,2,1,0:T(8,128)(2,1)S(1)} copy-done((bf16[3,3,3,64,512]{4,3,2,1,0:T(8,128)(2,1)S(1)}, bf16[3,3,3,64,512]{4,3,2,1,0:T(8,128)(2,1)}, u32[]{:S(2)}) %copy-start.1) | copy-done | bytes 1769496
  40.0 0.0 copy-done.2
  40.0 4.7 %convolution_select_fusion = f32[2,8,8,5,64]{4,2,3,1,0:T(8,128)S(1)} fusion(bf16[3,3,3,64,512]{4,3,2,1,0:T(8,128)(2,1)S(1)} %copy-done.1, bf16[512,2,8,1,7,2]{0,4,5,2,1,3:T(8,128)(2,1)S(1)} %slice.70, bf16[512,2,8,1,8,5]{0,4,5,2,1,3:T(8,128)(2,1)S(1)} %copy.50, pred[8,5]{0,1:T(8,128)(4,1)S(1)} %copy-done.2), kind=kOutput, calls=%fused_computation.2 | convolution fusion | flops 694853632 | bytes 2818088 | tf_op jit(solution)/shard_map/conv_general_dilated | solution.py:38
  44.7 0.1 copy.51
  44.9 1.9 %collective-permute-start.1 = (bf16[512,1,1,32]{0,3,2,1:T(8,128)(2,1)S(1)}, bf16[512,1,1,32]{0,3,2,1:T(8,128)(2,1)S(1)}, u32[]{:S(2)}, u32[]{:S(2)}) collective-permute-start(bf16[512,1,1,32]{0,3,2,1:T(8,128)(2,1)S(1)} %get-tuple-element.23), channel_id=1, source_target_pairs={{0,56},{1,461},{2,58},{3,463},{4,60},{5,457},{6,62},{7,459},{8,68}... | collective-permute-start | bytes 98312 | tf_op jit(solution)/shard_map/ppermute | solution.py:27
  46.8 4.8 %collective-permute-start = (bf16[512,1,1,32]{0,3,2,1:T(8,128)(2,1)S(1)}, bf16[512,1,1,32]{0,3,2,1:T(8,128)(2,1)S(1)}, u32[]{:S(2)}, u32[]{:S(2)}) collective-permute-start(bf16[512,1,1,32]{0,3,2,1:T(8,128)(2,1)S(1)} %get-tuple-element.24), channel_id=1, source_target_pairs={{0,76},{1,441},{2,78},{3,443},{4,72},{5,445},{6,74},{7,447},{8,84}... | collective-permute-start | bytes 98312 | tf_op jit(solution)/shard_map/ppermute | solution.py:27
  51.7 0.1 pad.11.clone
  51.8 0.0 collective-permute-done.2
  51.8 0.1 copy.83
  51.9 0.1 copy.54
  52.1 0.0 collective-permute-done.3
  52.1 1.9 %collective-permute-start.4 = (bf16[512,320]{0,1:T(8,128)(2,1)S(1)}, bf16[512,320]{0,1:T(8,128)(2,1)S(1)}, u32[]{:S(2)}, u32[]{:S(2)}) collective-permute-start(bf16[512,320]{0,1:T(8,128)(2,1)S(1)} %pad_maximum_fusion), channel_id=1, source_target_pairs={{0,1},{1,0},{2,3},{3,2},{4,5},{5,4},{6,7},{7,6},{8,9},{9,8},{10,11... | collective-permute-start | bytes 983048 | tf_op jit(solution)/shard_map/ppermute | solution.py:75
  54.1 0.9 %convolution_select_fusion.2 = f32[1,8,8,5,64]{4,2,3,1,0:T(8,128)S(1)} fusion(bf16[3,3,3,64,512]{4,3,2,1,0:T(8,128)(2,1)S(1)} %copy-done.1, s32[]{:T(128)S(6)} %select_n.123, bf16[512,1,8,1,7,2]{0,4,5,2,3,1:T(8,128)(2,1)S(1)} %slice.74, bf16[512,1,8,1,8,5]{0,4,5,2,3,1:T(8,128)(2,1)S(1)} %copy.54, pred[8,5]{0,1:T(8,128)(4,1)S(1)} %copy-done.2), kind=kOutput, calls=%fused_computation.4 | convolution fusion | flops 174411776 | bytes 1131524 | tf_op jit(solution)/shard_map/conv_general_dilated | solution.py:38
  55.1 0.6 collective-permute-done.4
  55.7 0.2 copy.84
  55.9 0.1 copy.59
  56.0 0.9 %convolution_select_fusion.1 = f32[1,8,8,5,64]{4,2,3,1,0:T(8,128)S(1)} fusion(bf16[3,3,3,64,512]{4,3,2,1,0:T(8,128)(2,1)S(1)} %copy-done.1, s32[]{:T(128)S(6)} %select_n.126, bf16[512,1,8,1,7,2]{0,4,5,2,3,1:T(8,128)(2,1)S(1)} %slice.79, bf16[512,1,8,1,8,5]{0,4,5,2,3,1:T(8,128)(2,1)S(1)} %copy.59, pred[8,5]{0,1:T(8,128)(4,1)S(1)} %copy-done.2), kind=kOutput, calls=%fused_computation.3 | convolution fusion | flops 174411776 | bytes 1131524 | tf_op jit(solution)/shard_map/conv_general_dilated | solution.py:38
  57.0 0.0 collective-permute-done.1
  57.0 0.0 collective-permute-done
  57.1 2.0 %collective-permute-start.5 = (bf16[512,64]{0,1:T(8,128)(2,1)S(1)}, bf16[512,64]{0,1:T(8,128)(2,1)S(1)}, u32[]{:S(2)}, u32[]{:S(2)}) collective-permute-start(bf16[512,64]{0,1:T(8,128)(2,1)S(1)} %pad_maximum_fusion.1), channel_id=1, source_target_pairs={{0,1},{1,0},{2,3},{3,2},{4,5},{5,4},{6,7},{7,6},{8,9},{9,8},{10,11... | collective-permute-start | bytes 196616 | tf_op jit(solution)/shard_map/ppermute | solution.py:85
  59.1 1.1 %collective-permute-done.5 = bf16[512,64]{0,1:T(8,128)(2,1)S(1)} collective-permute-done((bf16[512,64]{0,1:T(8,128)(2,1)S(1)}, bf16[512,64]{0,1:T(8,128)(2,1)S(1)}, u32[]{:S(2)}, u32[]{:S(2)}) %collective-permute-start.5) | collective-permute-done | bytes 65568 | tf_op jit(solution)/shard_map/ppermute | solution.py:85
  60.3 0.1 copy.85
  60.4 0.1 pad.6.clone
  60.5 0.3 convolution_select_fusion.4
  60.9 0.0 copy-start
  60.9 0.1 copy.86
  61.0 0.1 pad.8.clone
  61.2 0.3 convolution_select_fusion.3
  61.6 0.0 copy-done
  61.6 0.2 multiply_maximum_fusion
  61.8 0.1 copy.78
  61.8 0.8 %copy.79 = f32[1,2,64,256]{3,2,1,0:T(8,128)} copy(f32[1,2,64,256]{2,3,1,0:T(8,128)S(1)} %bitcast.116) | data formatting | bytes 262144 | tf_op jit(solution)/shard_map/reshape | solution.py:111
  (32 shorter events, 0.6 us)
Async XLA Ops:
  23.5 28.6 %collective-permute-start.3 = (bf16[512,2,1,32]{0,3,2,1:T(8,128)(2,1)S(1)}, bf16[512,2,1,32]{0,3,2,1:T(8,128)(2,1)S(1)}, u32[]{:S(2)}, u32[]{:S(2)}) collective-permute-start(bf16[512,2,1,32]{0,3,2,1:T(8,128)(2,1)S(1)} %slice_select_fusion.1), channel_id=1, source_target_pairs={{0,8},{1,507},{2,10},{3,509},{4,12},{5,511},{6,14},{7,505},{8,16},... | collective-permute-start | bytes 196616 | tf_op jit(solution)/shard_map/ppermute | solution.py:27
  33.6 18.1 %collective-permute-start.2 = (bf16[512,1,8,32]{0,3,2,1:T(8,128)(2,1)S(1)}, bf16[512,1,8,32]{0,3,2,1:T(8,128)(2,1)S(1)}, u32[]{:S(2)}, u32[]{:S(2)}) collective-permute-start(bf16[512,1,8,32]{0,3,2,1:T(8,128)(2,1)S(1)} %slice_select_fusion), channel_id=1, source_target_pairs={{0,68},{1,453},{2,70},{3,455},{4,64},{5,449},{6,66},{7,451},{8,76}... | collective-permute-start | bytes 786440 | tf_op jit(solution)/shard_map/ppermute | solution.py:27
  38.5 1.5 %copy-start.1 = (bf16[3,3,3,64,512]{4,3,2,1,0:T(8,128)(2,1)S(1)}, bf16[3,3,3,64,512]{4,3,2,1,0:T(8,128)(2,1)}, u32[]{:S(2)}) copy-start(bf16[3,3,3,64,512]{4,3,2,1,0:T(8,128)(2,1)} %param.4) | copy-start | bytes 5308420
  38.6 1.5 %copy-start.2 = (pred[8,5]{0,1:T(8,128)(4,1)S(1)}, pred[8,5]{0,1:T(8,128)(4,1)}, u32[]{:S(2)}) copy-start(pred[8,5]{0,1:T(8,128)(4,1)} %constant.75) | copy-start | bytes 124
  44.9 12.2 %collective-permute-start.1 = (bf16[512,1,1,32]{0,3,2,1:T(8,128)(2,1)S(1)}, bf16[512,1,1,32]{0,3,2,1:T(8,128)(2,1)S(1)}, u32[]{:S(2)}, u32[]{:S(2)}) collective-permute-start(bf16[512,1,1,32]{0,3,2,1:T(8,128)(2,1)S(1)} %get-tuple-element.23), channel_id=1, source_target_pairs={{0,56},{1,461},{2,58},{3,463},{4,60},{5,457},{6,62},{7,459},{8,68}... | collective-permute-start | bytes 98312 | tf_op jit(solution)/shard_map/ppermute | solution.py:27
  46.8 10.2 %collective-permute-start = (bf16[512,1,1,32]{0,3,2,1:T(8,128)(2,1)S(1)}, bf16[512,1,1,32]{0,3,2,1:T(8,128)(2,1)S(1)}, u32[]{:S(2)}, u32[]{:S(2)}) collective-permute-start(bf16[512,1,1,32]{0,3,2,1:T(8,128)(2,1)S(1)} %get-tuple-element.24), channel_id=1, source_target_pairs={{0,76},{1,441},{2,78},{3,443},{4,72},{5,445},{6,74},{7,447},{8,84}... | collective-permute-start | bytes 98312 | tf_op jit(solution)/shard_map/ppermute | solution.py:27
  52.1 3.5 %collective-permute-start.4 = (bf16[512,320]{0,1:T(8,128)(2,1)S(1)}, bf16[512,320]{0,1:T(8,128)(2,1)S(1)}, u32[]{:S(2)}, u32[]{:S(2)}) collective-permute-start(bf16[512,320]{0,1:T(8,128)(2,1)S(1)} %pad_maximum_fusion), channel_id=1, source_target_pairs={{0,1},{1,0},{2,3},{3,2},{4,5},{5,4},{6,7},{7,6},{8,9},{9,8},{10,11... | collective-permute-start | bytes 983048 | tf_op jit(solution)/shard_map/ppermute | solution.py:75
  57.1 3.1 %collective-permute-start.5 = (bf16[512,64]{0,1:T(8,128)(2,1)S(1)}, bf16[512,64]{0,1:T(8,128)(2,1)S(1)}, u32[]{:S(2)}, u32[]{:S(2)}) collective-permute-start(bf16[512,64]{0,1:T(8,128)(2,1)S(1)} %pad_maximum_fusion.1), channel_id=1, source_target_pairs={{0,1},{1,0},{2,3},{3,2},{4,5},{5,4},{6,7},{7,6},{8,9},{9,8},{10,11... | collective-permute-start | bytes 196616 | tf_op jit(solution)/shard_map/ppermute | solution.py:85
  60.9 0.7 %copy-start = (f32[64]{0:T(128)S(1)}, f32[64]{0:T(128)}, u32[]{:S(2)}) copy-start(f32[64]{0:T(128)} %param.5) | copy-start | bytes 772

commit v25 on v24

--- a/solution.py
+++ b/solution.py
@@ -55,8 +55,8 @@
     own_part = conv(gathered, weight, ((1, 1), (1, 1), (1, 1)))
     width_in = gathered.shape[0]
     got = [
-        cross(gathered[:, -1:], gathered[:, :1], "space", CY),
-        cross(gathered[:, :, -1:], gathered[:, :, :1], "space", 1, shift=1),
+        cross(gathered[:, -1:], gathered[:, :1], "space", CY, shift=3),
+        cross(gathered[:, :, -1:], gathered[:, :, :1], "space", 1),
     ]
     corners_from, own_part = lax.optimization_barrier((gathered[:, ::size_x - 1, ::size_y - 1], own_part))
     got += [

time: 62.9 us -> 61.3 us (0.975)
  starting transfers between devices: 25.4 us -> 23.5 us
    ppermute x4, starting transfers between devices: 21.5 us -> 19.6 us  [cross(): return lax.ppermute(sent, (axis, 'chan'), pairs)]
where the time goes in v25:
time: 61.3 us; the launch traced here: 60.7 us
  starting transfers between devices  23.5 us (38%)
  blocking collectives  21.7 us (35%)
  matrix products  7.23 us (12%)
  local copies, waits for them, and re-layouts  4.76 us (8%)
  waiting for transfers between devices  1.69 us (3%)
  other arithmetic  1.23 us (2%)
    all_gather x1, blocking collectives, body(): gathered = lax.all_gather(own_block, 'chan', axis=0, tiled=True)  21.7 us
    ppermute x4, starting transfers between devices, cross(): return lax.ppermute(sent, (axis, 'chan'), pairs)  19.6 us
    conv_general_dilated x5, matrix products, conv(): lax.conv_general_dilated(field[None], taps, window_strides=(1, 1, 1), pad...  7.23 us
    ppermute x1, starting transfers between devices, body(): late_other = lax.ppermute(late, 'chan', pairs_core)  2.04 us
    unnamed x14, local copies, waits for them, and re-layouts  2.03 us
    ppermute x1, starting transfers between devices, body(): early_other = lax.ppermute(early, 'chan', pairs_core)  1.92 us
  transfers between devices with their start and end apart: 6, of which 2 were waited for; matrix products, arithmetic and copies ran while one was open for 13% of the time, Pallas kernels for 0%

profile of v25, /device:TPU:1, one launch (start us, length us, event | category | flops | bytes accessed | tf_op | source)
XLA Modules:
  0.0 60.7 jit_solution(3638856314638939471)
XLA Ops:
  0.0 0.9 %convert_element_type.8 = bf16[1,2,64,256]{3,2,1,0:T(8,128)(2,1)S(1)} convert(f32[1,2,64,256]{3,2,1,0:T(8,128)} %param.3) | non-fusion elementwise | flops 32768 | bytes 196608 | tf_op jit(solution)/shard_map/convert_element_type | solution.py:52
  0.9 0.1 copy.89
  1.0 21.7 %all_gather.3 = bf16[512,2,256]{2,1,0:T(2,128)(2,1)S(1)} all-gather(bf16[64,2,256]{2,1,0:T(2,128)(2,1)S(1)} %bitcast.122), channel_id=1, replica_groups=mesh['space'=64,'chan'=8] {'chan'}, dimensions={0}, use_global_device_ids=true | all-gather | bytes 589824 | tf_op jit(solution)/shard_map/all_gather | solution.py:53
  22.7 0.7 %copy.46 = bf16[512,2,256]{0,2,1:T(8,128)(2,1)S(1)} copy(bf16[512,2,256]{2,1,0:T(2,128)(2,1)S(1)} %all_gather.3) | data formatting | bytes 1048576 | tf_op jit(solution)/shard_map/all_gather | solution.py:53
  23.5 10.9 %collective-permute-start.3 = (bf16[512,2,1,32]{0,3,2,1:T(8,128)(2,1)S(1)}, bf16[512,2,1,32]{0,3,2,1:T(8,128)(2,1)S(1)}, u32[]{:S(2)}, u32[]{:S(2)}) collective-permute-start(bf16[512,2,1,32]{0,3,2,1:T(8,128)(2,1)S(1)} %slice_select_fusion.1), channel_id=1, source_target_pairs={{0,8},{1,509},{2,10},{3,511},{4,12},{5,505},{6,14},{7,507},{8,16},... | collective-permute-start | bytes 196616 | tf_op jit(solution)/shard_map/ppermute | solution.py:27
  34.4 1.9 %collective-permute-start.2 = (bf16[512,1,8,32]{0,3,2,1:T(8,128)(2,1)S(1)}, bf16[512,1,8,32]{0,3,2,1:T(8,128)(2,1)S(1)}, u32[]{:S(2)}, u32[]{:S(2)}) collective-permute-start(bf16[512,1,8,32]{0,3,2,1:T(8,128)(2,1)S(1)} %slice_select_fusion), channel_id=1, source_target_pairs={{0,70},{1,455},{2,64},{3,449},{4,66},{5,451},{6,68},{7,453},{8,78}... | collective-permute-start | bytes 786440 | tf_op jit(solution)/shard_map/ppermute | solution.py:27
  36.4 0.3 copy.82
  36.7 0.0 copy-start.1
  36.7 0.0 copy-start.2
  36.7 0.2 copy.50
  36.9 0.1 slice.70
  37.0 1.1 %copy-done.1 = bf16[3,3,3,64,512]{4,3,2,1,0:T(8,128)(2,1)S(1)} copy-done((bf16[3,3,3,64,512]{4,3,2,1,0:T(8,128)(2,1)S(1)}, bf16[3,3,3,64,512]{4,3,2,1,0:T(8,128)(2,1)}, u32[]{:S(2)}) %copy-start.1) | copy-done | bytes 1769496
  38.1 0.0 copy-done.2
  38.1 4.7 %convolution_select_fusion = f32[2,8,8,5,64]{4,2,3,1,0:T(8,128)S(1)} fusion(bf16[3,3,3,64,512]{4,3,2,1,0:T(8,128)(2,1)S(1)} %copy-done.1, bf16[512,2,8,1,7,2]{0,4,5,2,1,3:T(8,128)(2,1)S(1)} %slice.70, bf16[512,2,8,1,8,5]{0,4,5,2,1,3:T(8,128)(2,1)S(1)} %copy.50, pred[8,5]{0,1:T(8,128)(4,1)S(1)} %copy-done.2), kind=kOutput, calls=%fused_computation.2 | convolution fusion | flops 694853632 | bytes 2818088 | tf_op jit(solution)/shard_map/conv_general_dilated | solution.py:38
  42.8 0.1 copy.51
  43.0 1.9 %collective-permute-start.1 = (bf16[512,1,1,32]{0,3,2,1:T(8,128)(2,1)S(1)}, bf16[512,1,1,32]{0,3,2,1:T(8,128)(2,1)S(1)}, u32[]{:S(2)}, u32[]{:S(2)}) collective-permute-start(bf16[512,1,1,32]{0,3,2,1:T(8,128)(2,1)S(1)} %get-tuple-element.23), channel_id=1, source_target_pairs={{0,56},{1,461},{2,58},{3,463},{4,60},{5,457},{6,62},{7,459},{8,68}... | collective-permute-start | bytes 98312 | tf_op jit(solution)/shard_map/ppermute | solution.py:27
  44.9 4.8 %collective-permute-start = (bf16[512,1,1,32]{0,3,2,1:T(8,128)(2,1)S(1)}, bf16[512,1,1,32]{0,3,2,1:T(8,128)(2,1)S(1)}, u32[]{:S(2)}, u32[]{:S(2)}) collective-permute-start(bf16[512,1,1,32]{0,3,2,1:T(8,128)(2,1)S(1)} %get-tuple-element.24), channel_id=1, source_target_pairs={{0,76},{1,441},{2,78},{3,443},{4,72},{5,445},{6,74},{7,447},{8,84}... | collective-permute-start | bytes 98312 | tf_op jit(solution)/shard_map/ppermute | solution.py:27
  49.8 0.1 pad.11.clone
  49.9 0.0 collective-permute-done.2
  49.9 0.1 copy.83
  50.1 0.1 copy.54
  50.2 0.0 collective-permute-done.3
  50.3 1.9 %collective-permute-start.4 = (bf16[512,320]{0,1:T(8,128)(2,1)S(1)}, bf16[512,320]{0,1:T(8,128)(2,1)S(1)}, u32[]{:S(2)}, u32[]{:S(2)}) collective-permute-start(bf16[512,320]{0,1:T(8,128)(2,1)S(1)} %pad_maximum_fusion), channel_id=1, source_target_pairs={{0,1},{1,0},{2,3},{3,2},{4,5},{5,4},{6,7},{7,6},{8,9},{9,8},{10,11... | collective-permute-start | bytes 983048 | tf_op jit(solution)/shard_map/ppermute | solution.py:75
  52.2 0.9 %convolution_select_fusion.2 = f32[1,8,8,5,64]{4,2,3,1,0:T(8,128)S(1)} fusion(bf16[3,3,3,64,512]{4,3,2,1,0:T(8,128)(2,1)S(1)} %copy-done.1, s32[]{:T(128)S(6)} %select_n.123, bf16[512,1,8,1,7,2]{0,4,5,2,3,1:T(8,128)(2,1)S(1)} %slice.74, bf16[512,1,8,1,8,5]{0,4,5,2,3,1:T(8,128)(2,1)S(1)} %copy.54, pred[8,5]{0,1:T(8,128)(4,1)S(1)} %copy-done.2), kind=kOutput, calls=%fused_computation.4 | convolution fusion | flops 174411776 | bytes 1131524 | tf_op jit(solution)/shard_map/conv_general_dilated | solution.py:38
  53.2 0.6 collective-permute-done.4
  53.8 0.2 copy.84
  54.0 0.1 copy.59
  54.1 0.9 %convolution_select_fusion.1 = f32[1,8,8,5,64]{4,2,3,1,0:T(8,128)S(1)} fusion(bf16[3,3,3,64,512]{4,3,2,1,0:T(8,128)(2,1)S(1)} %copy-done.1, s32[]{:T(128)S(6)} %select_n.126, bf16[512,1,8,1,7,2]{0,4,5,2,3,1:T(8,128)(2,1)S(1)} %slice.79, bf16[512,1,8,1,8,5]{0,4,5,2,3,1:T(8,128)(2,1)S(1)} %copy.59, pred[8,5]{0,1:T(8,128)(4,1)S(1)} %copy-done.2), kind=kOutput, calls=%fused_computation.3 | convolution fusion | flops 174411776 | bytes 1131524 | tf_op jit(solution)/shard_map/conv_general_dilated | solution.py:38
  55.1 0.0 collective-permute-done.1
  55.1 0.0 collective-permute-done
  55.2 2.0 %collective-permute-start.5 = (bf16[512,64]{0,1:T(8,128)(2,1)S(1)}, bf16[512,64]{0,1:T(8,128)(2,1)S(1)}, u32[]{:S(2)}, u32[]{:S(2)}) collective-permute-start(bf16[512,64]{0,1:T(8,128)(2,1)S(1)} %pad_maximum_fusion.1), channel_id=1, source_target_pairs={{0,1},{1,0},{2,3},{3,2},{4,5},{5,4},{6,7},{7,6},{8,9},{9,8},{10,11... | collective-permute-start | bytes 196616 | tf_op jit(solution)/shard_map/ppermute | solution.py:85
  57.2 1.1 %collective-permute-done.5 = bf16[512,64]{0,1:T(8,128)(2,1)S(1)} collective-permute-done((bf16[512,64]{0,1:T(8,128)(2,1)S(1)}, bf16[512,64]{0,1:T(8,128)(2,1)S(1)}, u32[]{:S(2)}, u32[]{:S(2)}) %collective-permute-start.5) | collective-permute-done | bytes 65568 | tf_op jit(solution)/shard_map/ppermute | solution.py:85
  58.4 0.1 copy.85
  58.5 0.1 pad.6.clone
  58.6 0.3 convolution_select_fusion.4
  59.0 0.0 copy-start
  59.0 0.1 copy.86
  59.2 0.1 pad.8.clone
  59.3 0.3 convolution_select_fusion.3
  59.7 0.0 copy-done
  59.7 0.2 multiply_maximum_fusion
  59.9 0.1 copy.78
  59.9 0.8 %copy.79 = f32[1,2,64,256]{3,2,1,0:T(8,128)} copy(f32[1,2,64,256]{2,3,1,0:T(8,128)S(1)} %bitcast.116) | data formatting | bytes 262144 | tf_op jit(solution)/shard_map/reshape | solution.py:111
  (32 shorter events, 0.6 us)
Async XLA Ops:
  23.5 26.7 %collective-permute-start.3 = (bf16[512,2,1,32]{0,3,2,1:T(8,128)(2,1)S(1)}, bf16[512,2,1,32]{0,3,2,1:T(8,128)(2,1)S(1)}, u32[]{:S(2)}, u32[]{:S(2)}) collective-permute-start(bf16[512,2,1,32]{0,3,2,1:T(8,128)(2,1)S(1)} %slice_select_fusion.1), channel_id=1, source_target_pairs={{0,8},{1,509},{2,10},{3,511},{4,12},{5,505},{6,14},{7,507},{8,16},... | collective-permute-start | bytes 196616 | tf_op jit(solution)/shard_map/ppermute | solution.py:27
  34.4 15.5 %collective-permute-start.2 = (bf16[512,1,8,32]{0,3,2,1:T(8,128)(2,1)S(1)}, bf16[512,1,8,32]{0,3,2,1:T(8,128)(2,1)S(1)}, u32[]{:S(2)}, u32[]{:S(2)}) collective-permute-start(bf16[512,1,8,32]{0,3,2,1:T(8,128)(2,1)S(1)} %slice_select_fusion), channel_id=1, source_target_pairs={{0,70},{1,455},{2,64},{3,449},{4,66},{5,451},{6,68},{7,453},{8,78}... | collective-permute-start | bytes 786440 | tf_op jit(solution)/shard_map/ppermute | solution.py:27
  36.7 1.5 %copy-start.1 = (bf16[3,3,3,64,512]{4,3,2,1,0:T(8,128)(2,1)S(1)}, bf16[3,3,3,64,512]{4,3,2,1,0:T(8,128)(2,1)}, u32[]{:S(2)}) copy-start(bf16[3,3,3,64,512]{4,3,2,1,0:T(8,128)(2,1)} %param.4) | copy-start | bytes 5308420
  36.7 1.5 %copy-start.2 = (pred[8,5]{0,1:T(8,128)(4,1)S(1)}, pred[8,5]{0,1:T(8,128)(4,1)}, u32[]{:S(2)}) copy-start(pred[8,5]{0,1:T(8,128)(4,1)} %constant.75) | copy-start | bytes 124
  43.0 12.2 %collective-permute-start.1 = (bf16[512,1,1,32]{0,3,2,1:T(8,128)(2,1)S(1)}, bf16[512,1,1,32]{0,3,2,1:T(8,128)(2,1)S(1)}, u32[]{:S(2)}, u32[]{:S(2)}) collective-permute-start(bf16[512,1,1,32]{0,3,2,1:T(8,128)(2,1)S(1)} %get-tuple-element.23), channel_id=1, source_target_pairs={{0,56},{1,461},{2,58},{3,463},{4,60},{5,457},{6,62},{7,459},{8,68}... | collective-permute-start | bytes 98312 | tf_op jit(solution)/shard_map/ppermute | solution.py:27
  44.9 10.2 %collective-permute-start = (bf16[512,1,1,32]{0,3,2,1:T(8,128)(2,1)S(1)}, bf16[512,1,1,32]{0,3,2,1:T(8,128)(2,1)S(1)}, u32[]{:S(2)}, u32[]{:S(2)}) collective-permute-start(bf16[512,1,1,32]{0,3,2,1:T(8,128)(2,1)S(1)} %get-tuple-element.24), channel_id=1, source_target_pairs={{0,76},{1,441},{2,78},{3,443},{4,72},{5,445},{6,74},{7,447},{8,84}... | collective-permute-start | bytes 98312 | tf_op jit(solution)/shard_map/ppermute | solution.py:27
  50.3 3.5 %collective-permute-start.4 = (bf16[512,320]{0,1:T(8,128)(2,1)S(1)}, bf16[512,320]{0,1:T(8,128)(2,1)S(1)}, u32[]{:S(2)}, u32[]{:S(2)}) collective-permute-start(bf16[512,320]{0,1:T(8,128)(2,1)S(1)} %pad_maximum_fusion), channel_id=1, source_target_pairs={{0,1},{1,0},{2,3},{3,2},{4,5},{5,4},{6,7},{7,6},{8,9},{9,8},{10,11... | collective-permute-start | bytes 983048 | tf_op jit(solution)/shard_map/ppermute | solution.py:75
  55.2 3.1 %collective-permute-start.5 = (bf16[512,64]{0,1:T(8,128)(2,1)S(1)}, bf16[512,64]{0,1:T(8,128)(2,1)S(1)}, u32[]{:S(2)}, u32[]{:S(2)}) collective-permute-start(bf16[512,64]{0,1:T(8,128)(2,1)S(1)} %pad_maximum_fusion.1), channel_id=1, source_target_pairs={{0,1},{1,0},{2,3},{3,2},{4,5},{5,4},{6,7},{7,6},{8,9},{9,8},{10,11... | collective-permute-start | bytes 196616 | tf_op jit(solution)/shard_map/ppermute | solution.py:85
  59.0 0.7 %copy-start = (f32[64]{0:T(128)S(1)}, f32[64]{0:T(128)}, u32[]{:S(2)}) copy-start(f32[64]{0:T(128)} %param.5) | copy-start | bytes 772
